TPU v7x, 32 devices: a whole 2x2x4 slice. The times are simulated.
32 devices in a mesh: space: 4 (over y, core), tm: 8 (over z, x).
Axes of the slice: x: 2, y: 2, z: 4, core: 2. Of those that a mesh axis runs over, the one named last changes fastest.
Arguments:
- probe_field: bfloat16 [4096, 2048], P('space', 'tm'), may hold values from -5 to 5
- kappa: float32 [4096], P('space'), may hold values from 0.1 to 1
- theta_space: float32 [32], P('tm'), may hold values from 0.3 to 1
- theta_time: float32 [32], P('tm'), may hold values from 0.2 to 0.8
- diag_blocks: bfloat16 [32, 128, 128], P('space'), may hold values from -0.05 to 1.05
- off_blocks: bfloat16 [32, 8, 128, 128], P('space'), may hold values from -0.375 to 0.375
- block_cols: int32 [32, 8], P('space'), may hold values from 0 to 11
- halo_needs: int32 [16], P('space'), may hold values from 0 to 7
- covariates: bfloat16 [65536, 256], P(('space', 'tm')), may hold values from -4 to 4
- obs_owner: int32 [65536, 1], P(('space', 'tm')), may hold values from 0 to 3; in each aligned block of 2048 rows (0 to 2047, 2048 to 4095, ...) at most 1024 rows name the same one
- obs_cell: int32 [65536], P(('space', 'tm')), may hold values from 0 to 4095
- svc_coef: bfloat16 [4096, 256], P('space'), may hold values from -0.375 to 0.375
Outputs:
- solution: float32 [4096, 2048], P('space', 'tm')
- grads: float32 [2, 2048], P(None, 'tm')
Inputs may be any that keep to these rules, and one draw needn't show every extreme that they name: `obs_owner`: in each aligned block of 2048 rows (the rows of one device) no owner is named by more than 1024 rows, a bound that some block reaches.
All inputs are finite; a program needn't handle non-finite values.
Results may differ from a plain program's by a relative error of at most 0.0021.
Values may be sent and summed in bfloat16 or wider, within the bound.
No kernel may reach another device: no remote copies, remote signals or barrier semaphores. Data moves between devices by JAX's collectives and lax.ppermute only.
A program may use at most 64 MiB of HBM per device.

v0:
```python
import jax
import jax.numpy as jnp
from jax import lax
from jax.sharding import PartitionSpec as P

NB_DEV = 8
BLOCK = 128
HALO_B = 2
T_DEV = 4
PROBES = 64
NCOV = 256
OBS_DEV = 2048
ITERS = 4
NODES_DEV = 1024


relaxation = 0.6


def with_halo(array, sides, width):
    for axis, dim in sides:
        peers, length = (lax.axis_size(axis), array.shape[dim])
        up = [(i, (i + 1) % peers) for i in range(peers - 1)]
        down = [(j, i) for i, j in up]
        last = lax.slice_in_dim(array, length - width, length, axis=dim)
        initial = lax.slice_in_dim(array, 0, width, axis=dim)
        before = lax.ppermute(last, axis, up)
        after = lax.ppermute(initial, axis, down)
        array = jnp.concatenate([before, array, after], axis=dim)
    return array


def shards(
    probe_field,
    kappa,
    theta_space,
    theta_time,
    diag_blocks,
    off_blocks,
    block_cols,
    halo_needs,
    covariates,
    obs_owner,
    obs_cell,
    svc_coef,
):
    space_count = lax.axis_size("space")
    columns = probe_field.shape[1]
    width_local = NB_DEV + 2 * HALO_B
    probe_vals = probe_field.astype(jnp.float32)
    sdiag = jnp.diagonal(diag_blocks, axis1=1, axis2=2).astype(jnp.float32).reshape(NODES_DEV)
    scale_space = jnp.repeat(theta_space, PROBES)[None, :]
    scale_time = jnp.repeat(theta_time, PROBES)[None, :]
    base_diag = scale_space * sdiag[:, None] + 2.0 * scale_time + kappa[:, None]
    local_ids = jnp.arange(width_local, dtype=jnp.int32)
    picks = (block_cols[:, :, None] == local_ids[None, None, :]).astype(jnp.float32)
    own_pick = (jnp.arange(NB_DEV, dtype=jnp.int32)[:, None] == local_ids[None, :]).astype(
        jnp.float32
    )
    combined = jnp.einsum("bkm,bkij->bimj", picks, off_blocks.astype(jnp.float32))
    combined = combined + jnp.einsum("bm,bij->bimj", own_pick, diag_blocks.astype(jnp.float32))
    combined = combined.astype(jnp.bfloat16).reshape(NODES_DEV, width_local * BLOCK)
    own_part = combined[:, :NODES_DEV]
    lower_part = combined[:, NODES_DEV : NODES_DEV + HALO_B * BLOCK]
    upper_part = combined[:, NODES_DEV + HALO_B * BLOCK :]

    def spatial(field):
        arrived = with_halo(field, (("space", 0),), NODES_DEV)
        lower = (
            arrived[:NODES_DEV]
            .reshape(NB_DEV, BLOCK, columns)[halo_needs[:HALO_B]]
            .reshape(HALO_B * BLOCK, columns)
        )
        upper = (
            arrived[2 * NODES_DEV :]
            .reshape(NB_DEV, BLOCK, columns)[halo_needs[HALO_B:]]
            .reshape(HALO_B * BLOCK, columns)
        )
        total = jnp.dot(own_part, field, preferred_element_type=jnp.float32)
        total = total + jnp.dot(lower_part, lower, preferred_element_type=jnp.float32)
        total = total + jnp.dot(upper_part, upper, preferred_element_type=jnp.float32)
        return total

    def temporal(field):
        arrived = with_halo(field, (("tm", 1),), PROBES)
        return (
            2.0 * field.astype(jnp.float32)
            - arrived[:, :columns].astype(jnp.float32)
            - arrived[:, 2 * PROBES :].astype(jnp.float32)
        )

    solution = relaxation * probe_vals / base_diag
    rounded = lax.optimization_barrier(solution.astype(jnp.bfloat16))
    first_space = spatial(rounded)
    first_time = temporal(rounded)
    capacity = 2 * OBS_DEV // space_count
    owner = obs_owner[:, 0]
    hits = (owner[:, None] == jnp.arange(space_count, dtype=jnp.int32)[None, :]).astype(jnp.int32)
    earlier = jnp.cumsum(hits, axis=0) - hits
    rank = jnp.sum(earlier * hits, axis=1)
    slot = owner * capacity + rank
    send_rows = jnp.zeros((space_count * capacity, NCOV), jnp.bfloat16).at[slot].set(covariates)
    send_cells = jnp.full((space_count * capacity,), -1, jnp.int32).at[slot].set(obs_cell)
    recv_rows, recv_cells = (
        lax.all_to_all(send_rows, "space", split_axis=0, concat_axis=0, tiled=True),
        lax.all_to_all(send_cells, "space", split_axis=0, concat_axis=0, tiled=True),
    )
    live = recv_cells >= 0
    cell_ids = jnp.where(live, recv_cells, 0)
    coef_rows = svc_coef[cell_ids // T_DEV]
    eta = jnp.einsum("rc,rc->r", recv_rows, coef_rows, preferred_element_type=jnp.float32)
    obs_weight = jnp.where(live, jnp.exp(eta), 0.0)
    counted = jax.ops.segment_sum(obs_weight, cell_ids, num_segments=NODES_DEV * T_DEV)
    obs_diag = jnp.repeat(counted.reshape(NODES_DEV, T_DEV), PROBES, axis=1)
    full_diag = base_diag + obs_diag
    local_diag = kappa[:, None] + obs_diag
    applied = (
        scale_space * first_space
        + scale_time * first_time
        + local_diag * rounded.astype(jnp.float32)
    )
    solution = solution + relaxation * (probe_vals - applied) / full_diag
    for sweep in range(ITERS - 1):
        rounded = lax.optimization_barrier(solution.astype(jnp.bfloat16))
        applied = (
            scale_space * spatial(rounded)
            + scale_time * temporal(rounded)
            + local_diag * rounded.astype(jnp.float32)
        )
        solution = solution + relaxation * (probe_vals - applied) / full_diag
    rounded = solution.astype(jnp.bfloat16)
    partial_sums = jnp.stack(
        [
            jnp.sum(probe_vals * spatial(rounded), axis=0),
            jnp.sum(probe_vals * temporal(rounded), axis=0),
        ]
    )
    totals = lax.psum(partial_sums, "space")
    grads = totals / (NODES_DEV * space_count)
    return (solution, grads)


def solution(mesh):
    return jax.shard_map(
        shards,
        mesh=mesh,
        in_specs=(
            P("space", "tm"),
            P("space"),
            P("tm"),
            P("tm"),
            P("space", None, None),
            P("space", None, None, None),
            P("space", None),
            P("space"),
            P(("space", "tm"), None),
            P(("space", "tm"), None),
            P(("space", "tm")),
            P("space", None),
        ),
        out_specs=(P("space", "tm"), P(None, "tm")),
        check_vma=False,
    )
```

profile of v0, /device:TPU:0, one launch (start us, length us, event | category | flops | bytes accessed | tf_op | source)
XLA Modules:
  0.0 245.6 jit_solution(10058885374834791966)
XLA Ops:
  3.0 1.2 copy.41
  4.3 4.4 %copy.42 = bf16[8,128,128]{0,2,1:T(8,128)(2,1)} copy(bf16[8,128,128]{2,1,0:T(8,128)(2,1)} %param.16) | data formatting | bytes 524288 | tf_op args[4]
  8.7 1.9 gather_fusion
  11.9 1.3 collective-permute-start.1
  13.2 3.9 %collective-permute-start = (bf16[1024,256]{0,1:T(8,128)(2,1)}, bf16[1024,256]{0,1:T(8,128)(2,1)}, u32[]{:S(2)}, u32[]{:S(2)}) collective-permute-start(bf16[1024,256]{0,1:T(8,128)(2,1)} %fusion.57), channel_id=1, source_target_pairs={{0,8},{8,16},{16,24},{1,9},{9,17},{17,25},{2,10},{10,18},{18,26},{... | collective-permute-start | bytes 1572872 | tf_op jit(solution)/shard_map/ppermute | solution.py:27
  18.8 8.8 %scatter_custom_fusion = s32[4096]{0:T(1024)} fusion(s32[2048]{0:T(1024)S(1)} %bitcast.146, s32[2048]{0:T(1024)} %param.22, s32[]{:T(128)} %constant.23.clone.1), kind=kCustom, calls=%fused_computation.143 | custom fusion | bytes 16896 | tf_op jit(solution)/shard_map/scatter | solution.py:103
  27.6 4.3 %all-to-all-start = ((s32[4,1024,1]{1,2,0:T(1,128)}), s32[4,1024,1]{1,2,0:T(1,128)S(1)}, u32[]{:S(2)}, u32[]{:S(2)}) async-start(s32[4,1024,1]{1,2,0:T(1,128)} %bitcast.15), calls=%async_computation | async-start | bytes 32768 | tf_op jit(solution)/shard_map/all_to_all | solution.py:106
  31.8 1.6 fusion.84
  33.5 4.5 %collective-permute-start.2 = (bf16[1024,64]{0,1:T(8,128)(2,1)}, bf16[1024,64]{0,1:T(8,128)(2,1)}, u32[]{:S(2)}, u32[]{:S(2)}) collective-permute-start(bf16[1024,64]{0,1:T(8,128)(2,1)} %get-tuple-element.16), channel_id=1, source_target_pairs={{0,1},{1,2},{2,3},{3,4},{4,5},{5,6},{6,7},{8,9},{9,10},{10,11},{11... | collective-permute-start | bytes 393224 | tf_op jit(solution)/shard_map/ppermute | solution.py:27
  38.0 1.3 collective-permute-start.3
  39.4 2.2 add_convert_fusion
  41.6 1.6 copy.93
  43.3 3.2 %fusion.37 = f32[1024,256]{0,1:T(8,128)} fusion(bf16[1024,256]{0,1:T(8,128)(2,1)} %fusion.57, bf16[1024,1536]{1,0:T(8,128)(2,1)S(1)} %bitcast.100), kind=kOutput, calls=%fused_computation.78 | convolution fusion | flops 536870912 | bytes 3670016 | tf_op jit(solution)/shard_map/dot_general | solution.py:79
  46.4 11.3 %scatter_custom_fusion.1 = bf16[4096,256]{1,0:T(8,128)(2,1)} fusion(s32[2048]{0:T(1024)S(1)} %bitcast.147, bf16[2048,256]{1,0:T(8,128)(2,1)} %param.20, bf16[]{:T(256)} %constant.45.clone.1), kind=kCustom, calls=%fused_computation.96 | custom fusion | bytes 2097664 | tf_op jit(solution)/shard_map/scatter | solution.py:102
  57.7 4.6 %all-to-all-start.1 = ((bf16[4,1024,256]{2,1,0:T(8,128)(2,1)}), bf16[4,1024,256]{2,1,0:T(8,128)(2,1)}, u32[]{:S(2)}, u32[]{:S(2)}) async-start(bf16[4,1024,256]{2,1,0:T(8,128)(2,1)} %bitcast.115), calls=%async_computation.1 | async-start | bytes 4194304 | tf_op jit(solution)/shard_map/all_to_all | solution.py:105
  63.1 17.0 %gather_fusion.3 = bf16[4096,256]{1,0:T(8,128)(2,1)} fusion(bf16[1024,256]{1,0:T(8,128)(2,1)S(1)} %copy-done.1, s32[4096]{0:T(1024)S(1)} %broadcast_clamp_fusion), kind=kCustom, calls=%fused_computation.3 | custom fusion | bytes 4210688 | tf_op jit(solution)/shard_map/gather | solution.py:110
  82.6 1.2 copy.71
  84.6 2.7 %convolution_add_fusion.9 = f32[1024,256]{0,1:T(8,128)} fusion(f32[1024,256]{0,1:T(8,128)} %fusion.37, bf16[256,256]{1,0:T(8,128)(2,1)S(1)} %bitcast.128, bf16[1024,1536]{1,0:T(8,128)(2,1)} %bitcast.101), kind=kOutput, calls=%fused_computation.54 | convolution fusion | flops 134479872 | bytes 2752512 | tf_op jit(solution)/shard_map/dot_general | solution.py:80
  87.9 2.9 %fusion = f32[4096]{0:T(1024)S(1)} fusion(bf16[4096,256]{1,0:T(8,128)(2,1)} %gather_fusion.3, bf16[4,1024,256]{2,1,0:T(8,128)(2,1)} %all-to-all-done.1), kind=kLoop, calls=%fused_computation.17 | loop fusion | flops 4190208 | bytes 4210688 | tf_op jit(solution)/shard_map/rc,rc->r/dot_general | solution.py:111
  90.8 25.3 %scatter_custom_fusion.2 = f32[4096]{0:T(1024)S(1)} fusion(s32[4096]{0:T(1024)S(1)} %bitcast.144, f32[4096]{0:T(1024)S(1)} %exponential_select_fusion, f32[]{:T(128)} %constant.21.clone.1), kind=kCustom, calls=%fused_computation.145 | custom fusion | flops 4096 | bytes 16388 | tf_op jit(solution)/shard_map/scatter-add | solution.py:113
  116.8 1.4 fusion.5
  118.3 4.2 %fusion.85 = (bf16[1024,256]{0,1:T(8,128)(2,1)S(1)}, f32[1024,256]{0,1:T(8,128)}) fusion(f32[1024,256]{0,1:T(8,128)S(1)} %get-tuple-element.19, f32[1024,256]{0,1:T(8,128)S(1)} %get-tuple-element.18, bf16[1024,64]{0,1:T(8,128)(2,1)} %collective-permute-done.3, bf16[1024,256]{0,1:T(8,128)(2,1)} %fusion.57, bf16[1024,64]{0,1:T(8,128)(2,1)} %collective-permute-done.2, ...), kind=kOutput, calls=%fused_computation.162 | convolution fusion | flops 141557760 | bytes 6695936 | tf_op jit(solution)/shard_map/dot_general | solution.py:81
  122.5 1.3 collective-permute-start.5
  123.8 4.5 %collective-permute-start.4 = (bf16[1024,256]{0,1:T(8,128)(2,1)S(1)}, bf16[1024,256]{0,1:T(8,128)(2,1)}, u32[]{:S(2)}, u32[]{:S(2)}) collective-permute-start(bf16[1024,256]{0,1:T(8,128)(2,1)S(1)} %get-tuple-element.24), channel_id=1, source_target_pairs={{0,8},{8,16},{16,24},{1,9},{9,17},{17,25},{2,10},{10,18},{18,26},{... | collective-permute-start | bytes 1572872 | tf_op jit(solution)/shard_map/ppermute | solution.py:27
  129.4 5.2 %collective-permute-start.6 = (bf16[1024,64]{0,1:T(8,128)(2,1)S(1)}, bf16[1024,64]{0,1:T(8,128)(2,1)}, u32[]{:S(2)}, u32[]{:S(2)}) collective-permute-start(bf16[1024,64]{0,1:T(8,128)(2,1)S(1)} %get-tuple-element.14), channel_id=1, source_target_pairs={{0,1},{1,2},{2,3},{3,4},{4,5},{5,6},{6,7},{8,9},{9,10},{10,11},{11... | collective-permute-start | bytes 393224 | tf_op jit(solution)/shard_map/ppermute | solution.py:27
  134.6 1.3 collective-permute-start.7
  135.9 1.7 fusion.35
  137.6 2.1 copy.74
  139.7 1.7 gather_fusion.4
  141.4 2.7 %convolution_add_fusion.7 = f32[1024,256]{0,1:T(8,128)} fusion(f32[1024,256]{0,1:T(8,128)} %fusion.35, bf16[256,256]{1,0:T(8,128)(2,1)S(1)} %bitcast.129, bf16[1024,1536]{1,0:T(8,128)(2,1)} %bitcast.103), kind=kOutput, calls=%fused_computation.49 | convolution fusion | flops 134479872 | bytes 2752512 | tf_op jit(solution)/shard_map/dot_general | solution.py:80
  144.2 2.0 copy.75
  146.2 1.7 gather_fusion.5
  148.0 4.4 %fusion.86 = (bf16[1024,256]{0,1:T(8,128)(2,1)}, f32[1024,256]{0,1:T(8,128)}) fusion(f32[1024,256]{0,1:T(8,128)} %get-tuple-element.25, f32[1024,256]{0,1:T(8,128)} %copy-done.8, f32[1024,256]{0,1:T(8,128)} %fusion.4, bf16[1024,64]{0,1:T(8,128)(2,1)} %collective-permute-done.7, bf16[1024,256]{0,1:T(8,128)(2,1)S(1)} %get-tuple-element.24, ...), kind=kOutput, calls=%fused_computation.163 | convolution fusion | flops 140247040 | bytes 7735296 | tf_op jit(solution)/shard_map/dot_general | solution.py:81
  152.4 1.3 collective-permute-start.9
  153.7 4.0 %collective-permute-start.8 = (bf16[1024,256]{0,1:T(8,128)(2,1)}, bf16[1024,256]{0,1:T(8,128)(2,1)}, u32[]{:S(2)}, u32[]{:S(2)}) collective-permute-start(bf16[1024,256]{0,1:T(8,128)(2,1)} %get-tuple-element.26), channel_id=1, source_target_pairs={{0,8},{8,16},{16,24},{1,9},{9,17},{17,25},{2,10},{10,18},{18,26},{... | collective-permute-start | bytes 1572872 | tf_op jit(solution)/shard_map/ppermute | solution.py:27
  157.7 2.2 fusion.3
  160.9 5.0 %collective-permute-start.10 = (bf16[1024,64]{0,1:T(8,128)(2,1)S(1)}, bf16[1024,64]{0,1:T(8,128)(2,1)}, u32[]{:S(2)}, u32[]{:S(2)}) collective-permute-start(bf16[1024,64]{0,1:T(8,128)(2,1)S(1)} %get-tuple-element.12), channel_id=1, source_target_pairs={{0,1},{1,2},{2,3},{3,4},{4,5},{5,6},{6,7},{8,9},{9,10},{10,11},{11... | collective-permute-start | bytes 393224 | tf_op jit(solution)/shard_map/ppermute | solution.py:27
  165.9 1.3 collective-permute-start.11
  167.2 2.8 %fusion.33 = f32[1024,256]{0,1:T(8,128)} fusion(bf16[1024,256]{0,1:T(8,128)(2,1)} %get-tuple-element.26, bf16[1024,1536]{1,0:T(8,128)(2,1)S(1)} %bitcast.112), kind=kOutput, calls=%fused_computation.74 | convolution fusion | flops 536870912 | bytes 3670016 | tf_op jit(solution)/shard_map/dot_general | solution.py:79
  171.9 2.7 %convolution_add_fusion.5 = f32[1024,256]{0,1:T(8,128)} fusion(f32[1024,256]{0,1:T(8,128)} %fusion.33, bf16[256,256]{1,0:T(8,128)(2,1)S(1)} %bitcast.130, bf16[1024,1536]{1,0:T(8,128)(2,1)} %bitcast.105), kind=kOutput, calls=%fused_computation.44 | convolution fusion | flops 134479872 | bytes 2752512 | tf_op jit(solution)/shard_map/dot_general | solution.py:80
  176.6 4.7 %fusion.87 = (bf16[1024,256]{0,1:T(8,128)(2,1)S(1)}, f32[1024,256]{0,1:T(8,128)}) fusion(f32[1024,256]{0,1:T(8,128)} %get-tuple-element.27, f32[1024,256]{0,1:T(8,128)} %copy-done.8, f32[1024,256]{0,1:T(8,128)} %fusion.3, bf16[1024,64]{0,1:T(8,128)(2,1)} %collective-permute-done.11, bf16[1024,256]{0,1:T(8,128)(2,1)} %get-tuple-element.26, ...), kind=kOutput, calls=%fused_computation.164 | convolution fusion | flops 140247040 | bytes 7735296 | tf_op jit(solution)/shard_map/dot_general | solution.py:81
  181.3 1.3 collective-permute-start.13
  182.6 3.9 %collective-permute-start.12 = (bf16[1024,256]{0,1:T(8,128)(2,1)S(1)}, bf16[1024,256]{0,1:T(8,128)(2,1)}, u32[]{:S(2)}, u32[]{:S(2)}) collective-permute-start(bf16[1024,256]{0,1:T(8,128)(2,1)S(1)} %get-tuple-element.28), channel_id=1, source_target_pairs={{0,8},{8,16},{16,24},{1,9},{9,17},{17,25},{2,10},{10,18},{18,26},{... | collective-permute-start | bytes 1572872 | tf_op jit(solution)/shard_map/ppermute | solution.py:27
  187.7 5.2 %collective-permute-start.14 = (bf16[1024,64]{0,1:T(8,128)(2,1)S(1)}, bf16[1024,64]{0,1:T(8,128)(2,1)}, u32[]{:S(2)}, u32[]{:S(2)}) collective-permute-start(bf16[1024,64]{0,1:T(8,128)(2,1)S(1)} %get-tuple-element.10), channel_id=1, source_target_pairs={{0,1},{1,2},{2,3},{3,4},{4,5},{5,6},{6,7},{8,9},{9,10},{10,11},{11... | collective-permute-start | bytes 393224 | tf_op jit(solution)/shard_map/ppermute | solution.py:27
  192.8 1.5 collective-permute-start.15
  194.3 1.7 fusion.31
  196.1 2.1 copy.78
  198.1 1.7 gather_fusion.8
  199.9 2.7 %convolution_add_fusion.3 = f32[1024,256]{0,1:T(8,128)} fusion(f32[1024,256]{0,1:T(8,128)} %fusion.31, bf16[256,256]{1,0:T(8,128)(2,1)S(1)} %bitcast.131, bf16[1024,1536]{1,0:T(8,128)(2,1)} %bitcast.107), kind=kOutput, calls=%fused_computation.39 | convolution fusion | flops 134479872 | bytes 2752512 | tf_op jit(solution)/shard_map/dot_general | solution.py:80
  202.6 2.0 copy.79
  204.6 1.7 gather_fusion.9
  206.4 4.5 %fusion.88 = (bf16[1024,256]{0,1:T(8,128)(2,1)}, f32[1024,256]{0,1:T(8,128)}) fusion(f32[1024,256]{0,1:T(8,128)} %get-tuple-element.29, f32[1024,256]{0,1:T(8,128)} %copy-done.8, f32[1024,256]{0,1:T(8,128)} %fusion.2, bf16[1024,64]{0,1:T(8,128)(2,1)} %collective-permute-done.15, bf16[1024,256]{0,1:T(8,128)(2,1)S(1)} %get-tuple-element.28, ...), kind=kOutput, calls=%fused_computation.165 | convolution fusion | flops 140247040 | bytes 7735296 | tf_op jit(solution)/shard_map/dot_general | solution.py:81
  211.9 1.3 collective-permute-start.17
  213.2 3.8 %collective-permute-start.16 = (bf16[1024,256]{0,1:T(8,128)(2,1)}, bf16[1024,256]{0,1:T(8,128)(2,1)}, u32[]{:S(2)}, u32[]{:S(2)}) collective-permute-start(bf16[1024,256]{0,1:T(8,128)(2,1)} %get-tuple-element.30), channel_id=1, source_target_pairs={{0,8},{8,16},{16,24},{1,9},{9,17},{17,25},{2,10},{10,18},{18,26},{... | collective-permute-start | bytes 1572872 | tf_op jit(solution)/shard_map/ppermute | solution.py:27
  217.0 4.5 %collective-permute-start.18 = (bf16[1024,64]{0,1:T(8,128)(2,1)S(1)}, bf16[1024,64]{0,1:T(8,128)(2,1)S(1)}, u32[]{:S(2)}, u32[]{:S(2)}) collective-permute-start(bf16[1024,64]{0,1:T(8,128)(2,1)S(1)} %get-tuple-element.8), channel_id=1, source_target_pairs={{0,1},{1,2},{2,3},{3,4},{4,5},{5,6},{6,7},{8,9},{9,10},{10,11},{11... | collective-permute-start | bytes 393224 | tf_op jit(solution)/shard_map/ppermute | solution.py:27
  221.6 1.3 collective-permute-start.19
  222.9 2.7 %fusion.39 = f32[1024,256]{0,1:T(8,128)} fusion(bf16[1024,256]{0,1:T(8,128)(2,1)} %get-tuple-element.30, bf16[1024,1536]{1,0:T(8,128)(2,1)S(1)} %bitcast.114), kind=kOutput, calls=%fused_computation.80 | convolution fusion | flops 536870912 | bytes 3670016 | tf_op jit(solution)/shard_map/dot_general | solution.py:79
  225.6 2.5 %copy.61 = f32[1024,256]{1,0:T(8,128)} copy(f32[1024,256]{0,1:T(8,128)} %get-tuple-element.31) | data formatting | bytes 2097152
  228.2 2.1 collective-permute-done.19
  230.3 1.9 fusion.54
  232.2 1.2 copy.81
  236.0 1.7 convolution_add_fusion.1
  237.8 1.5 fusion.30
  239.3 5.8 %psum.7 = f32[2,256]{1,0:T(2,128)S(1)} all-reduce(f32[2,256]{1,0:T(2,128)S(1)} %pad_maximum_fusion.10), channel_id=1, replica_groups=mesh['space'=4,'tm'=8] {'space'}, use_global_device_ids=true, to_apply=%region_8.9 | all-reduce | flops 512 | bytes 4096 | tf_op jit(solution)/shard_map/psum | solution.py:138
  (122 shorter events, 22.0 us)
Async XLA Ops:
  0.6 38.8 %copy-start = (bf16[8,8,128,128]{3,2,1,0:T(8,128)(2,1)S(1)}, bf16[8,8,128,128]{3,2,1,0:T(8,128)(2,1)}, u32[]{:S(2)}) copy-start(bf16[8,8,128,128]{3,2,1,0:T(8,128)(2,1)} %param.17) | copy-start | bytes 6291460
  0.6 10.0 %copy-start.9 = (f32[1024]{0:T(1024)S(1)}, f32[1024]{0:T(1024)}, u32[]{:S(2)}) copy-start(f32[1024]{0:T(1024)} %param.13) | copy-start | bytes 12292
  1.6 10.3 %copy-start.18 = (f32[256]{0:T(256)}, f32[256]{0:T(256)S(1)}, u32[]{:S(2)}) copy-start(f32[256]{0:T(256)S(1)} %mul.135) | copy-start | bytes 3076
  2.4 0.5 copy-start.23
  3.0 8.9 %copy-start.21 = (f32[256]{0:T(256)}, f32[256]{0:T(256)S(1)}, u32[]{:S(2)}) copy-start(f32[256]{0:T(256)S(1)} %broadcast_multiply_fusion.1) | copy-start | bytes 3076
  4.2 12.8 %copy-start.13 = (s32[2048,1]{0,1:T(1,128)S(1)}, s32[2048,1]{0,1:T(1,128)}, u32[]{:S(2)}) copy-start(s32[2048,1]{0,1:T(1,128)} %param.21) | copy-start | bytes 24580
  4.2 35.0 %copy-start.7 = (bf16[8,128,128]{2,1,0:T(8,128)(2,1)S(1)}, bf16[8,128,128]{2,1,0:T(8,128)(2,1)}, u32[]{:S(2)}) copy-start(bf16[8,128,128]{2,1,0:T(8,128)(2,1)} %param.16) | copy-start | bytes 786436
  4.3 35.1 %copy-start.27 = (s32[4]{0:T(128)S(1)}, s32[4]{0:T(128)}, u32[]{:S(2)}) copy-start(s32[4]{0:T(128)} %param.19) | copy-start | bytes 52
  4.3 35.1 %copy-start.26 = (s32[8,8]{1,0:T(8,128)S(1)}, s32[8,8]{1,0:T(8,128)}, u32[]{:S(2)}) copy-start(s32[8,8]{1,0:T(8,128)} %param.18) | copy-start | bytes 772
  10.7 31.0 %copy-start.14 = (f32[8,128]{1,0:T(8,128)}, f32[8,128]{1,0:T(8,128)S(1)}, u32[]{:S(2)}) copy-start(f32[8,128]{1,0:T(8,128)S(1)} %copy.43) | copy-start | bytes 12292
  11.9 68.9 %collective-permute-start.1 = (bf16[1024,256]{0,1:T(8,128)(2,1)}, bf16[1024,256]{0,1:T(8,128)(2,1)}, u32[]{:S(2)}, u32[]{:S(2)}) collective-permute-start(bf16[1024,256]{0,1:T(8,128)(2,1)} %fusion.57), channel_id=1, source_target_pairs={{8,0},{16,8},{24,16},{9,1},{17,9},{25,17},{10,2},{18,10},{26,18},{... | collective-permute-start | bytes 1572872 | tf_op jit(solution)/shard_map/ppermute | solution.py:28
  13.2 69.4 %collective-permute-start = (bf16[1024,256]{0,1:T(8,128)(2,1)}, bf16[1024,256]{0,1:T(8,128)(2,1)}, u32[]{:S(2)}, u32[]{:S(2)}) collective-permute-start(bf16[1024,256]{0,1:T(8,128)(2,1)} %fusion.57), channel_id=1, source_target_pairs={{0,8},{8,16},{16,24},{1,9},{9,17},{17,25},{2,10},{10,18},{18,26},{... | collective-permute-start | bytes 1572872 | tf_op jit(solution)/shard_map/ppermute | solution.py:27
  27.6 30.2 %all-to-all-start = ((s32[4,1024,1]{1,2,0:T(1,128)}), s32[4,1024,1]{1,2,0:T(1,128)S(1)}, u32[]{:S(2)}, u32[]{:S(2)}) async-start(s32[4,1024,1]{1,2,0:T(1,128)} %bitcast.15), calls=%async_computation | async-start | bytes 32768 | tf_op jit(solution)/shard_map/all_to_all | solution.py:106
  33.5 84.8 %collective-permute-start.2 = (bf16[1024,64]{0,1:T(8,128)(2,1)}, bf16[1024,64]{0,1:T(8,128)(2,1)}, u32[]{:S(2)}, u32[]{:S(2)}) collective-permute-start(bf16[1024,64]{0,1:T(8,128)(2,1)} %get-tuple-element.16), channel_id=1, source_target_pairs={{0,1},{1,2},{2,3},{3,4},{4,5},{5,6},{6,7},{8,9},{9,10},{10,11},{11... | collective-permute-start | bytes 393224 | tf_op jit(solution)/shard_map/ppermute | solution.py:27
  38.0 80.3 %collective-permute-start.3 = (bf16[1024,64]{0,1:T(8,128)(2,1)S(1)}, bf16[1024,64]{0,1:T(8,128)(2,1)}, u32[]{:S(2)}, u32[]{:S(2)}) collective-permute-start(bf16[1024,64]{0,1:T(8,128)(2,1)S(1)} %get-tuple-element.17), channel_id=1, source_target_pairs={{1,0},{2,1},{3,2},{4,3},{5,4},{6,5},{7,6},{9,8},{10,9},{11,10},{12... | collective-permute-start | bytes 393224 | tf_op jit(solution)/shard_map/ppermute | solution.py:28
  43.2 3.2 %copy-start.2 = (bf16[128,8,12,128]{3,1,2,0:T(8,128)(2,1)}, bf16[128,8,12,128]{3,1,2,0:T(8,128)(2,1)S(1)}, u32[]{:S(2)}) copy-start(bf16[128,8,12,128]{3,1,2,0:T(8,128)(2,1)S(1)} %copy.93) | copy-start | bytes 9437188
  46.4 35.6 %copy-start.17 = (s32[1024]{0:T(1024)}, s32[1024]{0:T(1024)S(1)}, u32[]{:S(2)}) copy-start(s32[1024]{0:T(1024)S(1)} %pad_clamp_fusion) | copy-start | bytes 12292
  46.4 16.7 %copy-start.1 = (bf16[1024,256]{1,0:T(8,128)(2,1)S(1)}, bf16[1024,256]{1,0:T(8,128)(2,1)}, u32[]{:S(2)}) copy-start(bf16[1024,256]{1,0:T(8,128)(2,1)} %param.23) | copy-start | bytes 1572868
  57.7 30.2 %all-to-all-start.1 = ((bf16[4,1024,256]{2,1,0:T(8,128)(2,1)}), bf16[4,1024,256]{2,1,0:T(8,128)(2,1)}, u32[]{:S(2)}, u32[]{:S(2)}) async-start(bf16[4,1024,256]{2,1,0:T(8,128)(2,1)} %bitcast.115), calls=%async_computation.1 | async-start | bytes 4194304 | tf_op jit(solution)/shard_map/all_to_all | solution.py:105
  84.5 6.2 %copy-start.16 = (pred[4,1024]{1,0:T(4,128)(4,1)S(1)}, pred[4,1024]{1,0:T(4,128)(4,1)}, u32[]{:S(2)}) copy-start(pred[4,1024]{1,0:T(4,128)(4,1)} %compare_reduce_fusion) | copy-start | bytes 12292
  87.3 29.5 %copy-start.10 = (f32[1024]{0:T(1024)S(1)}, f32[1024]{0:T(1024)}, u32[]{:S(2)}) copy-start(f32[1024]{0:T(1024)} %param.13) | copy-start | bytes 12292
  87.3 29.5 %copy-start.15 = (f32[8,128]{1,0:T(8,128)S(1)}, f32[8,128]{1,0:T(8,128)}, u32[]{:S(2)}) copy-start(f32[8,128]{1,0:T(8,128)} %copy-done.14) | copy-start | bytes 12292
  87.3 29.5 %copy-start.19 = (f32[256]{0:T(256)S(1)}, f32[256]{0:T(256)}, u32[]{:S(2)}) copy-start(f32[256]{0:T(256)} %copy-done.18) | copy-start | bytes 3076
  87.3 29.5 %copy-start.22 = (f32[256]{0:T(256)S(1)}, f32[256]{0:T(256)}, u32[]{:S(2)}) copy-start(f32[256]{0:T(256)} %copy-done.21) | copy-start | bytes 3076
  87.3 31.0 %copy-start.24 = (f32[256]{0:T(256)S(1)}, f32[256]{0:T(256)}, u32[]{:S(2)}) copy-start(f32[256]{0:T(256)} %copy-done.23) | copy-start | bytes 3076
  118.2 4.3 %copy-start.8 = (f32[1024,256]{0,1:T(8,128)}, f32[1024,256]{0,1:T(8,128)S(1)}, u32[]{:S(2)}) copy-start(f32[1024,256]{0,1:T(8,128)S(1)} %get-tuple-element.19) | copy-start | bytes 3145732
  118.3 17.7 %copy-start.3 = (bf16[128,8,12,128]{3,1,2,0:T(8,128)(2,1)S(1)}, bf16[128,8,12,128]{3,1,2,0:T(8,128)(2,1)}, u32[]{:S(2)}) copy-start(bf16[128,8,12,128]{3,1,2,0:T(8,128)(2,1)} %copy-done.2) | copy-start | bytes 9437188
  122.5 21.6 %collective-permute-start.5 = (bf16[1024,256]{0,1:T(8,128)(2,1)S(1)}, bf16[1024,256]{0,1:T(8,128)(2,1)}, u32[]{:S(2)}, u32[]{:S(2)}) collective-permute-start(bf16[1024,256]{0,1:T(8,128)(2,1)S(1)} %get-tuple-element.24), channel_id=1, source_target_pairs={{8,0},{16,8},{24,16},{9,1},{17,9},{25,17},{10,2},{18,10},{26,18},{... | collective-permute-start | bytes 1572872 | tf_op jit(solution)/shard_map/ppermute | solution.py:28
  123.8 13.8 %collective-permute-start.4 = (bf16[1024,256]{0,1:T(8,128)(2,1)S(1)}, bf16[1024,256]{0,1:T(8,128)(2,1)}, u32[]{:S(2)}, u32[]{:S(2)}) collective-permute-start(bf16[1024,256]{0,1:T(8,128)(2,1)S(1)} %get-tuple-element.24), channel_id=1, source_target_pairs={{0,8},{8,16},{16,24},{1,9},{9,17},{17,25},{2,10},{10,18},{18,26},{... | collective-permute-start | bytes 1572872 | tf_op jit(solution)/shard_map/ppermute | solution.py:27
  129.4 18.5 %collective-permute-start.6 = (bf16[1024,64]{0,1:T(8,128)(2,1)S(1)}, bf16[1024,64]{0,1:T(8,128)(2,1)}, u32[]{:S(2)}, u32[]{:S(2)}) collective-permute-start(bf16[1024,64]{0,1:T(8,128)(2,1)S(1)} %get-tuple-element.14), channel_id=1, source_target_pairs={{0,1},{1,2},{2,3},{3,4},{4,5},{5,6},{6,7},{8,9},{9,10},{10,11},{11... | collective-permute-start | bytes 393224 | tf_op jit(solution)/shard_map/ppermute | solution.py:27
  134.6 13.3 %collective-permute-start.7 = (bf16[1024,64]{0,1:T(8,128)(2,1)S(1)}, bf16[1024,64]{0,1:T(8,128)(2,1)}, u32[]{:S(2)}, u32[]{:S(2)}) collective-permute-start(bf16[1024,64]{0,1:T(8,128)(2,1)S(1)} %get-tuple-element.15), channel_id=1, source_target_pairs={{1,0},{2,1},{3,2},{4,3},{5,4},{6,5},{7,6},{9,8},{10,9},{11,10},{12... | collective-permute-start | bytes 393224 | tf_op jit(solution)/shard_map/ppermute | solution.py:28
  147.9 9.8 %copy-start.11 = (f32[1024]{0:T(1024)S(1)}, f32[1024]{0:T(1024)}, u32[]{:S(2)}) copy-start(f32[1024]{0:T(1024)} %param.13) | copy-start | bytes 12292
  148.0 19.3 %copy-start.4 = (bf16[128,8,12,128]{3,1,2,0:T(8,128)(2,1)S(1)}, bf16[128,8,12,128]{3,1,2,0:T(8,128)(2,1)}, u32[]{:S(2)}) copy-start(bf16[128,8,12,128]{3,1,2,0:T(8,128)(2,1)} %copy-done.2) | copy-start | bytes 9437188
  152.4 22.3 %collective-permute-start.9 = (bf16[1024,256]{0,1:T(8,128)(2,1)}, bf16[1024,256]{0,1:T(8,128)(2,1)}, u32[]{:S(2)}, u32[]{:S(2)}) collective-permute-start(bf16[1024,256]{0,1:T(8,128)(2,1)} %get-tuple-element.26), channel_id=1, source_target_pairs={{8,0},{16,8},{24,16},{9,1},{17,9},{25,17},{10,2},{18,10},{26,18},{... | collective-permute-start | bytes 1572872 | tf_op jit(solution)/shard_map/ppermute | solution.py:28
  153.7 16.3 %collective-permute-start.8 = (bf16[1024,256]{0,1:T(8,128)(2,1)}, bf16[1024,256]{0,1:T(8,128)(2,1)}, u32[]{:S(2)}, u32[]{:S(2)}) collective-permute-start(bf16[1024,256]{0,1:T(8,128)(2,1)} %get-tuple-element.26), channel_id=1, source_target_pairs={{0,8},{8,16},{16,24},{1,9},{9,17},{17,25},{2,10},{10,18},{18,26},{... | collective-permute-start | bytes 1572872 | tf_op jit(solution)/shard_map/ppermute | solution.py:27
  160.9 15.7 %collective-permute-start.10 = (bf16[1024,64]{0,1:T(8,128)(2,1)S(1)}, bf16[1024,64]{0,1:T(8,128)(2,1)}, u32[]{:S(2)}, u32[]{:S(2)}) collective-permute-start(bf16[1024,64]{0,1:T(8,128)(2,1)S(1)} %get-tuple-element.12), channel_id=1, source_target_pairs={{0,1},{1,2},{2,3},{3,4},{4,5},{5,6},{6,7},{8,9},{9,10},{10,11},{11... | collective-permute-start | bytes 393224 | tf_op jit(solution)/shard_map/ppermute | solution.py:27
  165.9 10.7 %collective-permute-start.11 = (bf16[1024,64]{0,1:T(8,128)(2,1)S(1)}, bf16[1024,64]{0,1:T(8,128)(2,1)}, u32[]{:S(2)}, u32[]{:S(2)}) collective-permute-start(bf16[1024,64]{0,1:T(8,128)(2,1)S(1)} %get-tuple-element.13), channel_id=1, source_target_pairs={{1,0},{2,1},{3,2},{4,3},{5,4},{6,5},{7,6},{9,8},{10,9},{11,10},{12... | collective-permute-start | bytes 393224 | tf_op jit(solution)/shard_map/ppermute | solution.py:28
  176.6 9.9 %copy-start.12 = (f32[1024]{0:T(1024)S(1)}, f32[1024]{0:T(1024)}, u32[]{:S(2)}) copy-start(f32[1024]{0:T(1024)} %param.13) | copy-start | bytes 12292
  176.6 17.7 %copy-start.5 = (bf16[128,8,12,128]{3,1,2,0:T(8,128)(2,1)S(1)}, bf16[128,8,12,128]{3,1,2,0:T(8,128)(2,1)}, u32[]{:S(2)}) copy-start(bf16[128,8,12,128]{3,1,2,0:T(8,128)(2,1)} %copy-done.2) | copy-start | bytes 9437188
  181.3 21.2 %collective-permute-start.13 = (bf16[1024,256]{0,1:T(8,128)(2,1)S(1)}, bf16[1024,256]{0,1:T(8,128)(2,1)}, u32[]{:S(2)}, u32[]{:S(2)}) collective-permute-start(bf16[1024,256]{0,1:T(8,128)(2,1)S(1)} %get-tuple-element.28), channel_id=1, source_target_pairs={{8,0},{16,8},{24,16},{9,1},{17,9},{25,17},{10,2},{18,10},{26,18},{... | collective-permute-start | bytes 1572872 | tf_op jit(solution)/shard_map/ppermute | solution.py:28
  182.6 13.4 %collective-permute-start.12 = (bf16[1024,256]{0,1:T(8,128)(2,1)S(1)}, bf16[1024,256]{0,1:T(8,128)(2,1)}, u32[]{:S(2)}, u32[]{:S(2)}) collective-permute-start(bf16[1024,256]{0,1:T(8,128)(2,1)S(1)} %get-tuple-element.28), channel_id=1, source_target_pairs={{0,8},{8,16},{16,24},{1,9},{9,17},{17,25},{2,10},{10,18},{18,26},{... | collective-permute-start | bytes 1572872 | tf_op jit(solution)/shard_map/ppermute | solution.py:27
  187.7 18.7 %collective-permute-start.14 = (bf16[1024,64]{0,1:T(8,128)(2,1)S(1)}, bf16[1024,64]{0,1:T(8,128)(2,1)}, u32[]{:S(2)}, u32[]{:S(2)}) collective-permute-start(bf16[1024,64]{0,1:T(8,128)(2,1)S(1)} %get-tuple-element.10), channel_id=1, source_target_pairs={{0,1},{1,2},{2,3},{3,4},{4,5},{5,6},{6,7},{8,9},{9,10},{10,11},{11... | collective-permute-start | bytes 393224 | tf_op jit(solution)/shard_map/ppermute | solution.py:27
  192.8 13.5 %collective-permute-start.15 = (bf16[1024,64]{0,1:T(8,128)(2,1)S(1)}, bf16[1024,64]{0,1:T(8,128)(2,1)}, u32[]{:S(2)}, u32[]{:S(2)}) collective-permute-start(bf16[1024,64]{0,1:T(8,128)(2,1)S(1)} %get-tuple-element.11), channel_id=1, source_target_pairs={{1,0},{2,1},{3,2},{4,3},{5,4},{6,5},{7,6},{9,8},{10,9},{11,10},{12... | collective-permute-start | bytes 393224 | tf_op jit(solution)/shard_map/ppermute | solution.py:28
  196.1 10.3 %copy-start.20 = (f32[256]{0:T(256)S(1)}, f32[256]{0:T(256)}, u32[]{:S(2)}) copy-start(f32[256]{0:T(256)} %copy-done.18) | copy-start | bytes 3076
  196.1 10.3 %copy-start.25 = (f32[256]{0:T(256)S(1)}, f32[256]{0:T(256)}, u32[]{:S(2)}) copy-start(f32[256]{0:T(256)} %copy-done.23) | copy-start | bytes 3076
  206.4 16.5 %copy-start.6 = (bf16[128,8,12,128]{3,1,2,0:T(8,128)(2,1)S(1)}, bf16[128,8,12,128]{3,1,2,0:T(8,128)(2,1)}, u32[]{:S(2)}) copy-start(bf16[128,8,12,128]{3,1,2,0:T(8,128)(2,1)} %copy-done.2) | copy-start | bytes 9437188
  211.9 20.3 %collective-permute-start.17 = (bf16[1024,256]{0,1:T(8,128)(2,1)}, bf16[1024,256]{0,1:T(8,128)(2,1)}, u32[]{:S(2)}, u32[]{:S(2)}) collective-permute-start(bf16[1024,256]{0,1:T(8,128)(2,1)} %get-tuple-element.30), channel_id=1, source_target_pairs={{8,0},{16,8},{24,16},{9,1},{17,9},{25,17},{10,2},{18,10},{26,18},{... | collective-permute-start | bytes 1572872 | tf_op jit(solution)/shard_map/ppermute | solution.py:28
  213.2 20.9 %collective-permute-start.16 = (bf16[1024,256]{0,1:T(8,128)(2,1)}, bf16[1024,256]{0,1:T(8,128)(2,1)}, u32[]{:S(2)}, u32[]{:S(2)}) collective-permute-start(bf16[1024,256]{0,1:T(8,128)(2,1)} %get-tuple-element.30), channel_id=1, source_target_pairs={{0,8},{8,16},{16,24},{1,9},{9,17},{17,25},{2,10},{10,18},{18,26},{... | collective-permute-start | bytes 1572872 | tf_op jit(solution)/shard_map/ppermute | solution.py:27
  217.0 11.1 %collective-permute-start.18 = (bf16[1024,64]{0,1:T(8,128)(2,1)S(1)}, bf16[1024,64]{0,1:T(8,128)(2,1)S(1)}, u32[]{:S(2)}, u32[]{:S(2)}) collective-permute-start(bf16[1024,64]{0,1:T(8,128)(2,1)S(1)} %get-tuple-element.8), channel_id=1, source_target_pairs={{0,1},{1,2},{2,3},{3,4},{4,5},{5,6},{6,7},{8,9},{9,10},{10,11},{11... | collective-permute-start | bytes 393224 | tf_op jit(solution)/shard_map/ppermute | solution.py:27
  221.6 8.7 %collective-permute-start.19 = (bf16[1024,64]{0,1:T(8,128)(2,1)S(1)}, bf16[1024,64]{0,1:T(8,128)(2,1)S(1)}, u32[]{:S(2)}, u32[]{:S(2)}) collective-permute-start(bf16[1024,64]{0,1:T(8,128)(2,1)S(1)} %get-tuple-element.9), channel_id=1, source_target_pairs={{1,0},{2,1},{3,2},{4,3},{5,4},{6,5},{7,6},{9,8},{10,9},{11,10},{12... | collective-permute-start | bytes 393224 | tf_op jit(solution)/shard_map/ppermute | solution.py:28
where the time goes:
time: 248 us; the launch traced here: 246 us
  local copies, waits for them, and re-layouts  82.4 us (33%)
  starting transfers between devices  66.5 us (27%)
  matrix products  46.3 us (19%)
  other arithmetic  40.6 us (16%)
  blocking collectives  5.76 us (2%)
  waiting for transfers between devices  2.81 us (1%)
    ppermute x10, starting transfers between devices, with_halo(): before = lax.ppermute(last, axis, up)  44.5 us
    scatter-add x1, other arithmetic, shards(): jax.ops.segment_sum(obs_weight, cell_ids, num_segments=NODES_DEV * T_DEV)  25.3 us
    dot_general x5, matrix products, spatial(): jnp.dot(upper_part, upper, preferred_element_type=jnp.float32)  19.3 us
    gather x1, local copies, waits for them, and re-layouts, shards(): coef_rows = svc_coef[cell_ids // T_DEV]  17 us
    ppermute x10, starting transfers between devices, with_halo(): after = lax.ppermute(initial, axis, down)  13 us
    dot_general x5, matrix products, spatial(): jnp.dot(lower_part, lower, preferred_element_type=jnp.float32)  12.6 us
    dot_general x5, matrix products, spatial(): total = jnp.dot(own_part, field, preferred_element_type=jnp.float32)  12.1 us
    scatter x1, local copies, waits for them, and re-layouts, shards(): jnp.zeros((space_count * capacity, NCOV), jnp.bfloat16).at[slot]  11.3 us
  transfers between devices with their start and end apart: 22, of which 2 were waited for; matrix products, arithmetic and copies ran while one was open for 54% of the time, Pallas kernels for 0%

commit v1 on v0

--- a/solution.py
+++ b/solution.py
@@ -64,18 +64,22 @@
     lower_part = combined[:, NODES_DEV : NODES_DEV + HALO_B * BLOCK]
     upper_part = combined[:, NODES_DEV + HALO_B * BLOCK :]
 
+    space_index = lax.axis_index("space")
+    up = [(i, i + 1) for i in range(space_count - 1)]
+    down = [(i + 1, i) for i in range(space_count - 1)]
+    upper_wants = lax.ppermute(halo_needs[:HALO_B], "space", down)
+    lower_wants = lax.ppermute(halo_needs[HALO_B:], "space", up)
+
+    def pick_blocks(blocks, wanted):
+        return jnp.concatenate(
+            [lax.dynamic_index_in_dim(blocks, wanted[j], axis=0, keepdims=False) for j in range(HALO_B)],
+            axis=0,
+        )
+
     def spatial(field):
-        arrived = with_halo(field, (("space", 0),), NODES_DEV)
-        lower = (
-            arrived[:NODES_DEV]
-            .reshape(NB_DEV, BLOCK, columns)[halo_needs[:HALO_B]]
-            .reshape(HALO_B * BLOCK, columns)
-        )
-        upper = (
-            arrived[2 * NODES_DEV :]
-            .reshape(NB_DEV, BLOCK, columns)[halo_needs[HALO_B:]]
-            .reshape(HALO_B * BLOCK, columns)
-        )
+        blocks = field.reshape(NB_DEV, BLOCK, columns)
+        lower = lax.ppermute(pick_blocks(blocks, upper_wants), "space", up)
+        upper = lax.ppermute(pick_blocks(blocks, lower_wants), "space", down)
         total = jnp.dot(own_part, field, preferred_element_type=jnp.float32)
         total = total + jnp.dot(lower_part, lower, preferred_element_type=jnp.float32)
         total = total + jnp.dot(upper_part, upper, preferred_element_type=jnp.float32)
@@ -93,24 +97,17 @@
     rounded = lax.optimization_barrier(solution.astype(jnp.bfloat16))
     first_space = spatial(rounded)
     first_time = temporal(rounded)
-    capacity = 2 * OBS_DEV // space_count
+    nodes_dev = svc_coef.shape[0]
+    svc_all = lax.all_gather(svc_coef, "space", axis=0, tiled=True)
     owner = obs_owner[:, 0]
-    hits = (owner[:, None] == jnp.arange(space_count, dtype=jnp.int32)[None, :]).astype(jnp.int32)
-    earlier = jnp.cumsum(hits, axis=0) - hits
-    rank = jnp.sum(earlier * hits, axis=1)
-    slot = owner * capacity + rank
-    send_rows = jnp.zeros((space_count * capacity, NCOV), jnp.bfloat16).at[slot].set(covariates)
-    send_cells = jnp.full((space_count * capacity,), -1, jnp.int32).at[slot].set(obs_cell)
-    recv_rows, recv_cells = (
-        lax.all_to_all(send_rows, "space", split_axis=0, concat_axis=0, tiled=True),
-        lax.all_to_all(send_cells, "space", split_axis=0, concat_axis=0, tiled=True),
+    coef_rows = svc_all[owner * nodes_dev + obs_cell // T_DEV]
+    eta = jnp.einsum("rc,rc->r", covariates, coef_rows, preferred_element_type=jnp.float32)
+    obs_weight = jnp.exp(eta)
+    bins = owner * (nodes_dev * T_DEV) + obs_cell
+    local_counts = jax.ops.segment_sum(
+        obs_weight, bins, num_segments=space_count * nodes_dev * T_DEV
     )
-    live = recv_cells >= 0
-    cell_ids = jnp.where(live, recv_cells, 0)
-    coef_rows = svc_coef[cell_ids // T_DEV]
-    eta = jnp.einsum("rc,rc->r", recv_rows, coef_rows, preferred_element_type=jnp.float32)
-    obs_weight = jnp.where(live, jnp.exp(eta), 0.0)
-    counted = jax.ops.segment_sum(obs_weight, cell_ids, num_segments=NODES_DEV * T_DEV)
+    counted = lax.psum_scatter(local_counts, "space", scatter_dimension=0, tiled=True)
     obs_diag = jnp.repeat(counted.reshape(NODES_DEV, T_DEV), PROBES, axis=1)
     full_diag = base_diag + obs_diag
     local_diag = kappa[:, None] + obs_diag

time: 248 us -> 235 us (0.948)
  waiting for transfers between devices: 2.81 us -> 48.4 us
  local copies, waits for them, and re-layouts: 82.4 us -> 44.4 us
  other arithmetic: 40.6 us -> 18.2 us
  between operations: 1.35 us -> 23.1 us
  starting transfers between devices: 66.5 us -> 51.8 us
  matrix products: 46.3 us -> 40.6 us
    unnamed x0 -> x3, waiting for transfers between devices: none -> 34 us
    ppermute x0 -> x12, starting transfers between devices: none -> 23.2 us  [the longest x5 12.4 us: spatial(): lower = lax.ppermute(pick_blocks(blocks, upper_wants), 'space', up)]
    ppermute x10 -> x5, starting transfers between devices: 44.5 us -> 22.1 us  [with_halo(): before = lax.ppermute(last, axis, up)]
    scatter x2 -> x0, local copies, waits for them, and re-layouts: 20.1 us -> none  [the longest x1 11.3 us: shards(): jnp.zeros((space_count * capacity, NCOV), jnp.bfloat16).at[slot]]
    gather x11 -> x1, local copies, waits for them, and re-layouts: 27.8 us -> 10.4 us  [shards(): coef_rows = svc_all[owner * nodes_dev + obs_cell // T_DEV]]
    scatter-add x1, other arithmetic: 25.3 us -> 12 us  [shards(): jax.ops.segment_sum(obs_weight, bins, num_segments=space_count * nodes_de...]
    ppermute x10 -> x5, waiting for transfers between devices: 2.16 us -> 14.4 us  [with_halo(): after = lax.ppermute(initial, axis, down)]
    all_to_all x2 -> x0, starting transfers between devices: 8.9 us -> none  [the longest x1 4.63 us: shards(): lax.all_to_all(send_rows, 'space', split_axis=0, concat_axis=0, tiled=True)]
  transfers between devices with their start and end apart: 22 -> 24, of which waited for: 2 -> 5; matrix products, arithmetic and copies ran while one was open for 54% -> 30% of each run, Pallas kernels for 0% -> 0%
where the time goes in v1:
time: 235 us; the launch traced here: 232 us
  starting transfers between devices  51.8 us (22%)
  waiting for transfers between devices  48.4 us (21%)
  local copies, waits for them, and re-layouts  44.4 us (19%)
  matrix products  40.6 us (17%)
  between operations  23.1 us (10%)
  other arithmetic  18.2 us (8%)
  blocking collectives  5.76 us (2%)
    unnamed x3, waiting for transfers between devices  34 us
    ppermute x5, starting transfers between devices, with_halo(): before = lax.ppermute(last, axis, up)  22.1 us
    ppermute x5, waiting for transfers between devices, with_halo(): after = lax.ppermute(initial, axis, down)  14.4 us
    dot_general x5, matrix products, spatial(): total = jnp.dot(own_part, field, preferred_element_type=jnp.float32)  14.4 us
    dot_general x5, matrix products, spatial(): jnp.dot(upper_part, upper, preferred_element_type=jnp.float32)  14.4 us
    unnamed x70, local copies, waits for them, and re-layouts  12.9 us
    ppermute x5, starting transfers between devices, spatial(): lower = lax.ppermute(pick_blocks(blocks, upper_wants), 'space', up)  12.4 us
    scatter-add x1, other arithmetic, shards(): jax.ops.segment_sum(obs_weight, bins, num_segments=space_count * nodes_de...  12 us
  transfers between devices with their start and end apart: 24, of which 5 were waited for; matrix products, arithmetic and copies ran while one was open for 30% of the time, Pallas kernels for 0%

profile of v1, /device:TPU:0, one launch (start us, length us, event | category | flops | bytes accessed | tf_op | source)
XLA Modules:
  0.0 232.3 jit_solution(14687740390695803875)
XLA Ops:
  8.0 1.4 fusion.82
  9.4 2.9 %collective-permute-start.2 = (s32[2]{0:T(128)}, s32[2]{0:T(128)}, u32[]{:S(2)}, u32[]{:S(2)}) collective-permute-start(s32[2]{0:T(128)} %get-tuple-element.46), channel_id=1, source_target_pairs={{0,8},{8,16},{16,24},{1,9},{9,17},{17,25},{2,10},{10,18},{18,26},{... | collective-permute-start | bytes 32 | tf_op jit(solution)/shard_map/ppermute | solution.py:71
  12.3 1.3 collective-permute-start
  15.2 1.2 copy.51
  16.5 4.5 %copy.52 = bf16[8,128,128]{0,2,1:T(8,128)(2,1)} copy(bf16[8,128,128]{2,1,0:T(8,128)(2,1)} %param.16) | data formatting | bytes 524288 | tf_op args[4]
  21.0 1.9 gather_fusion
  24.1 4.9 %collective-permute-start.4 = (bf16[1024,64]{0,1:T(8,128)(2,1)}, bf16[1024,64]{0,1:T(8,128)(2,1)}, u32[]{:S(2)}, u32[]{:S(2)}) collective-permute-start(bf16[1024,64]{0,1:T(8,128)(2,1)} %get-tuple-element.32), channel_id=1, source_target_pairs={{0,1},{1,2},{2,3},{3,4},{4,5},{5,6},{6,7},{8,9},{9,10},{10,11},{11... | collective-permute-start | bytes 393224 | tf_op jit(solution)/shard_map/ppermute | solution.py:27
  28.9 1.3 collective-permute-start.5
  31.1 1.0 copy.91
  32.1 3.1 %add_convert_fusion = bf16[8,12,128,128]{3,1,2,0:T(8,128)(2,1)S(1)} fusion(f32[8,128,128]{2,1,0:T(8,128)} %convert.8, f32[8,12]{1,0:T(8,128)S(1)} %fusion.75, bf16[8,8,128,128]{3,2,1,0:T(8,128)(2,1)S(1)} %copy-done, s32[8,8]{1,0:T(8,128)S(1)} %copy-done.27), kind=kOutput, calls=%fused_computation.3 | convolution fusion | flops 29885184 | bytes 5767808 | tf_op jit(solution)/shard_map/bkm,bkij->bimj/dot_general | solution.py:60
  35.3 3.2 %copy.103 = bf16[128,8,12,128]{3,1,2,0:T(8,128)(2,1)} copy(bf16[128,8,12,128]{3,2,1,0:T(8,128)(2,1)S(1)} %bitcast.96) | data formatting | bytes 6291456
  40.4 3.3 %fusion.37 = f32[1024,256]{0,1:T(8,128)} fusion(bf16[1024,256]{0,1:T(8,128)(2,1)S(1)} %fusion.55, bf16[1024,1536]{1,0:T(8,128)(2,1)} %bitcast.97), kind=kOutput, calls=%fused_computation.66 | convolution fusion | flops 536870912 | bytes 3670016 | tf_op jit(solution)/shard_map/dot_general | solution.py:83
  43.7 1.3 fusion.81
  47.7 1.3 fusion.83
  53.9 1.0 dynamic-slice_bitcast_fusion.17
  54.9 4.2 %collective-permute-start.1 = (bf16[256,256]{1,0:T(8,128)(2,1)S(1)}, bf16[256,256]{1,0:T(8,128)(2,1)}, u32[]{:S(2)}, u32[]{:S(2)}) collective-permute-start(bf16[256,256]{1,0:T(8,128)(2,1)S(1)} %pad_maximum_fusion.10), channel_id=1, source_target_pairs={{0,8},{8,16},{16,24},{1,9},{9,17},{17,25},{2,10},{10,18},{18,26},{... | collective-permute-start | bytes 393224 | tf_op jit(solution)/shard_map/ppermute | solution.py:81
  59.2 1.3 collective-permute-start.3
  60.5 10.4 %gather_fusion.1 = bf16[2048,256]{1,0:T(8,128)(2,1)} fusion(bf16[4096,256]{1,0:T(8,128)(2,1)} %all-gather.2.cloned.1.call-done, s32[2048]{0:T(1024)S(1)} %copy-done.18), kind=kCustom, calls=%fused_computation.1 | custom fusion | bytes 2105344 | tf_op jit(solution)/shard_map/gather | solution.py:103
  70.9 1.9 fusion
  72.8 12.0 %scatter_custom_fusion = f32[16384]{0:T(1024)} fusion(s32[2048]{0:T(1024)} %get-tuple-element.41, f32[2048]{0:T(1024)S(1)} %exp.3, f32[]{:T(128)} %constant.72.clone.1), kind=kCustom, calls=%fused_computation.137 | custom fusion | flops 2048 | bytes 66048 | tf_op jit(solution)/shard_map/scatter-add | solution.py:107
  84.8 2.8 %convolution_add_fusion.9 = f32[1024,256]{0,1:T(8,128)} fusion(f32[1024,256]{0,1:T(8,128)} %fusion.37, bf16[256,256]{1,0:T(8,128)(2,1)} %collective-permute-done.1, bf16[1024,1536]{1,0:T(8,128)(2,1)} %bitcast.98), kind=kOutput, calls=%fused_computation.42 | convolution fusion | flops 134479872 | bytes 2752512 | tf_op jit(solution)/shard_map/dot_general | solution.py:84
  87.6 33.3 %all-reduce.3.cloned.1.call-done = f32[16384]{0:T(1024)} async-done(((f32[16384]{0:T(1024)}), f32[16384]{0:T(1024)}) %all-reduce.3.cloned.1.call-update) | async-done | bytes 65552
  121.6 1.3 reshape.52
  122.9 1.2 copy.60
  124.2 1.1 fusion.5
  125.3 4.0 %fusion.84 = (bf16[1024,256]{0,1:T(8,128)(2,1)}, f32[1024,256]{0,1:T(8,128)}) fusion(f32[1024,256]{0,1:T(8,128)S(1)} %get-tuple-element.39, f32[1024,256]{0,1:T(8,128)S(1)} %get-tuple-element.38, bf16[1024,64]{0,1:T(8,128)(2,1)} %collective-permute-done.5, bf16[1024,256]{0,1:T(8,128)(2,1)S(1)} %fusion.55, bf16[1024,64]{0,1:T(8,128)(2,1)} %collective-permute-done.4, ...), kind=kOutput, calls=%fused_computation.168 | convolution fusion | flops 141557760 | bytes 6695936 | tf_op jit(solution)/shard_map/dot_general | solution.py:85
  129.3 2.1 copy.92
  131.4 2.5 %fusion.35 = f32[1024,256]{0,1:T(8,128)S(1)} fusion(bf16[1024,256]{0,1:T(8,128)(2,1)} %get-tuple-element.50, bf16[1024,1536]{1,0:T(8,128)(2,1)} %bitcast.100), kind=kOutput, calls=%fused_computation.64 | convolution fusion | flops 536870912 | bytes 3670016 | tf_op jit(solution)/shard_map/dot_general | solution.py:83
  134.1 1.4 collective-permute-start.6
  135.7 3.4 %collective-permute-start.8 = (bf16[1024,64]{0,1:T(8,128)(2,1)S(1)}, bf16[1024,64]{0,1:T(8,128)(2,1)S(1)}, u32[]{:S(2)}, u32[]{:S(2)}) collective-permute-start(bf16[1024,64]{0,1:T(8,128)(2,1)S(1)} %get-tuple-element.26), channel_id=1, source_target_pairs={{0,1},{1,2},{2,3},{3,4},{4,5},{5,6},{6,7},{8,9},{9,10},{10,11},{11... | collective-permute-start | bytes 393224 | tf_op jit(solution)/shard_map/ppermute | solution.py:27
  139.1 1.3 collective-permute-start.9
  140.4 1.5 collective-permute-start.7
  141.9 1.4 convolution_add_fusion.7
  143.3 4.0 %collective-permute-done.9 = bf16[1024,64]{0,1:T(8,128)(2,1)S(1)} collective-permute-done((bf16[1024,64]{0,1:T(8,128)(2,1)S(1)}, bf16[1024,64]{0,1:T(8,128)(2,1)S(1)}, u32[]{:S(2)}, u32[]{:S(2)}) %collective-permute-start.9) | collective-permute-done | bytes 131104 | tf_op jit(solution)/shard_map/ppermute | solution.py:28
  147.3 3.0 %fusion.85 = (bf16[1024,256]{0,1:T(8,128)(2,1)}, f32[1024,256]{0,1:T(8,128)}) fusion(f32[1024,256]{0,1:T(8,128)S(1)} %copy-done.30, f32[1024,256]{0,1:T(8,128)S(1)} %copy-done.11, f32[1024,256]{0,1:T(8,128)S(1)} %fusion.4, bf16[1024,64]{0,1:T(8,128)(2,1)S(1)} %collective-permute-done.9, bf16[1024,256]{0,1:T(8,128)(2,1)S(1)} %copy-done.1, ...), kind=kOutput, calls=%fused_computation.169 | convolution fusion | flops 140247040 | bytes 7735296 | tf_op jit(solution)/shard_map/dot_general | solution.py:85
  150.4 2.1 copy.93
  152.5 2.5 %fusion.33 = f32[1024,256]{0,1:T(8,128)S(1)} fusion(bf16[1024,256]{0,1:T(8,128)(2,1)} %get-tuple-element.52, bf16[1024,1536]{1,0:T(8,128)(2,1)} %bitcast.103), kind=kOutput, calls=%fused_computation.62 | convolution fusion | flops 536870912 | bytes 3670016 | tf_op jit(solution)/shard_map/dot_general | solution.py:83
  155.2 2.3 %collective-permute-start.10 = (bf16[256,256]{1,0:T(8,128)(2,1)S(1)}, bf16[256,256]{1,0:T(8,128)(2,1)S(1)}, u32[]{:S(2)}, u32[]{:S(2)}) collective-permute-start(bf16[256,256]{1,0:T(8,128)(2,1)S(1)} %pad_maximum_fusion.14), channel_id=1, source_target_pairs={{0,8},{8,16},{16,24},{1,9},{9,17},{17,25},{2,10},{10,18},{18,26},{... | collective-permute-start | bytes 393224 | tf_op jit(solution)/shard_map/ppermute | solution.py:81
  157.7 4.3 %collective-permute-start.12 = (bf16[1024,64]{0,1:T(8,128)(2,1)S(1)}, bf16[1024,64]{0,1:T(8,128)(2,1)S(1)}, u32[]{:S(2)}, u32[]{:S(2)}) collective-permute-start(bf16[1024,64]{0,1:T(8,128)(2,1)S(1)} %get-tuple-element.20), channel_id=1, source_target_pairs={{0,1},{1,2},{2,3},{3,4},{4,5},{5,6},{6,7},{8,9},{9,10},{10,11},{11... | collective-permute-start | bytes 393224 | tf_op jit(solution)/shard_map/ppermute | solution.py:27
  162.0 1.3 collective-permute-start.13
  163.3 1.3 collective-permute-start.11
  164.6 1.4 convolution_add_fusion.5
  166.0 3.6 %collective-permute-done.13 = bf16[1024,64]{0,1:T(8,128)(2,1)S(1)} collective-permute-done((bf16[1024,64]{0,1:T(8,128)(2,1)S(1)}, bf16[1024,64]{0,1:T(8,128)(2,1)S(1)}, u32[]{:S(2)}, u32[]{:S(2)}) %collective-permute-start.13) | collective-permute-done | bytes 131104 | tf_op jit(solution)/shard_map/ppermute | solution.py:28
  169.6 2.8 %fusion.86 = (bf16[1024,256]{0,1:T(8,128)(2,1)S(1)}, f32[1024,256]{0,1:T(8,128)}) fusion(f32[1024,256]{0,1:T(8,128)S(1)} %copy-done.31, f32[1024,256]{0,1:T(8,128)S(1)} %copy-done.12, f32[1024,256]{0,1:T(8,128)S(1)} %fusion.3, bf16[1024,64]{0,1:T(8,128)(2,1)S(1)} %collective-permute-done.13, bf16[1024,256]{0,1:T(8,128)(2,1)S(1)} %copy-done.4, ...), kind=kOutput, calls=%fused_computation.170 | convolution fusion | flops 140247040 | bytes 7735296 | tf_op jit(solution)/shard_map/dot_general | solution.py:85
  172.5 1.0 copy.94
  173.5 2.4 %fusion.31 = f32[1024,256]{0,1:T(8,128)S(1)} fusion(bf16[1024,256]{0,1:T(8,128)(2,1)S(1)} %get-tuple-element.54, bf16[1024,1536]{1,0:T(8,128)(2,1)} %bitcast.106), kind=kOutput, calls=%fused_computation.60 | convolution fusion | flops 536870912 | bytes 3670016 | tf_op jit(solution)/shard_map/dot_general | solution.py:83
  176.0 2.0 collective-permute-start.14
  178.1 4.7 %collective-permute-start.16 = (bf16[1024,64]{0,1:T(8,128)(2,1)S(1)}, bf16[1024,64]{0,1:T(8,128)(2,1)S(1)}, u32[]{:S(2)}, u32[]{:S(2)}) collective-permute-start(bf16[1024,64]{0,1:T(8,128)(2,1)S(1)} %get-tuple-element.14), channel_id=1, source_target_pairs={{0,1},{1,2},{2,3},{3,4},{4,5},{5,6},{6,7},{8,9},{9,10},{10,11},{11... | collective-permute-start | bytes 393224 | tf_op jit(solution)/shard_map/ppermute | solution.py:27
  182.8 1.3 collective-permute-start.17
  184.2 1.3 collective-permute-start.15
  185.5 1.4 convolution_add_fusion.3
  186.9 3.8 %collective-permute-done.17 = bf16[1024,64]{0,1:T(8,128)(2,1)S(1)} collective-permute-done((bf16[1024,64]{0,1:T(8,128)(2,1)S(1)}, bf16[1024,64]{0,1:T(8,128)(2,1)S(1)}, u32[]{:S(2)}, u32[]{:S(2)}) %collective-permute-start.17) | collective-permute-done | bytes 131104 | tf_op jit(solution)/shard_map/ppermute | solution.py:28
  190.7 3.0 %fusion.87 = (bf16[1024,256]{0,1:T(8,128)(2,1)}, f32[1024,256]{0,1:T(8,128)}) fusion(f32[1024,256]{0,1:T(8,128)S(1)} %copy-done.29, f32[1024,256]{0,1:T(8,128)S(1)} %copy-done.13, f32[1024,256]{0,1:T(8,128)S(1)} %fusion.2, bf16[1024,64]{0,1:T(8,128)(2,1)S(1)} %collective-permute-done.17, bf16[1024,256]{0,1:T(8,128)(2,1)S(1)} %get-tuple-element.54, ...), kind=kOutput, calls=%fused_computation.171 | convolution fusion | flops 140247040 | bytes 7735296 | tf_op jit(solution)/shard_map/dot_general | solution.py:85
  193.7 2.1 copy.95
  195.8 3.6 %fusion.39 = f32[1024,256]{0,1:T(8,128)} fusion(bf16[1024,256]{0,1:T(8,128)(2,1)} %get-tuple-element.56, bf16[1024,1536]{1,0:T(8,128)(2,1)} %bitcast.109), kind=kOutput, calls=%fused_computation.68 | convolution fusion | flops 536870912 | bytes 3670016 | tf_op jit(solution)/shard_map/dot_general | solution.py:83
  199.4 2.4 %collective-permute-start.18 = (bf16[256,256]{1,0:T(8,128)(2,1)S(1)}, bf16[256,256]{1,0:T(8,128)(2,1)}, u32[]{:S(2)}, u32[]{:S(2)}) collective-permute-start(bf16[256,256]{1,0:T(8,128)(2,1)S(1)} %pad_maximum_fusion.18), channel_id=1, source_target_pairs={{0,8},{8,16},{16,24},{1,9},{9,17},{17,25},{2,10},{10,18},{18,26},{... | collective-permute-start | bytes 393224 | tf_op jit(solution)/shard_map/ppermute | solution.py:81
  202.5 2.5 %copy.80 = f32[1024,256]{1,0:T(8,128)} copy(f32[1024,256]{0,1:T(8,128)} %get-tuple-element.57) | data formatting | bytes 2097152
  205.0 4.9 %collective-permute-start.20 = (bf16[1024,64]{0,1:T(8,128)(2,1)}, bf16[1024,64]{0,1:T(8,128)(2,1)S(1)}, u32[]{:S(2)}, u32[]{:S(2)}) collective-permute-start(bf16[1024,64]{0,1:T(8,128)(2,1)} %get-tuple-element.12), channel_id=1, source_target_pairs={{0,1},{1,2},{2,3},{3,4},{4,5},{5,6},{6,7},{8,9},{9,10},{10,11},{11... | collective-permute-start | bytes 393224 | tf_op jit(solution)/shard_map/ppermute | solution.py:27
  209.9 1.3 collective-permute-start.21
  211.2 1.3 collective-permute-start.19
  212.5 1.8 convolution_add_fusion.1
  214.3 2.9 %collective-permute-done.21 = bf16[1024,64]{0,1:T(8,128)(2,1)S(1)} collective-permute-done((bf16[1024,64]{0,1:T(8,128)(2,1)S(1)}, bf16[1024,64]{0,1:T(8,128)(2,1)S(1)}, u32[]{:S(2)}, u32[]{:S(2)}) %collective-permute-start.21) | collective-permute-done | bytes 131104 | tf_op jit(solution)/shard_map/ppermute | solution.py:28
  217.6 1.5 fusion.30
  219.1 5.8 %psum.7 = f32[2,256]{1,0:T(2,128)S(1)} all-reduce(f32[2,256]{1,0:T(2,128)S(1)} %pad_maximum_fusion.20), channel_id=1, replica_groups=mesh['space'=4,'tm'=8] {'space'}, use_global_device_ids=true, to_apply=%region_4.5 | all-reduce | flops 512 | bytes 4096 | tf_op jit(solution)/shard_map/psum | solution.py:135
  (128 shorter events, 8.8 us)
Async XLA Ops:
  7.2 24.9 %copy-start = (bf16[8,8,128,128]{3,2,1,0:T(8,128)(2,1)S(1)}, bf16[8,8,128,128]{3,2,1,0:T(8,128)(2,1)}, u32[]{:S(2)}) copy-start(bf16[8,8,128,128]{3,2,1,0:T(8,128)(2,1)} %param.17) | copy-start | bytes 6291460
  7.2 15.8 %copy-start.14 = (f32[1024]{0:T(1024)S(1)}, f32[1024]{0:T(1024)}, u32[]{:S(2)}) copy-start(f32[1024]{0:T(1024)} %param.13) | copy-start | bytes 12292
  7.2 53.3 %all-gather.2.cloned.1.call-start = ((), (), s32[]{:S(2)}) async-start(), calls=%async_computation | async-start | bytes 2621440 | tf_op jit(solution)/shard_map/all_gather | solution.py:101
  7.9 113.0 %all-reduce.3.cloned.1.call-start = ((), (), s32[]{:S(2)}) async-start(), calls=%async_computation.1 | async-start | bytes 131072
  9.4 34.4 %collective-permute-start.2 = (s32[2]{0:T(128)}, s32[2]{0:T(128)}, u32[]{:S(2)}, u32[]{:S(2)}) collective-permute-start(s32[2]{0:T(128)} %get-tuple-element.46), channel_id=1, source_target_pairs={{0,8},{8,16},{16,24},{1,9},{9,17},{17,25},{2,10},{10,18},{18,26},{... | collective-permute-start | bytes 32 | tf_op jit(solution)/shard_map/ppermute | solution.py:71
  12.3 35.4 %collective-permute-start = (s32[2]{0:T(128)}, s32[2]{0:T(128)}, u32[]{:S(2)}, u32[]{:S(2)}) collective-permute-start(s32[2]{0:T(128)} %get-tuple-element.47), channel_id=1, source_target_pairs={{8,0},{16,8},{24,16},{9,1},{17,9},{25,17},{10,2},{18,10},{26,18},{... | collective-permute-start | bytes 32 | tf_op jit(solution)/shard_map/ppermute | solution.py:70
  14.4 9.0 %copy-start.19 = (f32[256]{0:T(256)}, f32[256]{0:T(256)S(1)}, u32[]{:S(2)}) copy-start(f32[256]{0:T(256)S(1)} %mul.140) | copy-start | bytes 3076
  15.2 7.8 %copy-start.25 = (f32[256]{0:T(256)}, f32[256]{0:T(256)S(1)}, u32[]{:S(2)}) copy-start(f32[256]{0:T(256)S(1)} %broadcast_in_dim_reshape.2) | copy-start | bytes 3076
  16.4 13.8 %copy-start.9 = (bf16[8,128,128]{2,1,0:T(8,128)(2,1)S(1)}, bf16[8,128,128]{2,1,0:T(8,128)(2,1)}, u32[]{:S(2)}) copy-start(bf16[8,128,128]{2,1,0:T(8,128)(2,1)} %param.16) | copy-start | bytes 786436
  16.5 15.6 %copy-start.27 = (s32[8,8]{1,0:T(8,128)S(1)}, s32[8,8]{1,0:T(8,128)}, u32[]{:S(2)}) copy-start(s32[8,8]{1,0:T(8,128)} %param.18) | copy-start | bytes 772
  23.0 12.3 %copy-start.16 = (f32[8,128]{1,0:T(8,128)}, f32[8,128]{1,0:T(8,128)S(1)}, u32[]{:S(2)}) copy-start(f32[8,128]{1,0:T(8,128)S(1)} %copy.53) | copy-start | bytes 12292
  23.0 7.3 %copy-start.21 = (f32[256]{0:T(256)}, f32[256]{0:T(256)S(1)}, u32[]{:S(2)}) copy-start(f32[256]{0:T(256)S(1)} %broadcast_multiply_fusion.3) | copy-start | bytes 3076
  24.1 101.2 %collective-permute-start.4 = (bf16[1024,64]{0,1:T(8,128)(2,1)}, bf16[1024,64]{0,1:T(8,128)(2,1)}, u32[]{:S(2)}, u32[]{:S(2)}) collective-permute-start(bf16[1024,64]{0,1:T(8,128)(2,1)} %get-tuple-element.32), channel_id=1, source_target_pairs={{0,1},{1,2},{2,3},{3,4},{4,5},{5,6},{6,7},{8,9},{9,10},{10,11},{11... | collective-permute-start | bytes 393224 | tf_op jit(solution)/shard_map/ppermute | solution.py:27
  28.9 96.3 %collective-permute-start.5 = (bf16[1024,64]{0,1:T(8,128)(2,1)S(1)}, bf16[1024,64]{0,1:T(8,128)(2,1)}, u32[]{:S(2)}, u32[]{:S(2)}) collective-permute-start(bf16[1024,64]{0,1:T(8,128)(2,1)S(1)} %get-tuple-element.33), channel_id=1, source_target_pairs={{1,0},{2,1},{3,2},{4,3},{5,4},{6,5},{7,6},{9,8},{10,9},{11,10},{12... | collective-permute-start | bytes 393224 | tf_op jit(solution)/shard_map/ppermute | solution.py:28
  35.3 3.2 %copy-start.28 = (u32[32]{0:T(128)S(1)}, u32[32]{0:T(128)}, u32[]{:S(2)}) copy-start(u32[32]{0:T(128)} %constant.98) | copy-start | bytes 388
  35.3 4.5 %copy-start.23 = (s32[2048,1]{0,1:T(1,128)S(1)}, s32[2048,1]{0,1:T(1,128)}, u32[]{:S(2)}) copy-start(s32[2048,1]{0,1:T(1,128)} %param.21) | copy-start | bytes 24580
  35.3 4.5 %copy-start.24 = (s32[2048]{0:T(1024)S(1)}, s32[2048]{0:T(1024)}, u32[]{:S(2)}) copy-start(s32[2048]{0:T(1024)} %param.22) | copy-start | bytes 24580
  40.4 20.1 %copy-start.18 = (s32[2048]{0:T(1024)S(1)}, s32[2048]{0:T(1024)}, u32[]{:S(2)}) copy-start(s32[2048]{0:T(1024)} %get-tuple-element.40) | copy-start | bytes 24580
  54.9 29.9 %collective-permute-start.1 = (bf16[256,256]{1,0:T(8,128)(2,1)S(1)}, bf16[256,256]{1,0:T(8,128)(2,1)}, u32[]{:S(2)}, u32[]{:S(2)}) collective-permute-start(bf16[256,256]{1,0:T(8,128)(2,1)S(1)} %pad_maximum_fusion.10), channel_id=1, source_target_pairs={{0,8},{8,16},{16,24},{1,9},{9,17},{17,25},{2,10},{10,18},{18,26},{... | collective-permute-start | bytes 393224 | tf_op jit(solution)/shard_map/ppermute | solution.py:81
  59.2 66.1 %collective-permute-start.3 = (bf16[256,256]{1,0:T(8,128)(2,1)S(1)}, bf16[256,256]{1,0:T(8,128)(2,1)}, u32[]{:S(2)}, u32[]{:S(2)}) collective-permute-start(bf16[256,256]{1,0:T(8,128)(2,1)S(1)} %pad_maximum_fusion.11), channel_id=1, source_target_pairs={{8,0},{16,8},{24,16},{9,1},{17,9},{25,17},{10,2},{18,10},{26,18},{... | collective-permute-start | bytes 393224 | tf_op jit(solution)/shard_map/ppermute | solution.py:82
  84.8 40.5 %copy-start.15 = (f32[1024]{0:T(1024)S(1)}, f32[1024]{0:T(1024)}, u32[]{:S(2)}) copy-start(f32[1024]{0:T(1024)} %param.13) | copy-start | bytes 12292
  84.8 40.5 %copy-start.17 = (f32[8,128]{1,0:T(8,128)S(1)}, f32[8,128]{1,0:T(8,128)}, u32[]{:S(2)}) copy-start(f32[8,128]{1,0:T(8,128)} %copy-done.16) | copy-start | bytes 12292
  84.8 40.5 %copy-start.20 = (f32[256]{0:T(256)S(1)}, f32[256]{0:T(256)}, u32[]{:S(2)}) copy-start(f32[256]{0:T(256)} %copy-done.19) | copy-start | bytes 3076
  84.8 40.5 %copy-start.22 = (f32[256]{0:T(256)S(1)}, f32[256]{0:T(256)}, u32[]{:S(2)}) copy-start(f32[256]{0:T(256)} %copy-done.21) | copy-start | bytes 3076
  84.8 40.5 %copy-start.26 = (f32[256]{0:T(256)S(1)}, f32[256]{0:T(256)}, u32[]{:S(2)}) copy-start(f32[256]{0:T(256)} %copy-done.25) | copy-start | bytes 3076
  125.2 4.1 %copy-start.10 = (f32[1024,256]{0,1:T(8,128)}, f32[1024,256]{0,1:T(8,128)S(1)}, u32[]{:S(2)}) copy-start(f32[1024,256]{0,1:T(8,128)S(1)} %get-tuple-element.39) | copy-start | bytes 3145732
  129.3 6.2 %copy-start.1 = (bf16[1024,256]{0,1:T(8,128)(2,1)S(1)}, bf16[1024,256]{0,1:T(8,128)(2,1)}, u32[]{:S(2)}) copy-start(bf16[1024,256]{0,1:T(8,128)(2,1)} %get-tuple-element.50) | copy-start | bytes 1572868
  131.4 2.6 %copy-start.6 = (bf16[1024,256]{1,0:T(8,128)(2,1)S(1)}, bf16[1024,256]{1,0:T(8,128)(2,1)}, u32[]{:S(2)}) copy-start(bf16[1024,256]{1,0:T(8,128)(2,1)} %copy.92) | copy-start | bytes 1572868
  134.0 13.3 %copy-start.11 = (f32[1024,256]{0,1:T(8,128)S(1)}, f32[1024,256]{0,1:T(8,128)}, u32[]{:S(2)}) copy-start(f32[1024,256]{0,1:T(8,128)} %copy-done.10) | copy-start | bytes 3145732
  134.0 13.3 %copy-start.30 = (f32[1024,256]{0,1:T(8,128)S(1)}, f32[1024,256]{0,1:T(8,128)}, u32[]{:S(2)}) copy-start(f32[1024,256]{0,1:T(8,128)} %get-tuple-element.51) | copy-start | bytes 3145732
  134.1 7.8 %collective-permute-start.6 = (bf16[256,256]{1,0:T(8,128)(2,1)S(1)}, bf16[256,256]{1,0:T(8,128)(2,1)S(1)}, u32[]{:S(2)}, u32[]{:S(2)}) collective-permute-start(bf16[256,256]{1,0:T(8,128)(2,1)S(1)} %pad_maximum_fusion.12), channel_id=1, source_target_pairs={{0,8},{8,16},{16,24},{1,9},{9,17},{17,25},{2,10},{10,18},{18,26},{... | collective-permute-start | bytes 393224 | tf_op jit(solution)/shard_map/ppermute | solution.py:81
  135.7 7.6 %collective-permute-start.8 = (bf16[1024,64]{0,1:T(8,128)(2,1)S(1)}, bf16[1024,64]{0,1:T(8,128)(2,1)S(1)}, u32[]{:S(2)}, u32[]{:S(2)}) collective-permute-start(bf16[1024,64]{0,1:T(8,128)(2,1)S(1)} %get-tuple-element.26), channel_id=1, source_target_pairs={{0,1},{1,2},{2,3},{3,4},{4,5},{5,6},{6,7},{8,9},{9,10},{10,11},{11... | collective-permute-start | bytes 393224 | tf_op jit(solution)/shard_map/ppermute | solution.py:27
  139.1 8.2 %collective-permute-start.9 = (bf16[1024,64]{0,1:T(8,128)(2,1)S(1)}, bf16[1024,64]{0,1:T(8,128)(2,1)S(1)}, u32[]{:S(2)}, u32[]{:S(2)}) collective-permute-start(bf16[1024,64]{0,1:T(8,128)(2,1)S(1)} %get-tuple-element.27), channel_id=1, source_target_pairs={{1,0},{2,1},{3,2},{4,3},{5,4},{6,5},{7,6},{9,8},{10,9},{11,10},{12... | collective-permute-start | bytes 393224 | tf_op jit(solution)/shard_map/ppermute | solution.py:28
  140.4 6.9 %collective-permute-start.7 = (bf16[256,256]{1,0:T(8,128)(2,1)S(1)}, bf16[256,256]{1,0:T(8,128)(2,1)S(1)}, u32[]{:S(2)}, u32[]{:S(2)}) collective-permute-start(bf16[256,256]{1,0:T(8,128)(2,1)S(1)} %pad_maximum_fusion.13), channel_id=1, source_target_pairs={{8,0},{16,8},{24,16},{9,1},{17,9},{25,17},{10,2},{18,10},{26,18},{... | collective-permute-start | bytes 393224 | tf_op jit(solution)/shard_map/ppermute | solution.py:82
  150.4 7.1 %copy-start.3 = (bf16[1024,256]{0,1:T(8,128)(2,1)S(1)}, bf16[1024,256]{0,1:T(8,128)(2,1)}, u32[]{:S(2)}) copy-start(bf16[1024,256]{0,1:T(8,128)(2,1)} %get-tuple-element.52) | copy-start | bytes 1572868
  152.5 2.6 %copy-start.7 = (bf16[1024,256]{1,0:T(8,128)(2,1)S(1)}, bf16[1024,256]{1,0:T(8,128)(2,1)}, u32[]{:S(2)}) copy-start(bf16[1024,256]{1,0:T(8,128)(2,1)} %copy.93) | copy-start | bytes 1572868
  155.1 14.6 %copy-start.4 = (bf16[1024,256]{0,1:T(8,128)(2,1)S(1)}, bf16[1024,256]{0,1:T(8,128)(2,1)}, u32[]{:S(2)}) copy-start(bf16[1024,256]{0,1:T(8,128)(2,1)} %get-tuple-element.52) | copy-start | bytes 1572868
  155.1 14.6 %copy-start.12 = (f32[1024,256]{0,1:T(8,128)S(1)}, f32[1024,256]{0,1:T(8,128)}, u32[]{:S(2)}) copy-start(f32[1024,256]{0,1:T(8,128)} %copy-done.10) | copy-start | bytes 3145732
  155.1 14.6 %copy-start.31 = (f32[1024,256]{0,1:T(8,128)S(1)}, f32[1024,256]{0,1:T(8,128)}, u32[]{:S(2)}) copy-start(f32[1024,256]{0,1:T(8,128)} %get-tuple-element.53) | copy-start | bytes 3145732
  155.2 9.4 %collective-permute-start.10 = (bf16[256,256]{1,0:T(8,128)(2,1)S(1)}, bf16[256,256]{1,0:T(8,128)(2,1)S(1)}, u32[]{:S(2)}, u32[]{:S(2)}) collective-permute-start(bf16[256,256]{1,0:T(8,128)(2,1)S(1)} %pad_maximum_fusion.14), channel_id=1, source_target_pairs={{0,8},{8,16},{16,24},{1,9},{9,17},{17,25},{2,10},{10,18},{18,26},{... | collective-permute-start | bytes 393224 | tf_op jit(solution)/shard_map/ppermute | solution.py:81
  157.7 8.3 %collective-permute-start.12 = (bf16[1024,64]{0,1:T(8,128)(2,1)S(1)}, bf16[1024,64]{0,1:T(8,128)(2,1)S(1)}, u32[]{:S(2)}, u32[]{:S(2)}) collective-permute-start(bf16[1024,64]{0,1:T(8,128)(2,1)S(1)} %get-tuple-element.20), channel_id=1, source_target_pairs={{0,1},{1,2},{2,3},{3,4},{4,5},{5,6},{6,7},{8,9},{9,10},{10,11},{11... | collective-permute-start | bytes 393224 | tf_op jit(solution)/shard_map/ppermute | solution.py:27
  162.0 7.7 %collective-permute-start.13 = (bf16[1024,64]{0,1:T(8,128)(2,1)S(1)}, bf16[1024,64]{0,1:T(8,128)(2,1)S(1)}, u32[]{:S(2)}, u32[]{:S(2)}) collective-permute-start(bf16[1024,64]{0,1:T(8,128)(2,1)S(1)} %get-tuple-element.21), channel_id=1, source_target_pairs={{1,0},{2,1},{3,2},{4,3},{5,4},{6,5},{7,6},{9,8},{10,9},{11,10},{12... | collective-permute-start | bytes 393224 | tf_op jit(solution)/shard_map/ppermute | solution.py:28
  163.3 6.3 %collective-permute-start.11 = (bf16[256,256]{1,0:T(8,128)(2,1)S(1)}, bf16[256,256]{1,0:T(8,128)(2,1)S(1)}, u32[]{:S(2)}, u32[]{:S(2)}) collective-permute-start(bf16[256,256]{1,0:T(8,128)(2,1)S(1)} %pad_maximum_fusion.15), channel_id=1, source_target_pairs={{8,0},{16,8},{24,16},{9,1},{17,9},{25,17},{10,2},{18,10},{26,18},{... | collective-permute-start | bytes 393224 | tf_op jit(solution)/shard_map/ppermute | solution.py:82
  173.5 2.4 %copy-start.8 = (bf16[1024,256]{1,0:T(8,128)(2,1)S(1)}, bf16[1024,256]{1,0:T(8,128)(2,1)}, u32[]{:S(2)}) copy-start(bf16[1024,256]{1,0:T(8,128)(2,1)} %copy.94) | copy-start | bytes 1572868
  175.9 14.8 %copy-start.13 = (f32[1024,256]{0,1:T(8,128)S(1)}, f32[1024,256]{0,1:T(8,128)}, u32[]{:S(2)}) copy-start(f32[1024,256]{0,1:T(8,128)} %copy-done.10) | copy-start | bytes 3145732
  175.9 14.8 %copy-start.29 = (f32[1024,256]{0,1:T(8,128)S(1)}, f32[1024,256]{0,1:T(8,128)}, u32[]{:S(2)}) copy-start(f32[1024,256]{0,1:T(8,128)} %get-tuple-element.55) | copy-start | bytes 3145732
  176.0 9.5 %collective-permute-start.14 = (bf16[256,256]{1,0:T(8,128)(2,1)S(1)}, bf16[256,256]{1,0:T(8,128)(2,1)S(1)}, u32[]{:S(2)}, u32[]{:S(2)}) collective-permute-start(bf16[256,256]{1,0:T(8,128)(2,1)S(1)} %pad_maximum_fusion.16), channel_id=1, source_target_pairs={{0,8},{8,16},{16,24},{1,9},{9,17},{17,25},{2,10},{10,18},{18,26},{... | collective-permute-start | bytes 393224 | tf_op jit(solution)/shard_map/ppermute | solution.py:81
  178.1 8.7 %collective-permute-start.16 = (bf16[1024,64]{0,1:T(8,128)(2,1)S(1)}, bf16[1024,64]{0,1:T(8,128)(2,1)S(1)}, u32[]{:S(2)}, u32[]{:S(2)}) collective-permute-start(bf16[1024,64]{0,1:T(8,128)(2,1)S(1)} %get-tuple-element.14), channel_id=1, source_target_pairs={{0,1},{1,2},{2,3},{3,4},{4,5},{5,6},{6,7},{8,9},{9,10},{10,11},{11... | collective-permute-start | bytes 393224 | tf_op jit(solution)/shard_map/ppermute | solution.py:27
  182.8 7.8 %collective-permute-start.17 = (bf16[1024,64]{0,1:T(8,128)(2,1)S(1)}, bf16[1024,64]{0,1:T(8,128)(2,1)S(1)}, u32[]{:S(2)}, u32[]{:S(2)}) collective-permute-start(bf16[1024,64]{0,1:T(8,128)(2,1)S(1)} %get-tuple-element.15), channel_id=1, source_target_pairs={{1,0},{2,1},{3,2},{4,3},{5,4},{6,5},{7,6},{9,8},{10,9},{11,10},{12... | collective-permute-start | bytes 393224 | tf_op jit(solution)/shard_map/ppermute | solution.py:28
  184.2 6.5 %collective-permute-start.15 = (bf16[256,256]{1,0:T(8,128)(2,1)S(1)}, bf16[256,256]{1,0:T(8,128)(2,1)S(1)}, u32[]{:S(2)}, u32[]{:S(2)}) collective-permute-start(bf16[256,256]{1,0:T(8,128)(2,1)S(1)} %pad_maximum_fusion.17), channel_id=1, source_target_pairs={{8,0},{16,8},{24,16},{9,1},{17,9},{25,17},{10,2},{18,10},{26,18},{... | collective-permute-start | bytes 393224 | tf_op jit(solution)/shard_map/ppermute | solution.py:82
  193.7 8.1 %copy-start.2 = (bf16[1024,256]{0,1:T(8,128)(2,1)S(1)}, bf16[1024,256]{0,1:T(8,128)(2,1)}, u32[]{:S(2)}) copy-start(bf16[1024,256]{0,1:T(8,128)(2,1)} %get-tuple-element.56) | copy-start | bytes 1572868
  195.8 3.6 %copy-start.5 = (bf16[1024,256]{1,0:T(8,128)(2,1)S(1)}, bf16[1024,256]{1,0:T(8,128)(2,1)}, u32[]{:S(2)}) copy-start(bf16[1024,256]{1,0:T(8,128)(2,1)} %copy.95) | copy-start | bytes 1572868
  199.4 13.0 %collective-permute-start.18 = (bf16[256,256]{1,0:T(8,128)(2,1)S(1)}, bf16[256,256]{1,0:T(8,128)(2,1)}, u32[]{:S(2)}, u32[]{:S(2)}) collective-permute-start(bf16[256,256]{1,0:T(8,128)(2,1)S(1)} %pad_maximum_fusion.18), channel_id=1, source_target_pairs={{0,8},{8,16},{16,24},{1,9},{9,17},{17,25},{2,10},{10,18},{18,26},{... | collective-permute-start | bytes 393224 | tf_op jit(solution)/shard_map/ppermute | solution.py:81
  205.0 9.3 %collective-permute-start.20 = (bf16[1024,64]{0,1:T(8,128)(2,1)}, bf16[1024,64]{0,1:T(8,128)(2,1)S(1)}, u32[]{:S(2)}, u32[]{:S(2)}) collective-permute-start(bf16[1024,64]{0,1:T(8,128)(2,1)} %get-tuple-element.12), channel_id=1, source_target_pairs={{0,1},{1,2},{2,3},{3,4},{4,5},{5,6},{6,7},{8,9},{9,10},{10,11},{11... | collective-permute-start | bytes 393224 | tf_op jit(solution)/shard_map/ppermute | solution.py:27
  209.9 7.4 %collective-permute-start.21 = (bf16[1024,64]{0,1:T(8,128)(2,1)S(1)}, bf16[1024,64]{0,1:T(8,128)(2,1)S(1)}, u32[]{:S(2)}, u32[]{:S(2)}) collective-permute-start(bf16[1024,64]{0,1:T(8,128)(2,1)S(1)} %get-tuple-element.13), channel_id=1, source_target_pairs={{1,0},{2,1},{3,2},{4,3},{5,4},{6,5},{7,6},{9,8},{10,9},{11,10},{12... | collective-permute-start | bytes 393224 | tf_op jit(solution)/shard_map/ppermute | solution.py:28
  211.2 6.5 %collective-permute-start.19 = (bf16[256,256]{1,0:T(8,128)(2,1)S(1)}, bf16[256,256]{1,0:T(8,128)(2,1)S(1)}, u32[]{:S(2)}, u32[]{:S(2)}) collective-permute-start(bf16[256,256]{1,0:T(8,128)(2,1)S(1)} %pad_maximum_fusion.19), channel_id=1, source_target_pairs={{8,0},{16,8},{24,16},{9,1},{17,9},{25,17},{10,2},{18,10},{26,18},{... | collective-permute-start | bytes 393224 | tf_op jit(solution)/shard_map/ppermute | solution.py:82
Sparse Core Ops, SparseCore 0:
  9.6 25.2 all-gather.1
  84.9 35.9 all-reduce.2

commit v2 on v1

--- a/solution.py
+++ b/solution.py
@@ -106,8 +106,10 @@
     bins = owner * (nodes_dev * T_DEV) + obs_cell
     local_counts = jax.ops.segment_sum(
         obs_weight, bins, num_segments=space_count * nodes_dev * T_DEV
+    ).reshape(space_count, nodes_dev * T_DEV)
+    counted = jnp.sum(
+        lax.all_to_all(local_counts, "space", split_axis=0, concat_axis=0, tiled=True), axis=0
     )
-    counted = lax.psum_scatter(local_counts, "space", scatter_dimension=0, tiled=True)
     obs_diag = jnp.repeat(counted.reshape(NODES_DEV, T_DEV), PROBES, axis=1)
     full_diag = base_diag + obs_diag
     local_diag = kappa[:, None] + obs_diag

time: 235 us -> 202 us (0.86)
  waiting for transfers between devices: 48.4 us -> 16.7 us
  starting transfers between devices: 51.8 us -> 58.1 us
  local copies, waits for them, and re-layouts: 44.4 us -> 41 us
    unnamed x3 -> x1, waiting for transfers between devices: 34 us -> 0.68 us
    all_to_all x0 -> x1, starting transfers between devices: none -> 4.83 us  [shards(): lax.all_to_all(local_counts, 'space', split_axis=0, concat_axis=0, tiled=...]
    unnamed x70 -> x48, local copies, waits for them, and re-layouts: 12.9 us -> 11.5 us
  transfers between devices with their start and end apart: 24 -> 24, of which waited for: 5 -> 5; matrix products, arithmetic and copies ran while one was open for 30% -> 31% of each run, Pallas kernels for 0% -> 0%
where the time goes in v2:
time: 202 us; the launch traced here: 200 us
  starting transfers between devices  58.1 us (29%)
  local copies, waits for them, and re-layouts  41 us (20%)
  matrix products  39.1 us (19%)
  between operations  22.2 us (11%)
  other arithmetic  16.9 us (8%)
  waiting for transfers between devices  16.7 us (8%)
  blocking collectives  5.76 us (3%)
    ppermute x5, starting transfers between devices, with_halo(): before = lax.ppermute(last, axis, up)  23.6 us
    ppermute x5, waiting for transfers between devices, with_halo(): after = lax.ppermute(initial, axis, down)  14.6 us
    dot_general x5, matrix products, spatial(): jnp.dot(upper_part, upper, preferred_element_type=jnp.float32)  14.4 us
    ppermute x5, starting transfers between devices, spatial(): lower = lax.ppermute(pick_blocks(blocks, upper_wants), 'space', up)  12.9 us
    dot_general x5, matrix products, spatial(): total = jnp.dot(own_part, field, preferred_element_type=jnp.float32)  12.8 us
    scatter-add x1, other arithmetic, shards(): jax.ops.segment_sum(obs_weight, bins, num_segments=space_count * nodes_de...  11.8 us
    unnamed x48, local copies, waits for them, and re-layouts  11.5 us
    gather x1, local copies, waits for them, and re-layouts, shards(): coef_rows = svc_all[owner * nodes_dev + obs_cell // T_DEV]  10.4 us
  transfers between devices with their start and end apart: 24, of which 5 were waited for; matrix products, arithmetic and copies ran while one was open for 31% of the time, Pallas kernels for 0%

profile of v2, /device:TPU:0, one launch (start us, length us, event | category | flops | bytes accessed | tf_op | source)
XLA Modules:
  0.0 199.6 jit_solution(16367063319526638481)
XLA Ops:
  7.9 0.8 fusion.82
  8.7 2.4 %collective-permute-start.2 = (s32[2]{0:T(128)S(1)}, s32[2]{0:T(128)S(1)}, u32[]{:S(2)}, u32[]{:S(2)}) collective-permute-start(s32[2]{0:T(128)S(1)} %get-tuple-element.48), channel_id=1, source_target_pairs={{0,8},{8,16},{16,24},{1,9},{9,17},{17,25},{2,10},{10,18},{18,26},{... | collective-permute-start | bytes 32 | tf_op jit(solution)/shard_map/ppermute | solution.py:71
  11.1 1.3 collective-permute-start
  14.0 1.2 copy.81
  15.3 4.4 %copy.82 = bf16[8,128,128]{0,2,1:T(8,128)(2,1)} copy(bf16[8,128,128]{2,1,0:T(8,128)(2,1)} %param.16) | data formatting | bytes 524288 | tf_op args[4]
  19.7 1.9 gather_fusion
  22.9 4.9 %collective-permute-start.4 = (bf16[1024,64]{0,1:T(8,128)(2,1)}, bf16[1024,64]{0,1:T(8,128)(2,1)}, u32[]{:S(2)}, u32[]{:S(2)}) collective-permute-start(bf16[1024,64]{0,1:T(8,128)(2,1)} %get-tuple-element.34), channel_id=1, source_target_pairs={{0,1},{1,2},{2,3},{3,4},{4,5},{5,6},{6,7},{8,9},{9,10},{10,11},{11... | collective-permute-start | bytes 393224 | tf_op jit(solution)/shard_map/ppermute | solution.py:27
  27.7 1.3 collective-permute-start.5
  29.0 0.8 convert.8
  29.9 1.0 copy.122
  30.9 3.1 %add_convert_fusion = bf16[8,12,128,128]{3,1,2,0:T(8,128)(2,1)S(1)} fusion(f32[8,128,128]{2,1,0:T(8,128)} %convert.8, f32[8,12]{1,0:T(8,128)S(1)} %fusion.75, bf16[8,8,128,128]{3,2,1,0:T(8,128)(2,1)S(1)} %copy-done, s32[8,8]{1,0:T(8,128)S(1)} %copy-done.18), kind=kOutput, calls=%fused_computation.3 | convolution fusion | flops 29885184 | bytes 5767808 | tf_op jit(solution)/shard_map/bkm,bkij->bimj/dot_general | solution.py:60
  34.1 1.6 copy.135
  35.7 1.6 copy-done.1
  37.3 1.7 fusion.37
  47.6 1.0 dynamic-slice_bitcast_fusion.17
  48.6 4.7 %collective-permute-start.1 = (bf16[256,256]{1,0:T(8,128)(2,1)S(1)}, bf16[256,256]{1,0:T(8,128)(2,1)}, u32[]{:S(2)}, u32[]{:S(2)}) collective-permute-start(bf16[256,256]{1,0:T(8,128)(2,1)S(1)} %pad_maximum_fusion.10), channel_id=1, source_target_pairs={{0,8},{8,16},{16,24},{1,9},{9,17},{17,25},{2,10},{10,18},{18,26},{... | collective-permute-start | bytes 393224 | tf_op jit(solution)/shard_map/ppermute | solution.py:81
  53.4 1.3 collective-permute-start.3
  54.7 10.4 %gather_fusion.1 = bf16[2048,256]{1,0:T(8,128)(2,1)} fusion(bf16[4096,256]{1,0:T(8,128)(2,1)} %all-gather.2.cloned.1.call-done, s32[2048]{0:T(1024)S(1)} %get-tuple-element.42), kind=kCustom, calls=%fused_computation.1 | custom fusion | bytes 2105344 | tf_op jit(solution)/shard_map/gather | solution.py:103
  65.1 1.9 fusion
  67.0 11.8 %scatter_custom_fusion = f32[16384]{0:T(1024)} fusion(s32[2048]{0:T(1024)S(1)} %get-tuple-element.43, f32[2048]{0:T(1024)S(1)} %exp.3, f32[]{:T(128)} %constant.72.clone.1), kind=kCustom, calls=%fused_computation.137 | custom fusion | flops 2048 | bytes 65540 | tf_op jit(solution)/shard_map/scatter-add | solution.py:107
  78.8 4.8 %all-to-all-start = ((f32[4,1,4096]{2,1,0:T(1,128)}), f32[4,1,4096]{2,1,0:T(1,128)S(1)}, u32[]{:S(2)}, u32[]{:S(2)}) async-start(f32[4,1,4096]{2,1,0:T(1,128)} %bitcast.16), calls=%async_computation | async-start | bytes 131072 | tf_op jit(solution)/shard_map/all_to_all | solution.py:111
  83.6 2.8 %convolution_add_fusion.9 = f32[1024,256]{0,1:T(8,128)} fusion(f32[1024,256]{0,1:T(8,128)} %fusion.37, bf16[256,256]{1,0:T(8,128)(2,1)} %collective-permute-done.1, bf16[1024,1536]{1,0:T(8,128)(2,1)} %bitcast.98), kind=kOutput, calls=%fused_computation.42 | convolution fusion | flops 134479872 | bytes 2752512 | tf_op jit(solution)/shard_map/dot_general | solution.py:84
  86.4 1.3 all-to-all-done
  87.8 1.3 reshape.56
  89.2 1.2 copy.91
  90.8 4.0 %fusion.84 = (bf16[1024,256]{0,1:T(8,128)(2,1)}, f32[1024,256]{0,1:T(8,128)}) fusion(f32[1024,256]{0,1:T(8,128)S(1)} %get-tuple-element.41, f32[1024,256]{0,1:T(8,128)S(1)} %get-tuple-element.40, bf16[1024,64]{0,1:T(8,128)(2,1)} %collective-permute-done.5, bf16[1024,256]{0,1:T(8,128)(2,1)S(1)} %fusion.55, bf16[1024,64]{0,1:T(8,128)(2,1)} %collective-permute-done.4, ...), kind=kOutput, calls=%fused_computation.168 | convolution fusion | flops 141557760 | bytes 6695936 | tf_op jit(solution)/shard_map/dot_general | solution.py:85
  94.8 2.2 %copy.123 = bf16[1024,256]{1,0:T(8,128)(2,1)} copy(bf16[1024,256]{0,1:T(8,128)(2,1)} %get-tuple-element.52) | data formatting | bytes 1048576 | tf_op jit(solution)/shard_map/reshape | solution.py:80
  97.0 2.6 %fusion.35 = f32[1024,256]{0,1:T(8,128)S(1)} fusion(bf16[1024,256]{0,1:T(8,128)(2,1)} %get-tuple-element.52, bf16[1024,1536]{1,0:T(8,128)(2,1)} %bitcast.100), kind=kOutput, calls=%fused_computation.64 | convolution fusion | flops 536870912 | bytes 3670016 | tf_op jit(solution)/shard_map/dot_general | solution.py:83
  99.6 1.7 collective-permute-start.6
  101.5 4.6 %collective-permute-start.8 = (bf16[1024,64]{0,1:T(8,128)(2,1)S(1)}, bf16[1024,64]{0,1:T(8,128)(2,1)S(1)}, u32[]{:S(2)}, u32[]{:S(2)}) collective-permute-start(bf16[1024,64]{0,1:T(8,128)(2,1)S(1)} %get-tuple-element.28), channel_id=1, source_target_pairs={{0,1},{1,2},{2,3},{3,4},{4,5},{5,6},{6,7},{8,9},{9,10},{10,11},{11... | collective-permute-start | bytes 393224 | tf_op jit(solution)/shard_map/ppermute | solution.py:27
  106.0 1.3 collective-permute-start.9
  107.4 1.5 collective-permute-start.7
  108.8 1.4 convolution_add_fusion.7
  110.2 4.0 %collective-permute-done.9 = bf16[1024,64]{0,1:T(8,128)(2,1)S(1)} collective-permute-done((bf16[1024,64]{0,1:T(8,128)(2,1)S(1)}, bf16[1024,64]{0,1:T(8,128)(2,1)S(1)}, u32[]{:S(2)}, u32[]{:S(2)}) %collective-permute-start.9) | collective-permute-done | bytes 131104 | tf_op jit(solution)/shard_map/ppermute | solution.py:28
  114.3 3.0 %fusion.85 = (bf16[1024,256]{0,1:T(8,128)(2,1)}, f32[1024,256]{0,1:T(8,128)}) fusion(f32[1024,256]{0,1:T(8,128)S(1)} %copy-done.20, f32[1024,256]{0,1:T(8,128)S(1)} %copy-done.12, f32[1024,256]{0,1:T(8,128)S(1)} %fusion.4, bf16[1024,64]{0,1:T(8,128)(2,1)S(1)} %collective-permute-done.9, bf16[1024,256]{0,1:T(8,128)(2,1)S(1)} %copy-done.2, ...), kind=kOutput, calls=%fused_computation.169 | convolution fusion | flops 140247040 | bytes 7735296 | tf_op jit(solution)/shard_map/dot_general | solution.py:85
  117.3 2.2 %copy.124 = bf16[1024,256]{1,0:T(8,128)(2,1)} copy(bf16[1024,256]{0,1:T(8,128)(2,1)} %get-tuple-element.54) | data formatting | bytes 1048576 | tf_op jit(solution)/shard_map/reshape | solution.py:80
  119.5 2.5 %fusion.33 = f32[1024,256]{0,1:T(8,128)S(1)} fusion(bf16[1024,256]{0,1:T(8,128)(2,1)} %get-tuple-element.54, bf16[1024,1536]{1,0:T(8,128)(2,1)} %bitcast.103), kind=kOutput, calls=%fused_computation.62 | convolution fusion | flops 536870912 | bytes 3670016 | tf_op jit(solution)/shard_map/dot_general | solution.py:83
  122.2 2.3 %collective-permute-start.10 = (bf16[256,256]{1,0:T(8,128)(2,1)S(1)}, bf16[256,256]{1,0:T(8,128)(2,1)S(1)}, u32[]{:S(2)}, u32[]{:S(2)}) collective-permute-start(bf16[256,256]{1,0:T(8,128)(2,1)S(1)} %pad_maximum_fusion.14), channel_id=1, source_target_pairs={{0,8},{8,16},{16,24},{1,9},{9,17},{17,25},{2,10},{10,18},{18,26},{... | collective-permute-start | bytes 393224 | tf_op jit(solution)/shard_map/ppermute | solution.py:81
  124.6 4.4 %collective-permute-start.12 = (bf16[1024,64]{0,1:T(8,128)(2,1)S(1)}, bf16[1024,64]{0,1:T(8,128)(2,1)S(1)}, u32[]{:S(2)}, u32[]{:S(2)}) collective-permute-start(bf16[1024,64]{0,1:T(8,128)(2,1)S(1)} %get-tuple-element.22), channel_id=1, source_target_pairs={{0,1},{1,2},{2,3},{3,4},{4,5},{5,6},{6,7},{8,9},{9,10},{10,11},{11... | collective-permute-start | bytes 393224 | tf_op jit(solution)/shard_map/ppermute | solution.py:27
  129.0 1.3 collective-permute-start.13
  130.4 1.3 collective-permute-start.11
  131.7 1.4 convolution_add_fusion.5
  133.1 3.8 %collective-permute-done.13 = bf16[1024,64]{0,1:T(8,128)(2,1)S(1)} collective-permute-done((bf16[1024,64]{0,1:T(8,128)(2,1)S(1)}, bf16[1024,64]{0,1:T(8,128)(2,1)S(1)}, u32[]{:S(2)}, u32[]{:S(2)}) %collective-permute-start.13) | collective-permute-done | bytes 131104 | tf_op jit(solution)/shard_map/ppermute | solution.py:28
  136.9 2.8 %fusion.86 = (bf16[1024,256]{0,1:T(8,128)(2,1)S(1)}, f32[1024,256]{0,1:T(8,128)}) fusion(f32[1024,256]{0,1:T(8,128)S(1)} %copy-done.21, f32[1024,256]{0,1:T(8,128)S(1)} %copy-done.13, f32[1024,256]{0,1:T(8,128)S(1)} %fusion.3, bf16[1024,64]{0,1:T(8,128)(2,1)S(1)} %collective-permute-done.13, bf16[1024,256]{0,1:T(8,128)(2,1)S(1)} %copy-done.5, ...), kind=kOutput, calls=%fused_computation.170 | convolution fusion | flops 140247040 | bytes 7735296 | tf_op jit(solution)/shard_map/dot_general | solution.py:85
  139.7 1.0 copy.125
  140.7 2.4 %fusion.31 = f32[1024,256]{0,1:T(8,128)S(1)} fusion(bf16[1024,256]{0,1:T(8,128)(2,1)S(1)} %get-tuple-element.56, bf16[1024,1536]{1,0:T(8,128)(2,1)} %bitcast.106), kind=kOutput, calls=%fused_computation.60 | convolution fusion | flops 536870912 | bytes 3670016 | tf_op jit(solution)/shard_map/dot_general | solution.py:83
  143.2 1.8 collective-permute-start.14
  145.2 4.9 %collective-permute-start.16 = (bf16[1024,64]{0,1:T(8,128)(2,1)S(1)}, bf16[1024,64]{0,1:T(8,128)(2,1)S(1)}, u32[]{:S(2)}, u32[]{:S(2)}) collective-permute-start(bf16[1024,64]{0,1:T(8,128)(2,1)S(1)} %get-tuple-element.16), channel_id=1, source_target_pairs={{0,1},{1,2},{2,3},{3,4},{4,5},{5,6},{6,7},{8,9},{9,10},{10,11},{11... | collective-permute-start | bytes 393224 | tf_op jit(solution)/shard_map/ppermute | solution.py:27
  150.1 1.3 collective-permute-start.17
  151.4 1.3 collective-permute-start.15
  152.7 1.4 convolution_add_fusion.3
  154.1 3.8 %collective-permute-done.17 = bf16[1024,64]{0,1:T(8,128)(2,1)S(1)} collective-permute-done((bf16[1024,64]{0,1:T(8,128)(2,1)S(1)}, bf16[1024,64]{0,1:T(8,128)(2,1)S(1)}, u32[]{:S(2)}, u32[]{:S(2)}) %collective-permute-start.17) | collective-permute-done | bytes 131104 | tf_op jit(solution)/shard_map/ppermute | solution.py:28
  157.9 3.0 %fusion.87 = (bf16[1024,256]{0,1:T(8,128)(2,1)}, f32[1024,256]{0,1:T(8,128)}) fusion(f32[1024,256]{0,1:T(8,128)S(1)} %copy-done.19, f32[1024,256]{0,1:T(8,128)S(1)} %copy-done.14, f32[1024,256]{0,1:T(8,128)S(1)} %fusion.2, bf16[1024,64]{0,1:T(8,128)(2,1)S(1)} %collective-permute-done.17, bf16[1024,256]{0,1:T(8,128)(2,1)S(1)} %get-tuple-element.56, ...), kind=kOutput, calls=%fused_computation.171 | convolution fusion | flops 140247040 | bytes 7735296 | tf_op jit(solution)/shard_map/dot_general | solution.py:85
  161.0 2.1 %copy.126 = bf16[1024,256]{1,0:T(8,128)(2,1)} copy(bf16[1024,256]{0,1:T(8,128)(2,1)} %get-tuple-element.58) | data formatting | bytes 1048576 | tf_op jit(solution)/shard_map/reshape | solution.py:80
  163.1 3.6 %fusion.39 = f32[1024,256]{0,1:T(8,128)} fusion(bf16[1024,256]{0,1:T(8,128)(2,1)} %get-tuple-element.58, bf16[1024,1536]{1,0:T(8,128)(2,1)} %bitcast.109), kind=kOutput, calls=%fused_computation.68 | convolution fusion | flops 536870912 | bytes 3670016 | tf_op jit(solution)/shard_map/dot_general | solution.py:83
  166.7 2.3 %collective-permute-start.18 = (bf16[256,256]{1,0:T(8,128)(2,1)S(1)}, bf16[256,256]{1,0:T(8,128)(2,1)}, u32[]{:S(2)}, u32[]{:S(2)}) collective-permute-start(bf16[256,256]{1,0:T(8,128)(2,1)S(1)} %pad_maximum_fusion.18), channel_id=1, source_target_pairs={{0,8},{8,16},{16,24},{1,9},{9,17},{17,25},{2,10},{10,18},{18,26},{... | collective-permute-start | bytes 393224 | tf_op jit(solution)/shard_map/ppermute | solution.py:81
  169.7 2.5 %copy.111 = f32[1024,256]{1,0:T(8,128)} copy(f32[1024,256]{0,1:T(8,128)} %get-tuple-element.59) | data formatting | bytes 2097152
  172.3 4.9 %collective-permute-start.20 = (bf16[1024,64]{0,1:T(8,128)(2,1)}, bf16[1024,64]{0,1:T(8,128)(2,1)S(1)}, u32[]{:S(2)}, u32[]{:S(2)}) collective-permute-start(bf16[1024,64]{0,1:T(8,128)(2,1)} %get-tuple-element.14), channel_id=1, source_target_pairs={{0,1},{1,2},{2,3},{3,4},{4,5},{5,6},{6,7},{8,9},{9,10},{10,11},{11... | collective-permute-start | bytes 393224 | tf_op jit(solution)/shard_map/ppermute | solution.py:27
  177.1 1.3 collective-permute-start.21
  178.4 1.3 collective-permute-start.19
  179.7 1.8 convolution_add_fusion.1
  181.6 2.9 %collective-permute-done.21 = bf16[1024,64]{0,1:T(8,128)(2,1)S(1)} collective-permute-done((bf16[1024,64]{0,1:T(8,128)(2,1)S(1)}, bf16[1024,64]{0,1:T(8,128)(2,1)S(1)}, u32[]{:S(2)}, u32[]{:S(2)}) %collective-permute-start.21) | collective-permute-done | bytes 131104 | tf_op jit(solution)/shard_map/ppermute | solution.py:28
  184.9 1.5 fusion.30
  186.4 5.8 %psum.7 = f32[2,256]{1,0:T(2,128)S(1)} all-reduce(f32[2,256]{1,0:T(2,128)S(1)} %pad_maximum_fusion.20), channel_id=1, replica_groups=mesh['space'=4,'tm'=8] {'space'}, use_global_device_ids=true, to_apply=%region_4.5 | all-reduce | flops 512 | bytes 4096 | tf_op jit(solution)/shard_map/psum | solution.py:137
  (106 shorter events, 7.6 us)
Async XLA Ops:
  7.2 23.7 %copy-start = (bf16[8,8,128,128]{3,2,1,0:T(8,128)(2,1)S(1)}, bf16[8,8,128,128]{3,2,1,0:T(8,128)(2,1)}, u32[]{:S(2)}) copy-start(bf16[8,8,128,128]{3,2,1,0:T(8,128)(2,1)} %param.17) | copy-start | bytes 6291460
  7.2 14.6 %copy-start.15 = (f32[1024]{0:T(1024)S(1)}, f32[1024]{0:T(1024)}, u32[]{:S(2)}) copy-start(f32[1024]{0:T(1024)} %param.13) | copy-start | bytes 12292
  7.2 47.5 %all-gather.2.cloned.1.call-start = ((), (), s32[]{:S(2)}) async-start(), calls=%async_computation.1 | async-start | bytes 2621440 | tf_op jit(solution)/shard_map/all_gather | solution.py:101
  8.7 30.3 %collective-permute-start.2 = (s32[2]{0:T(128)S(1)}, s32[2]{0:T(128)S(1)}, u32[]{:S(2)}, u32[]{:S(2)}) collective-permute-start(s32[2]{0:T(128)S(1)} %get-tuple-element.48), channel_id=1, source_target_pairs={{0,8},{8,16},{16,24},{1,9},{9,17},{17,25},{2,10},{10,18},{18,26},{... | collective-permute-start | bytes 32 | tf_op jit(solution)/shard_map/ppermute | solution.py:71
  11.1 31.1 %collective-permute-start = (s32[2]{0:T(128)S(1)}, s32[2]{0:T(128)S(1)}, u32[]{:S(2)}, u32[]{:S(2)}) collective-permute-start(s32[2]{0:T(128)S(1)} %get-tuple-element.49), channel_id=1, source_target_pairs={{8,0},{16,8},{24,16},{9,1},{17,9},{25,17},{10,2},{18,10},{26,18},{... | collective-permute-start | bytes 32 | tf_op jit(solution)/shard_map/ppermute | solution.py:70
  15.3 13.8 %copy-start.10 = (bf16[8,128,128]{2,1,0:T(8,128)(2,1)S(1)}, bf16[8,128,128]{2,1,0:T(8,128)(2,1)}, u32[]{:S(2)}) copy-start(bf16[8,128,128]{2,1,0:T(8,128)(2,1)} %param.16) | copy-start | bytes 786436
  15.3 15.6 %copy-start.18 = (s32[8,8]{1,0:T(8,128)S(1)}, s32[8,8]{1,0:T(8,128)}, u32[]{:S(2)}) copy-start(s32[8,8]{1,0:T(8,128)} %param.18) | copy-start | bytes 772
  22.9 67.9 %collective-permute-start.4 = (bf16[1024,64]{0,1:T(8,128)(2,1)}, bf16[1024,64]{0,1:T(8,128)(2,1)}, u32[]{:S(2)}, u32[]{:S(2)}) collective-permute-start(bf16[1024,64]{0,1:T(8,128)(2,1)} %get-tuple-element.34), channel_id=1, source_target_pairs={{0,1},{1,2},{2,3},{3,4},{4,5},{5,6},{6,7},{8,9},{9,10},{10,11},{11... | collective-permute-start | bytes 393224 | tf_op jit(solution)/shard_map/ppermute | solution.py:27
  27.7 63.0 %collective-permute-start.5 = (bf16[1024,64]{0,1:T(8,128)(2,1)}, bf16[1024,64]{0,1:T(8,128)(2,1)}, u32[]{:S(2)}, u32[]{:S(2)}) collective-permute-start(bf16[1024,64]{0,1:T(8,128)(2,1)} %get-tuple-element.35), channel_id=1, source_target_pairs={{1,0},{2,1},{3,2},{4,3},{5,4},{6,5},{7,6},{9,8},{10,9},{11,10},{12... | collective-permute-start | bytes 393224 | tf_op jit(solution)/shard_map/ppermute | solution.py:28
  34.0 1.6 copy-start.16
  34.1 1.7 copy-start.17
  35.7 1.6 copy-start.1
  48.6 35.0 %collective-permute-start.1 = (bf16[256,256]{1,0:T(8,128)(2,1)S(1)}, bf16[256,256]{1,0:T(8,128)(2,1)}, u32[]{:S(2)}, u32[]{:S(2)}) collective-permute-start(bf16[256,256]{1,0:T(8,128)(2,1)S(1)} %pad_maximum_fusion.10), channel_id=1, source_target_pairs={{0,8},{8,16},{16,24},{1,9},{9,17},{17,25},{2,10},{10,18},{18,26},{... | collective-permute-start | bytes 393224 | tf_op jit(solution)/shard_map/ppermute | solution.py:81
  53.4 37.4 %collective-permute-start.3 = (bf16[256,256]{1,0:T(8,128)(2,1)S(1)}, bf16[256,256]{1,0:T(8,128)(2,1)}, u32[]{:S(2)}, u32[]{:S(2)}) collective-permute-start(bf16[256,256]{1,0:T(8,128)(2,1)S(1)} %pad_maximum_fusion.11), channel_id=1, source_target_pairs={{8,0},{16,8},{24,16},{9,1},{17,9},{25,17},{10,2},{18,10},{26,18},{... | collective-permute-start | bytes 393224 | tf_op jit(solution)/shard_map/ppermute | solution.py:82
  78.8 9.0 %all-to-all-start = ((f32[4,1,4096]{2,1,0:T(1,128)}), f32[4,1,4096]{2,1,0:T(1,128)S(1)}, u32[]{:S(2)}, u32[]{:S(2)}) async-start(f32[4,1,4096]{2,1,0:T(1,128)} %bitcast.16), calls=%async_computation | async-start | bytes 131072 | tf_op jit(solution)/shard_map/all_to_all | solution.py:111
  90.7 4.1 %copy-start.11 = (f32[1024,256]{0,1:T(8,128)}, f32[1024,256]{0,1:T(8,128)S(1)}, u32[]{:S(2)}) copy-start(f32[1024,256]{0,1:T(8,128)S(1)} %get-tuple-element.41) | copy-start | bytes 3145732
  94.8 6.5 %copy-start.2 = (bf16[1024,256]{0,1:T(8,128)(2,1)S(1)}, bf16[1024,256]{0,1:T(8,128)(2,1)}, u32[]{:S(2)}) copy-start(bf16[1024,256]{0,1:T(8,128)(2,1)} %get-tuple-element.52) | copy-start | bytes 1572868
  97.0 2.6 %copy-start.7 = (bf16[1024,256]{1,0:T(8,128)(2,1)S(1)}, bf16[1024,256]{1,0:T(8,128)(2,1)}, u32[]{:S(2)}) copy-start(bf16[1024,256]{1,0:T(8,128)(2,1)} %copy.123) | copy-start | bytes 1572868
  99.5 14.8 %copy-start.12 = (f32[1024,256]{0,1:T(8,128)S(1)}, f32[1024,256]{0,1:T(8,128)}, u32[]{:S(2)}) copy-start(f32[1024,256]{0,1:T(8,128)} %copy-done.11) | copy-start | bytes 3145732
  99.5 14.8 %copy-start.20 = (f32[1024,256]{0,1:T(8,128)S(1)}, f32[1024,256]{0,1:T(8,128)}, u32[]{:S(2)}) copy-start(f32[1024,256]{0,1:T(8,128)} %get-tuple-element.53) | copy-start | bytes 3145732
  99.6 9.2 %collective-permute-start.6 = (bf16[256,256]{1,0:T(8,128)(2,1)S(1)}, bf16[256,256]{1,0:T(8,128)(2,1)S(1)}, u32[]{:S(2)}, u32[]{:S(2)}) collective-permute-start(bf16[256,256]{1,0:T(8,128)(2,1)S(1)} %pad_maximum_fusion.12), channel_id=1, source_target_pairs={{0,8},{8,16},{16,24},{1,9},{9,17},{17,25},{2,10},{10,18},{18,26},{... | collective-permute-start | bytes 393224 | tf_op jit(solution)/shard_map/ppermute | solution.py:81
  101.5 8.8 %collective-permute-start.8 = (bf16[1024,64]{0,1:T(8,128)(2,1)S(1)}, bf16[1024,64]{0,1:T(8,128)(2,1)S(1)}, u32[]{:S(2)}, u32[]{:S(2)}) collective-permute-start(bf16[1024,64]{0,1:T(8,128)(2,1)S(1)} %get-tuple-element.28), channel_id=1, source_target_pairs={{0,1},{1,2},{2,3},{3,4},{4,5},{5,6},{6,7},{8,9},{9,10},{10,11},{11... | collective-permute-start | bytes 393224 | tf_op jit(solution)/shard_map/ppermute | solution.py:27
  106.0 8.3 %collective-permute-start.9 = (bf16[1024,64]{0,1:T(8,128)(2,1)S(1)}, bf16[1024,64]{0,1:T(8,128)(2,1)S(1)}, u32[]{:S(2)}, u32[]{:S(2)}) collective-permute-start(bf16[1024,64]{0,1:T(8,128)(2,1)S(1)} %get-tuple-element.29), channel_id=1, source_target_pairs={{1,0},{2,1},{3,2},{4,3},{5,4},{6,5},{7,6},{9,8},{10,9},{11,10},{12... | collective-permute-start | bytes 393224 | tf_op jit(solution)/shard_map/ppermute | solution.py:28
  107.4 6.9 %collective-permute-start.7 = (bf16[256,256]{1,0:T(8,128)(2,1)S(1)}, bf16[256,256]{1,0:T(8,128)(2,1)S(1)}, u32[]{:S(2)}, u32[]{:S(2)}) collective-permute-start(bf16[256,256]{1,0:T(8,128)(2,1)S(1)} %pad_maximum_fusion.13), channel_id=1, source_target_pairs={{8,0},{16,8},{24,16},{9,1},{17,9},{25,17},{10,2},{18,10},{26,18},{... | collective-permute-start | bytes 393224 | tf_op jit(solution)/shard_map/ppermute | solution.py:82
  117.3 7.1 %copy-start.4 = (bf16[1024,256]{0,1:T(8,128)(2,1)S(1)}, bf16[1024,256]{0,1:T(8,128)(2,1)}, u32[]{:S(2)}) copy-start(bf16[1024,256]{0,1:T(8,128)(2,1)} %get-tuple-element.54) | copy-start | bytes 1572868
  119.5 2.6 %copy-start.8 = (bf16[1024,256]{1,0:T(8,128)(2,1)S(1)}, bf16[1024,256]{1,0:T(8,128)(2,1)}, u32[]{:S(2)}) copy-start(bf16[1024,256]{1,0:T(8,128)(2,1)} %copy.124) | copy-start | bytes 1572868
  122.1 14.8 %copy-start.5 = (bf16[1024,256]{0,1:T(8,128)(2,1)S(1)}, bf16[1024,256]{0,1:T(8,128)(2,1)}, u32[]{:S(2)}) copy-start(bf16[1024,256]{0,1:T(8,128)(2,1)} %get-tuple-element.54) | copy-start | bytes 1572868
  122.1 14.8 %copy-start.13 = (f32[1024,256]{0,1:T(8,128)S(1)}, f32[1024,256]{0,1:T(8,128)}, u32[]{:S(2)}) copy-start(f32[1024,256]{0,1:T(8,128)} %copy-done.11) | copy-start | bytes 3145732
  122.1 14.8 %copy-start.21 = (f32[1024,256]{0,1:T(8,128)S(1)}, f32[1024,256]{0,1:T(8,128)}, u32[]{:S(2)}) copy-start(f32[1024,256]{0,1:T(8,128)} %get-tuple-element.55) | copy-start | bytes 3145732
  122.2 9.5 %collective-permute-start.10 = (bf16[256,256]{1,0:T(8,128)(2,1)S(1)}, bf16[256,256]{1,0:T(8,128)(2,1)S(1)}, u32[]{:S(2)}, u32[]{:S(2)}) collective-permute-start(bf16[256,256]{1,0:T(8,128)(2,1)S(1)} %pad_maximum_fusion.14), channel_id=1, source_target_pairs={{0,8},{8,16},{16,24},{1,9},{9,17},{17,25},{2,10},{10,18},{18,26},{... | collective-permute-start | bytes 393224 | tf_op jit(solution)/shard_map/ppermute | solution.py:81
  124.6 8.5 %collective-permute-start.12 = (bf16[1024,64]{0,1:T(8,128)(2,1)S(1)}, bf16[1024,64]{0,1:T(8,128)(2,1)S(1)}, u32[]{:S(2)}, u32[]{:S(2)}) collective-permute-start(bf16[1024,64]{0,1:T(8,128)(2,1)S(1)} %get-tuple-element.22), channel_id=1, source_target_pairs={{0,1},{1,2},{2,3},{3,4},{4,5},{5,6},{6,7},{8,9},{9,10},{10,11},{11... | collective-permute-start | bytes 393224 | tf_op jit(solution)/shard_map/ppermute | solution.py:27
  129.0 7.8 %collective-permute-start.13 = (bf16[1024,64]{0,1:T(8,128)(2,1)S(1)}, bf16[1024,64]{0,1:T(8,128)(2,1)S(1)}, u32[]{:S(2)}, u32[]{:S(2)}) collective-permute-start(bf16[1024,64]{0,1:T(8,128)(2,1)S(1)} %get-tuple-element.23), channel_id=1, source_target_pairs={{1,0},{2,1},{3,2},{4,3},{5,4},{6,5},{7,6},{9,8},{10,9},{11,10},{12... | collective-permute-start | bytes 393224 | tf_op jit(solution)/shard_map/ppermute | solution.py:28
  130.4 6.5 %collective-permute-start.11 = (bf16[256,256]{1,0:T(8,128)(2,1)S(1)}, bf16[256,256]{1,0:T(8,128)(2,1)S(1)}, u32[]{:S(2)}, u32[]{:S(2)}) collective-permute-start(bf16[256,256]{1,0:T(8,128)(2,1)S(1)} %pad_maximum_fusion.15), channel_id=1, source_target_pairs={{8,0},{16,8},{24,16},{9,1},{17,9},{25,17},{10,2},{18,10},{26,18},{... | collective-permute-start | bytes 393224 | tf_op jit(solution)/shard_map/ppermute | solution.py:82
  140.7 2.4 %copy-start.9 = (bf16[1024,256]{1,0:T(8,128)(2,1)S(1)}, bf16[1024,256]{1,0:T(8,128)(2,1)}, u32[]{:S(2)}) copy-start(bf16[1024,256]{1,0:T(8,128)(2,1)} %copy.125) | copy-start | bytes 1572868
  143.1 14.8 %copy-start.14 = (f32[1024,256]{0,1:T(8,128)S(1)}, f32[1024,256]{0,1:T(8,128)}, u32[]{:S(2)}) copy-start(f32[1024,256]{0,1:T(8,128)} %copy-done.11) | copy-start | bytes 3145732
  143.1 14.8 %copy-start.19 = (f32[1024,256]{0,1:T(8,128)S(1)}, f32[1024,256]{0,1:T(8,128)}, u32[]{:S(2)}) copy-start(f32[1024,256]{0,1:T(8,128)} %get-tuple-element.57) | copy-start | bytes 3145732
  143.2 9.5 %collective-permute-start.14 = (bf16[256,256]{1,0:T(8,128)(2,1)S(1)}, bf16[256,256]{1,0:T(8,128)(2,1)S(1)}, u32[]{:S(2)}, u32[]{:S(2)}) collective-permute-start(bf16[256,256]{1,0:T(8,128)(2,1)S(1)} %pad_maximum_fusion.16), channel_id=1, source_target_pairs={{0,8},{8,16},{16,24},{1,9},{9,17},{17,25},{2,10},{10,18},{18,26},{... | collective-permute-start | bytes 393224 | tf_op jit(solution)/shard_map/ppermute | solution.py:81
  145.2 8.9 %collective-permute-start.16 = (bf16[1024,64]{0,1:T(8,128)(2,1)S(1)}, bf16[1024,64]{0,1:T(8,128)(2,1)S(1)}, u32[]{:S(2)}, u32[]{:S(2)}) collective-permute-start(bf16[1024,64]{0,1:T(8,128)(2,1)S(1)} %get-tuple-element.16), channel_id=1, source_target_pairs={{0,1},{1,2},{2,3},{3,4},{4,5},{5,6},{6,7},{8,9},{9,10},{10,11},{11... | collective-permute-start | bytes 393224 | tf_op jit(solution)/shard_map/ppermute | solution.py:27
  150.1 7.8 %collective-permute-start.17 = (bf16[1024,64]{0,1:T(8,128)(2,1)S(1)}, bf16[1024,64]{0,1:T(8,128)(2,1)S(1)}, u32[]{:S(2)}, u32[]{:S(2)}) collective-permute-start(bf16[1024,64]{0,1:T(8,128)(2,1)S(1)} %get-tuple-element.17), channel_id=1, source_target_pairs={{1,0},{2,1},{3,2},{4,3},{5,4},{6,5},{7,6},{9,8},{10,9},{11,10},{12... | collective-permute-start | bytes 393224 | tf_op jit(solution)/shard_map/ppermute | solution.py:28
  151.4 6.5 %collective-permute-start.15 = (bf16[256,256]{1,0:T(8,128)(2,1)S(1)}, bf16[256,256]{1,0:T(8,128)(2,1)S(1)}, u32[]{:S(2)}, u32[]{:S(2)}) collective-permute-start(bf16[256,256]{1,0:T(8,128)(2,1)S(1)} %pad_maximum_fusion.17), channel_id=1, source_target_pairs={{8,0},{16,8},{24,16},{9,1},{17,9},{25,17},{10,2},{18,10},{26,18},{... | collective-permute-start | bytes 393224 | tf_op jit(solution)/shard_map/ppermute | solution.py:82
  161.0 8.1 %copy-start.3 = (bf16[1024,256]{0,1:T(8,128)(2,1)S(1)}, bf16[1024,256]{0,1:T(8,128)(2,1)}, u32[]{:S(2)}) copy-start(bf16[1024,256]{0,1:T(8,128)(2,1)} %get-tuple-element.58) | copy-start | bytes 1572868
  163.1 3.6 %copy-start.6 = (bf16[1024,256]{1,0:T(8,128)(2,1)S(1)}, bf16[1024,256]{1,0:T(8,128)(2,1)}, u32[]{:S(2)}) copy-start(bf16[1024,256]{1,0:T(8,128)(2,1)} %copy.126) | copy-start | bytes 1572868
  166.7 13.0 %collective-permute-start.18 = (bf16[256,256]{1,0:T(8,128)(2,1)S(1)}, bf16[256,256]{1,0:T(8,128)(2,1)}, u32[]{:S(2)}, u32[]{:S(2)}) collective-permute-start(bf16[256,256]{1,0:T(8,128)(2,1)S(1)} %pad_maximum_fusion.18), channel_id=1, source_target_pairs={{0,8},{8,16},{16,24},{1,9},{9,17},{17,25},{2,10},{10,18},{18,26},{... | collective-permute-start | bytes 393224 | tf_op jit(solution)/shard_map/ppermute | solution.py:81
  172.3 9.3 %collective-permute-start.20 = (bf16[1024,64]{0,1:T(8,128)(2,1)}, bf16[1024,64]{0,1:T(8,128)(2,1)S(1)}, u32[]{:S(2)}, u32[]{:S(2)}) collective-permute-start(bf16[1024,64]{0,1:T(8,128)(2,1)} %get-tuple-element.14), channel_id=1, source_target_pairs={{0,1},{1,2},{2,3},{3,4},{4,5},{5,6},{6,7},{8,9},{9,10},{10,11},{11... | collective-permute-start | bytes 393224 | tf_op jit(solution)/shard_map/ppermute | solution.py:27
  177.1 7.4 %collective-permute-start.21 = (bf16[1024,64]{0,1:T(8,128)(2,1)S(1)}, bf16[1024,64]{0,1:T(8,128)(2,1)S(1)}, u32[]{:S(2)}, u32[]{:S(2)}) collective-permute-start(bf16[1024,64]{0,1:T(8,128)(2,1)S(1)} %get-tuple-element.15), channel_id=1, source_target_pairs={{1,0},{2,1},{3,2},{4,3},{5,4},{6,5},{7,6},{9,8},{10,9},{11,10},{12... | collective-permute-start | bytes 393224 | tf_op jit(solution)/shard_map/ppermute | solution.py:28
  178.4 6.5 %collective-permute-start.19 = (bf16[256,256]{1,0:T(8,128)(2,1)S(1)}, bf16[256,256]{1,0:T(8,128)(2,1)S(1)}, u32[]{:S(2)}, u32[]{:S(2)}) collective-permute-start(bf16[256,256]{1,0:T(8,128)(2,1)S(1)} %pad_maximum_fusion.19), channel_id=1, source_target_pairs={{8,0},{16,8},{24,16},{9,1},{17,9},{25,17},{10,2},{18,10},{26,18},{... | collective-permute-start | bytes 393224 | tf_op jit(solution)/shard_map/ppermute | solution.py:82
Sparse Core Ops, SparseCore 0:
  9.6 25.2 all-gather.1

commit v3 on v2

--- a/solution.py
+++ b/solution.py
@@ -48,17 +48,23 @@
     columns = probe_field.shape[1]
     width_local = NB_DEV + 2 * HALO_B
     probe_vals = probe_field.astype(jnp.float32)
-    sdiag = jnp.diagonal(diag_blocks, axis1=1, axis2=2).astype(jnp.float32).reshape(NODES_DEV)
+    eye = jnp.arange(BLOCK)[:, None] == jnp.arange(BLOCK)[None, :]
+    sdiag = jnp.sum(
+        jnp.where(eye[None], diag_blocks.astype(jnp.float32), 0.0), axis=2
+    ).reshape(NODES_DEV)
     scale_space = jnp.repeat(theta_space, PROBES)[None, :]
     scale_time = jnp.repeat(theta_time, PROBES)[None, :]
     base_diag = scale_space * sdiag[:, None] + 2.0 * scale_time + kappa[:, None]
     local_ids = jnp.arange(width_local, dtype=jnp.int32)
-    picks = (block_cols[:, :, None] == local_ids[None, None, :]).astype(jnp.float32)
-    own_pick = (jnp.arange(NB_DEV, dtype=jnp.int32)[:, None] == local_ids[None, :]).astype(
-        jnp.float32
+    picks = block_cols[:, None, None, :] == local_ids[None, None, :, None]
+    off_f32 = off_blocks.astype(jnp.float32).transpose(0, 2, 1, 3)
+    combined = jnp.sum(
+        jnp.where(picks[..., None], off_f32[:, :, None, :, :], 0.0), axis=3
     )
-    combined = jnp.einsum("bkm,bkij->bimj", picks, off_blocks.astype(jnp.float32))
-    combined = combined + jnp.einsum("bm,bij->bimj", own_pick, diag_blocks.astype(jnp.float32))
+    own_pick = jnp.arange(NB_DEV, dtype=jnp.int32)[:, None] == local_ids[None, :]
+    combined = combined + jnp.where(
+        own_pick[:, None, :, None], diag_blocks.astype(jnp.float32)[:, :, None, :], 0.0
+    )
     combined = combined.astype(jnp.bfloat16).reshape(NODES_DEV, width_local * BLOCK)
     own_part = combined[:, :NODES_DEV]
     lower_part = combined[:, NODES_DEV : NODES_DEV + HALO_B * BLOCK]

time: 202 us -> 258 us (1.28)
  other arithmetic: 16.9 us -> 80.7 us
  matrix products: 39.1 us -> 27.3 us
  waiting for transfers between devices: 16.7 us -> 21.6 us
  local copies, waits for them, and re-layouts: 41 us -> 38.4 us
    reduce_sum x0 -> x2, other arithmetic: none -> 55.7 us  [the longest x1 54.6 us: shards(): jnp.sum(jnp.where(picks[..., None], off_f32[:, :, None, :, :], 0.0), axis=3)]
    ppermute x5, waiting for transfers between devices: 0.01 us -> 6.09 us  [with_halo(): before = lax.ppermute(last, axis, up)]
    unnamed x48 -> x63, local copies, waits for them, and re-layouts: 11.5 us -> 5.52 us
    convert_element_type x1 -> x2, other arithmetic: 0.01 us -> 5.41 us  [the longest x1 4.58 us: shards(): combined.astype(jnp.bfloat16).reshape(NODES_DEV, width_local * BLOCK)]
    transpose x0 -> x1, local copies, waits for them, and re-layouts: none -> 4.44 us  [shards(): off_f32 = off_blocks.astype(jnp.float32).transpose(0, 2, 1, 3)]
    dot_general x5, matrix products: 8.76 us -> 5.38 us  [spatial(): jnp.dot(lower_part, lower, preferred_element_type=jnp.float32)]
    ppermute x5, starting transfers between devices: 12.9 us -> 16.2 us  [spatial(): lower = lax.ppermute(pick_blocks(blocks, upper_wants), 'space', up)]
    dot_general x1 -> x0, matrix products: 3.15 us -> none  [shards(): jnp.einsum('bkm,bkij->bimj', picks, off_blocks.astype(jnp.float32))]
  transfers between devices with their start and end apart: 24 -> 24, of which waited for: 5 -> 8; matrix products, arithmetic and copies ran while one was open for 31% -> 45% of each run, Pallas kernels for 0% -> 0%
where the time goes in v3:
time: 258 us; the launch traced here: 257 us
  other arithmetic  80.7 us (31%)
  starting transfers between devices  60.3 us (23%)
  local copies, waits for them, and re-layouts  38.4 us (15%)
  matrix products  27.3 us (11%)
  between operations  22.5 us (9%)
  waiting for transfers between devices  21.6 us (8%)
  blocking collectives  5.76 us (2%)
    reduce_sum x1, other arithmetic, shards(): jnp.sum(jnp.where(picks[..., None], off_f32[:, :, None, :, :], 0.0), axis=3)  54.6 us
    ppermute x5, starting transfers between devices, with_halo(): before = lax.ppermute(last, axis, up)  22.6 us
    ppermute x5, starting transfers between devices, spatial(): lower = lax.ppermute(pick_blocks(blocks, upper_wants), 'space', up)  16.2 us
    ppermute x5, waiting for transfers between devices, with_halo(): after = lax.ppermute(initial, axis, down)  13.9 us
    scatter-add x1, other arithmetic, shards(): jax.ops.segment_sum(obs_weight, bins, num_segments=space_count * nodes_de...  11.8 us
    dot_general x5, matrix products, spatial(): jnp.dot(upper_part, upper, preferred_element_type=jnp.float32)  11.8 us
    gather x1, local copies, waits for them, and re-layouts, shards(): coef_rows = svc_all[owner * nodes_dev + obs_cell // T_DEV]  10.4 us
    dot_general x5, matrix products, spatial(): total = jnp.dot(own_part, field, preferred_element_type=jnp.float32)  10.2 us
  transfers between devices with their start and end apart: 24, of which 8 were waited for; matrix products, arithmetic and copies ran while one was open for 45% of the time, Pallas kernels for 0%

profile of v3, /device:TPU:0, one launch (start us, length us, event | category | flops | bytes accessed | tf_op | source)
XLA Modules:
  0.0 256.6 jit_solution(16152687584168393158)
XLA Ops:
  7.2 0.9 fusion.77
  8.1 1.3 collective-permute-start
  9.4 3.0 %collective-permute-start.2 = (s32[2]{0:T(128)S(1)}, s32[2]{0:T(128)S(1)}, u32[]{:S(2)}, u32[]{:S(2)}) collective-permute-start(s32[2]{0:T(128)S(1)} %get-tuple-element.48), channel_id=1, source_target_pairs={{0,8},{8,16},{16,24},{1,9},{9,17},{17,25},{2,10},{10,18},{18,26},{... | collective-permute-start | bytes 32 | tf_op jit(solution)/shard_map/ppermute | solution.py:77
  12.5 1.2 copy.76
  15.4 1.1 select_reduce_fusion.1
  16.5 1.1 fusion.54
  18.4 5.5 %collective-permute-start.4 = (bf16[1024,64]{0,1:T(8,128)(2,1)}, bf16[1024,64]{0,1:T(8,128)(2,1)}, u32[]{:S(2)}, u32[]{:S(2)}) collective-permute-start(bf16[1024,64]{0,1:T(8,128)(2,1)} %get-tuple-element.34), channel_id=1, source_target_pairs={{0,1},{1,2},{2,3},{3,4},{4,5},{5,6},{6,7},{8,9},{9,10},{10,11},{11... | collective-permute-start | bytes 393224 | tf_op jit(solution)/shard_map/ppermute | solution.py:27
  23.9 1.3 collective-permute-start.5
  25.2 1.0 copy.114
  27.6 4.4 %copy.77 = f32[8,128,8,128]{3,2,1,0:T(8,128)} copy(f32[8,128,8,128]{3,1,2,0:T(8,128)S(1)} %convert_bitcast_fusion) | data formatting | bytes 8388608 | tf_op jit(solution)/shard_map/transpose | solution.py:60
  32.0 54.6 %select_reduce_fusion = f32[8,128,12,128]{3,2,1,0:T(8,128)} fusion(f32[8,128,8,128]{3,2,1,0:T(8,128)} %copy.77, pred[8,12,8]{2,1,0:T(8,128)(4,1)S(1)} %iota_compare_fusion), kind=kLoop, calls=%fused_computation.2 | loop fusion | flops 23592960 | bytes 10486528 | tf_op jit(solution)/shard_map/reduce_sum | solution.py:61
  86.7 4.6 %add_convert_fusion = bf16[8,128,12,128]{3,2,1,0:T(8,128)(2,1)S(1)} fusion(f32[8,128,12,128]{3,2,1,0:T(8,128)} %select_reduce_fusion, f32[8,128,128]{2,1,0:T(8,128)S(1)} %copy-done.13, pred[8,12]{1,0:T(8,128)(4,1)S(1)} %iota_compare_fusion.2), kind=kLoop, calls=%fused_computation.3 | loop fusion | flops 4718592 | bytes 9961568 | tf_op jit(solution)/shard_map/convert_element_type | solution.py:68
  91.3 1.6 copy.125
  93.0 1.7 fusion.36
  103.6 1.0 dynamic-slice_bitcast_fusion.17
  104.6 3.4 %collective-permute-start.1 = (bf16[256,256]{1,0:T(8,128)(2,1)S(1)}, bf16[256,256]{1,0:T(8,128)(2,1)}, u32[]{:S(2)}, u32[]{:S(2)}) collective-permute-start(bf16[256,256]{1,0:T(8,128)(2,1)S(1)} %pad_maximum_fusion.10), channel_id=1, source_target_pairs={{0,8},{8,16},{16,24},{1,9},{9,17},{17,25},{2,10},{10,18},{18,26},{... | collective-permute-start | bytes 393224 | tf_op jit(solution)/shard_map/ppermute | solution.py:87
  108.0 1.5 collective-permute-start.3
  109.6 10.4 %gather_fusion = bf16[2048,256]{1,0:T(8,128)(2,1)} fusion(bf16[4096,256]{1,0:T(8,128)(2,1)} %all-gather.2.cloned.1.call-done, s32[2048]{0:T(1024)S(1)} %get-tuple-element.42), kind=kCustom, calls=%fused_computation | custom fusion | bytes 2105344 | tf_op jit(solution)/shard_map/gather | solution.py:109
  119.9 1.9 fusion
  121.8 11.8 %scatter_custom_fusion = f32[16384]{0:T(1024)} fusion(s32[2048]{0:T(1024)S(1)} %get-tuple-element.43, f32[2048]{0:T(1024)S(1)} %exp.3, f32[]{:T(128)} %constant.64.clone.1), kind=kCustom, calls=%fused_computation.139 | custom fusion | flops 2048 | bytes 65540 | tf_op jit(solution)/shard_map/scatter-add | solution.py:113
  133.7 3.6 %all-to-all-start = ((f32[4,1,4096]{2,1,0:T(1,128)}), f32[4,1,4096]{2,1,0:T(1,128)S(1)}, u32[]{:S(2)}, u32[]{:S(2)}) async-start(f32[4,1,4096]{2,1,0:T(1,128)} %bitcast.12), calls=%async_computation | async-start | bytes 131072 | tf_op jit(solution)/shard_map/all_to_all | solution.py:117
  137.3 2.6 %convolution_add_fusion.9 = f32[1024,256]{0,1:T(8,128)} fusion(f32[1024,256]{0,1:T(8,128)} %fusion.36, bf16[256,256]{1,0:T(8,128)(2,1)} %collective-permute-done.1, bf16[1024,1536]{1,0:T(8,128)(2,1)S(1)} %bitcast.90), kind=kOutput, calls=%fused_computation.42 | convolution fusion | flops 134479872 | bytes 2752512 | tf_op jit(solution)/shard_map/dot_general | solution.py:90
  139.9 1.5 all-to-all-done
  141.5 1.3 reshape.87
  142.8 1.2 copy.84
  144.1 1.4 fusion.4
  145.5 4.4 %fusion.79 = (bf16[1024,256]{0,1:T(8,128)(2,1)}, f32[1024,256]{0,1:T(8,128)}) fusion(f32[1024,256]{0,1:T(8,128)S(1)} %get-tuple-element.41, f32[1024,256]{0,1:T(8,128)S(1)} %get-tuple-element.40, bf16[1024,64]{0,1:T(8,128)(2,1)} %collective-permute-done.5, bf16[1024,256]{0,1:T(8,128)(2,1)} %copy-done.5, bf16[1024,64]{0,1:T(8,128)(2,1)} %collective-permute-done.4, ...), kind=kOutput, calls=%fused_computation.165 | convolution fusion | flops 141557760 | bytes 6695936 | tf_op jit(solution)/shard_map/dot_general | solution.py:91
  149.9 2.0 copy.115
  152.0 1.9 fusion.34
  154.1 1.4 collective-permute-start.7
  155.5 3.0 %collective-permute-start.6 = (bf16[256,256]{1,0:T(8,128)(2,1)S(1)}, bf16[256,256]{1,0:T(8,128)(2,1)S(1)}, u32[]{:S(2)}, u32[]{:S(2)}) collective-permute-start(bf16[256,256]{1,0:T(8,128)(2,1)S(1)} %pad_maximum_fusion.12), channel_id=1, source_target_pairs={{0,8},{8,16},{16,24},{1,9},{9,17},{17,25},{2,10},{10,18},{18,26},{... | collective-permute-start | bytes 393224 | tf_op jit(solution)/shard_map/ppermute | solution.py:87
  158.6 4.6 %collective-permute-start.8 = (bf16[1024,64]{0,1:T(8,128)(2,1)S(1)}, bf16[1024,64]{0,1:T(8,128)(2,1)S(1)}, u32[]{:S(2)}, u32[]{:S(2)}) collective-permute-start(bf16[1024,64]{0,1:T(8,128)(2,1)S(1)} %get-tuple-element.28), channel_id=1, source_target_pairs={{0,1},{1,2},{2,3},{3,4},{4,5},{5,6},{6,7},{8,9},{9,10},{10,11},{11... | collective-permute-start | bytes 393224 | tf_op jit(solution)/shard_map/ppermute | solution.py:27
  163.2 1.3 collective-permute-start.9
  164.9 2.1 collective-permute-done.8
  166.9 4.2 %collective-permute-done.9 = bf16[1024,64]{0,1:T(8,128)(2,1)S(1)} collective-permute-done((bf16[1024,64]{0,1:T(8,128)(2,1)S(1)}, bf16[1024,64]{0,1:T(8,128)(2,1)S(1)}, u32[]{:S(2)}, u32[]{:S(2)}) %collective-permute-start.9) | collective-permute-done | bytes 131104 | tf_op jit(solution)/shard_map/ppermute | solution.py:28
  171.2 2.0 fusion.80
  173.1 2.0 copy.116
  175.2 1.9 fusion.32
  177.3 1.4 collective-permute-start.11
  178.7 3.0 %collective-permute-start.10 = (bf16[256,256]{1,0:T(8,128)(2,1)S(1)}, bf16[256,256]{1,0:T(8,128)(2,1)S(1)}, u32[]{:S(2)}, u32[]{:S(2)}) collective-permute-start(bf16[256,256]{1,0:T(8,128)(2,1)S(1)} %pad_maximum_fusion.14), channel_id=1, source_target_pairs={{0,8},{8,16},{16,24},{1,9},{9,17},{17,25},{2,10},{10,18},{18,26},{... | collective-permute-start | bytes 393224 | tf_op jit(solution)/shard_map/ppermute | solution.py:87
  181.8 4.5 %collective-permute-start.12 = (bf16[1024,64]{0,1:T(8,128)(2,1)S(1)}, bf16[1024,64]{0,1:T(8,128)(2,1)S(1)}, u32[]{:S(2)}, u32[]{:S(2)}) collective-permute-start(bf16[1024,64]{0,1:T(8,128)(2,1)S(1)} %get-tuple-element.22), channel_id=1, source_target_pairs={{0,1},{1,2},{2,3},{3,4},{4,5},{5,6},{6,7},{8,9},{9,10},{10,11},{11... | collective-permute-start | bytes 393224 | tf_op jit(solution)/shard_map/ppermute | solution.py:27
  186.4 1.3 collective-permute-start.13
  188.0 2.2 collective-permute-done.12
  190.2 4.1 %collective-permute-done.13 = bf16[1024,64]{0,1:T(8,128)(2,1)S(1)} collective-permute-done((bf16[1024,64]{0,1:T(8,128)(2,1)S(1)}, bf16[1024,64]{0,1:T(8,128)(2,1)S(1)}, u32[]{:S(2)}, u32[]{:S(2)}) %collective-permute-start.13) | collective-permute-done | bytes 131104 | tf_op jit(solution)/shard_map/ppermute | solution.py:28
  194.4 2.0 fusion.81
  196.3 2.0 copy.117
  198.4 1.9 fusion.30
  200.5 1.4 collective-permute-start.15
  201.9 3.0 %collective-permute-start.14 = (bf16[256,256]{1,0:T(8,128)(2,1)S(1)}, bf16[256,256]{1,0:T(8,128)(2,1)S(1)}, u32[]{:S(2)}, u32[]{:S(2)}) collective-permute-start(bf16[256,256]{1,0:T(8,128)(2,1)S(1)} %pad_maximum_fusion.16), channel_id=1, source_target_pairs={{0,8},{8,16},{16,24},{1,9},{9,17},{17,25},{2,10},{10,18},{18,26},{... | collective-permute-start | bytes 393224 | tf_op jit(solution)/shard_map/ppermute | solution.py:87
  205.0 4.2 %collective-permute-start.16 = (bf16[1024,64]{0,1:T(8,128)(2,1)S(1)}, bf16[1024,64]{0,1:T(8,128)(2,1)S(1)}, u32[]{:S(2)}, u32[]{:S(2)}) collective-permute-start(bf16[1024,64]{0,1:T(8,128)(2,1)S(1)} %get-tuple-element.16), channel_id=1, source_target_pairs={{0,1},{1,2},{2,3},{3,4},{4,5},{5,6},{6,7},{8,9},{9,10},{10,11},{11... | collective-permute-start | bytes 393224 | tf_op jit(solution)/shard_map/ppermute | solution.py:27
  209.2 1.3 collective-permute-start.17
  210.8 1.8 collective-permute-done.16
  212.6 4.7 %collective-permute-done.17 = bf16[1024,64]{0,1:T(8,128)(2,1)S(1)} collective-permute-done((bf16[1024,64]{0,1:T(8,128)(2,1)S(1)}, bf16[1024,64]{0,1:T(8,128)(2,1)S(1)}, u32[]{:S(2)}, u32[]{:S(2)}) %collective-permute-start.17) | collective-permute-done | bytes 131104 | tf_op jit(solution)/shard_map/ppermute | solution.py:28
  217.3 2.0 fusion.82
  219.3 2.0 copy.118
  221.3 2.8 %fusion.38 = f32[1024,256]{0,1:T(8,128)} fusion(bf16[1024,256]{0,1:T(8,128)(2,1)} %get-tuple-element.58, bf16[1024,1536]{1,0:T(8,128)(2,1)S(1)} %bitcast.101), kind=kOutput, calls=%fused_computation.68 | convolution fusion | flops 536870912 | bytes 3670016 | tf_op jit(solution)/shard_map/dot_general | solution.py:89
  224.9 1.3 collective-permute-start.19
  226.8 3.7 %collective-permute-start.18 = (bf16[256,256]{1,0:T(8,128)(2,1)}, bf16[256,256]{1,0:T(8,128)(2,1)}, u32[]{:S(2)}, u32[]{:S(2)}) collective-permute-start(bf16[256,256]{1,0:T(8,128)(2,1)} %pad_maximum_fusion.18), channel_id=1, source_target_pairs={{0,8},{8,16},{16,24},{1,9},{9,17},{17,25},{2,10},{10,18},{18,26},{... | collective-permute-start | bytes 393224 | tf_op jit(solution)/shard_map/ppermute | solution.py:87
  231.2 3.9 %collective-permute-start.20 = (bf16[1024,64]{0,1:T(8,128)(2,1)}, bf16[1024,64]{0,1:T(8,128)(2,1)S(1)}, u32[]{:S(2)}, u32[]{:S(2)}) collective-permute-start(bf16[1024,64]{0,1:T(8,128)(2,1)} %get-tuple-element.14), channel_id=1, source_target_pairs={{0,1},{1,2},{2,3},{3,4},{4,5},{5,6},{6,7},{8,9},{9,10},{10,11},{11... | collective-permute-start | bytes 393224 | tf_op jit(solution)/shard_map/ppermute | solution.py:27
  235.1 1.3 collective-permute-start.21
  236.4 2.5 copy.104
  238.9 1.7 convolution_add_fusion.1
  240.7 1.5 fusion.29
  243.4 5.8 %psum.7 = f32[2,256]{1,0:T(2,128)S(1)} all-reduce(f32[2,256]{1,0:T(2,128)S(1)} %pad_maximum_fusion.20), channel_id=1, replica_groups=mesh['space'=4,'tm'=8] {'space'}, use_global_device_ids=true, to_apply=%region_6.7 | all-reduce | flops 512 | bytes 4096 | tf_op jit(solution)/shard_map/psum | solution.py:143
  (123 shorter events, 10.9 us)
Async XLA Ops:
  7.2 19.0 %copy-start.18 = (bf16[8,128,128]{2,1,0:T(8,128)(2,1)S(1)}, bf16[8,128,128]{2,1,0:T(8,128)(2,1)}, u32[]{:S(2)}) copy-start(bf16[8,128,128]{2,1,0:T(8,128)(2,1)} %param.16) | copy-start | bytes 786436
  7.2 19.8 %copy-start.12 = (bf16[8,8,128,128]{3,2,1,0:T(8,128)(2,1)S(1)}, bf16[8,8,128,128]{3,2,1,0:T(8,128)(2,1)}, u32[]{:S(2)}) copy-start(bf16[8,8,128,128]{3,2,1,0:T(8,128)(2,1)} %param.17) | copy-start | bytes 6291460
  7.2 102.4 %all-gather.2.cloned.1.call-start = ((), (), s32[]{:S(2)}) async-start(), calls=%async_computation.1 | async-start | bytes 2621440 | tf_op jit(solution)/shard_map/all_gather | solution.py:107
  8.1 86.6 %collective-permute-start = (s32[2]{0:T(128)S(1)}, s32[2]{0:T(128)S(1)}, u32[]{:S(2)}, u32[]{:S(2)}) collective-permute-start(s32[2]{0:T(128)S(1)} %get-tuple-element.49), channel_id=1, source_target_pairs={{8,0},{16,8},{24,16},{9,1},{17,9},{25,17},{10,2},{18,10},{26,18},{... | collective-permute-start | bytes 32 | tf_op jit(solution)/shard_map/ppermute | solution.py:76
  9.4 88.5 %collective-permute-start.2 = (s32[2]{0:T(128)S(1)}, s32[2]{0:T(128)S(1)}, u32[]{:S(2)}, u32[]{:S(2)}) collective-permute-start(s32[2]{0:T(128)S(1)} %get-tuple-element.48), channel_id=1, source_target_pairs={{0,8},{8,16},{16,24},{1,9},{9,17},{17,25},{2,10},{10,18},{18,26},{... | collective-permute-start | bytes 32 | tf_op jit(solution)/shard_map/ppermute | solution.py:77
  13.8 13.8 %copy-start = (bf16[1024,256]{0,1:T(8,128)(2,1)}, bf16[1024,256]{0,1:T(8,128)(2,1)S(1)}, u32[]{:S(2)}) copy-start(bf16[1024,256]{0,1:T(8,128)(2,1)S(1)} %copy.76) | copy-start | bytes 1572868
  17.6 10.0 %copy-start.5 = (bf16[1024,256]{0,1:T(8,128)(2,1)}, bf16[1024,256]{0,1:T(8,128)(2,1)S(1)}, u32[]{:S(2)}) copy-start(bf16[1024,256]{0,1:T(8,128)(2,1)S(1)} %fusion.54) | copy-start | bytes 1572868
  18.4 127.1 %collective-permute-start.4 = (bf16[1024,64]{0,1:T(8,128)(2,1)}, bf16[1024,64]{0,1:T(8,128)(2,1)}, u32[]{:S(2)}, u32[]{:S(2)}) collective-permute-start(bf16[1024,64]{0,1:T(8,128)(2,1)} %get-tuple-element.34), channel_id=1, source_target_pairs={{0,1},{1,2},{2,3},{3,4},{4,5},{5,6},{6,7},{8,9},{9,10},{10,11},{11... | collective-permute-start | bytes 393224 | tf_op jit(solution)/shard_map/ppermute | solution.py:27
  23.9 121.6 %collective-permute-start.5 = (bf16[1024,64]{0,1:T(8,128)(2,1)}, bf16[1024,64]{0,1:T(8,128)(2,1)}, u32[]{:S(2)}, u32[]{:S(2)}) collective-permute-start(bf16[1024,64]{0,1:T(8,128)(2,1)} %get-tuple-element.35), channel_id=1, source_target_pairs={{1,0},{2,1},{3,2},{4,3},{5,4},{6,5},{7,6},{9,8},{10,9},{11,10},{12... | collective-permute-start | bytes 393224 | tf_op jit(solution)/shard_map/ppermute | solution.py:28
  27.5 4.5 %copy-start.26 = (s32[8,8]{1,0:T(8,128)S(1)}, s32[8,8]{1,0:T(8,128)}, u32[]{:S(2)}) copy-start(s32[8,8]{1,0:T(8,128)} %param.18) | copy-start | bytes 772
  32.0 54.7 %copy-start.13 = (f32[8,128,128]{2,1,0:T(8,128)S(1)}, f32[8,128,128]{2,1,0:T(8,128)}, u32[]{:S(2)}) copy-start(f32[8,128,128]{2,1,0:T(8,128)} %convert_element_type.80) | copy-start | bytes 1572868
  91.3 1.6 copy-start.24
  91.3 1.7 copy-start.25
  91.3 1.7 copy-start.6
  104.6 32.7 %collective-permute-start.1 = (bf16[256,256]{1,0:T(8,128)(2,1)S(1)}, bf16[256,256]{1,0:T(8,128)(2,1)}, u32[]{:S(2)}, u32[]{:S(2)}) collective-permute-start(bf16[256,256]{1,0:T(8,128)(2,1)S(1)} %pad_maximum_fusion.10), channel_id=1, source_target_pairs={{0,8},{8,16},{16,24},{1,9},{9,17},{17,25},{2,10},{10,18},{18,26},{... | collective-permute-start | bytes 393224 | tf_op jit(solution)/shard_map/ppermute | solution.py:87
  108.0 37.4 %collective-permute-start.3 = (bf16[256,256]{1,0:T(8,128)(2,1)S(1)}, bf16[256,256]{1,0:T(8,128)(2,1)}, u32[]{:S(2)}, u32[]{:S(2)}) collective-permute-start(bf16[256,256]{1,0:T(8,128)(2,1)S(1)} %pad_maximum_fusion.11), channel_id=1, source_target_pairs={{8,0},{16,8},{24,16},{9,1},{17,9},{25,17},{10,2},{18,10},{26,18},{... | collective-permute-start | bytes 393224 | tf_op jit(solution)/shard_map/ppermute | solution.py:88
  119.9 24.1 %copy-start.23 = (f32[1024]{0:T(1024)S(1)}, f32[1024]{0:T(1024)}, u32[]{:S(2)}) copy-start(f32[1024]{0:T(1024)} %param.13) | copy-start | bytes 12292
  133.7 7.8 %all-to-all-start = ((f32[4,1,4096]{2,1,0:T(1,128)}), f32[4,1,4096]{2,1,0:T(1,128)S(1)}, u32[]{:S(2)}, u32[]{:S(2)}) async-start(f32[4,1,4096]{2,1,0:T(1,128)} %bitcast.12), calls=%async_computation | async-start | bytes 131072 | tf_op jit(solution)/shard_map/all_to_all | solution.py:117
  145.5 4.5 %copy-start.19 = (f32[1024,256]{0,1:T(8,128)}, f32[1024,256]{0,1:T(8,128)S(1)}, u32[]{:S(2)}) copy-start(f32[1024,256]{0,1:T(8,128)S(1)} %get-tuple-element.41) | copy-start | bytes 3145732
  152.0 1.9 copy-start.10
  152.0 2.0 copy-start.16
  153.9 17.3 %copy-start.1 = (bf16[1024,256]{0,1:T(8,128)(2,1)S(1)}, bf16[1024,256]{0,1:T(8,128)(2,1)}, u32[]{:S(2)}) copy-start(bf16[1024,256]{0,1:T(8,128)(2,1)} %copy-done) | copy-start | bytes 1572868
  153.9 17.3 %copy-start.20 = (f32[1024,256]{0,1:T(8,128)S(1)}, f32[1024,256]{0,1:T(8,128)}, u32[]{:S(2)}) copy-start(f32[1024,256]{0,1:T(8,128)} %copy-done.19) | copy-start | bytes 3145732
  153.9 17.3 %copy-start.28 = (f32[1024,256]{0,1:T(8,128)S(1)}, f32[1024,256]{0,1:T(8,128)}, u32[]{:S(2)}) copy-start(f32[1024,256]{0,1:T(8,128)} %get-tuple-element.53) | copy-start | bytes 3145732
  154.1 10.8 %collective-permute-start.7 = (bf16[256,256]{1,0:T(8,128)(2,1)S(1)}, bf16[256,256]{1,0:T(8,128)(2,1)S(1)}, u32[]{:S(2)}, u32[]{:S(2)}) collective-permute-start(bf16[256,256]{1,0:T(8,128)(2,1)S(1)} %pad_maximum_fusion.13), channel_id=1, source_target_pairs={{8,0},{16,8},{24,16},{9,1},{17,9},{25,17},{10,2},{18,10},{26,18},{... | collective-permute-start | bytes 393224 | tf_op jit(solution)/shard_map/ppermute | solution.py:88
  155.5 8.9 %collective-permute-start.6 = (bf16[256,256]{1,0:T(8,128)(2,1)S(1)}, bf16[256,256]{1,0:T(8,128)(2,1)S(1)}, u32[]{:S(2)}, u32[]{:S(2)}) collective-permute-start(bf16[256,256]{1,0:T(8,128)(2,1)S(1)} %pad_maximum_fusion.12), channel_id=1, source_target_pairs={{0,8},{8,16},{16,24},{1,9},{9,17},{17,25},{2,10},{10,18},{18,26},{... | collective-permute-start | bytes 393224 | tf_op jit(solution)/shard_map/ppermute | solution.py:87
  158.6 8.3 %collective-permute-start.8 = (bf16[1024,64]{0,1:T(8,128)(2,1)S(1)}, bf16[1024,64]{0,1:T(8,128)(2,1)S(1)}, u32[]{:S(2)}, u32[]{:S(2)}) collective-permute-start(bf16[1024,64]{0,1:T(8,128)(2,1)S(1)} %get-tuple-element.28), channel_id=1, source_target_pairs={{0,1},{1,2},{2,3},{3,4},{4,5},{5,6},{6,7},{8,9},{9,10},{10,11},{11... | collective-permute-start | bytes 393224 | tf_op jit(solution)/shard_map/ppermute | solution.py:27
  163.2 8.0 %collective-permute-start.9 = (bf16[1024,64]{0,1:T(8,128)(2,1)S(1)}, bf16[1024,64]{0,1:T(8,128)(2,1)S(1)}, u32[]{:S(2)}, u32[]{:S(2)}) collective-permute-start(bf16[1024,64]{0,1:T(8,128)(2,1)S(1)} %get-tuple-element.29), channel_id=1, source_target_pairs={{1,0},{2,1},{3,2},{4,3},{5,4},{6,5},{7,6},{9,8},{10,9},{11,10},{12... | collective-permute-start | bytes 393224 | tf_op jit(solution)/shard_map/ppermute | solution.py:28
  175.2 1.9 copy-start.11
  175.2 2.0 copy-start.17
  177.0 17.3 %copy-start.2 = (bf16[1024,256]{0,1:T(8,128)(2,1)S(1)}, bf16[1024,256]{0,1:T(8,128)(2,1)}, u32[]{:S(2)}) copy-start(bf16[1024,256]{0,1:T(8,128)(2,1)} %copy-done) | copy-start | bytes 1572868
  177.1 17.3 %copy-start.21 = (f32[1024,256]{0,1:T(8,128)S(1)}, f32[1024,256]{0,1:T(8,128)}, u32[]{:S(2)}) copy-start(f32[1024,256]{0,1:T(8,128)} %copy-done.19) | copy-start | bytes 3145732
  177.1 17.3 %copy-start.29 = (f32[1024,256]{0,1:T(8,128)S(1)}, f32[1024,256]{0,1:T(8,128)}, u32[]{:S(2)}) copy-start(f32[1024,256]{0,1:T(8,128)} %get-tuple-element.55) | copy-start | bytes 3145732
  177.3 10.7 %collective-permute-start.11 = (bf16[256,256]{1,0:T(8,128)(2,1)S(1)}, bf16[256,256]{1,0:T(8,128)(2,1)S(1)}, u32[]{:S(2)}, u32[]{:S(2)}) collective-permute-start(bf16[256,256]{1,0:T(8,128)(2,1)S(1)} %pad_maximum_fusion.15), channel_id=1, source_target_pairs={{8,0},{16,8},{24,16},{9,1},{17,9},{25,17},{10,2},{18,10},{26,18},{... | collective-permute-start | bytes 393224 | tf_op jit(solution)/shard_map/ppermute | solution.py:88
  178.7 8.9 %collective-permute-start.10 = (bf16[256,256]{1,0:T(8,128)(2,1)S(1)}, bf16[256,256]{1,0:T(8,128)(2,1)S(1)}, u32[]{:S(2)}, u32[]{:S(2)}) collective-permute-start(bf16[256,256]{1,0:T(8,128)(2,1)S(1)} %pad_maximum_fusion.14), channel_id=1, source_target_pairs={{0,8},{8,16},{16,24},{1,9},{9,17},{17,25},{2,10},{10,18},{18,26},{... | collective-permute-start | bytes 393224 | tf_op jit(solution)/shard_map/ppermute | solution.py:87
  181.8 8.4 %collective-permute-start.12 = (bf16[1024,64]{0,1:T(8,128)(2,1)S(1)}, bf16[1024,64]{0,1:T(8,128)(2,1)S(1)}, u32[]{:S(2)}, u32[]{:S(2)}) collective-permute-start(bf16[1024,64]{0,1:T(8,128)(2,1)S(1)} %get-tuple-element.22), channel_id=1, source_target_pairs={{0,1},{1,2},{2,3},{3,4},{4,5},{5,6},{6,7},{8,9},{9,10},{10,11},{11... | collective-permute-start | bytes 393224 | tf_op jit(solution)/shard_map/ppermute | solution.py:27
  186.4 8.0 %collective-permute-start.13 = (bf16[1024,64]{0,1:T(8,128)(2,1)S(1)}, bf16[1024,64]{0,1:T(8,128)(2,1)S(1)}, u32[]{:S(2)}, u32[]{:S(2)}) collective-permute-start(bf16[1024,64]{0,1:T(8,128)(2,1)S(1)} %get-tuple-element.23), channel_id=1, source_target_pairs={{1,0},{2,1},{3,2},{4,3},{5,4},{6,5},{7,6},{9,8},{10,9},{11,10},{12... | collective-permute-start | bytes 393224 | tf_op jit(solution)/shard_map/ppermute | solution.py:28
  198.4 1.9 copy-start.9
  198.4 2.0 copy-start.15
  200.2 17.1 %copy-start.3 = (bf16[1024,256]{0,1:T(8,128)(2,1)S(1)}, bf16[1024,256]{0,1:T(8,128)(2,1)}, u32[]{:S(2)}) copy-start(bf16[1024,256]{0,1:T(8,128)(2,1)} %copy-done) | copy-start | bytes 1572868
  200.2 17.1 %copy-start.22 = (f32[1024,256]{0,1:T(8,128)S(1)}, f32[1024,256]{0,1:T(8,128)}, u32[]{:S(2)}) copy-start(f32[1024,256]{0,1:T(8,128)} %copy-done.19) | copy-start | bytes 3145732
  200.3 17.1 %copy-start.27 = (f32[1024,256]{0,1:T(8,128)S(1)}, f32[1024,256]{0,1:T(8,128)}, u32[]{:S(2)}) copy-start(f32[1024,256]{0,1:T(8,128)} %get-tuple-element.57) | copy-start | bytes 3145732
  200.5 10.3 %collective-permute-start.15 = (bf16[256,256]{1,0:T(8,128)(2,1)S(1)}, bf16[256,256]{1,0:T(8,128)(2,1)S(1)}, u32[]{:S(2)}, u32[]{:S(2)}) collective-permute-start(bf16[256,256]{1,0:T(8,128)(2,1)S(1)} %pad_maximum_fusion.17), channel_id=1, source_target_pairs={{8,0},{16,8},{24,16},{9,1},{17,9},{25,17},{10,2},{18,10},{26,18},{... | collective-permute-start | bytes 393224 | tf_op jit(solution)/shard_map/ppermute | solution.py:88
  201.9 8.5 %collective-permute-start.14 = (bf16[256,256]{1,0:T(8,128)(2,1)S(1)}, bf16[256,256]{1,0:T(8,128)(2,1)S(1)}, u32[]{:S(2)}, u32[]{:S(2)}) collective-permute-start(bf16[256,256]{1,0:T(8,128)(2,1)S(1)} %pad_maximum_fusion.16), channel_id=1, source_target_pairs={{0,8},{8,16},{16,24},{1,9},{9,17},{17,25},{2,10},{10,18},{18,26},{... | collective-permute-start | bytes 393224 | tf_op jit(solution)/shard_map/ppermute | solution.py:87
  205.0 7.6 %collective-permute-start.16 = (bf16[1024,64]{0,1:T(8,128)(2,1)S(1)}, bf16[1024,64]{0,1:T(8,128)(2,1)S(1)}, u32[]{:S(2)}, u32[]{:S(2)}) collective-permute-start(bf16[1024,64]{0,1:T(8,128)(2,1)S(1)} %get-tuple-element.16), channel_id=1, source_target_pairs={{0,1},{1,2},{2,3},{3,4},{4,5},{5,6},{6,7},{8,9},{9,10},{10,11},{11... | collective-permute-start | bytes 393224 | tf_op jit(solution)/shard_map/ppermute | solution.py:27
  209.2 8.2 %collective-permute-start.17 = (bf16[1024,64]{0,1:T(8,128)(2,1)S(1)}, bf16[1024,64]{0,1:T(8,128)(2,1)S(1)}, u32[]{:S(2)}, u32[]{:S(2)}) collective-permute-start(bf16[1024,64]{0,1:T(8,128)(2,1)S(1)} %get-tuple-element.17), channel_id=1, source_target_pairs={{1,0},{2,1},{3,2},{4,3},{5,4},{6,5},{7,6},{9,8},{10,9},{11,10},{12... | collective-permute-start | bytes 393224 | tf_op jit(solution)/shard_map/ppermute | solution.py:28
  221.3 2.9 %copy-start.14 = (bf16[1024,256]{1,0:T(8,128)(2,1)S(1)}, bf16[1024,256]{1,0:T(8,128)(2,1)}, u32[]{:S(2)}) copy-start(bf16[1024,256]{1,0:T(8,128)(2,1)} %copy.118) | copy-start | bytes 1572868
  221.3 9.2 %copy-start.7 = (bf16[1024,256]{0,1:T(8,128)(2,1)S(1)}, bf16[1024,256]{0,1:T(8,128)(2,1)}, u32[]{:S(2)}) copy-start(bf16[1024,256]{0,1:T(8,128)(2,1)} %get-tuple-element.58) | copy-start | bytes 1572868
  224.9 15.8 %collective-permute-start.19 = (bf16[256,256]{1,0:T(8,128)(2,1)}, bf16[256,256]{1,0:T(8,128)(2,1)S(1)}, u32[]{:S(2)}, u32[]{:S(2)}) collective-permute-start(bf16[256,256]{1,0:T(8,128)(2,1)} %pad_maximum_fusion.19), channel_id=1, source_target_pairs={{8,0},{16,8},{24,16},{9,1},{17,9},{25,17},{10,2},{18,10},{26,18},{... | collective-permute-start | bytes 393224 | tf_op jit(solution)/shard_map/ppermute | solution.py:88
  226.8 12.1 %collective-permute-start.18 = (bf16[256,256]{1,0:T(8,128)(2,1)}, bf16[256,256]{1,0:T(8,128)(2,1)}, u32[]{:S(2)}, u32[]{:S(2)}) collective-permute-start(bf16[256,256]{1,0:T(8,128)(2,1)} %pad_maximum_fusion.18), channel_id=1, source_target_pairs={{0,8},{8,16},{16,24},{1,9},{9,17},{17,25},{2,10},{10,18},{18,26},{... | collective-permute-start | bytes 393224 | tf_op jit(solution)/shard_map/ppermute | solution.py:87
  231.2 10.9 %collective-permute-start.20 = (bf16[1024,64]{0,1:T(8,128)(2,1)}, bf16[1024,64]{0,1:T(8,128)(2,1)S(1)}, u32[]{:S(2)}, u32[]{:S(2)}) collective-permute-start(bf16[1024,64]{0,1:T(8,128)(2,1)} %get-tuple-element.14), channel_id=1, source_target_pairs={{0,1},{1,2},{2,3},{3,4},{4,5},{5,6},{6,7},{8,9},{9,10},{10,11},{11... | collective-permute-start | bytes 393224 | tf_op jit(solution)/shard_map/ppermute | solution.py:27
  235.1 7.9 %collective-permute-start.21 = (bf16[1024,64]{0,1:T(8,128)(2,1)}, bf16[1024,64]{0,1:T(8,128)(2,1)S(1)}, u32[]{:S(2)}, u32[]{:S(2)}) collective-permute-start(bf16[1024,64]{0,1:T(8,128)(2,1)} %get-tuple-element.15), channel_id=1, source_target_pairs={{1,0},{2,1},{3,2},{4,3},{5,4},{6,5},{7,6},{9,8},{10,9},{11,10},{12... | collective-permute-start | bytes 393224 | tf_op jit(solution)/shard_map/ppermute | solution.py:28
  238.9 4.1 %copy-start.4 = (bf16[1024,256]{0,1:T(8,128)(2,1)S(1)}, bf16[1024,256]{0,1:T(8,128)(2,1)}, u32[]{:S(2)}) copy-start(bf16[1024,256]{0,1:T(8,128)(2,1)} %copy-done) | copy-start | bytes 1572868
  238.9 4.1 %copy-start.8 = (bf16[1024,256]{0,1:T(8,128)(2,1)S(1)}, bf16[1024,256]{0,1:T(8,128)(2,1)}, u32[]{:S(2)}) copy-start(bf16[1024,256]{0,1:T(8,128)(2,1)} %get-tuple-element.58) | copy-start | bytes 1572868
Sparse Core Ops, SparseCore 0:
  12.6 25.2 all-gather.1

commit v4 on v2

--- a/solution.py
+++ b/solution.py
@@ -98,9 +98,14 @@
     first_space = spatial(rounded)
     first_time = temporal(rounded)
     nodes_dev = svc_coef.shape[0]
-    svc_all = lax.all_gather(svc_coef, "space", axis=0, tiled=True)
+    tables = [svc_coef] + [
+        lax.ppermute(svc_coef, "space", [(i, (i + k) % space_count) for i in range(space_count)])
+        for k in range(1, space_count)
+    ]
+    svc_all = jnp.concatenate(tables, axis=0)
     owner = obs_owner[:, 0]
-    coef_rows = svc_all[owner * nodes_dev + obs_cell // T_DEV]
+    shift = (lax.axis_index("space") - owner) % space_count
+    coef_rows = svc_all[shift * nodes_dev + obs_cell // T_DEV]
     eta = jnp.einsum("rc,rc->r", covariates, coef_rows, preferred_element_type=jnp.float32)
     obs_weight = jnp.exp(eta)
     bins = owner * (nodes_dev * T_DEV) + obs_cell

time: 202 us -> 192 us (0.950)
  between operations: 22.2 us -> 9.41 us
  other arithmetic: 16.9 us -> 20.8 us
  local copies, waits for them, and re-layouts: 41 us -> 38.6 us
  starting transfers between devices: 58.1 us -> 60.4 us
    ppermute x0 -> x3, starting transfers between devices: none -> 4.81 us  [shards(): lax.ppermute(svc_coef, 'space', [(i, (i + k) % space_count) for i in rang...]
    concatenate x0 -> x1, other arithmetic: none -> 3 us  [shards(): svc_all = jnp.concatenate(tables, axis=0)]
    unnamed x48 -> x52, local copies, waits for them, and re-layouts: 11.5 us -> 10.4 us
  transfers between devices with their start and end apart: 24 -> 26, of which waited for: 5 -> 5; matrix products, arithmetic and copies ran while one was open for 31% -> 33% of each run, Pallas kernels for 0% -> 0%
where the time goes in v4:
time: 192 us; the launch traced here: 190 us
  starting transfers between devices  60.4 us (31%)
  matrix products  39 us (20%)
  local copies, waits for them, and re-layouts  38.6 us (20%)
  other arithmetic  20.8 us (11%)
  waiting for transfers between devices  16.2 us (8%)
  between operations  9.41 us (5%)
  blocking collectives  5.76 us (3%)
    ppermute x5, starting transfers between devices, with_halo(): before = lax.ppermute(last, axis, up)  22.8 us
    ppermute x5, waiting for transfers between devices, with_halo(): after = lax.ppermute(initial, axis, down)  14.8 us
    dot_general x5, matrix products, spatial(): jnp.dot(upper_part, upper, preferred_element_type=jnp.float32)  14.4 us
    dot_general x5, matrix products, spatial(): total = jnp.dot(own_part, field, preferred_element_type=jnp.float32)  12.8 us
    ppermute x5, starting transfers between devices, spatial(): lower = lax.ppermute(pick_blocks(blocks, upper_wants), 'space', up)  12.3 us
    scatter-add x1, other arithmetic, shards(): jax.ops.segment_sum(obs_weight, bins, num_segments=space_count * nodes_de...  11.8 us
    unnamed x52, local copies, waits for them, and re-layouts  10.4 us
    gather x1, local copies, waits for them, and re-layouts, shards(): coef_rows = svc_all[shift * nodes_dev + obs_cell // T_DEV]  10.4 us
  transfers between devices with their start and end apart: 26, of which 5 were waited for; matrix products, arithmetic and copies ran while one was open for 33% of the time, Pallas kernels for 0%

profile of v4, /device:TPU:0, one launch (start us, length us, event | category | flops | bytes accessed | tf_op | source)
XLA Modules:
  0.0 190.2 jit_solution(14879145280327207192)
XLA Ops:
  0.7 3.1 %collective-permute-start.7 = (bf16[1024,256]{1,0:T(8,128)(2,1)}, bf16[1024,256]{1,0:T(8,128)(2,1)}, u32[]{:S(2)}, u32[]{:S(2)}) collective-permute-start(bf16[1024,256]{1,0:T(8,128)(2,1)} %param.23), channel_id=1, source_target_pairs={{0,16},{8,24},{16,0},{24,8},{1,17},{9,25},{17,1},{25,9},{2,18},{10... | collective-permute-start | bytes 1572872 | tf_op jit(solution)/shard_map/ppermute | solution.py:102
  3.7 1.7 collective-permute-start.8
  6.3 1.3 collective-permute-start.2
  7.6 1.3 collective-permute-start
  8.9 1.8 convert.8
  10.7 4.4 %copy.82 = bf16[8,128,128]{0,2,1:T(8,128)(2,1)} copy(bf16[8,128,128]{2,1,0:T(8,128)(2,1)} %param.16) | data formatting | bytes 524288 | tf_op args[4]
  15.6 2.0 %gather_fusion = bf16[128,8]{1,0:T(8,128)(2,1)S(1)} fusion(bf16[8,128,128]{0,2,1:T(8,128)(2,1)} %copy.82, s32[128]{0:T(128)S(1)} %or_bitcast_fusion), kind=kCustom, calls=%fused_computation | custom fusion | bytes 5120 | tf_op jit(solution)/shard_map/jit(diagonal)/gather | solution.py:51
  18.8 1.0 copy.122
  19.8 3.1 %add_convert_fusion = bf16[8,12,128,128]{3,1,2,0:T(8,128)(2,1)S(1)} fusion(f32[8,128,128]{2,1,0:T(8,128)} %convert.8, f32[8,12]{1,0:T(8,128)S(1)} %fusion.77, bf16[8,8,128,128]{3,2,1,0:T(8,128)(2,1)S(1)} %copy-done, s32[8,8]{1,0:T(8,128)S(1)} %copy-done.18), kind=kOutput, calls=%fused_computation.3 | convolution fusion | flops 29885184 | bytes 5767808 | tf_op jit(solution)/shard_map/bkm,bkij->bimj/dot_general | solution.py:60
  22.9 1.6 copy.135
  24.6 1.6 copy-done.1
  26.1 1.7 fusion.37
  27.9 4.1 %collective-permute-start.4 = (bf16[1024,64]{0,1:T(8,128)(2,1)}, bf16[1024,64]{0,1:T(8,128)(2,1)}, u32[]{:S(2)}, u32[]{:S(2)}) collective-permute-start(bf16[1024,64]{0,1:T(8,128)(2,1)} %get-tuple-element.34), channel_id=1, source_target_pairs={{0,1},{1,2},{2,3},{3,4},{4,5},{5,6},{6,7},{8,9},{9,10},{10,11},{11... | collective-permute-start | bytes 393224 | tf_op jit(solution)/shard_map/ppermute | solution.py:27
  35.2 1.3 collective-permute-start.5
  43.6 4.1 %collective-permute-start.1 = (bf16[256,256]{1,0:T(8,128)(2,1)S(1)}, bf16[256,256]{1,0:T(8,128)(2,1)}, u32[]{:S(2)}, u32[]{:S(2)}) collective-permute-start(bf16[256,256]{1,0:T(8,128)(2,1)S(1)} %pad_maximum_fusion.11), channel_id=1, source_target_pairs={{0,8},{8,16},{16,24},{1,9},{9,17},{17,25},{2,10},{10,18},{18,26},{... | collective-permute-start | bytes 393224 | tf_op jit(solution)/shard_map/ppermute | solution.py:81
  47.7 1.3 collective-permute-start.3
  49.0 3.0 %pad_maximum_fusion = bf16[4096,256]{1,0:T(8,128)(2,1)} fusion(bf16[1024,256]{1,0:T(8,128)(2,1)} %collective-permute-done.8, bf16[1024,256]{1,0:T(8,128)(2,1)} %collective-permute-done.7, bf16[1024,256]{1,0:T(8,128)(2,1)} %collective-permute-done.6, bf16[1024,256]{1,0:T(8,128)(2,1)} %param.23), kind=kLoop, calls=%fused_computation.12 | loop fusion | flops 8388608 | bytes 4194304 | tf_op jit(solution)/shard_map/concatenate | solution.py:105
  52.0 10.4 %gather_fusion.1 = bf16[2048,256]{1,0:T(8,128)(2,1)} fusion(bf16[4096,256]{1,0:T(8,128)(2,1)} %pad_maximum_fusion, s32[2048]{0:T(1024)S(1)} %get-tuple-element.42), kind=kCustom, calls=%fused_computation.1 | custom fusion | bytes 2105344 | tf_op jit(solution)/shard_map/gather | solution.py:108
  62.4 1.9 fusion
  64.3 11.8 %scatter_custom_fusion = f32[16384]{0:T(1024)} fusion(s32[2048]{0:T(1024)S(1)} %get-tuple-element.43, f32[2048]{0:T(1024)S(1)} %exp.3, f32[]{:T(128)} %constant.87.clone.1), kind=kCustom, calls=%fused_computation.138 | custom fusion | flops 2048 | bytes 65540 | tf_op jit(solution)/shard_map/scatter-add | solution.py:112
  76.1 4.9 %all-to-all-start = ((f32[4,1,4096]{2,1,0:T(1,128)}), f32[4,1,4096]{2,1,0:T(1,128)S(1)}, u32[]{:S(2)}, u32[]{:S(2)}) async-start(f32[4,1,4096]{2,1,0:T(1,128)} %bitcast.16), calls=%async_computation | async-start | bytes 131072 | tf_op jit(solution)/shard_map/all_to_all | solution.py:116
  81.0 2.8 %convolution_add_fusion.9 = f32[1024,256]{0,1:T(8,128)} fusion(f32[1024,256]{0,1:T(8,128)} %fusion.37, bf16[256,256]{1,0:T(8,128)(2,1)} %collective-permute-done.1, bf16[1024,1536]{1,0:T(8,128)(2,1)} %bitcast.98), kind=kOutput, calls=%fused_computation.43 | convolution fusion | flops 134479872 | bytes 2752512 | tf_op jit(solution)/shard_map/dot_general | solution.py:84
  83.8 1.3 all-to-all-done
  85.2 1.3 reshape.56
  86.5 1.2 copy.91
  88.2 4.0 %fusion.86 = (bf16[1024,256]{0,1:T(8,128)(2,1)}, f32[1024,256]{0,1:T(8,128)}) fusion(f32[1024,256]{0,1:T(8,128)S(1)} %get-tuple-element.41, f32[1024,256]{0,1:T(8,128)S(1)} %get-tuple-element.40, bf16[1024,64]{0,1:T(8,128)(2,1)} %collective-permute-done.5, bf16[1024,256]{0,1:T(8,128)(2,1)S(1)} %fusion.55, bf16[1024,64]{0,1:T(8,128)(2,1)} %collective-permute-done.4, ...), kind=kOutput, calls=%fused_computation.174 | convolution fusion | flops 141557760 | bytes 6695936 | tf_op jit(solution)/shard_map/dot_general | solution.py:85
  92.2 2.1 %copy.123 = bf16[1024,256]{1,0:T(8,128)(2,1)} copy(bf16[1024,256]{0,1:T(8,128)(2,1)} %get-tuple-element.52) | data formatting | bytes 1048576 | tf_op jit(solution)/shard_map/reshape | solution.py:80
  94.3 2.5 %fusion.35 = f32[1024,256]{0,1:T(8,128)S(1)} fusion(bf16[1024,256]{0,1:T(8,128)(2,1)} %get-tuple-element.52, bf16[1024,1536]{1,0:T(8,128)(2,1)} %bitcast.100), kind=kOutput, calls=%fused_computation.65 | convolution fusion | flops 536870912 | bytes 3670016 | tf_op jit(solution)/shard_map/dot_general | solution.py:83
  96.9 1.7 collective-permute-start.9
  98.8 4.6 %collective-permute-start.11 = (bf16[1024,64]{0,1:T(8,128)(2,1)S(1)}, bf16[1024,64]{0,1:T(8,128)(2,1)S(1)}, u32[]{:S(2)}, u32[]{:S(2)}) collective-permute-start(bf16[1024,64]{0,1:T(8,128)(2,1)S(1)} %get-tuple-element.28), channel_id=1, source_target_pairs={{0,1},{1,2},{2,3},{3,4},{4,5},{5,6},{6,7},{8,9},{9,10},{10,11},{11... | collective-permute-start | bytes 393224 | tf_op jit(solution)/shard_map/ppermute | solution.py:27
  103.4 1.5 collective-permute-start.12
  104.9 1.3 collective-permute-start.10
  106.2 1.4 convolution_add_fusion.7
  107.6 4.2 %collective-permute-done.12 = bf16[1024,64]{0,1:T(8,128)(2,1)S(1)} collective-permute-done((bf16[1024,64]{0,1:T(8,128)(2,1)S(1)}, bf16[1024,64]{0,1:T(8,128)(2,1)S(1)}, u32[]{:S(2)}, u32[]{:S(2)}) %collective-permute-start.12) | collective-permute-done | bytes 131104 | tf_op jit(solution)/shard_map/ppermute | solution.py:28
  111.8 3.0 %fusion.87 = (bf16[1024,256]{0,1:T(8,128)(2,1)}, f32[1024,256]{0,1:T(8,128)}) fusion(f32[1024,256]{0,1:T(8,128)S(1)} %copy-done.22, f32[1024,256]{0,1:T(8,128)S(1)} %copy-done.11, f32[1024,256]{0,1:T(8,128)S(1)} %fusion.4, bf16[1024,64]{0,1:T(8,128)(2,1)S(1)} %collective-permute-done.12, bf16[1024,256]{0,1:T(8,128)(2,1)S(1)} %copy-done.2, ...), kind=kOutput, calls=%fused_computation.175 | convolution fusion | flops 140247040 | bytes 7735296 | tf_op jit(solution)/shard_map/dot_general | solution.py:85
  114.8 2.1 %copy.124 = bf16[1024,256]{1,0:T(8,128)(2,1)} copy(bf16[1024,256]{0,1:T(8,128)(2,1)} %get-tuple-element.54) | data formatting | bytes 1048576 | tf_op jit(solution)/shard_map/reshape | solution.py:80
  117.0 2.5 %fusion.33 = f32[1024,256]{0,1:T(8,128)S(1)} fusion(bf16[1024,256]{0,1:T(8,128)(2,1)} %get-tuple-element.54, bf16[1024,1536]{1,0:T(8,128)(2,1)} %bitcast.103), kind=kOutput, calls=%fused_computation.63 | convolution fusion | flops 536870912 | bytes 3670016 | tf_op jit(solution)/shard_map/dot_general | solution.py:83
  119.6 2.3 %collective-permute-start.13 = (bf16[256,256]{1,0:T(8,128)(2,1)S(1)}, bf16[256,256]{1,0:T(8,128)(2,1)S(1)}, u32[]{:S(2)}, u32[]{:S(2)}) collective-permute-start(bf16[256,256]{1,0:T(8,128)(2,1)S(1)} %pad_maximum_fusion.15), channel_id=1, source_target_pairs={{0,8},{8,16},{16,24},{1,9},{9,17},{17,25},{2,10},{10,18},{18,26},{... | collective-permute-start | bytes 393224 | tf_op jit(solution)/shard_map/ppermute | solution.py:81
  122.1 4.4 %collective-permute-start.15 = (bf16[1024,64]{0,1:T(8,128)(2,1)S(1)}, bf16[1024,64]{0,1:T(8,128)(2,1)S(1)}, u32[]{:S(2)}, u32[]{:S(2)}) collective-permute-start(bf16[1024,64]{0,1:T(8,128)(2,1)S(1)} %get-tuple-element.22), channel_id=1, source_target_pairs={{0,1},{1,2},{2,3},{3,4},{4,5},{5,6},{6,7},{8,9},{9,10},{10,11},{11... | collective-permute-start | bytes 393224 | tf_op jit(solution)/shard_map/ppermute | solution.py:27
  126.5 1.3 collective-permute-start.16
  127.8 1.3 collective-permute-start.14
  129.1 1.4 convolution_add_fusion.5
  130.5 3.8 %collective-permute-done.16 = bf16[1024,64]{0,1:T(8,128)(2,1)S(1)} collective-permute-done((bf16[1024,64]{0,1:T(8,128)(2,1)S(1)}, bf16[1024,64]{0,1:T(8,128)(2,1)S(1)}, u32[]{:S(2)}, u32[]{:S(2)}) %collective-permute-start.16) | collective-permute-done | bytes 131104 | tf_op jit(solution)/shard_map/ppermute | solution.py:28
  134.4 2.8 %fusion.88 = (bf16[1024,256]{0,1:T(8,128)(2,1)S(1)}, f32[1024,256]{0,1:T(8,128)}) fusion(f32[1024,256]{0,1:T(8,128)S(1)} %copy-done.23, f32[1024,256]{0,1:T(8,128)S(1)} %copy-done.12, f32[1024,256]{0,1:T(8,128)S(1)} %fusion.3, bf16[1024,64]{0,1:T(8,128)(2,1)S(1)} %collective-permute-done.16, bf16[1024,256]{0,1:T(8,128)(2,1)S(1)} %copy-done.5, ...), kind=kOutput, calls=%fused_computation.176 | convolution fusion | flops 140247040 | bytes 7735296 | tf_op jit(solution)/shard_map/dot_general | solution.py:85
  137.2 1.0 copy.125
  138.2 2.4 %fusion.31 = f32[1024,256]{0,1:T(8,128)S(1)} fusion(bf16[1024,256]{0,1:T(8,128)(2,1)S(1)} %get-tuple-element.56, bf16[1024,1536]{1,0:T(8,128)(2,1)} %bitcast.106), kind=kOutput, calls=%fused_computation.61 | convolution fusion | flops 536870912 | bytes 3670016 | tf_op jit(solution)/shard_map/dot_general | solution.py:83
  140.7 1.8 collective-permute-start.17
  142.6 4.9 %collective-permute-start.19 = (bf16[1024,64]{0,1:T(8,128)(2,1)S(1)}, bf16[1024,64]{0,1:T(8,128)(2,1)S(1)}, u32[]{:S(2)}, u32[]{:S(2)}) collective-permute-start(bf16[1024,64]{0,1:T(8,128)(2,1)S(1)} %get-tuple-element.16), channel_id=1, source_target_pairs={{0,1},{1,2},{2,3},{3,4},{4,5},{5,6},{6,7},{8,9},{9,10},{10,11},{11... | collective-permute-start | bytes 393224 | tf_op jit(solution)/shard_map/ppermute | solution.py:27
  147.5 1.3 collective-permute-start.20
  148.8 1.3 collective-permute-start.18
  150.2 1.4 convolution_add_fusion.3
  151.6 3.8 %collective-permute-done.20 = bf16[1024,64]{0,1:T(8,128)(2,1)S(1)} collective-permute-done((bf16[1024,64]{0,1:T(8,128)(2,1)S(1)}, bf16[1024,64]{0,1:T(8,128)(2,1)S(1)}, u32[]{:S(2)}, u32[]{:S(2)}) %collective-permute-start.20) | collective-permute-done | bytes 131104 | tf_op jit(solution)/shard_map/ppermute | solution.py:28
  155.4 3.0 %fusion.89 = (bf16[1024,256]{0,1:T(8,128)(2,1)}, f32[1024,256]{0,1:T(8,128)}) fusion(f32[1024,256]{0,1:T(8,128)S(1)} %copy-done.21, f32[1024,256]{0,1:T(8,128)S(1)} %copy-done.13, f32[1024,256]{0,1:T(8,128)S(1)} %fusion.2, bf16[1024,64]{0,1:T(8,128)(2,1)S(1)} %collective-permute-done.20, bf16[1024,256]{0,1:T(8,128)(2,1)S(1)} %get-tuple-element.56, ...), kind=kOutput, calls=%fused_computation.177 | convolution fusion | flops 140247040 | bytes 7735296 | tf_op jit(solution)/shard_map/dot_general | solution.py:85
  158.4 2.1 %copy.126 = bf16[1024,256]{1,0:T(8,128)(2,1)} copy(bf16[1024,256]{0,1:T(8,128)(2,1)} %get-tuple-element.58) | data formatting | bytes 1048576 | tf_op jit(solution)/shard_map/reshape | solution.py:80
  160.5 3.6 %fusion.39 = f32[1024,256]{0,1:T(8,128)} fusion(bf16[1024,256]{0,1:T(8,128)(2,1)} %get-tuple-element.58, bf16[1024,1536]{1,0:T(8,128)(2,1)} %bitcast.109), kind=kOutput, calls=%fused_computation.69 | convolution fusion | flops 536870912 | bytes 3670016 | tf_op jit(solution)/shard_map/dot_general | solution.py:83
  164.1 2.3 %collective-permute-start.21 = (bf16[256,256]{1,0:T(8,128)(2,1)S(1)}, bf16[256,256]{1,0:T(8,128)(2,1)}, u32[]{:S(2)}, u32[]{:S(2)}) collective-permute-start(bf16[256,256]{1,0:T(8,128)(2,1)S(1)} %pad_maximum_fusion.19), channel_id=1, source_target_pairs={{0,8},{8,16},{16,24},{1,9},{9,17},{17,25},{2,10},{10,18},{18,26},{... | collective-permute-start | bytes 393224 | tf_op jit(solution)/shard_map/ppermute | solution.py:81
  167.1 2.5 %copy.111 = f32[1024,256]{1,0:T(8,128)} copy(f32[1024,256]{0,1:T(8,128)} %get-tuple-element.59) | data formatting | bytes 2097152
  169.7 4.9 %collective-permute-start.23 = (bf16[1024,64]{0,1:T(8,128)(2,1)}, bf16[1024,64]{0,1:T(8,128)(2,1)S(1)}, u32[]{:S(2)}, u32[]{:S(2)}) collective-permute-start(bf16[1024,64]{0,1:T(8,128)(2,1)} %get-tuple-element.14), channel_id=1, source_target_pairs={{0,1},{1,2},{2,3},{3,4},{4,5},{5,6},{6,7},{8,9},{9,10},{10,11},{11... | collective-permute-start | bytes 393224 | tf_op jit(solution)/shard_map/ppermute | solution.py:27
  174.5 1.3 collective-permute-start.24
  175.9 1.3 collective-permute-start.22
  177.2 1.8 convolution_add_fusion.1
  179.0 2.9 %collective-permute-done.24 = bf16[1024,64]{0,1:T(8,128)(2,1)S(1)} collective-permute-done((bf16[1024,64]{0,1:T(8,128)(2,1)S(1)}, bf16[1024,64]{0,1:T(8,128)(2,1)S(1)}, u32[]{:S(2)}, u32[]{:S(2)}) %collective-permute-start.24) | collective-permute-done | bytes 131104 | tf_op jit(solution)/shard_map/ppermute | solution.py:28
  182.3 1.5 fusion.30
  183.8 5.8 %psum.7 = f32[2,256]{1,0:T(2,128)S(1)} all-reduce(f32[2,256]{1,0:T(2,128)S(1)} %pad_maximum_fusion.21), channel_id=1, replica_groups=mesh['space'=4,'tm'=8] {'space'}, use_global_device_ids=true, to_apply=%region_4.5 | all-reduce | flops 512 | bytes 4096 | tf_op jit(solution)/shard_map/psum | solution.py:142
  (114 shorter events, 7.6 us)
Async XLA Ops:
  0.6 19.1 %copy-start = (bf16[8,8,128,128]{3,2,1,0:T(8,128)(2,1)S(1)}, bf16[8,8,128,128]{3,2,1,0:T(8,128)(2,1)}, u32[]{:S(2)}) copy-start(bf16[8,8,128,128]{3,2,1,0:T(8,128)(2,1)} %param.17) | copy-start | bytes 6291460
  0.6 14.4 %copy-start.19 = (f32[4]{0:T(128)S(1)}, f32[4]{0:T(128)}, u32[]{:S(2)}) copy-start(f32[4]{0:T(128)} %param.14) | copy-start | bytes 52
  0.7 14.6 %copy-start.20 = (f32[4]{0:T(128)S(1)}, f32[4]{0:T(128)}, u32[]{:S(2)}) copy-start(f32[4]{0:T(128)} %param.15) | copy-start | bytes 52
  0.7 14.7 %copy-start.14 = (bf16[1024,256]{1,0:T(8,128)(2,1)S(1)}, bf16[1024,256]{1,0:T(8,128)(2,1)}, u32[]{:S(2)}) copy-start(bf16[1024,256]{1,0:T(8,128)(2,1)} %param.12) | copy-start | bytes 1572868
  0.7 42.9 %collective-permute-start.7 = (bf16[1024,256]{1,0:T(8,128)(2,1)}, bf16[1024,256]{1,0:T(8,128)(2,1)}, u32[]{:S(2)}, u32[]{:S(2)}) collective-permute-start(bf16[1024,256]{1,0:T(8,128)(2,1)} %param.23), channel_id=1, source_target_pairs={{0,16},{8,24},{16,0},{24,8},{1,17},{9,25},{17,1},{25,9},{2,18},{10... | collective-permute-start | bytes 1572872 | tf_op jit(solution)/shard_map/ppermute | solution.py:102
  3.7 44.0 %collective-permute-start.6 = (bf16[1024,256]{1,0:T(8,128)(2,1)}, bf16[1024,256]{1,0:T(8,128)(2,1)}, u32[]{:S(2)}, u32[]{:S(2)}) collective-permute-start(bf16[1024,256]{1,0:T(8,128)(2,1)} %param.23), channel_id=1, source_target_pairs={{0,8},{8,16},{16,24},{24,0},{1,9},{9,17},{17,25},{25,1},{2,10},{10... | collective-permute-start | bytes 1572872 | tf_op jit(solution)/shard_map/ppermute | solution.py:102
  3.7 45.3 %collective-permute-start.8 = (bf16[1024,256]{1,0:T(8,128)(2,1)}, bf16[1024,256]{1,0:T(8,128)(2,1)}, u32[]{:S(2)}, u32[]{:S(2)}) collective-permute-start(bf16[1024,256]{1,0:T(8,128)(2,1)} %param.23), channel_id=1, source_target_pairs={{0,24},{8,0},{16,8},{24,16},{1,25},{9,1},{17,9},{25,17},{2,26},{10... | collective-permute-start | bytes 1572872 | tf_op jit(solution)/shard_map/ppermute | solution.py:102
  6.3 21.6 %collective-permute-start.2 = (s32[2]{0:T(128)S(1)}, s32[2]{0:T(128)S(1)}, u32[]{:S(2)}, u32[]{:S(2)}) collective-permute-start(s32[2]{0:T(128)S(1)} %get-tuple-element.48), channel_id=1, source_target_pairs={{0,8},{8,16},{16,24},{1,9},{9,17},{17,25},{2,10},{10,18},{18,26},{... | collective-permute-start | bytes 32 | tf_op jit(solution)/shard_map/ppermute | solution.py:71
  7.6 27.6 %collective-permute-start = (s32[2]{0:T(128)S(1)}, s32[2]{0:T(128)S(1)}, u32[]{:S(2)}, u32[]{:S(2)}) collective-permute-start(s32[2]{0:T(128)S(1)} %get-tuple-element.49), channel_id=1, source_target_pairs={{8,0},{16,8},{24,16},{9,1},{17,9},{25,17},{10,2},{18,10},{26,18},{... | collective-permute-start | bytes 32 | tf_op jit(solution)/shard_map/ppermute | solution.py:70
  8.9 8.7 %copy-start.15 = (f32[1024]{0:T(1024)S(1)}, f32[1024]{0:T(1024)}, u32[]{:S(2)}) copy-start(f32[1024]{0:T(1024)} %param.13) | copy-start | bytes 12292
  10.7 9.1 %copy-start.18 = (s32[8,8]{1,0:T(8,128)S(1)}, s32[8,8]{1,0:T(8,128)}, u32[]{:S(2)}) copy-start(s32[8,8]{1,0:T(8,128)} %param.18) | copy-start | bytes 772
  24.5 1.6 copy-start.1
  24.5 3.3 %copy-start.16 = (s32[2048,1]{0,1:T(1,128)S(1)}, s32[2048,1]{0,1:T(1,128)}, u32[]{:S(2)}) copy-start(s32[2048,1]{0,1:T(1,128)} %param.21) | copy-start | bytes 24580
  24.5 3.3 %copy-start.17 = (s32[2048]{0:T(1024)S(1)}, s32[2048]{0:T(1024)}, u32[]{:S(2)}) copy-start(s32[2048]{0:T(1024)} %param.22) | copy-start | bytes 24580
  27.9 60.2 %collective-permute-start.4 = (bf16[1024,64]{0,1:T(8,128)(2,1)}, bf16[1024,64]{0,1:T(8,128)(2,1)}, u32[]{:S(2)}, u32[]{:S(2)}) collective-permute-start(bf16[1024,64]{0,1:T(8,128)(2,1)} %get-tuple-element.34), channel_id=1, source_target_pairs={{0,1},{1,2},{2,3},{3,4},{4,5},{5,6},{6,7},{8,9},{9,10},{10,11},{11... | collective-permute-start | bytes 393224 | tf_op jit(solution)/shard_map/ppermute | solution.py:27
  35.2 53.0 %collective-permute-start.5 = (bf16[1024,64]{0,1:T(8,128)(2,1)}, bf16[1024,64]{0,1:T(8,128)(2,1)}, u32[]{:S(2)}, u32[]{:S(2)}) collective-permute-start(bf16[1024,64]{0,1:T(8,128)(2,1)} %get-tuple-element.35), channel_id=1, source_target_pairs={{1,0},{2,1},{3,2},{4,3},{5,4},{6,5},{7,6},{9,8},{10,9},{11,10},{12... | collective-permute-start | bytes 393224 | tf_op jit(solution)/shard_map/ppermute | solution.py:28
  43.6 37.4 %collective-permute-start.1 = (bf16[256,256]{1,0:T(8,128)(2,1)S(1)}, bf16[256,256]{1,0:T(8,128)(2,1)}, u32[]{:S(2)}, u32[]{:S(2)}) collective-permute-start(bf16[256,256]{1,0:T(8,128)(2,1)S(1)} %pad_maximum_fusion.11), channel_id=1, source_target_pairs={{0,8},{8,16},{16,24},{1,9},{9,17},{17,25},{2,10},{10,18},{18,26},{... | collective-permute-start | bytes 393224 | tf_op jit(solution)/shard_map/ppermute | solution.py:81
  47.7 40.4 %collective-permute-start.3 = (bf16[256,256]{1,0:T(8,128)(2,1)S(1)}, bf16[256,256]{1,0:T(8,128)(2,1)}, u32[]{:S(2)}, u32[]{:S(2)}) collective-permute-start(bf16[256,256]{1,0:T(8,128)(2,1)S(1)} %pad_maximum_fusion.12), channel_id=1, source_target_pairs={{8,0},{16,8},{24,16},{9,1},{17,9},{25,17},{10,2},{18,10},{26,18},{... | collective-permute-start | bytes 393224 | tf_op jit(solution)/shard_map/ppermute | solution.py:82
  76.1 9.0 %all-to-all-start = ((f32[4,1,4096]{2,1,0:T(1,128)}), f32[4,1,4096]{2,1,0:T(1,128)S(1)}, u32[]{:S(2)}, u32[]{:S(2)}) async-start(f32[4,1,4096]{2,1,0:T(1,128)} %bitcast.16), calls=%async_computation | async-start | bytes 131072 | tf_op jit(solution)/shard_map/all_to_all | solution.py:116
  88.1 4.1 %copy-start.10 = (f32[1024,256]{0,1:T(8,128)}, f32[1024,256]{0,1:T(8,128)S(1)}, u32[]{:S(2)}) copy-start(f32[1024,256]{0,1:T(8,128)S(1)} %get-tuple-element.41) | copy-start | bytes 3145732
  92.2 6.5 %copy-start.2 = (bf16[1024,256]{0,1:T(8,128)(2,1)S(1)}, bf16[1024,256]{0,1:T(8,128)(2,1)}, u32[]{:S(2)}) copy-start(bf16[1024,256]{0,1:T(8,128)(2,1)} %get-tuple-element.52) | copy-start | bytes 1572868
  94.3 2.6 %copy-start.7 = (bf16[1024,256]{1,0:T(8,128)(2,1)S(1)}, bf16[1024,256]{1,0:T(8,128)(2,1)}, u32[]{:S(2)}) copy-start(bf16[1024,256]{1,0:T(8,128)(2,1)} %copy.123) | copy-start | bytes 1572868
  96.9 14.9 %copy-start.11 = (f32[1024,256]{0,1:T(8,128)S(1)}, f32[1024,256]{0,1:T(8,128)}, u32[]{:S(2)}) copy-start(f32[1024,256]{0,1:T(8,128)} %copy-done.10) | copy-start | bytes 3145732
  96.9 14.9 %copy-start.22 = (f32[1024,256]{0,1:T(8,128)S(1)}, f32[1024,256]{0,1:T(8,128)}, u32[]{:S(2)}) copy-start(f32[1024,256]{0,1:T(8,128)} %get-tuple-element.53) | copy-start | bytes 3145732
  96.9 9.2 %collective-permute-start.9 = (bf16[256,256]{1,0:T(8,128)(2,1)S(1)}, bf16[256,256]{1,0:T(8,128)(2,1)S(1)}, u32[]{:S(2)}, u32[]{:S(2)}) collective-permute-start(bf16[256,256]{1,0:T(8,128)(2,1)S(1)} %pad_maximum_fusion.13), channel_id=1, source_target_pairs={{0,8},{8,16},{16,24},{1,9},{9,17},{17,25},{2,10},{10,18},{18,26},{... | collective-permute-start | bytes 393224 | tf_op jit(solution)/shard_map/ppermute | solution.py:81
  98.8 8.8 %collective-permute-start.11 = (bf16[1024,64]{0,1:T(8,128)(2,1)S(1)}, bf16[1024,64]{0,1:T(8,128)(2,1)S(1)}, u32[]{:S(2)}, u32[]{:S(2)}) collective-permute-start(bf16[1024,64]{0,1:T(8,128)(2,1)S(1)} %get-tuple-element.28), channel_id=1, source_target_pairs={{0,1},{1,2},{2,3},{3,4},{4,5},{5,6},{6,7},{8,9},{9,10},{10,11},{11... | collective-permute-start | bytes 393224 | tf_op jit(solution)/shard_map/ppermute | solution.py:27
  103.4 8.4 %collective-permute-start.12 = (bf16[1024,64]{0,1:T(8,128)(2,1)S(1)}, bf16[1024,64]{0,1:T(8,128)(2,1)S(1)}, u32[]{:S(2)}, u32[]{:S(2)}) collective-permute-start(bf16[1024,64]{0,1:T(8,128)(2,1)S(1)} %get-tuple-element.29), channel_id=1, source_target_pairs={{1,0},{2,1},{3,2},{4,3},{5,4},{6,5},{7,6},{9,8},{10,9},{11,10},{12... | collective-permute-start | bytes 393224 | tf_op jit(solution)/shard_map/ppermute | solution.py:28
  104.9 6.9 %collective-permute-start.10 = (bf16[256,256]{1,0:T(8,128)(2,1)S(1)}, bf16[256,256]{1,0:T(8,128)(2,1)S(1)}, u32[]{:S(2)}, u32[]{:S(2)}) collective-permute-start(bf16[256,256]{1,0:T(8,128)(2,1)S(1)} %pad_maximum_fusion.14), channel_id=1, source_target_pairs={{8,0},{16,8},{24,16},{9,1},{17,9},{25,17},{10,2},{18,10},{26,18},{... | collective-permute-start | bytes 393224 | tf_op jit(solution)/shard_map/ppermute | solution.py:82
  114.8 7.1 %copy-start.4 = (bf16[1024,256]{0,1:T(8,128)(2,1)S(1)}, bf16[1024,256]{0,1:T(8,128)(2,1)}, u32[]{:S(2)}) copy-start(bf16[1024,256]{0,1:T(8,128)(2,1)} %get-tuple-element.54) | copy-start | bytes 1572868
  117.0 2.6 %copy-start.8 = (bf16[1024,256]{1,0:T(8,128)(2,1)S(1)}, bf16[1024,256]{1,0:T(8,128)(2,1)}, u32[]{:S(2)}) copy-start(bf16[1024,256]{1,0:T(8,128)(2,1)} %copy.124) | copy-start | bytes 1572868
  119.5 14.8 %copy-start.5 = (bf16[1024,256]{0,1:T(8,128)(2,1)S(1)}, bf16[1024,256]{0,1:T(8,128)(2,1)}, u32[]{:S(2)}) copy-start(bf16[1024,256]{0,1:T(8,128)(2,1)} %get-tuple-element.54) | copy-start | bytes 1572868
  119.5 14.8 %copy-start.12 = (f32[1024,256]{0,1:T(8,128)S(1)}, f32[1024,256]{0,1:T(8,128)}, u32[]{:S(2)}) copy-start(f32[1024,256]{0,1:T(8,128)} %copy-done.10) | copy-start | bytes 3145732
  119.5 14.8 %copy-start.23 = (f32[1024,256]{0,1:T(8,128)S(1)}, f32[1024,256]{0,1:T(8,128)}, u32[]{:S(2)}) copy-start(f32[1024,256]{0,1:T(8,128)} %get-tuple-element.55) | copy-start | bytes 3145732
  119.6 9.5 %collective-permute-start.13 = (bf16[256,256]{1,0:T(8,128)(2,1)S(1)}, bf16[256,256]{1,0:T(8,128)(2,1)S(1)}, u32[]{:S(2)}, u32[]{:S(2)}) collective-permute-start(bf16[256,256]{1,0:T(8,128)(2,1)S(1)} %pad_maximum_fusion.15), channel_id=1, source_target_pairs={{0,8},{8,16},{16,24},{1,9},{9,17},{17,25},{2,10},{10,18},{18,26},{... | collective-permute-start | bytes 393224 | tf_op jit(solution)/shard_map/ppermute | solution.py:81
  122.1 8.4 %collective-permute-start.15 = (bf16[1024,64]{0,1:T(8,128)(2,1)S(1)}, bf16[1024,64]{0,1:T(8,128)(2,1)S(1)}, u32[]{:S(2)}, u32[]{:S(2)}) collective-permute-start(bf16[1024,64]{0,1:T(8,128)(2,1)S(1)} %get-tuple-element.22), channel_id=1, source_target_pairs={{0,1},{1,2},{2,3},{3,4},{4,5},{5,6},{6,7},{8,9},{9,10},{10,11},{11... | collective-permute-start | bytes 393224 | tf_op jit(solution)/shard_map/ppermute | solution.py:27
  126.5 7.8 %collective-permute-start.16 = (bf16[1024,64]{0,1:T(8,128)(2,1)S(1)}, bf16[1024,64]{0,1:T(8,128)(2,1)S(1)}, u32[]{:S(2)}, u32[]{:S(2)}) collective-permute-start(bf16[1024,64]{0,1:T(8,128)(2,1)S(1)} %get-tuple-element.23), channel_id=1, source_target_pairs={{1,0},{2,1},{3,2},{4,3},{5,4},{6,5},{7,6},{9,8},{10,9},{11,10},{12... | collective-permute-start | bytes 393224 | tf_op jit(solution)/shard_map/ppermute | solution.py:28
  127.8 6.5 %collective-permute-start.14 = (bf16[256,256]{1,0:T(8,128)(2,1)S(1)}, bf16[256,256]{1,0:T(8,128)(2,1)S(1)}, u32[]{:S(2)}, u32[]{:S(2)}) collective-permute-start(bf16[256,256]{1,0:T(8,128)(2,1)S(1)} %pad_maximum_fusion.16), channel_id=1, source_target_pairs={{8,0},{16,8},{24,16},{9,1},{17,9},{25,17},{10,2},{18,10},{26,18},{... | collective-permute-start | bytes 393224 | tf_op jit(solution)/shard_map/ppermute | solution.py:82
  138.2 2.4 %copy-start.9 = (bf16[1024,256]{1,0:T(8,128)(2,1)S(1)}, bf16[1024,256]{1,0:T(8,128)(2,1)}, u32[]{:S(2)}) copy-start(bf16[1024,256]{1,0:T(8,128)(2,1)} %copy.125) | copy-start | bytes 1572868
  140.6 14.8 %copy-start.13 = (f32[1024,256]{0,1:T(8,128)S(1)}, f32[1024,256]{0,1:T(8,128)}, u32[]{:S(2)}) copy-start(f32[1024,256]{0,1:T(8,128)} %copy-done.10) | copy-start | bytes 3145732
  140.6 14.8 %copy-start.21 = (f32[1024,256]{0,1:T(8,128)S(1)}, f32[1024,256]{0,1:T(8,128)}, u32[]{:S(2)}) copy-start(f32[1024,256]{0,1:T(8,128)} %get-tuple-element.57) | copy-start | bytes 3145732
  140.7 9.5 %collective-permute-start.17 = (bf16[256,256]{1,0:T(8,128)(2,1)S(1)}, bf16[256,256]{1,0:T(8,128)(2,1)S(1)}, u32[]{:S(2)}, u32[]{:S(2)}) collective-permute-start(bf16[256,256]{1,0:T(8,128)(2,1)S(1)} %pad_maximum_fusion.17), channel_id=1, source_target_pairs={{0,8},{8,16},{16,24},{1,9},{9,17},{17,25},{2,10},{10,18},{18,26},{... | collective-permute-start | bytes 393224 | tf_op jit(solution)/shard_map/ppermute | solution.py:81
  142.6 8.9 %collective-permute-start.19 = (bf16[1024,64]{0,1:T(8,128)(2,1)S(1)}, bf16[1024,64]{0,1:T(8,128)(2,1)S(1)}, u32[]{:S(2)}, u32[]{:S(2)}) collective-permute-start(bf16[1024,64]{0,1:T(8,128)(2,1)S(1)} %get-tuple-element.16), channel_id=1, source_target_pairs={{0,1},{1,2},{2,3},{3,4},{4,5},{5,6},{6,7},{8,9},{9,10},{10,11},{11... | collective-permute-start | bytes 393224 | tf_op jit(solution)/shard_map/ppermute | solution.py:27
  147.5 7.8 %collective-permute-start.20 = (bf16[1024,64]{0,1:T(8,128)(2,1)S(1)}, bf16[1024,64]{0,1:T(8,128)(2,1)S(1)}, u32[]{:S(2)}, u32[]{:S(2)}) collective-permute-start(bf16[1024,64]{0,1:T(8,128)(2,1)S(1)} %get-tuple-element.17), channel_id=1, source_target_pairs={{1,0},{2,1},{3,2},{4,3},{5,4},{6,5},{7,6},{9,8},{10,9},{11,10},{12... | collective-permute-start | bytes 393224 | tf_op jit(solution)/shard_map/ppermute | solution.py:28
  148.8 6.5 %collective-permute-start.18 = (bf16[256,256]{1,0:T(8,128)(2,1)S(1)}, bf16[256,256]{1,0:T(8,128)(2,1)S(1)}, u32[]{:S(2)}, u32[]{:S(2)}) collective-permute-start(bf16[256,256]{1,0:T(8,128)(2,1)S(1)} %pad_maximum_fusion.18), channel_id=1, source_target_pairs={{8,0},{16,8},{24,16},{9,1},{17,9},{25,17},{10,2},{18,10},{26,18},{... | collective-permute-start | bytes 393224 | tf_op jit(solution)/shard_map/ppermute | solution.py:82
  158.4 8.1 %copy-start.3 = (bf16[1024,256]{0,1:T(8,128)(2,1)S(1)}, bf16[1024,256]{0,1:T(8,128)(2,1)}, u32[]{:S(2)}) copy-start(bf16[1024,256]{0,1:T(8,128)(2,1)} %get-tuple-element.58) | copy-start | bytes 1572868
  160.5 3.6 %copy-start.6 = (bf16[1024,256]{1,0:T(8,128)(2,1)S(1)}, bf16[1024,256]{1,0:T(8,128)(2,1)}, u32[]{:S(2)}) copy-start(bf16[1024,256]{1,0:T(8,128)(2,1)} %copy.126) | copy-start | bytes 1572868
  164.1 13.0 %collective-permute-start.21 = (bf16[256,256]{1,0:T(8,128)(2,1)S(1)}, bf16[256,256]{1,0:T(8,128)(2,1)}, u32[]{:S(2)}, u32[]{:S(2)}) collective-permute-start(bf16[256,256]{1,0:T(8,128)(2,1)S(1)} %pad_maximum_fusion.19), channel_id=1, source_target_pairs={{0,8},{8,16},{16,24},{1,9},{9,17},{17,25},{2,10},{10,18},{18,26},{... | collective-permute-start | bytes 393224 | tf_op jit(solution)/shard_map/ppermute | solution.py:81
  169.7 9.3 %collective-permute-start.23 = (bf16[1024,64]{0,1:T(8,128)(2,1)}, bf16[1024,64]{0,1:T(8,128)(2,1)S(1)}, u32[]{:S(2)}, u32[]{:S(2)}) collective-permute-start(bf16[1024,64]{0,1:T(8,128)(2,1)} %get-tuple-element.14), channel_id=1, source_target_pairs={{0,1},{1,2},{2,3},{3,4},{4,5},{5,6},{6,7},{8,9},{9,10},{10,11},{11... | collective-permute-start | bytes 393224 | tf_op jit(solution)/shard_map/ppermute | solution.py:27
  174.5 7.4 %collective-permute-start.24 = (bf16[1024,64]{0,1:T(8,128)(2,1)S(1)}, bf16[1024,64]{0,1:T(8,128)(2,1)S(1)}, u32[]{:S(2)}, u32[]{:S(2)}) collective-permute-start(bf16[1024,64]{0,1:T(8,128)(2,1)S(1)} %get-tuple-element.15), channel_id=1, source_target_pairs={{1,0},{2,1},{3,2},{4,3},{5,4},{6,5},{7,6},{9,8},{10,9},{11,10},{12... | collective-permute-start | bytes 393224 | tf_op jit(solution)/shard_map/ppermute | solution.py:28
  175.9 6.5 %collective-permute-start.22 = (bf16[256,256]{1,0:T(8,128)(2,1)S(1)}, bf16[256,256]{1,0:T(8,128)(2,1)S(1)}, u32[]{:S(2)}, u32[]{:S(2)}) collective-permute-start(bf16[256,256]{1,0:T(8,128)(2,1)S(1)} %pad_maximum_fusion.20), channel_id=1, source_target_pairs={{8,0},{16,8},{24,16},{9,1},{17,9},{25,17},{10,2},{18,10},{26,18},{... | collective-permute-start | bytes 393224 | tf_op jit(solution)/shard_map/ppermute | solution.py:82

commit v5 on v4

--- a/solution.py
+++ b/solution.py
@@ -48,7 +48,10 @@
     columns = probe_field.shape[1]
     width_local = NB_DEV + 2 * HALO_B
     probe_vals = probe_field.astype(jnp.float32)
-    sdiag = jnp.diagonal(diag_blocks, axis1=1, axis2=2).astype(jnp.float32).reshape(NODES_DEV)
+    eye = jnp.arange(BLOCK)[:, None] == jnp.arange(BLOCK)[None, :]
+    sdiag = jnp.sum(jnp.where(eye[None], diag_blocks.astype(jnp.float32), 0.0), axis=2).reshape(
+        NODES_DEV
+    )
     scale_space = jnp.repeat(theta_space, PROBES)[None, :]
     scale_time = jnp.repeat(theta_time, PROBES)[None, :]
     base_diag = scale_space * sdiag[:, None] + 2.0 * scale_time + kappa[:, None]
@@ -63,6 +66,7 @@
     own_part = combined[:, :NODES_DEV]
     lower_part = combined[:, NODES_DEV : NODES_DEV + HALO_B * BLOCK]
     upper_part = combined[:, NODES_DEV + HALO_B * BLOCK :]
+    own_t, lower_t, upper_t = own_part.T, lower_part.T, upper_part.T
 
     space_index = lax.axis_index("space")
     up = [(i, i + 1) for i in range(space_count - 1)]
@@ -70,20 +74,19 @@
     upper_wants = lax.ppermute(halo_needs[:HALO_B], "space", down)
     lower_wants = lax.ppermute(halo_needs[HALO_B:], "space", up)
 
-    def pick_blocks(blocks, wanted):
+    def pick_blocks(field, wanted):
         return jnp.concatenate(
-            [lax.dynamic_index_in_dim(blocks, wanted[j], axis=0, keepdims=False) for j in range(HALO_B)],
+            [lax.dynamic_slice_in_dim(field, wanted[j] * BLOCK, BLOCK, axis=0) for j in range(HALO_B)],
             axis=0,
         )
 
     def spatial(field):
-        blocks = field.reshape(NB_DEV, BLOCK, columns)
-        lower = lax.ppermute(pick_blocks(blocks, upper_wants), "space", up)
-        upper = lax.ppermute(pick_blocks(blocks, lower_wants), "space", down)
-        total = jnp.dot(own_part, field, preferred_element_type=jnp.float32)
-        total = total + jnp.dot(lower_part, lower, preferred_element_type=jnp.float32)
-        total = total + jnp.dot(upper_part, upper, preferred_element_type=jnp.float32)
-        return total
+        lower = lax.ppermute(pick_blocks(field, upper_wants), "space", up)
+        upper = lax.ppermute(pick_blocks(field, lower_wants), "space", down)
+        total = jnp.dot(field.T, own_t, preferred_element_type=jnp.float32)
+        total = total + jnp.dot(lower.T, lower_t, preferred_element_type=jnp.float32)
+        total = total + jnp.dot(upper.T, upper_t, preferred_element_type=jnp.float32)
+        return total.T
 
     def temporal(field):
         arrived = with_halo(field, (("tm", 1),), PROBES)

time: 192 us -> 166 us (0.86)
  matrix products: 39 us -> 21 us
  local copies, waits for them, and re-layouts: 38.6 us -> 24.8 us
  between operations: 9.41 us -> 3.94 us
  waiting for transfers between devices: 16.2 us -> 21.4 us
  starting transfers between devices: 60.4 us -> 65.1 us
  other arithmetic: 20.8 us -> 23.2 us
    dot_general x15, matrix products: 35.9 us -> 18.7 us  [the longest x5 7.57 us: spatial(): jnp.dot(upper.T, upper_t, preferred_element_type=jnp.float32)]
    reshape x5 -> x0, local copies, waits for them, and re-layouts: 8.37 us -> none  [spatial(): blocks = field.reshape(NB_DEV, BLOCK, columns)]
    ppermute x10, starting transfers between devices: 18.7 us -> 25.5 us  [the longest x5 19.1 us: spatial(): lower = lax.ppermute(pick_blocks(field, upper_wants), 'space', up)]
    ppermute x5, waiting for transfers between devices: 0.01 us -> 5.93 us  [with_halo(): before = lax.ppermute(last, axis, up)]
    unnamed x52 -> x17, local copies, waits for them, and re-layouts: 10.4 us -> 6.37 us
    gather x1 -> x0, local copies, waits for them, and re-layouts: 1.96 us -> none  [shards(): jnp.diagonal(diag_blocks, axis1=1, axis2=2).astype(jnp.float32)]
    ppermute x5, starting transfers between devices: 22.8 us -> 20.8 us  [with_halo(): before = lax.ppermute(last, axis, up)]
  transfers between devices with their start and end apart: 26 -> 26, of which waited for: 5 -> 8; matrix products, arithmetic and copies ran while one was open for 33% -> 34% of each run, Pallas kernels for 0% -> 0%
where the time goes in v5:
time: 166 us; the launch traced here: 165 us
  starting transfers between devices  65.1 us (39%)
  local copies, waits for them, and re-layouts  24.8 us (15%)
  other arithmetic  23.2 us (14%)
  waiting for transfers between devices  21.4 us (13%)
  matrix products  21 us (13%)
  blocking collectives  5.76 us (3%)
  between operations  3.94 us (2%)
    ppermute x5, starting transfers between devices, with_halo(): before = lax.ppermute(last, axis, up)  20.8 us
    ppermute x5, starting transfers between devices, spatial(): lower = lax.ppermute(pick_blocks(field, upper_wants), 'space', up)  19.1 us
    ppermute x5, waiting for transfers between devices, with_halo(): after = lax.ppermute(initial, axis, down)  14.1 us
    scatter-add x1, other arithmetic, shards(): jax.ops.segment_sum(obs_weight, bins, num_segments=space_count * nodes_de...  11.8 us
    gather x1, local copies, waits for them, and re-layouts, shards(): coef_rows = svc_all[shift * nodes_dev + obs_cell // T_DEV]  10.4 us
    dot_general x5, matrix products, spatial(): jnp.dot(upper.T, upper_t, preferred_element_type=jnp.float32)  7.57 us
    ppermute x5, starting transfers between devices, with_halo(): after = lax.ppermute(initial, axis, down)  6.64 us
    ppermute x5, starting transfers between devices, spatial(): upper = lax.ppermute(pick_blocks(field, lower_wants), 'space', down)  6.44 us
  transfers between devices with their start and end apart: 26, of which 8 were waited for; matrix products, arithmetic and copies ran while one was open for 34% of the time, Pallas kernels for 0%

profile of v5, /device:TPU:0, one launch (start us, length us, event | category | flops | bytes accessed | tf_op | source)
XLA Modules:
  0.0 165.0 jit_solution(7312707293220596472)
XLA Ops:
  1.2 2.6 %collective-permute-start.7 = (bf16[1024,256]{1,0:T(8,128)(2,1)}, bf16[1024,256]{1,0:T(8,128)(2,1)}, u32[]{:S(2)}, u32[]{:S(2)}) collective-permute-start(bf16[1024,256]{1,0:T(8,128)(2,1)} %param.23), channel_id=1, source_target_pairs={{0,16},{8,24},{16,0},{24,8},{1,17},{9,25},{17,1},{25,9},{2,18},{10... | collective-permute-start | bytes 1572872 | tf_op jit(solution)/shard_map/ppermute | solution.py:105
  3.8 1.4 collective-permute-start.8
  5.2 0.8 fusion.84
  6.0 1.3 collective-permute-start
  7.3 3.0 %collective-permute-start.2 = (s32[2]{0:T(128)S(1)}, s32[2]{0:T(128)S(1)}, u32[]{:S(2)}, u32[]{:S(2)}) collective-permute-start(s32[2]{0:T(128)S(1)} %get-tuple-element.48), channel_id=1, source_target_pairs={{0,8},{8,16},{16,24},{1,9},{9,17},{17,25},{2,10},{10,18},{18,26},{... | collective-permute-start | bytes 32 | tf_op jit(solution)/shard_map/ppermute | solution.py:75
  10.3 1.2 copy.36
  11.6 0.7 broadcast_in_dim.42
  12.4 0.7 broadcast_in_dim.39
  13.2 1.0 convert_element_type.81
  14.2 1.1 select_reduce_fusion
  15.3 1.1 fusion.55
  16.4 2.2 %add_convert_fusion = bf16[8,12,128,128]{3,1,2,0:T(8,128)(2,1)S(1)} fusion(f32[8,128,128]{2,1,0:T(8,128)S(1)} %convert_element_type.81, f32[8,12]{1,0:T(8,128)S(1)} %fusion.77, bf16[8,8,128,128]{3,2,1,0:T(8,128)(2,1)S(1)} %copy-done, s32[8,8]{1,0:T(8,128)S(1)} %copy-done.6), kind=kOutput, calls=%fused_computation.2 | convolution fusion | flops 29885184 | bytes 5767808 | tf_op jit(solution)/shard_map/bkm,bkij->bimj/dot_general | solution.py:63
  18.7 1.6 copy.63
  20.3 0.7 fusion.82
  21.0 1.0 copy-done.1
  22.0 1.7 %fusion.37 = f32[1024,256]{0,1:T(8,128)} fusion(bf16[1024,256]{0,1:T(8,128)(2,1)S(1)} %fusion.55, bf16[1024,1536]{1,0:T(8,128)(2,1)S(1)} %bitcast.48), kind=kOutput, calls=%fused_computation.66 | convolution fusion | flops 536870912 | bytes 3670016 | tf_op jit(solution)/shard_map/dot_general | solution.py:86
  23.8 4.1 %collective-permute-start.4 = (bf16[1024,64]{0,1:T(8,128)(2,1)}, bf16[1024,64]{0,1:T(8,128)(2,1)}, u32[]{:S(2)}, u32[]{:S(2)}) collective-permute-start(bf16[1024,64]{0,1:T(8,128)(2,1)} %get-tuple-element.34), channel_id=1, source_target_pairs={{0,1},{1,2},{2,3},{3,4},{4,5},{5,6},{6,7},{8,9},{9,10},{10,11},{11... | collective-permute-start | bytes 393224 | tf_op jit(solution)/shard_map/ppermute | solution.py:27
  29.7 1.3 collective-permute-start.5
  33.1 6.3 %collective-permute-start.1 = (bf16[256,256]{0,1:T(8,128)(2,1)S(1)}, bf16[256,256]{0,1:T(8,128)(2,1)}, u32[]{:S(2)}, u32[]{:S(2)}) collective-permute-start(bf16[256,256]{0,1:T(8,128)(2,1)S(1)} %pad_maximum_fusion.11), channel_id=1, source_target_pairs={{0,8},{8,16},{16,24},{1,9},{9,17},{17,25},{2,10},{10,18},{18,26},{... | collective-permute-start | bytes 393224 | tf_op jit(solution)/shard_map/ppermute | solution.py:84
  39.4 1.3 collective-permute-start.3
  40.7 3.0 %pad_maximum_fusion = bf16[4096,256]{1,0:T(8,128)(2,1)} fusion(bf16[1024,256]{1,0:T(8,128)(2,1)} %collective-permute-done.8, bf16[1024,256]{1,0:T(8,128)(2,1)} %collective-permute-done.7, bf16[1024,256]{1,0:T(8,128)(2,1)} %collective-permute-done.6, bf16[1024,256]{1,0:T(8,128)(2,1)} %param.23), kind=kLoop, calls=%fused_computation.11 | loop fusion | flops 8388608 | bytes 4194304 | tf_op jit(solution)/shard_map/concatenate | solution.py:108
  43.7 10.4 %gather_fusion = bf16[2048,256]{1,0:T(8,128)(2,1)} fusion(bf16[4096,256]{1,0:T(8,128)(2,1)} %pad_maximum_fusion, s32[2048]{0:T(1024)S(1)} %get-tuple-element.42), kind=kCustom, calls=%fused_computation | custom fusion | bytes 2105344 | tf_op jit(solution)/shard_map/gather | solution.py:111
  54.0 1.9 %fusion = f32[2048]{0:T(1024)S(1)} fusion(bf16[2048,256]{1,0:T(8,128)(2,1)} %gather_fusion, bf16[2048,256]{1,0:T(8,128)(2,1)} %param.20), kind=kLoop, calls=%fused_computation.13 | loop fusion | flops 2095104 | bytes 2105344 | tf_op jit(solution)/shard_map/rc,rc->r/dot_general | solution.py:112
  55.9 11.8 %scatter_custom_fusion = f32[16384]{0:T(1024)} fusion(s32[2048]{0:T(1024)S(1)} %get-tuple-element.43, f32[2048]{0:T(1024)S(1)} %exp.3, f32[]{:T(128)} %constant.44.clone.1), kind=kCustom, calls=%fused_computation.118 | custom fusion | flops 2048 | bytes 65540 | tf_op jit(solution)/shard_map/scatter-add | solution.py:115
  67.8 3.3 %all-to-all-start = ((f32[4,1,4096]{2,1,0:T(1,128)}), f32[4,1,4096]{2,1,0:T(1,128)S(1)}, u32[]{:S(2)}, u32[]{:S(2)}) async-start(f32[4,1,4096]{2,1,0:T(1,128)} %bitcast.10), calls=%async_computation | async-start | bytes 131072 | tf_op jit(solution)/shard_map/all_to_all | solution.py:119
  71.1 2.7 %convolution_add_fusion.9 = f32[1024,256]{0,1:T(8,128)} fusion(f32[1024,256]{0,1:T(8,128)} %fusion.37, bf16[256,256]{0,1:T(8,128)(2,1)} %collective-permute-done.1, bf16[1024,1536]{1,0:T(8,128)(2,1)} %bitcast.49), kind=kOutput, calls=%fused_computation.42 | convolution fusion | flops 134479872 | bytes 2752512 | tf_op jit(solution)/shard_map/dot_general | solution.py:87
  73.8 1.3 all-to-all-done
  75.2 1.3 reshape.54
  76.6 1.2 copy.40
  78.2 2.7 %fusion.86 = (bf16[1024,256]{0,1:T(8,128)(2,1)S(1)}, f32[1024,256]{0,1:T(8,128)S(1)}) fusion(f32[1024,256]{0,1:T(8,128)S(1)} %get-tuple-element.41, f32[1024,256]{0,1:T(8,128)S(1)} %get-tuple-element.40, bf16[1024,64]{0,1:T(8,128)(2,1)} %collective-permute-done.5, bf16[1024,256]{0,1:T(8,128)(2,1)S(1)} %fusion.55, ...), kind=kOutput, calls=%fused_computation.173 | convolution fusion | flops 141557760 | bytes 6695936 | tf_op jit(solution)/shard_map/dot_general | solution.py:88
  81.0 0.7 fusion.35
  81.9 1.3 collective-permute-start.10
  83.2 3.0 %collective-permute-start.9 = (bf16[256,256]{0,1:T(8,128)(2,1)S(1)}, bf16[256,256]{0,1:T(8,128)(2,1)S(1)}, u32[]{:S(2)}, u32[]{:S(2)}) collective-permute-start(bf16[256,256]{0,1:T(8,128)(2,1)S(1)} %pad_maximum_fusion.13), channel_id=1, source_target_pairs={{0,8},{8,16},{16,24},{1,9},{9,17},{17,25},{2,10},{10,18},{18,26},{... | collective-permute-start | bytes 393224 | tf_op jit(solution)/shard_map/ppermute | solution.py:84
  86.3 4.3 %collective-permute-start.11 = (bf16[1024,64]{0,1:T(8,128)(2,1)S(1)}, bf16[1024,64]{0,1:T(8,128)(2,1)S(1)}, u32[]{:S(2)}, u32[]{:S(2)}) collective-permute-start(bf16[1024,64]{0,1:T(8,128)(2,1)S(1)} %get-tuple-element.28), channel_id=1, source_target_pairs={{0,1},{1,2},{2,3},{3,4},{4,5},{5,6},{6,7},{8,9},{9,10},{10,11},{11... | collective-permute-start | bytes 393224 | tf_op jit(solution)/shard_map/ppermute | solution.py:27
  90.6 1.5 collective-permute-start.12
  92.4 2.0 %collective-permute-done.11 = bf16[1024,64]{0,1:T(8,128)(2,1)S(1)} collective-permute-done((bf16[1024,64]{0,1:T(8,128)(2,1)S(1)}, bf16[1024,64]{0,1:T(8,128)(2,1)S(1)}, u32[]{:S(2)}, u32[]{:S(2)}) %collective-permute-start.11) | collective-permute-done | bytes 131104 | tf_op jit(solution)/shard_map/ppermute | solution.py:27
  94.5 4.2 %collective-permute-done.12 = bf16[1024,64]{0,1:T(8,128)(2,1)S(1)} collective-permute-done((bf16[1024,64]{0,1:T(8,128)(2,1)S(1)}, bf16[1024,64]{0,1:T(8,128)(2,1)S(1)}, u32[]{:S(2)}, u32[]{:S(2)}) %collective-permute-start.12) | collective-permute-done | bytes 131104 | tf_op jit(solution)/shard_map/ppermute | solution.py:28
  98.6 0.8 fusion.87
  99.5 0.7 fusion.33
  100.4 1.3 collective-permute-start.14
  101.8 3.0 %collective-permute-start.13 = (bf16[256,256]{0,1:T(8,128)(2,1)S(1)}, bf16[256,256]{0,1:T(8,128)(2,1)S(1)}, u32[]{:S(2)}, u32[]{:S(2)}) collective-permute-start(bf16[256,256]{0,1:T(8,128)(2,1)S(1)} %pad_maximum_fusion.15), channel_id=1, source_target_pairs={{0,8},{8,16},{16,24},{1,9},{9,17},{17,25},{2,10},{10,18},{18,26},{... | collective-permute-start | bytes 393224 | tf_op jit(solution)/shard_map/ppermute | solution.py:84
  104.8 4.5 %collective-permute-start.15 = (bf16[1024,64]{0,1:T(8,128)(2,1)S(1)}, bf16[1024,64]{0,1:T(8,128)(2,1)S(1)}, u32[]{:S(2)}, u32[]{:S(2)}) collective-permute-start(bf16[1024,64]{0,1:T(8,128)(2,1)S(1)} %get-tuple-element.22), channel_id=1, source_target_pairs={{0,1},{1,2},{2,3},{3,4},{4,5},{5,6},{6,7},{8,9},{9,10},{10,11},{11... | collective-permute-start | bytes 393224 | tf_op jit(solution)/shard_map/ppermute | solution.py:27
  109.4 1.3 collective-permute-start.16
  111.0 2.1 %collective-permute-done.15 = bf16[1024,64]{0,1:T(8,128)(2,1)S(1)} collective-permute-done((bf16[1024,64]{0,1:T(8,128)(2,1)S(1)}, bf16[1024,64]{0,1:T(8,128)(2,1)S(1)}, u32[]{:S(2)}, u32[]{:S(2)}) %collective-permute-start.15) | collective-permute-done | bytes 131104 | tf_op jit(solution)/shard_map/ppermute | solution.py:27
  113.1 4.4 %collective-permute-done.16 = bf16[1024,64]{0,1:T(8,128)(2,1)S(1)} collective-permute-done((bf16[1024,64]{0,1:T(8,128)(2,1)S(1)}, bf16[1024,64]{0,1:T(8,128)(2,1)S(1)}, u32[]{:S(2)}, u32[]{:S(2)}) %collective-permute-start.16) | collective-permute-done | bytes 131104 | tf_op jit(solution)/shard_map/ppermute | solution.py:28
  117.5 0.8 fusion.88
  118.4 0.7 fusion.31
  119.3 1.3 collective-permute-start.18
  120.6 3.0 %collective-permute-start.17 = (bf16[256,256]{0,1:T(8,128)(2,1)S(1)}, bf16[256,256]{0,1:T(8,128)(2,1)S(1)}, u32[]{:S(2)}, u32[]{:S(2)}) collective-permute-start(bf16[256,256]{0,1:T(8,128)(2,1)S(1)} %pad_maximum_fusion.17), channel_id=1, source_target_pairs={{0,8},{8,16},{16,24},{1,9},{9,17},{17,25},{2,10},{10,18},{18,26},{... | collective-permute-start | bytes 393224 | tf_op jit(solution)/shard_map/ppermute | solution.py:84
  123.7 4.0 %collective-permute-start.19 = (bf16[1024,64]{0,1:T(8,128)(2,1)S(1)}, bf16[1024,64]{0,1:T(8,128)(2,1)S(1)}, u32[]{:S(2)}, u32[]{:S(2)}) collective-permute-start(bf16[1024,64]{0,1:T(8,128)(2,1)S(1)} %get-tuple-element.16), channel_id=1, source_target_pairs={{0,1},{1,2},{2,3},{3,4},{4,5},{5,6},{6,7},{8,9},{9,10},{10,11},{11... | collective-permute-start | bytes 393224 | tf_op jit(solution)/shard_map/ppermute | solution.py:27
  127.7 1.3 collective-permute-start.20
  129.4 1.8 %collective-permute-done.19 = bf16[1024,64]{0,1:T(8,128)(2,1)S(1)} collective-permute-done((bf16[1024,64]{0,1:T(8,128)(2,1)S(1)}, bf16[1024,64]{0,1:T(8,128)(2,1)S(1)}, u32[]{:S(2)}, u32[]{:S(2)}) %collective-permute-start.19) | collective-permute-done | bytes 131104 | tf_op jit(solution)/shard_map/ppermute | solution.py:27
  131.2 4.7 %collective-permute-done.20 = bf16[1024,64]{0,1:T(8,128)(2,1)S(1)} collective-permute-done((bf16[1024,64]{0,1:T(8,128)(2,1)S(1)}, bf16[1024,64]{0,1:T(8,128)(2,1)S(1)}, u32[]{:S(2)}, u32[]{:S(2)}) %collective-permute-start.20) | collective-permute-done | bytes 131104 | tf_op jit(solution)/shard_map/ppermute | solution.py:28
  135.9 1.8 %fusion.89 = (bf16[1024,256]{0,1:T(8,128)(2,1)S(1)}, f32[1024,256]{0,1:T(8,128)}) fusion(f32[1024,256]{0,1:T(8,128)S(1)} %get-tuple-element.57, f32[1024,256]{0,1:T(8,128)S(1)} %get-tuple-element.41, f32[1024,256]{0,1:T(8,128)S(1)} %fusion.2, bf16[1024,64]{0,1:T(8,128)(2,1)S(1)} %collective-permute-done.20, bf16[1024,256]{0,1:T(8,128)(2,1)S(1)} %get-tuple-element.56, ...), kind=kOutput, calls=%fused_computation.176 | convolution fusion | flops 140247040 | bytes 7735296 | tf_op jit(solution)/shard_map/dot_general | solution.py:88
  137.8 1.7 %fusion.39 = f32[1024,256]{0,1:T(8,128)} fusion(bf16[1024,256]{0,1:T(8,128)(2,1)S(1)} %get-tuple-element.58, bf16[1024,1536]{1,0:T(8,128)(2,1)S(1)} %bitcast.62), kind=kOutput, calls=%fused_computation.68 | convolution fusion | flops 536870912 | bytes 3670016 | tf_op jit(solution)/shard_map/dot_general | solution.py:86
  140.1 1.3 collective-permute-start.22
  142.1 3.7 %collective-permute-start.21 = (bf16[256,256]{0,1:T(8,128)(2,1)}, bf16[256,256]{0,1:T(8,128)(2,1)}, u32[]{:S(2)}, u32[]{:S(2)}) collective-permute-start(bf16[256,256]{0,1:T(8,128)(2,1)} %pad_maximum_fusion.19), channel_id=1, source_target_pairs={{0,8},{8,16},{16,24},{1,9},{9,17},{17,25},{2,10},{10,18},{18,26},{... | collective-permute-start | bytes 393224 | tf_op jit(solution)/shard_map/ppermute | solution.py:84
  146.5 3.9 %collective-permute-start.23 = (bf16[1024,64]{0,1:T(8,128)(2,1)}, bf16[1024,64]{0,1:T(8,128)(2,1)S(1)}, u32[]{:S(2)}, u32[]{:S(2)}) collective-permute-start(bf16[1024,64]{0,1:T(8,128)(2,1)} %get-tuple-element.14), channel_id=1, source_target_pairs={{0,1},{1,2},{2,3},{3,4},{4,5},{5,6},{6,7},{8,9},{9,10},{10,11},{11... | collective-permute-start | bytes 393224 | tf_op jit(solution)/shard_map/ppermute | solution.py:27
  150.4 1.3 collective-permute-start.24
  151.7 2.5 %copy.44 = f32[1024,256]{1,0:T(8,128)} copy(f32[1024,256]{0,1:T(8,128)} %get-tuple-element.59) | data formatting | bytes 2097152
  154.2 1.8 %convolution_add_fusion.1 = f32[1024,256]{0,1:T(8,128)S(1)} fusion(f32[1024,256]{0,1:T(8,128)} %fusion.39, bf16[256,256]{0,1:T(8,128)(2,1)} %collective-permute-done.21, bf16[1024,1536]{1,0:T(8,128)(2,1)} %bitcast.51), kind=kOutput, calls=%fused_computation.22 | convolution fusion | flops 134479872 | bytes 2752512 | tf_op jit(solution)/shard_map/dot_general | solution.py:87
  156.0 1.5 fusion.30
  157.5 0.8 collective-permute-done.24
  158.7 5.8 %psum.7 = f32[2,256]{1,0:T(2,128)S(1)} all-reduce(f32[2,256]{1,0:T(2,128)S(1)} %pad_maximum_fusion.21), channel_id=1, replica_groups=mesh['space'=4,'tm'=8] {'space'}, use_global_device_ids=true, to_apply=%region_5.6 | all-reduce | flops 512 | bytes 4096 | tf_op jit(solution)/shard_map/psum | solution.py:145
  (72 shorter events, 7.4 us)
Async XLA Ops:
  0.6 15.8 %copy-start = (bf16[8,8,128,128]{3,2,1,0:T(8,128)(2,1)S(1)}, bf16[8,8,128,128]{3,2,1,0:T(8,128)(2,1)}, u32[]{:S(2)}) copy-start(bf16[8,8,128,128]{3,2,1,0:T(8,128)(2,1)} %param.17) | copy-start | bytes 6291460
  0.6 15.7 %copy-start.6 = (s32[8,8]{1,0:T(8,128)S(1)}, s32[8,8]{1,0:T(8,128)}, u32[]{:S(2)}) copy-start(s32[8,8]{1,0:T(8,128)} %param.18) | copy-start | bytes 772
  0.7 32.4 %collective-permute-start.6 = (bf16[1024,256]{1,0:T(8,128)(2,1)}, bf16[1024,256]{1,0:T(8,128)(2,1)}, u32[]{:S(2)}, u32[]{:S(2)}) collective-permute-start(bf16[1024,256]{1,0:T(8,128)(2,1)} %param.23), channel_id=1, source_target_pairs={{0,8},{8,16},{16,24},{24,0},{1,9},{9,17},{17,25},{25,1},{2,10},{10... | collective-permute-start | bytes 1572872 | tf_op jit(solution)/shard_map/ppermute | solution.py:105
  1.2 38.2 %collective-permute-start.7 = (bf16[1024,256]{1,0:T(8,128)(2,1)}, bf16[1024,256]{1,0:T(8,128)(2,1)}, u32[]{:S(2)}, u32[]{:S(2)}) collective-permute-start(bf16[1024,256]{1,0:T(8,128)(2,1)} %param.23), channel_id=1, source_target_pairs={{0,16},{8,24},{16,0},{24,8},{1,17},{9,25},{17,1},{25,9},{2,18},{10... | collective-permute-start | bytes 1572872 | tf_op jit(solution)/shard_map/ppermute | solution.py:105
  3.8 36.9 %collective-permute-start.8 = (bf16[1024,256]{1,0:T(8,128)(2,1)}, bf16[1024,256]{1,0:T(8,128)(2,1)}, u32[]{:S(2)}, u32[]{:S(2)}) collective-permute-start(bf16[1024,256]{1,0:T(8,128)(2,1)} %param.23), channel_id=1, source_target_pairs={{0,24},{8,0},{16,8},{24,16},{1,25},{9,1},{17,9},{25,17},{2,26},{10... | collective-permute-start | bytes 1572872 | tf_op jit(solution)/shard_map/ppermute | solution.py:105
  6.0 17.8 %collective-permute-start = (s32[2]{0:T(128)S(1)}, s32[2]{0:T(128)S(1)}, u32[]{:S(2)}, u32[]{:S(2)}) collective-permute-start(s32[2]{0:T(128)S(1)} %get-tuple-element.49), channel_id=1, source_target_pairs={{8,0},{16,8},{24,16},{9,1},{17,9},{25,17},{10,2},{18,10},{26,18},{... | collective-permute-start | bytes 32 | tf_op jit(solution)/shard_map/ppermute | solution.py:74
  7.3 22.5 %collective-permute-start.2 = (s32[2]{0:T(128)S(1)}, s32[2]{0:T(128)S(1)}, u32[]{:S(2)}, u32[]{:S(2)}) collective-permute-start(s32[2]{0:T(128)S(1)} %get-tuple-element.48), channel_id=1, source_target_pairs={{0,8},{8,16},{16,24},{1,9},{9,17},{17,25},{2,10},{10,18},{18,26},{... | collective-permute-start | bytes 32 | tf_op jit(solution)/shard_map/ppermute | solution.py:75
  20.3 1.7 %copy-start.1 = (bf16[128,8,12,128]{3,1,2,0:T(8,128)(2,1)}, bf16[128,8,12,128]{3,1,2,0:T(8,128)(2,1)S(1)}, u32[]{:S(2)}) copy-start(bf16[128,8,12,128]{3,1,2,0:T(8,128)(2,1)S(1)} %copy.63) | copy-start | bytes 9437188
  20.3 3.4 %copy-start.4 = (s32[2048,1]{0,1:T(1,128)S(1)}, s32[2048,1]{0,1:T(1,128)}, u32[]{:S(2)}) copy-start(s32[2048,1]{0,1:T(1,128)} %param.21) | copy-start | bytes 24580
  20.3 3.5 %copy-start.5 = (s32[2048]{0:T(1024)S(1)}, s32[2048]{0:T(1024)}, u32[]{:S(2)}) copy-start(s32[2048]{0:T(1024)} %param.22) | copy-start | bytes 24580
  23.8 54.4 %collective-permute-start.4 = (bf16[1024,64]{0,1:T(8,128)(2,1)}, bf16[1024,64]{0,1:T(8,128)(2,1)}, u32[]{:S(2)}, u32[]{:S(2)}) collective-permute-start(bf16[1024,64]{0,1:T(8,128)(2,1)} %get-tuple-element.34), channel_id=1, source_target_pairs={{0,1},{1,2},{2,3},{3,4},{4,5},{5,6},{6,7},{8,9},{9,10},{10,11},{11... | collective-permute-start | bytes 393224 | tf_op jit(solution)/shard_map/ppermute | solution.py:27
  29.7 48.4 %collective-permute-start.5 = (bf16[1024,64]{0,1:T(8,128)(2,1)}, bf16[1024,64]{0,1:T(8,128)(2,1)}, u32[]{:S(2)}, u32[]{:S(2)}) collective-permute-start(bf16[1024,64]{0,1:T(8,128)(2,1)} %get-tuple-element.35), channel_id=1, source_target_pairs={{1,0},{2,1},{3,2},{4,3},{5,4},{6,5},{7,6},{9,8},{10,9},{11,10},{12... | collective-permute-start | bytes 393224 | tf_op jit(solution)/shard_map/ppermute | solution.py:28
  33.1 38.0 %collective-permute-start.1 = (bf16[256,256]{0,1:T(8,128)(2,1)S(1)}, bf16[256,256]{0,1:T(8,128)(2,1)}, u32[]{:S(2)}, u32[]{:S(2)}) collective-permute-start(bf16[256,256]{0,1:T(8,128)(2,1)S(1)} %pad_maximum_fusion.11), channel_id=1, source_target_pairs={{0,8},{8,16},{16,24},{1,9},{9,17},{17,25},{2,10},{10,18},{18,26},{... | collective-permute-start | bytes 393224 | tf_op jit(solution)/shard_map/ppermute | solution.py:84
  39.4 38.8 %collective-permute-start.3 = (bf16[256,256]{0,1:T(8,128)(2,1)S(1)}, bf16[256,256]{0,1:T(8,128)(2,1)}, u32[]{:S(2)}, u32[]{:S(2)}) collective-permute-start(bf16[256,256]{0,1:T(8,128)(2,1)S(1)} %pad_maximum_fusion.12), channel_id=1, source_target_pairs={{8,0},{16,8},{24,16},{9,1},{17,9},{25,17},{10,2},{18,10},{26,18},{... | collective-permute-start | bytes 393224 | tf_op jit(solution)/shard_map/ppermute | solution.py:85
  54.0 23.8 %copy-start.3 = (f32[1024]{0:T(1024)S(1)}, f32[1024]{0:T(1024)}, u32[]{:S(2)}) copy-start(f32[1024]{0:T(1024)} %param.13) | copy-start | bytes 12292
  67.8 7.4 %all-to-all-start = ((f32[4,1,4096]{2,1,0:T(1,128)}), f32[4,1,4096]{2,1,0:T(1,128)S(1)}, u32[]{:S(2)}, u32[]{:S(2)}) async-start(f32[4,1,4096]{2,1,0:T(1,128)} %bitcast.10), calls=%async_computation | async-start | bytes 131072 | tf_op jit(solution)/shard_map/all_to_all | solution.py:119
  78.2 2.8 %copy-start.2 = (bf16[128,8,12,128]{3,1,2,0:T(8,128)(2,1)S(1)}, bf16[128,8,12,128]{3,1,2,0:T(8,128)(2,1)}, u32[]{:S(2)}) copy-start(bf16[128,8,12,128]{3,1,2,0:T(8,128)(2,1)} %copy-done.1) | copy-start | bytes 9437188
  81.9 10.6 %collective-permute-start.10 = (bf16[256,256]{0,1:T(8,128)(2,1)S(1)}, bf16[256,256]{0,1:T(8,128)(2,1)S(1)}, u32[]{:S(2)}, u32[]{:S(2)}) collective-permute-start(bf16[256,256]{0,1:T(8,128)(2,1)S(1)} %pad_maximum_fusion.14), channel_id=1, source_target_pairs={{8,0},{16,8},{24,16},{9,1},{17,9},{25,17},{10,2},{18,10},{26,18},{... | collective-permute-start | bytes 393224 | tf_op jit(solution)/shard_map/ppermute | solution.py:85
  83.2 8.9 %collective-permute-start.9 = (bf16[256,256]{0,1:T(8,128)(2,1)S(1)}, bf16[256,256]{0,1:T(8,128)(2,1)S(1)}, u32[]{:S(2)}, u32[]{:S(2)}) collective-permute-start(bf16[256,256]{0,1:T(8,128)(2,1)S(1)} %pad_maximum_fusion.13), channel_id=1, source_target_pairs={{0,8},{8,16},{16,24},{1,9},{9,17},{17,25},{2,10},{10,18},{18,26},{... | collective-permute-start | bytes 393224 | tf_op jit(solution)/shard_map/ppermute | solution.py:84
  86.3 8.2 %collective-permute-start.11 = (bf16[1024,64]{0,1:T(8,128)(2,1)S(1)}, bf16[1024,64]{0,1:T(8,128)(2,1)S(1)}, u32[]{:S(2)}, u32[]{:S(2)}) collective-permute-start(bf16[1024,64]{0,1:T(8,128)(2,1)S(1)} %get-tuple-element.28), channel_id=1, source_target_pairs={{0,1},{1,2},{2,3},{3,4},{4,5},{5,6},{6,7},{8,9},{9,10},{10,11},{11... | collective-permute-start | bytes 393224 | tf_op jit(solution)/shard_map/ppermute | solution.py:27
  90.6 8.1 %collective-permute-start.12 = (bf16[1024,64]{0,1:T(8,128)(2,1)S(1)}, bf16[1024,64]{0,1:T(8,128)(2,1)S(1)}, u32[]{:S(2)}, u32[]{:S(2)}) collective-permute-start(bf16[1024,64]{0,1:T(8,128)(2,1)S(1)} %get-tuple-element.29), channel_id=1, source_target_pairs={{1,0},{2,1},{3,2},{4,3},{5,4},{6,5},{7,6},{9,8},{10,9},{11,10},{12... | collective-permute-start | bytes 393224 | tf_op jit(solution)/shard_map/ppermute | solution.py:28
  100.4 10.6 %collective-permute-start.14 = (bf16[256,256]{0,1:T(8,128)(2,1)S(1)}, bf16[256,256]{0,1:T(8,128)(2,1)S(1)}, u32[]{:S(2)}, u32[]{:S(2)}) collective-permute-start(bf16[256,256]{0,1:T(8,128)(2,1)S(1)} %pad_maximum_fusion.16), channel_id=1, source_target_pairs={{8,0},{16,8},{24,16},{9,1},{17,9},{25,17},{10,2},{18,10},{26,18},{... | collective-permute-start | bytes 393224 | tf_op jit(solution)/shard_map/ppermute | solution.py:85
  101.8 8.9 %collective-permute-start.13 = (bf16[256,256]{0,1:T(8,128)(2,1)S(1)}, bf16[256,256]{0,1:T(8,128)(2,1)S(1)}, u32[]{:S(2)}, u32[]{:S(2)}) collective-permute-start(bf16[256,256]{0,1:T(8,128)(2,1)S(1)} %pad_maximum_fusion.15), channel_id=1, source_target_pairs={{0,8},{8,16},{16,24},{1,9},{9,17},{17,25},{2,10},{10,18},{18,26},{... | collective-permute-start | bytes 393224 | tf_op jit(solution)/shard_map/ppermute | solution.py:84
  104.8 8.3 %collective-permute-start.15 = (bf16[1024,64]{0,1:T(8,128)(2,1)S(1)}, bf16[1024,64]{0,1:T(8,128)(2,1)S(1)}, u32[]{:S(2)}, u32[]{:S(2)}) collective-permute-start(bf16[1024,64]{0,1:T(8,128)(2,1)S(1)} %get-tuple-element.22), channel_id=1, source_target_pairs={{0,1},{1,2},{2,3},{3,4},{4,5},{5,6},{6,7},{8,9},{9,10},{10,11},{11... | collective-permute-start | bytes 393224 | tf_op jit(solution)/shard_map/ppermute | solution.py:27
  109.4 8.1 %collective-permute-start.16 = (bf16[1024,64]{0,1:T(8,128)(2,1)S(1)}, bf16[1024,64]{0,1:T(8,128)(2,1)S(1)}, u32[]{:S(2)}, u32[]{:S(2)}) collective-permute-start(bf16[1024,64]{0,1:T(8,128)(2,1)S(1)} %get-tuple-element.23), channel_id=1, source_target_pairs={{1,0},{2,1},{3,2},{4,3},{5,4},{6,5},{7,6},{9,8},{10,9},{11,10},{12... | collective-permute-start | bytes 393224 | tf_op jit(solution)/shard_map/ppermute | solution.py:28
  119.3 10.1 %collective-permute-start.18 = (bf16[256,256]{0,1:T(8,128)(2,1)S(1)}, bf16[256,256]{0,1:T(8,128)(2,1)S(1)}, u32[]{:S(2)}, u32[]{:S(2)}) collective-permute-start(bf16[256,256]{0,1:T(8,128)(2,1)S(1)} %pad_maximum_fusion.18), channel_id=1, source_target_pairs={{8,0},{16,8},{24,16},{9,1},{17,9},{25,17},{10,2},{18,10},{26,18},{... | collective-permute-start | bytes 393224 | tf_op jit(solution)/shard_map/ppermute | solution.py:85
  120.6 8.4 %collective-permute-start.17 = (bf16[256,256]{0,1:T(8,128)(2,1)S(1)}, bf16[256,256]{0,1:T(8,128)(2,1)S(1)}, u32[]{:S(2)}, u32[]{:S(2)}) collective-permute-start(bf16[256,256]{0,1:T(8,128)(2,1)S(1)} %pad_maximum_fusion.17), channel_id=1, source_target_pairs={{0,8},{8,16},{16,24},{1,9},{9,17},{17,25},{2,10},{10,18},{18,26},{... | collective-permute-start | bytes 393224 | tf_op jit(solution)/shard_map/ppermute | solution.py:84
  123.7 7.5 %collective-permute-start.19 = (bf16[1024,64]{0,1:T(8,128)(2,1)S(1)}, bf16[1024,64]{0,1:T(8,128)(2,1)S(1)}, u32[]{:S(2)}, u32[]{:S(2)}) collective-permute-start(bf16[1024,64]{0,1:T(8,128)(2,1)S(1)} %get-tuple-element.16), channel_id=1, source_target_pairs={{0,1},{1,2},{2,3},{3,4},{4,5},{5,6},{6,7},{8,9},{9,10},{10,11},{11... | collective-permute-start | bytes 393224 | tf_op jit(solution)/shard_map/ppermute | solution.py:27
  127.7 8.2 %collective-permute-start.20 = (bf16[1024,64]{0,1:T(8,128)(2,1)S(1)}, bf16[1024,64]{0,1:T(8,128)(2,1)S(1)}, u32[]{:S(2)}, u32[]{:S(2)}) collective-permute-start(bf16[1024,64]{0,1:T(8,128)(2,1)S(1)} %get-tuple-element.17), channel_id=1, source_target_pairs={{1,0},{2,1},{3,2},{4,3},{5,4},{6,5},{7,6},{9,8},{10,9},{11,10},{12... | collective-permute-start | bytes 393224 | tf_op jit(solution)/shard_map/ppermute | solution.py:28
  140.1 15.8 %collective-permute-start.22 = (bf16[256,256]{0,1:T(8,128)(2,1)}, bf16[256,256]{0,1:T(8,128)(2,1)S(1)}, u32[]{:S(2)}, u32[]{:S(2)}) collective-permute-start(bf16[256,256]{0,1:T(8,128)(2,1)} %pad_maximum_fusion.20), channel_id=1, source_target_pairs={{8,0},{16,8},{24,16},{9,1},{17,9},{25,17},{10,2},{18,10},{26,18},{... | collective-permute-start | bytes 393224 | tf_op jit(solution)/shard_map/ppermute | solution.py:85
  142.1 12.1 %collective-permute-start.21 = (bf16[256,256]{0,1:T(8,128)(2,1)}, bf16[256,256]{0,1:T(8,128)(2,1)}, u32[]{:S(2)}, u32[]{:S(2)}) collective-permute-start(bf16[256,256]{0,1:T(8,128)(2,1)} %pad_maximum_fusion.19), channel_id=1, source_target_pairs={{0,8},{8,16},{16,24},{1,9},{9,17},{17,25},{2,10},{10,18},{18,26},{... | collective-permute-start | bytes 393224 | tf_op jit(solution)/shard_map/ppermute | solution.py:84
  146.5 11.0 %collective-permute-start.23 = (bf16[1024,64]{0,1:T(8,128)(2,1)}, bf16[1024,64]{0,1:T(8,128)(2,1)S(1)}, u32[]{:S(2)}, u32[]{:S(2)}) collective-permute-start(bf16[1024,64]{0,1:T(8,128)(2,1)} %get-tuple-element.14), channel_id=1, source_target_pairs={{0,1},{1,2},{2,3},{3,4},{4,5},{5,6},{6,7},{8,9},{9,10},{10,11},{11... | collective-permute-start | bytes 393224 | tf_op jit(solution)/shard_map/ppermute | solution.py:27
  150.4 7.9 %collective-permute-start.24 = (bf16[1024,64]{0,1:T(8,128)(2,1)}, bf16[1024,64]{0,1:T(8,128)(2,1)S(1)}, u32[]{:S(2)}, u32[]{:S(2)}) collective-permute-start(bf16[1024,64]{0,1:T(8,128)(2,1)} %get-tuple-element.15), channel_id=1, source_target_pairs={{1,0},{2,1},{3,2},{4,3},{5,4},{6,5},{7,6},{9,8},{10,9},{11,10},{12... | collective-permute-start | bytes 393224 | tf_op jit(solution)/shard_map/ppermute | solution.py:28

commit v6 on v5

--- a/solution.py
+++ b/solution.py
@@ -105,16 +105,28 @@
         lax.ppermute(svc_coef, "space", [(i, (i + k) % space_count) for i in range(space_count)])
         for k in range(1, space_count)
     ]
-    svc_all = jnp.concatenate(tables, axis=0)
+    shifts = (lax.axis_index("space") - jnp.arange(space_count)) % space_count
+    svc_all = jnp.stack(tables)[shifts].reshape(space_count * nodes_dev, svc_coef.shape[1])
     owner = obs_owner[:, 0]
-    shift = (lax.axis_index("space") - owner) % space_count
-    coef_rows = svc_all[shift * nodes_dev + obs_cell // T_DEV]
-    eta = jnp.einsum("rc,rc->r", covariates, coef_rows, preferred_element_type=jnp.float32)
+    node_ids = owner * nodes_dev + obs_cell // T_DEV
+    onehot = (node_ids[:, None] == jnp.arange(space_count * nodes_dev)[None, :]).astype(jnp.bfloat16)
+    coef_rows = jnp.dot(onehot, svc_all, preferred_element_type=jnp.float32)
+    eta = jnp.sum(covariates.astype(jnp.float32) * coef_rows, axis=1)
     obs_weight = jnp.exp(eta)
-    bins = owner * (nodes_dev * T_DEV) + obs_cell
-    local_counts = jax.ops.segment_sum(
-        obs_weight, bins, num_segments=space_count * nodes_dev * T_DEV
-    ).reshape(space_count, nodes_dev * T_DEV)
+    high = lax.reduce_precision(obs_weight, exponent_bits=8, mantissa_bits=7)
+    rest = obs_weight - high
+    middle = lax.reduce_precision(rest, exponent_bits=8, mantissa_bits=7)
+    low = rest - middle
+    in_step = obs_cell[:, None] % T_DEV == jnp.arange(T_DEV)[None, :]
+    parts = jnp.concatenate(
+        [jnp.where(in_step, piece[:, None], 0.0) for piece in (high, middle, low)], axis=1
+    ).astype(jnp.bfloat16)
+    sums = lax.dot_general(
+        onehot, parts, (((0,), (0,)), ((), ())), preferred_element_type=jnp.float32
+    )
+    local_counts = (sums[:, :T_DEV] + sums[:, T_DEV : 2 * T_DEV] + sums[:, 2 * T_DEV :]).reshape(
+        space_count, nodes_dev * T_DEV
+    )
     counted = jnp.sum(
         lax.all_to_all(local_counts, "space", split_axis=0, concat_axis=0, tiled=True), axis=0
     )

time: 166 us -> 168 us (1.012)
  matrix products: 21 us -> 36.4 us
  other arithmetic: 23.2 us -> 9.61 us
  starting transfers between devices: 65.1 us -> 62.6 us
    dot_general x0 -> x2, matrix products: none -> 15.3 us  [the longest x1 9.45 us: shards(): coef_rows = jnp.dot(onehot, svc_all, preferred_element_type=jnp.float32)]
    scatter-add x1 -> x0, other arithmetic: 11.8 us -> none  [shards(): jax.ops.segment_sum(obs_weight, bins, num_segments=space_count * nodes_de...]
    gather x1, local copies, waits for them, and re-layouts: 10.4 us -> 3.58 us  [shards(): jnp.stack(tables)[shifts]]
    all_to_all x0 -> x1, local copies, waits for them, and re-layouts: none -> 3.92 us  [shards(): lax.all_to_all(local_counts, 'space', split_axis=0, concat_axis=0, tiled=...]
    another operation x1 -> x3, other arithmetic: 0.01 us -> 3.15 us  [the longest x1 3.12 us: shards(): jnp.stack(tables)[shifts]]
    concatenate x1 -> x0, other arithmetic: 3 us -> none  [shards(): svc_all = jnp.concatenate(tables, axis=0)]
    ppermute x5, starting transfers between devices: 19.1 us -> 16.7 us  [spatial(): lower = lax.ppermute(pick_blocks(field, upper_wants), 'space', up)]
    unnamed x17 -> x18, local copies, waits for them, and re-layouts: 6.37 us -> 8.66 us
  transfers between devices with their start and end apart: 26 -> 26, of which waited for: 8 -> 8; matrix products, arithmetic and copies ran while one was open for 34% -> 33% of each run, Pallas kernels for 0% -> 0%
where the time goes in v6:
time: 168 us; the launch traced here: 166 us
  starting transfers between devices  62.6 us (37%)
  matrix products  36.4 us (22%)
  local copies, waits for them, and re-layouts  26.3 us (16%)
  waiting for transfers between devices  21.6 us (13%)
  other arithmetic  9.61 us (6%)
  blocking collectives  5.76 us (3%)
  between operations  3.9 us (2%)
    ppermute x5, starting transfers between devices, with_halo(): before = lax.ppermute(last, axis, up)  20.7 us
    ppermute x5, starting transfers between devices, spatial(): lower = lax.ppermute(pick_blocks(field, upper_wants), 'space', up)  16.7 us
    ppermute x5, waiting for transfers between devices, with_halo(): after = lax.ppermute(initial, axis, down)  14.2 us
    dot_general x1, matrix products, shards(): coef_rows = jnp.dot(onehot, svc_all, preferred_element_type=jnp.float32)  9.45 us
    unnamed x18, local copies, waits for them, and re-layouts  8.66 us
    dot_general x5, matrix products, spatial(): jnp.dot(upper.T, upper_t, preferred_element_type=jnp.float32)  7.56 us
    ppermute x5, starting transfers between devices, with_halo(): after = lax.ppermute(initial, axis, down)  6.46 us
    ppermute x5, starting transfers between devices, spatial(): upper = lax.ppermute(pick_blocks(field, lower_wants), 'space', down)  6.44 us
  transfers between devices with their start and end apart: 26, of which 8 were waited for; matrix products, arithmetic and copies ran while one was open for 33% of the time, Pallas kernels for 0%

profile of v6, /device:TPU:0, one launch (start us, length us, event | category | flops | bytes accessed | tf_op | source)
XLA Modules:
  0.0 166.2 jit_solution(7372805923818595142)
XLA Ops:
  1.2 2.6 %collective-permute-start.7 = (bf16[1024,256]{1,0:T(8,128)(2,1)}, bf16[1024,256]{1,0:T(8,128)(2,1)}, u32[]{:S(2)}, u32[]{:S(2)}) collective-permute-start(bf16[1024,256]{1,0:T(8,128)(2,1)} %param.23), channel_id=1, source_target_pairs={{0,16},{8,24},{16,0},{24,8},{1,17},{9,25},{17,1},{25,9},{2,18},{10... | collective-permute-start | bytes 1572872 | tf_op jit(solution)/shard_map/ppermute | solution.py:105
  3.8 1.4 collective-permute-start.8
  5.2 0.8 fusion.93
  6.0 1.3 collective-permute-start
  7.3 3.0 %collective-permute-start.2 = (s32[2]{0:T(128)S(1)}, s32[2]{0:T(128)S(1)}, u32[]{:S(2)}, u32[]{:S(2)}) collective-permute-start(s32[2]{0:T(128)S(1)} %get-tuple-element.50), channel_id=1, source_target_pairs={{0,8},{8,16},{16,24},{1,9},{9,17},{17,25},{2,10},{10,18},{18,26},{... | collective-permute-start | bytes 32 | tf_op jit(solution)/shard_map/ppermute | solution.py:75
  10.3 1.2 copy.31
  13.2 1.0 convert_element_type.86
  14.2 1.1 select_reduce_fusion
  15.3 1.1 fusion.60
  16.4 2.2 %add_convert_fusion = bf16[8,12,128,128]{3,1,2,0:T(8,128)(2,1)S(1)} fusion(f32[8,128,128]{2,1,0:T(8,128)S(1)} %convert_element_type.86, f32[8,12]{1,0:T(8,128)S(1)} %fusion.82, bf16[8,8,128,128]{3,2,1,0:T(8,128)(2,1)S(1)} %copy-done, s32[8,8]{1,0:T(8,128)S(1)} %copy-done.6), kind=kOutput, calls=%fused_computation.6 | convolution fusion | flops 29885184 | bytes 5767808 | tf_op jit(solution)/shard_map/bkm,bkij->bimj/dot_general | solution.py:63
  18.7 1.6 copy.54
  21.0 1.0 copy-done.1
  22.0 1.8 %fusion.42 = f32[1024,256]{0,1:T(8,128)} fusion(bf16[1024,256]{0,1:T(8,128)(2,1)S(1)} %fusion.60, bf16[1024,1536]{1,0:T(8,128)(2,1)S(1)} %bitcast.54), kind=kOutput, calls=%fused_computation.70 | convolution fusion | flops 536870912 | bytes 3670016 | tf_op jit(solution)/shard_map/dot_general | solution.py:86
  23.8 2.3 %copy.34 = bf16[2048,256]{0,1:T(8,128)(2,1)} copy(bf16[2048,256]{1,0:T(8,128)(2,1)} %param.20) | data formatting | bytes 2097152 | tf_op args[8]
  26.1 4.1 %collective-permute-start.4 = (bf16[1024,64]{0,1:T(8,128)(2,1)}, bf16[1024,64]{0,1:T(8,128)(2,1)}, u32[]{:S(2)}, u32[]{:S(2)}) collective-permute-start(bf16[1024,64]{0,1:T(8,128)(2,1)} %get-tuple-element.32), channel_id=1, source_target_pairs={{0,1},{1,2},{2,3},{3,4},{4,5},{5,6},{6,7},{8,9},{9,10},{10,11},{11... | collective-permute-start | bytes 393224 | tf_op jit(solution)/shard_map/ppermute | solution.py:27
  32.2 1.3 collective-permute-start.5
  35.5 3.9 %collective-permute-start.1 = (bf16[256,256]{0,1:T(8,128)(2,1)S(1)}, bf16[256,256]{0,1:T(8,128)(2,1)}, u32[]{:S(2)}, u32[]{:S(2)}) collective-permute-start(bf16[256,256]{0,1:T(8,128)(2,1)S(1)} %pad_maximum_fusion.11), channel_id=1, source_target_pairs={{0,8},{8,16},{16,24},{1,9},{9,17},{17,25},{2,10},{10,18},{18,26},{... | collective-permute-start | bytes 393224 | tf_op jit(solution)/shard_map/ppermute | solution.py:84
  39.4 1.3 collective-permute-start.3
  40.7 3.1 %pad_maximum_fusion = bf16[4,1024,256]{2,1,0:T(8,128)(2,1)} fusion(bf16[1,1024,256]{2,1,0:T(8,128)(2,1)} %bitcast.12, bf16[1,1024,256]{2,1,0:T(8,128)(2,1)} %bitcast.11, bf16[1,1024,256]{2,1,0:T(8,128)(2,1)} %bitcast.10, bf16[1,1024,256]{2,1,0:T(8,128)(2,1)} %bitcast.70), kind=kLoop, calls=%fused_computation.16 | loop fusion | flops 3145728 | bytes 4194304 | tf_op jit(solution)/shard_map/stack | solution.py:109
  43.8 3.6 %gather_fusion = bf16[4,1024,256]{2,1,0:T(8,128)(2,1)} fusion(bf16[4,1024,256]{2,1,0:T(8,128)(2,1)} %pad_maximum_fusion, s32[1024]{0:T(1024)S(1)} %pad_clamp_fusion), kind=kCustom, calls=%fused_computation | custom fusion | bytes 4194320 | tf_op jit(solution)/shard_map/gather | solution.py:109
  47.4 9.4 %fusion.10 = f32[2048]{0:T(1024)S(1)} fusion(bf16[4096,256]{1,0:T(8,128)(2,1)} %bitcast.69, s32[2048]{0:T(1024)S(1)} %get-tuple-element.47, bf16[2048,256]{0,1:T(8,128)(2,1)} %copy.34), kind=kOutput, calls=%fused_computation.24 | convolution fusion | flops 4304926720 | bytes 3162112 | tf_op jit(solution)/shard_map/dot_general | solution.py:113
  56.9 5.9 %fusion = f32[4096,12]{0,1:T(8,128)S(1)} fusion(s32[2048]{0:T(1024)S(1)} %get-tuple-element.47, bf16[2048,4]{0,1:T(4,128)(2,1)S(1)} %get-tuple-element.41, bf16[2048,4]{0,1:T(4,128)(2,1)S(1)} %get-tuple-element.42, bf16[2048,4]{0,1:T(4,128)(2,1)S(1)} %get-tuple-element.40), kind=kOutput, calls=%fused_computation.2 | convolution fusion | flops 209862656 | bytes 253952 | tf_op jit(solution)/shard_map/dot_general | solution.py:124
  62.8 2.0 %copy.35 = f32[4096,4]{1,0:T(8,128)} copy(f32[4096,4]{0,1:T(4,128)S(1)} %slice_add_fusion) | data formatting | bytes 131072 | tf_op jit(solution)/shard_map/add | solution.py:127
  64.8 3.9 %all_to_all.8 = f32[4,1,4096]{2,1,0:T(1,128)} reshape(f32[4096,4]{1,0:T(8,128)} %copy.35) | data formatting | bytes 131072 | tf_op jit(solution)/shard_map/all_to_all | solution.py:131
  68.7 3.5 %all-to-all-start = ((f32[4,1,4096]{2,1,0:T(1,128)}), f32[4,1,4096]{2,1,0:T(1,128)S(1)}, u32[]{:S(2)}, u32[]{:S(2)}) async-start(f32[4,1,4096]{2,1,0:T(1,128)} %all_to_all.8), calls=%async_computation | async-start | bytes 131072 | tf_op jit(solution)/shard_map/all_to_all | solution.py:131
  72.2 2.7 %convolution_add_fusion.9 = f32[1024,256]{0,1:T(8,128)} fusion(f32[1024,256]{0,1:T(8,128)} %fusion.42, bf16[256,256]{0,1:T(8,128)(2,1)} %collective-permute-done.1, bf16[1024,1536]{1,0:T(8,128)(2,1)} %bitcast.55), kind=kOutput, calls=%fused_computation.46 | convolution fusion | flops 134479872 | bytes 2752512 | tf_op jit(solution)/shard_map/dot_general | solution.py:87
  75.0 1.3 all-to-all-done
  76.4 1.3 reshape.124
  77.7 1.2 copy.37
  79.3 2.7 %fusion.95 = (bf16[1024,256]{0,1:T(8,128)(2,1)S(1)}, f32[1024,256]{0,1:T(8,128)S(1)}) fusion(f32[1024,256]{0,1:T(8,128)S(1)} %get-tuple-element.39, f32[1024,256]{0,1:T(8,128)S(1)} %get-tuple-element.38, bf16[1024,64]{0,1:T(8,128)(2,1)} %collective-permute-done.5, bf16[1024,256]{0,1:T(8,128)(2,1)S(1)} %fusion.60, ...), kind=kOutput, calls=%fused_computation.191 | convolution fusion | flops 141557760 | bytes 6695936 | tf_op jit(solution)/shard_map/dot_general | solution.py:88
  83.0 1.3 collective-permute-start.10
  84.3 3.0 %collective-permute-start.9 = (bf16[256,256]{0,1:T(8,128)(2,1)S(1)}, bf16[256,256]{0,1:T(8,128)(2,1)S(1)}, u32[]{:S(2)}, u32[]{:S(2)}) collective-permute-start(bf16[256,256]{0,1:T(8,128)(2,1)S(1)} %pad_maximum_fusion.13), channel_id=1, source_target_pairs={{0,8},{8,16},{16,24},{1,9},{9,17},{17,25},{2,10},{10,18},{18,26},{... | collective-permute-start | bytes 393224 | tf_op jit(solution)/shard_map/ppermute | solution.py:84
  87.4 4.3 %collective-permute-start.11 = (bf16[1024,64]{0,1:T(8,128)(2,1)S(1)}, bf16[1024,64]{0,1:T(8,128)(2,1)S(1)}, u32[]{:S(2)}, u32[]{:S(2)}) collective-permute-start(bf16[1024,64]{0,1:T(8,128)(2,1)S(1)} %get-tuple-element.26), channel_id=1, source_target_pairs={{0,1},{1,2},{2,3},{3,4},{4,5},{5,6},{6,7},{8,9},{9,10},{10,11},{11... | collective-permute-start | bytes 393224 | tf_op jit(solution)/shard_map/ppermute | solution.py:27
  91.7 1.3 collective-permute-start.12
  93.4 2.2 %collective-permute-done.11 = bf16[1024,64]{0,1:T(8,128)(2,1)S(1)} collective-permute-done((bf16[1024,64]{0,1:T(8,128)(2,1)S(1)}, bf16[1024,64]{0,1:T(8,128)(2,1)S(1)}, u32[]{:S(2)}, u32[]{:S(2)}) %collective-permute-start.11) | collective-permute-done | bytes 131104 | tf_op jit(solution)/shard_map/ppermute | solution.py:27
  95.5 4.3 %collective-permute-done.12 = bf16[1024,64]{0,1:T(8,128)(2,1)S(1)} collective-permute-done((bf16[1024,64]{0,1:T(8,128)(2,1)S(1)}, bf16[1024,64]{0,1:T(8,128)(2,1)S(1)}, u32[]{:S(2)}, u32[]{:S(2)}) %collective-permute-start.12) | collective-permute-done | bytes 131104 | tf_op jit(solution)/shard_map/ppermute | solution.py:28
  99.8 0.8 fusion.96
  100.7 0.7 fusion.38
  101.6 1.3 collective-permute-start.14
  102.9 3.0 %collective-permute-start.13 = (bf16[256,256]{0,1:T(8,128)(2,1)S(1)}, bf16[256,256]{0,1:T(8,128)(2,1)S(1)}, u32[]{:S(2)}, u32[]{:S(2)}) collective-permute-start(bf16[256,256]{0,1:T(8,128)(2,1)S(1)} %pad_maximum_fusion.15), channel_id=1, source_target_pairs={{0,8},{8,16},{16,24},{1,9},{9,17},{17,25},{2,10},{10,18},{18,26},{... | collective-permute-start | bytes 393224 | tf_op jit(solution)/shard_map/ppermute | solution.py:84
  106.0 4.5 %collective-permute-start.15 = (bf16[1024,64]{0,1:T(8,128)(2,1)S(1)}, bf16[1024,64]{0,1:T(8,128)(2,1)S(1)}, u32[]{:S(2)}, u32[]{:S(2)}) collective-permute-start(bf16[1024,64]{0,1:T(8,128)(2,1)S(1)} %get-tuple-element.20), channel_id=1, source_target_pairs={{0,1},{1,2},{2,3},{3,4},{4,5},{5,6},{6,7},{8,9},{9,10},{10,11},{11... | collective-permute-start | bytes 393224 | tf_op jit(solution)/shard_map/ppermute | solution.py:27
  110.5 1.3 collective-permute-start.16
  112.2 2.1 %collective-permute-done.15 = bf16[1024,64]{0,1:T(8,128)(2,1)S(1)} collective-permute-done((bf16[1024,64]{0,1:T(8,128)(2,1)S(1)}, bf16[1024,64]{0,1:T(8,128)(2,1)S(1)}, u32[]{:S(2)}, u32[]{:S(2)}) %collective-permute-start.15) | collective-permute-done | bytes 131104 | tf_op jit(solution)/shard_map/ppermute | solution.py:27
  114.3 4.4 %collective-permute-done.16 = bf16[1024,64]{0,1:T(8,128)(2,1)S(1)} collective-permute-done((bf16[1024,64]{0,1:T(8,128)(2,1)S(1)}, bf16[1024,64]{0,1:T(8,128)(2,1)S(1)}, u32[]{:S(2)}, u32[]{:S(2)}) %collective-permute-start.16) | collective-permute-done | bytes 131104 | tf_op jit(solution)/shard_map/ppermute | solution.py:28
  118.7 0.8 fusion.97
  119.5 0.7 fusion.36
  120.4 1.3 collective-permute-start.18
  121.8 3.0 %collective-permute-start.17 = (bf16[256,256]{0,1:T(8,128)(2,1)S(1)}, bf16[256,256]{0,1:T(8,128)(2,1)S(1)}, u32[]{:S(2)}, u32[]{:S(2)}) collective-permute-start(bf16[256,256]{0,1:T(8,128)(2,1)S(1)} %pad_maximum_fusion.17), channel_id=1, source_target_pairs={{0,8},{8,16},{16,24},{1,9},{9,17},{17,25},{2,10},{10,18},{18,26},{... | collective-permute-start | bytes 393224 | tf_op jit(solution)/shard_map/ppermute | solution.py:84
  124.8 4.0 %collective-permute-start.19 = (bf16[1024,64]{0,1:T(8,128)(2,1)S(1)}, bf16[1024,64]{0,1:T(8,128)(2,1)S(1)}, u32[]{:S(2)}, u32[]{:S(2)}) collective-permute-start(bf16[1024,64]{0,1:T(8,128)(2,1)S(1)} %get-tuple-element.14), channel_id=1, source_target_pairs={{0,1},{1,2},{2,3},{3,4},{4,5},{5,6},{6,7},{8,9},{9,10},{10,11},{11... | collective-permute-start | bytes 393224 | tf_op jit(solution)/shard_map/ppermute | solution.py:27
  128.8 1.3 collective-permute-start.20
  130.5 1.8 %collective-permute-done.19 = bf16[1024,64]{0,1:T(8,128)(2,1)S(1)} collective-permute-done((bf16[1024,64]{0,1:T(8,128)(2,1)S(1)}, bf16[1024,64]{0,1:T(8,128)(2,1)S(1)}, u32[]{:S(2)}, u32[]{:S(2)}) %collective-permute-start.19) | collective-permute-done | bytes 131104 | tf_op jit(solution)/shard_map/ppermute | solution.py:27
  132.3 4.7 %collective-permute-done.20 = bf16[1024,64]{0,1:T(8,128)(2,1)S(1)} collective-permute-done((bf16[1024,64]{0,1:T(8,128)(2,1)S(1)}, bf16[1024,64]{0,1:T(8,128)(2,1)S(1)}, u32[]{:S(2)}, u32[]{:S(2)}) %collective-permute-start.20) | collective-permute-done | bytes 131104 | tf_op jit(solution)/shard_map/ppermute | solution.py:28
  137.0 1.8 %fusion.98 = (bf16[1024,256]{0,1:T(8,128)(2,1)S(1)}, f32[1024,256]{0,1:T(8,128)}) fusion(f32[1024,256]{0,1:T(8,128)S(1)} %get-tuple-element.59, f32[1024,256]{0,1:T(8,128)S(1)} %get-tuple-element.39, f32[1024,256]{0,1:T(8,128)S(1)} %fusion.6, bf16[1024,64]{0,1:T(8,128)(2,1)S(1)} %collective-permute-done.20, bf16[1024,256]{0,1:T(8,128)(2,1)S(1)} %get-tuple-element.58, ...), kind=kOutput, calls=%fused_computation.194 | convolution fusion | flops 140247040 | bytes 7735296 | tf_op jit(solution)/shard_map/dot_general | solution.py:88
  138.9 1.7 %fusion.44 = f32[1024,256]{0,1:T(8,128)} fusion(bf16[1024,256]{0,1:T(8,128)(2,1)S(1)} %get-tuple-element.60, bf16[1024,1536]{1,0:T(8,128)(2,1)S(1)} %bitcast.68), kind=kOutput, calls=%fused_computation.72 | convolution fusion | flops 536870912 | bytes 3670016 | tf_op jit(solution)/shard_map/dot_general | solution.py:86
  141.3 1.3 collective-permute-start.22
  143.3 3.7 %collective-permute-start.21 = (bf16[256,256]{0,1:T(8,128)(2,1)}, bf16[256,256]{0,1:T(8,128)(2,1)}, u32[]{:S(2)}, u32[]{:S(2)}) collective-permute-start(bf16[256,256]{0,1:T(8,128)(2,1)} %pad_maximum_fusion.19), channel_id=1, source_target_pairs={{0,8},{8,16},{16,24},{1,9},{9,17},{17,25},{2,10},{10,18},{18,26},{... | collective-permute-start | bytes 393224 | tf_op jit(solution)/shard_map/ppermute | solution.py:84
  146.9 0.7 fusion.87
  147.7 3.9 %collective-permute-start.23 = (bf16[1024,64]{0,1:T(8,128)(2,1)}, bf16[1024,64]{0,1:T(8,128)(2,1)S(1)}, u32[]{:S(2)}, u32[]{:S(2)}) collective-permute-start(bf16[1024,64]{0,1:T(8,128)(2,1)} %get-tuple-element.12), channel_id=1, source_target_pairs={{0,1},{1,2},{2,3},{3,4},{4,5},{5,6},{6,7},{8,9},{9,10},{10,11},{11... | collective-permute-start | bytes 393224 | tf_op jit(solution)/shard_map/ppermute | solution.py:27
  151.5 1.3 collective-permute-start.24
  152.8 2.5 %copy.41 = f32[1024,256]{1,0:T(8,128)} copy(f32[1024,256]{0,1:T(8,128)} %get-tuple-element.61) | data formatting | bytes 2097152
  155.4 1.8 %convolution_add_fusion.1 = f32[1024,256]{0,1:T(8,128)S(1)} fusion(f32[1024,256]{0,1:T(8,128)} %fusion.44, bf16[256,256]{0,1:T(8,128)(2,1)} %collective-permute-done.21, bf16[1024,1536]{1,0:T(8,128)(2,1)} %bitcast.57), kind=kOutput, calls=%fused_computation.26 | convolution fusion | flops 134479872 | bytes 2752512 | tf_op jit(solution)/shard_map/dot_general | solution.py:87
  157.2 1.5 fusion.35
  158.6 0.8 collective-permute-done.24
  159.8 5.8 %psum.7 = f32[2,256]{1,0:T(2,128)S(1)} all-reduce(f32[2,256]{1,0:T(2,128)S(1)} %pad_maximum_fusion.21), channel_id=1, replica_groups=mesh['space'=4,'tm'=8] {'space'}, use_global_device_ids=true, to_apply=%region_5.6 | all-reduce | flops 512 | bytes 4096 | tf_op jit(solution)/shard_map/psum | solution.py:157
  (79 shorter events, 9.7 us)
Async XLA Ops:
  0.6 15.8 %copy-start = (bf16[8,8,128,128]{3,2,1,0:T(8,128)(2,1)S(1)}, bf16[8,8,128,128]{3,2,1,0:T(8,128)(2,1)}, u32[]{:S(2)}) copy-start(bf16[8,8,128,128]{3,2,1,0:T(8,128)(2,1)} %param.17) | copy-start | bytes 6291460
  0.6 15.7 %copy-start.6 = (s32[8,8]{1,0:T(8,128)S(1)}, s32[8,8]{1,0:T(8,128)}, u32[]{:S(2)}) copy-start(s32[8,8]{1,0:T(8,128)} %param.18) | copy-start | bytes 772
  0.7 34.8 %collective-permute-start.6 = (bf16[1024,256]{1,0:T(8,128)(2,1)}, bf16[1024,256]{1,0:T(8,128)(2,1)}, u32[]{:S(2)}, u32[]{:S(2)}) collective-permute-start(bf16[1024,256]{1,0:T(8,128)(2,1)} %param.23), channel_id=1, source_target_pairs={{0,8},{8,16},{16,24},{24,0},{1,9},{9,17},{17,25},{25,1},{2,10},{10... | collective-permute-start | bytes 1572872 | tf_op jit(solution)/shard_map/ppermute | solution.py:105
  1.2 38.2 %collective-permute-start.7 = (bf16[1024,256]{1,0:T(8,128)(2,1)}, bf16[1024,256]{1,0:T(8,128)(2,1)}, u32[]{:S(2)}, u32[]{:S(2)}) collective-permute-start(bf16[1024,256]{1,0:T(8,128)(2,1)} %param.23), channel_id=1, source_target_pairs={{0,16},{8,24},{16,0},{24,8},{1,17},{9,25},{17,1},{25,9},{2,18},{10... | collective-permute-start | bytes 1572872 | tf_op jit(solution)/shard_map/ppermute | solution.py:105
  3.8 36.9 %collective-permute-start.8 = (bf16[1024,256]{1,0:T(8,128)(2,1)}, bf16[1024,256]{1,0:T(8,128)(2,1)}, u32[]{:S(2)}, u32[]{:S(2)}) collective-permute-start(bf16[1024,256]{1,0:T(8,128)(2,1)} %param.23), channel_id=1, source_target_pairs={{0,24},{8,0},{16,8},{24,16},{1,25},{9,1},{17,9},{25,17},{2,26},{10... | collective-permute-start | bytes 1572872 | tf_op jit(solution)/shard_map/ppermute | solution.py:105
  6.0 20.2 %collective-permute-start = (s32[2]{0:T(128)S(1)}, s32[2]{0:T(128)S(1)}, u32[]{:S(2)}, u32[]{:S(2)}) collective-permute-start(s32[2]{0:T(128)S(1)} %get-tuple-element.51), channel_id=1, source_target_pairs={{8,0},{16,8},{24,16},{9,1},{17,9},{25,17},{10,2},{18,10},{26,18},{... | collective-permute-start | bytes 32 | tf_op jit(solution)/shard_map/ppermute | solution.py:74
  7.3 24.9 %collective-permute-start.2 = (s32[2]{0:T(128)S(1)}, s32[2]{0:T(128)S(1)}, u32[]{:S(2)}, u32[]{:S(2)}) collective-permute-start(s32[2]{0:T(128)S(1)} %get-tuple-element.50), channel_id=1, source_target_pairs={{0,8},{8,16},{16,24},{1,9},{9,17},{17,25},{2,10},{10,18},{18,26},{... | collective-permute-start | bytes 32 | tf_op jit(solution)/shard_map/ppermute | solution.py:75
  20.3 1.7 %copy-start.1 = (bf16[128,8,12,128]{3,1,2,0:T(8,128)(2,1)}, bf16[128,8,12,128]{3,1,2,0:T(8,128)(2,1)S(1)}, u32[]{:S(2)}) copy-start(bf16[128,8,12,128]{3,1,2,0:T(8,128)(2,1)S(1)} %copy.54) | copy-start | bytes 9437188
  20.3 3.5 %copy-start.4 = (s32[2048,1]{0,1:T(1,128)S(1)}, s32[2048,1]{0,1:T(1,128)}, u32[]{:S(2)}) copy-start(s32[2048,1]{0,1:T(1,128)} %param.21) | copy-start | bytes 24580
  21.0 5.1 %copy-start.5 = (s32[2048]{0:T(1024)S(1)}, s32[2048]{0:T(1024)}, u32[]{:S(2)}) copy-start(s32[2048]{0:T(1024)} %param.22) | copy-start | bytes 24580
  26.1 53.2 %collective-permute-start.4 = (bf16[1024,64]{0,1:T(8,128)(2,1)}, bf16[1024,64]{0,1:T(8,128)(2,1)}, u32[]{:S(2)}, u32[]{:S(2)}) collective-permute-start(bf16[1024,64]{0,1:T(8,128)(2,1)} %get-tuple-element.32), channel_id=1, source_target_pairs={{0,1},{1,2},{2,3},{3,4},{4,5},{5,6},{6,7},{8,9},{9,10},{10,11},{11... | collective-permute-start | bytes 393224 | tf_op jit(solution)/shard_map/ppermute | solution.py:27
  32.2 47.1 %collective-permute-start.5 = (bf16[1024,64]{0,1:T(8,128)(2,1)}, bf16[1024,64]{0,1:T(8,128)(2,1)}, u32[]{:S(2)}, u32[]{:S(2)}) collective-permute-start(bf16[1024,64]{0,1:T(8,128)(2,1)} %get-tuple-element.33), channel_id=1, source_target_pairs={{1,0},{2,1},{3,2},{4,3},{5,4},{6,5},{7,6},{9,8},{10,9},{11,10},{12... | collective-permute-start | bytes 393224 | tf_op jit(solution)/shard_map/ppermute | solution.py:28
  35.5 36.8 %collective-permute-start.1 = (bf16[256,256]{0,1:T(8,128)(2,1)S(1)}, bf16[256,256]{0,1:T(8,128)(2,1)}, u32[]{:S(2)}, u32[]{:S(2)}) collective-permute-start(bf16[256,256]{0,1:T(8,128)(2,1)S(1)} %pad_maximum_fusion.11), channel_id=1, source_target_pairs={{0,8},{8,16},{16,24},{1,9},{9,17},{17,25},{2,10},{10,18},{18,26},{... | collective-permute-start | bytes 393224 | tf_op jit(solution)/shard_map/ppermute | solution.py:84
  39.4 40.0 %collective-permute-start.3 = (bf16[256,256]{0,1:T(8,128)(2,1)S(1)}, bf16[256,256]{0,1:T(8,128)(2,1)}, u32[]{:S(2)}, u32[]{:S(2)}) collective-permute-start(bf16[256,256]{0,1:T(8,128)(2,1)S(1)} %pad_maximum_fusion.12), channel_id=1, source_target_pairs={{8,0},{16,8},{24,16},{9,1},{17,9},{25,17},{10,2},{18,10},{26,18},{... | collective-permute-start | bytes 393224 | tf_op jit(solution)/shard_map/ppermute | solution.py:85
  64.8 14.2 %copy-start.3 = (f32[1024]{0:T(1024)S(1)}, f32[1024]{0:T(1024)}, u32[]{:S(2)}) copy-start(f32[1024]{0:T(1024)} %param.13) | copy-start | bytes 12292
  68.7 7.6 %all-to-all-start = ((f32[4,1,4096]{2,1,0:T(1,128)}), f32[4,1,4096]{2,1,0:T(1,128)S(1)}, u32[]{:S(2)}, u32[]{:S(2)}) async-start(f32[4,1,4096]{2,1,0:T(1,128)} %all_to_all.8), calls=%async_computation | async-start | bytes 131072 | tf_op jit(solution)/shard_map/all_to_all | solution.py:131
  79.3 2.8 %copy-start.2 = (bf16[128,8,12,128]{3,1,2,0:T(8,128)(2,1)S(1)}, bf16[128,8,12,128]{3,1,2,0:T(8,128)(2,1)}, u32[]{:S(2)}) copy-start(bf16[128,8,12,128]{3,1,2,0:T(8,128)(2,1)} %copy-done.1) | copy-start | bytes 9437188
  83.0 10.3 %collective-permute-start.10 = (bf16[256,256]{0,1:T(8,128)(2,1)S(1)}, bf16[256,256]{0,1:T(8,128)(2,1)S(1)}, u32[]{:S(2)}, u32[]{:S(2)}) collective-permute-start(bf16[256,256]{0,1:T(8,128)(2,1)S(1)} %pad_maximum_fusion.14), channel_id=1, source_target_pairs={{8,0},{16,8},{24,16},{9,1},{17,9},{25,17},{10,2},{18,10},{26,18},{... | collective-permute-start | bytes 393224 | tf_op jit(solution)/shard_map/ppermute | solution.py:85
  84.3 8.7 %collective-permute-start.9 = (bf16[256,256]{0,1:T(8,128)(2,1)S(1)}, bf16[256,256]{0,1:T(8,128)(2,1)S(1)}, u32[]{:S(2)}, u32[]{:S(2)}) collective-permute-start(bf16[256,256]{0,1:T(8,128)(2,1)S(1)} %pad_maximum_fusion.13), channel_id=1, source_target_pairs={{0,8},{8,16},{16,24},{1,9},{9,17},{17,25},{2,10},{10,18},{18,26},{... | collective-permute-start | bytes 393224 | tf_op jit(solution)/shard_map/ppermute | solution.py:84
  87.4 8.1 %collective-permute-start.11 = (bf16[1024,64]{0,1:T(8,128)(2,1)S(1)}, bf16[1024,64]{0,1:T(8,128)(2,1)S(1)}, u32[]{:S(2)}, u32[]{:S(2)}) collective-permute-start(bf16[1024,64]{0,1:T(8,128)(2,1)S(1)} %get-tuple-element.26), channel_id=1, source_target_pairs={{0,1},{1,2},{2,3},{3,4},{4,5},{5,6},{6,7},{8,9},{9,10},{10,11},{11... | collective-permute-start | bytes 393224 | tf_op jit(solution)/shard_map/ppermute | solution.py:27
  91.7 8.1 %collective-permute-start.12 = (bf16[1024,64]{0,1:T(8,128)(2,1)S(1)}, bf16[1024,64]{0,1:T(8,128)(2,1)S(1)}, u32[]{:S(2)}, u32[]{:S(2)}) collective-permute-start(bf16[1024,64]{0,1:T(8,128)(2,1)S(1)} %get-tuple-element.27), channel_id=1, source_target_pairs={{1,0},{2,1},{3,2},{4,3},{5,4},{6,5},{7,6},{9,8},{10,9},{11,10},{12... | collective-permute-start | bytes 393224 | tf_op jit(solution)/shard_map/ppermute | solution.py:28
  101.6 10.6 %collective-permute-start.14 = (bf16[256,256]{0,1:T(8,128)(2,1)S(1)}, bf16[256,256]{0,1:T(8,128)(2,1)S(1)}, u32[]{:S(2)}, u32[]{:S(2)}) collective-permute-start(bf16[256,256]{0,1:T(8,128)(2,1)S(1)} %pad_maximum_fusion.16), channel_id=1, source_target_pairs={{8,0},{16,8},{24,16},{9,1},{17,9},{25,17},{10,2},{18,10},{26,18},{... | collective-permute-start | bytes 393224 | tf_op jit(solution)/shard_map/ppermute | solution.py:85
  102.9 8.9 %collective-permute-start.13 = (bf16[256,256]{0,1:T(8,128)(2,1)S(1)}, bf16[256,256]{0,1:T(8,128)(2,1)S(1)}, u32[]{:S(2)}, u32[]{:S(2)}) collective-permute-start(bf16[256,256]{0,1:T(8,128)(2,1)S(1)} %pad_maximum_fusion.15), channel_id=1, source_target_pairs={{0,8},{8,16},{16,24},{1,9},{9,17},{17,25},{2,10},{10,18},{18,26},{... | collective-permute-start | bytes 393224 | tf_op jit(solution)/shard_map/ppermute | solution.py:84
  106.0 8.3 %collective-permute-start.15 = (bf16[1024,64]{0,1:T(8,128)(2,1)S(1)}, bf16[1024,64]{0,1:T(8,128)(2,1)S(1)}, u32[]{:S(2)}, u32[]{:S(2)}) collective-permute-start(bf16[1024,64]{0,1:T(8,128)(2,1)S(1)} %get-tuple-element.20), channel_id=1, source_target_pairs={{0,1},{1,2},{2,3},{3,4},{4,5},{5,6},{6,7},{8,9},{9,10},{10,11},{11... | collective-permute-start | bytes 393224 | tf_op jit(solution)/shard_map/ppermute | solution.py:27
  110.5 8.1 %collective-permute-start.16 = (bf16[1024,64]{0,1:T(8,128)(2,1)S(1)}, bf16[1024,64]{0,1:T(8,128)(2,1)S(1)}, u32[]{:S(2)}, u32[]{:S(2)}) collective-permute-start(bf16[1024,64]{0,1:T(8,128)(2,1)S(1)} %get-tuple-element.21), channel_id=1, source_target_pairs={{1,0},{2,1},{3,2},{4,3},{5,4},{6,5},{7,6},{9,8},{10,9},{11,10},{12... | collective-permute-start | bytes 393224 | tf_op jit(solution)/shard_map/ppermute | solution.py:28
  120.4 10.1 %collective-permute-start.18 = (bf16[256,256]{0,1:T(8,128)(2,1)S(1)}, bf16[256,256]{0,1:T(8,128)(2,1)S(1)}, u32[]{:S(2)}, u32[]{:S(2)}) collective-permute-start(bf16[256,256]{0,1:T(8,128)(2,1)S(1)} %pad_maximum_fusion.18), channel_id=1, source_target_pairs={{8,0},{16,8},{24,16},{9,1},{17,9},{25,17},{10,2},{18,10},{26,18},{... | collective-permute-start | bytes 393224 | tf_op jit(solution)/shard_map/ppermute | solution.py:85
  121.8 8.4 %collective-permute-start.17 = (bf16[256,256]{0,1:T(8,128)(2,1)S(1)}, bf16[256,256]{0,1:T(8,128)(2,1)S(1)}, u32[]{:S(2)}, u32[]{:S(2)}) collective-permute-start(bf16[256,256]{0,1:T(8,128)(2,1)S(1)} %pad_maximum_fusion.17), channel_id=1, source_target_pairs={{0,8},{8,16},{16,24},{1,9},{9,17},{17,25},{2,10},{10,18},{18,26},{... | collective-permute-start | bytes 393224 | tf_op jit(solution)/shard_map/ppermute | solution.py:84
  124.8 7.5 %collective-permute-start.19 = (bf16[1024,64]{0,1:T(8,128)(2,1)S(1)}, bf16[1024,64]{0,1:T(8,128)(2,1)S(1)}, u32[]{:S(2)}, u32[]{:S(2)}) collective-permute-start(bf16[1024,64]{0,1:T(8,128)(2,1)S(1)} %get-tuple-element.14), channel_id=1, source_target_pairs={{0,1},{1,2},{2,3},{3,4},{4,5},{5,6},{6,7},{8,9},{9,10},{10,11},{11... | collective-permute-start | bytes 393224 | tf_op jit(solution)/shard_map/ppermute | solution.py:27
  128.8 8.2 %collective-permute-start.20 = (bf16[1024,64]{0,1:T(8,128)(2,1)S(1)}, bf16[1024,64]{0,1:T(8,128)(2,1)S(1)}, u32[]{:S(2)}, u32[]{:S(2)}) collective-permute-start(bf16[1024,64]{0,1:T(8,128)(2,1)S(1)} %get-tuple-element.15), channel_id=1, source_target_pairs={{1,0},{2,1},{3,2},{4,3},{5,4},{6,5},{7,6},{9,8},{10,9},{11,10},{12... | collective-permute-start | bytes 393224 | tf_op jit(solution)/shard_map/ppermute | solution.py:28
  141.3 15.8 %collective-permute-start.22 = (bf16[256,256]{0,1:T(8,128)(2,1)}, bf16[256,256]{0,1:T(8,128)(2,1)S(1)}, u32[]{:S(2)}, u32[]{:S(2)}) collective-permute-start(bf16[256,256]{0,1:T(8,128)(2,1)} %pad_maximum_fusion.20), channel_id=1, source_target_pairs={{8,0},{16,8},{24,16},{9,1},{17,9},{25,17},{10,2},{18,10},{26,18},{... | collective-permute-start | bytes 393224 | tf_op jit(solution)/shard_map/ppermute | solution.py:85
  143.3 12.1 %collective-permute-start.21 = (bf16[256,256]{0,1:T(8,128)(2,1)}, bf16[256,256]{0,1:T(8,128)(2,1)}, u32[]{:S(2)}, u32[]{:S(2)}) collective-permute-start(bf16[256,256]{0,1:T(8,128)(2,1)} %pad_maximum_fusion.19), channel_id=1, source_target_pairs={{0,8},{8,16},{16,24},{1,9},{9,17},{17,25},{2,10},{10,18},{18,26},{... | collective-permute-start | bytes 393224 | tf_op jit(solution)/shard_map/ppermute | solution.py:84
  147.7 11.0 %collective-permute-start.23 = (bf16[1024,64]{0,1:T(8,128)(2,1)}, bf16[1024,64]{0,1:T(8,128)(2,1)S(1)}, u32[]{:S(2)}, u32[]{:S(2)}) collective-permute-start(bf16[1024,64]{0,1:T(8,128)(2,1)} %get-tuple-element.12), channel_id=1, source_target_pairs={{0,1},{1,2},{2,3},{3,4},{4,5},{5,6},{6,7},{8,9},{9,10},{10,11},{11... | collective-permute-start | bytes 393224 | tf_op jit(solution)/shard_map/ppermute | solution.py:27
  151.5 7.9 %collective-permute-start.24 = (bf16[1024,64]{0,1:T(8,128)(2,1)}, bf16[1024,64]{0,1:T(8,128)(2,1)S(1)}, u32[]{:S(2)}, u32[]{:S(2)}) collective-permute-start(bf16[1024,64]{0,1:T(8,128)(2,1)} %get-tuple-element.13), channel_id=1, source_target_pairs={{1,0},{2,1},{3,2},{4,3},{5,4},{6,5},{7,6},{9,8},{10,9},{11,10},{12... | collective-permute-start | bytes 393224 | tf_op jit(solution)/shard_map/ppermute | solution.py:28

commit v7 on v6

--- a/solution.py
+++ b/solution.py
@@ -105,14 +105,14 @@
         lax.ppermute(svc_coef, "space", [(i, (i + k) % space_count) for i in range(space_count)])
         for k in range(1, space_count)
     ]
-    shifts = (lax.axis_index("space") - jnp.arange(space_count)) % space_count
-    svc_all = jnp.stack(tables)[shifts].reshape(space_count * nodes_dev, svc_coef.shape[1])
+    svc_all = jnp.concatenate(tables, axis=0)
     owner = obs_owner[:, 0]
+    shift = (lax.axis_index("space") - owner) % space_count
+    coef_rows = svc_all[shift * nodes_dev + obs_cell // T_DEV]
+    eta = jnp.einsum("rc,rc->r", covariates, coef_rows, preferred_element_type=jnp.float32)
+    obs_weight = jnp.exp(eta)
     node_ids = owner * nodes_dev + obs_cell // T_DEV
     onehot = (node_ids[:, None] == jnp.arange(space_count * nodes_dev)[None, :]).astype(jnp.bfloat16)
-    coef_rows = jnp.dot(onehot, svc_all, preferred_element_type=jnp.float32)
-    eta = jnp.sum(covariates.astype(jnp.float32) * coef_rows, axis=1)
-    obs_weight = jnp.exp(eta)
     high = lax.reduce_precision(obs_weight, exponent_bits=8, mantissa_bits=7)
     rest = obs_weight - high
     middle = lax.reduce_precision(rest, exponent_bits=8, mantissa_bits=7)

time: 168 us -> 167 us (level)
  matrix products: 36.4 us -> 26.8 us
  local copies, waits for them, and re-layouts: 26.3 us -> 30.7 us
  starting transfers between devices: 62.6 us -> 65.4 us
  other arithmetic: 9.61 us -> 11.4 us
    dot_general x1 -> x0, matrix products: 9.45 us -> none  [shards(): coef_rows = jnp.dot(onehot, svc_all, preferred_element_type=jnp.float32)]
    gather x1, local copies, waits for them, and re-layouts: 3.58 us -> 10.4 us  [shards(): coef_rows = svc_all[shift * nodes_dev + obs_cell // T_DEV]]
    another operation x3 -> x2, other arithmetic: 3.15 us -> 0.03 us  [the longest x1 3.12 us: shards(): jnp.stack(tables)[shifts]]
    concatenate x0 -> x1, other arithmetic: none -> 2.99 us  [shards(): svc_all = jnp.concatenate(tables, axis=0)]
    ppermute x5, starting transfers between devices: 16.7 us -> 19.1 us  [spatial(): lower = lax.ppermute(pick_blocks(field, upper_wants), 'space', up)]
    unnamed x18 -> x17, local copies, waits for them, and re-layouts: 8.66 us -> 6.38 us
    dot_general x0 -> x1, other arithmetic: none -> 1.89 us  [shards(): jnp.einsum('rc,rc->r', covariates, coef_rows, preferred_element_type=jnp....]
  transfers between devices with their start and end apart: 26 -> 26, of which waited for: 8 -> 8; matrix products, arithmetic and copies ran while one was open for 33% -> 31% of each run, Pallas kernels for 0% -> 0%
where the time goes in v7:
time: 167 us; the launch traced here: 165 us
  starting transfers between devices  65.4 us (39%)
  local copies, waits for them, and re-layouts  30.7 us (18%)
  matrix products  26.8 us (16%)
  waiting for transfers between devices  21.4 us (13%)
  other arithmetic  11.4 us (7%)
  blocking collectives  5.76 us (3%)
  between operations  3.96 us (2%)
    ppermute x5, starting transfers between devices, with_halo(): before = lax.ppermute(last, axis, up)  20.9 us
    ppermute x5, starting transfers between devices, spatial(): lower = lax.ppermute(pick_blocks(field, upper_wants), 'space', up)  19.1 us
    ppermute x5, waiting for transfers between devices, with_halo(): after = lax.ppermute(initial, axis, down)  14.2 us
    gather x1, local copies, waits for them, and re-layouts, shards(): coef_rows = svc_all[shift * nodes_dev + obs_cell // T_DEV]  10.4 us
    dot_general x5, matrix products, spatial(): jnp.dot(upper.T, upper_t, preferred_element_type=jnp.float32)  7.54 us
    ppermute x5, starting transfers between devices, spatial(): upper = lax.ppermute(pick_blocks(field, lower_wants), 'space', down)  6.62 us
    ppermute x5, starting transfers between devices, with_halo(): after = lax.ppermute(initial, axis, down)  6.46 us
    unnamed x17, local copies, waits for them, and re-layouts  6.38 us
  transfers between devices with their start and end apart: 26, of which 8 were waited for; matrix products, arithmetic and copies ran while one was open for 31% of the time, Pallas kernels for 0%

profile of v7, /device:TPU:0, one launch (start us, length us, event | category | flops | bytes accessed | tf_op | source)
XLA Modules:
  0.0 165.4 jit_solution(14597559550065144684)
XLA Ops:
  1.2 2.6 %collective-permute-start.7 = (bf16[1024,256]{1,0:T(8,128)(2,1)}, bf16[1024,256]{1,0:T(8,128)(2,1)}, u32[]{:S(2)}, u32[]{:S(2)}) collective-permute-start(bf16[1024,256]{1,0:T(8,128)(2,1)} %param.23), channel_id=1, source_target_pairs={{0,16},{8,24},{16,0},{24,8},{1,17},{9,25},{17,1},{25,9},{2,18},{10... | collective-permute-start | bytes 1572872 | tf_op jit(solution)/shard_map/ppermute | solution.py:105
  3.8 1.4 collective-permute-start.8
  5.2 0.8 fusion.92
  6.0 1.3 collective-permute-start
  7.3 3.0 %collective-permute-start.2 = (s32[2]{0:T(128)S(1)}, s32[2]{0:T(128)S(1)}, u32[]{:S(2)}, u32[]{:S(2)}) collective-permute-start(s32[2]{0:T(128)S(1)} %get-tuple-element.53), channel_id=1, source_target_pairs={{0,8},{8,16},{16,24},{1,9},{9,17},{17,25},{2,10},{10,18},{18,26},{... | collective-permute-start | bytes 32 | tf_op jit(solution)/shard_map/ppermute | solution.py:75
  10.3 1.2 copy.29
  13.2 1.0 convert_element_type.83
  14.2 1.1 select_reduce_fusion
  15.3 1.1 fusion.57
  16.4 2.2 %add_convert_fusion = bf16[8,12,128,128]{3,1,2,0:T(8,128)(2,1)S(1)} fusion(f32[8,128,128]{2,1,0:T(8,128)S(1)} %convert_element_type.83, f32[8,12]{1,0:T(8,128)S(1)} %fusion.82, bf16[8,8,128,128]{3,2,1,0:T(8,128)(2,1)S(1)} %copy-done, s32[8,8]{1,0:T(8,128)S(1)} %copy-done.6), kind=kOutput, calls=%fused_computation.4 | convolution fusion | flops 29885184 | bytes 5767808 | tf_op jit(solution)/shard_map/bkm,bkij->bimj/dot_general | solution.py:63
  18.7 1.6 copy.56
  21.0 1.0 copy-done.1
  22.0 1.7 %fusion.39 = f32[1024,256]{0,1:T(8,128)} fusion(bf16[1024,256]{0,1:T(8,128)(2,1)S(1)} %fusion.57, bf16[1024,1536]{1,0:T(8,128)(2,1)S(1)} %bitcast.47), kind=kOutput, calls=%fused_computation.68 | convolution fusion | flops 536870912 | bytes 3670016 | tf_op jit(solution)/shard_map/dot_general | solution.py:86
  23.8 4.1 %collective-permute-start.4 = (bf16[1024,64]{0,1:T(8,128)(2,1)}, bf16[1024,64]{0,1:T(8,128)(2,1)}, u32[]{:S(2)}, u32[]{:S(2)}) collective-permute-start(bf16[1024,64]{0,1:T(8,128)(2,1)} %get-tuple-element.32), channel_id=1, source_target_pairs={{0,1},{1,2},{2,3},{3,4},{4,5},{5,6},{6,7},{8,9},{9,10},{10,11},{11... | collective-permute-start | bytes 393224 | tf_op jit(solution)/shard_map/ppermute | solution.py:27
  29.7 1.3 collective-permute-start.5
  33.1 6.3 %collective-permute-start.1 = (bf16[256,256]{0,1:T(8,128)(2,1)S(1)}, bf16[256,256]{0,1:T(8,128)(2,1)}, u32[]{:S(2)}, u32[]{:S(2)}) collective-permute-start(bf16[256,256]{0,1:T(8,128)(2,1)S(1)} %pad_maximum_fusion.11), channel_id=1, source_target_pairs={{0,8},{8,16},{16,24},{1,9},{9,17},{17,25},{2,10},{10,18},{18,26},{... | collective-permute-start | bytes 393224 | tf_op jit(solution)/shard_map/ppermute | solution.py:84
  39.4 1.5 collective-permute-start.3
  40.8 3.0 %pad_maximum_fusion = bf16[4096,256]{1,0:T(8,128)(2,1)} fusion(bf16[1024,256]{1,0:T(8,128)(2,1)} %collective-permute-done.8, bf16[1024,256]{1,0:T(8,128)(2,1)} %collective-permute-done.7, bf16[1024,256]{1,0:T(8,128)(2,1)} %collective-permute-done.6, bf16[1024,256]{1,0:T(8,128)(2,1)} %param.23), kind=kLoop, calls=%fused_computation.13 | loop fusion | flops 8388608 | bytes 4194304 | tf_op jit(solution)/shard_map/concatenate | solution.py:108
  43.8 10.4 %gather_fusion = bf16[2048,256]{1,0:T(8,128)(2,1)} fusion(bf16[4096,256]{1,0:T(8,128)(2,1)} %pad_maximum_fusion, s32[2048]{0:T(1024)S(1)} %get-tuple-element.47), kind=kCustom, calls=%fused_computation | custom fusion | bytes 2105344 | tf_op jit(solution)/shard_map/gather | solution.py:111
  54.2 1.9 %fusion.2 = f32[2048]{0:T(1024)S(1)} fusion(bf16[2048,256]{1,0:T(8,128)(2,1)} %gather_fusion, bf16[2048,256]{1,0:T(8,128)(2,1)} %param.20), kind=kLoop, calls=%fused_computation.15 | loop fusion | flops 2095104 | bytes 2105344 | tf_op jit(solution)/shard_map/rc,rc->r/dot_general | solution.py:112
  56.1 5.9 %fusion = f32[4096,12]{0,1:T(8,128)S(1)} fusion(s32[2048]{0:T(1024)S(1)} %get-tuple-element.48, bf16[2048,4]{0,1:T(4,128)(2,1)S(1)} %get-tuple-element.41, bf16[2048,4]{0,1:T(4,128)(2,1)S(1)} %get-tuple-element.42, bf16[2048,4]{0,1:T(4,128)(2,1)S(1)} %get-tuple-element.40), kind=kOutput, calls=%fused_computation.2 | convolution fusion | flops 209862656 | bytes 253952 | tf_op jit(solution)/shard_map/dot_general | solution.py:124
  62.1 2.0 %copy.32 = f32[4096,4]{1,0:T(8,128)} copy(f32[4096,4]{0,1:T(4,128)S(1)} %slice_add_fusion) | data formatting | bytes 131072 | tf_op jit(solution)/shard_map/add | solution.py:127
  64.1 3.9 %all_to_all.8 = f32[4,1,4096]{2,1,0:T(1,128)} reshape(f32[4096,4]{1,0:T(8,128)} %copy.32) | data formatting | bytes 131072 | tf_op jit(solution)/shard_map/all_to_all | solution.py:131
  68.0 3.5 %all-to-all-start = ((f32[4,1,4096]{2,1,0:T(1,128)}), f32[4,1,4096]{2,1,0:T(1,128)S(1)}, u32[]{:S(2)}, u32[]{:S(2)}) async-start(f32[4,1,4096]{2,1,0:T(1,128)} %all_to_all.8), calls=%async_computation | async-start | bytes 131072 | tf_op jit(solution)/shard_map/all_to_all | solution.py:131
  71.5 2.7 %convolution_add_fusion.9 = f32[1024,256]{0,1:T(8,128)} fusion(f32[1024,256]{0,1:T(8,128)} %fusion.39, bf16[256,256]{0,1:T(8,128)(2,1)} %collective-permute-done.1, bf16[1024,1536]{1,0:T(8,128)(2,1)} %bitcast.48), kind=kOutput, calls=%fused_computation.44 | convolution fusion | flops 134479872 | bytes 2752512 | tf_op jit(solution)/shard_map/dot_general | solution.py:87
  74.3 1.1 all-to-all-done
  75.4 1.3 reshape.65
  76.8 1.2 copy.34
  78.4 2.7 %fusion.94 = (bf16[1024,256]{0,1:T(8,128)(2,1)S(1)}, f32[1024,256]{0,1:T(8,128)S(1)}) fusion(f32[1024,256]{0,1:T(8,128)S(1)} %get-tuple-element.39, f32[1024,256]{0,1:T(8,128)S(1)} %get-tuple-element.38, bf16[1024,64]{0,1:T(8,128)(2,1)} %collective-permute-done.5, bf16[1024,256]{0,1:T(8,128)(2,1)S(1)} %fusion.57, ...), kind=kOutput, calls=%fused_computation.191 | convolution fusion | flops 141557760 | bytes 6695936 | tf_op jit(solution)/shard_map/dot_general | solution.py:88
  81.2 0.7 fusion.37
  82.1 1.3 collective-permute-start.10
  83.4 3.0 %collective-permute-start.9 = (bf16[256,256]{0,1:T(8,128)(2,1)S(1)}, bf16[256,256]{0,1:T(8,128)(2,1)S(1)}, u32[]{:S(2)}, u32[]{:S(2)}) collective-permute-start(bf16[256,256]{0,1:T(8,128)(2,1)S(1)} %pad_maximum_fusion.13), channel_id=1, source_target_pairs={{0,8},{8,16},{16,24},{1,9},{9,17},{17,25},{2,10},{10,18},{18,26},{... | collective-permute-start | bytes 393224 | tf_op jit(solution)/shard_map/ppermute | solution.py:84
  86.5 4.5 %collective-permute-start.11 = (bf16[1024,64]{0,1:T(8,128)(2,1)S(1)}, bf16[1024,64]{0,1:T(8,128)(2,1)S(1)}, u32[]{:S(2)}, u32[]{:S(2)}) collective-permute-start(bf16[1024,64]{0,1:T(8,128)(2,1)S(1)} %get-tuple-element.26), channel_id=1, source_target_pairs={{0,1},{1,2},{2,3},{3,4},{4,5},{5,6},{6,7},{8,9},{9,10},{10,11},{11... | collective-permute-start | bytes 393224 | tf_op jit(solution)/shard_map/ppermute | solution.py:27
  91.0 1.3 collective-permute-start.12
  92.6 2.1 %collective-permute-done.11 = bf16[1024,64]{0,1:T(8,128)(2,1)S(1)} collective-permute-done((bf16[1024,64]{0,1:T(8,128)(2,1)S(1)}, bf16[1024,64]{0,1:T(8,128)(2,1)S(1)}, u32[]{:S(2)}, u32[]{:S(2)}) %collective-permute-start.11) | collective-permute-done | bytes 131104 | tf_op jit(solution)/shard_map/ppermute | solution.py:27
  94.8 4.3 %collective-permute-done.12 = bf16[1024,64]{0,1:T(8,128)(2,1)S(1)} collective-permute-done((bf16[1024,64]{0,1:T(8,128)(2,1)S(1)}, bf16[1024,64]{0,1:T(8,128)(2,1)S(1)}, u32[]{:S(2)}, u32[]{:S(2)}) %collective-permute-start.12) | collective-permute-done | bytes 131104 | tf_op jit(solution)/shard_map/ppermute | solution.py:28
  99.1 0.8 fusion.95
  100.0 0.7 fusion.35
  100.9 1.3 collective-permute-start.14
  102.2 3.0 %collective-permute-start.13 = (bf16[256,256]{0,1:T(8,128)(2,1)S(1)}, bf16[256,256]{0,1:T(8,128)(2,1)S(1)}, u32[]{:S(2)}, u32[]{:S(2)}) collective-permute-start(bf16[256,256]{0,1:T(8,128)(2,1)S(1)} %pad_maximum_fusion.15), channel_id=1, source_target_pairs={{0,8},{8,16},{16,24},{1,9},{9,17},{17,25},{2,10},{10,18},{18,26},{... | collective-permute-start | bytes 393224 | tf_op jit(solution)/shard_map/ppermute | solution.py:84
  105.3 4.5 %collective-permute-start.15 = (bf16[1024,64]{0,1:T(8,128)(2,1)S(1)}, bf16[1024,64]{0,1:T(8,128)(2,1)S(1)}, u32[]{:S(2)}, u32[]{:S(2)}) collective-permute-start(bf16[1024,64]{0,1:T(8,128)(2,1)S(1)} %get-tuple-element.20), channel_id=1, source_target_pairs={{0,1},{1,2},{2,3},{3,4},{4,5},{5,6},{6,7},{8,9},{9,10},{10,11},{11... | collective-permute-start | bytes 393224 | tf_op jit(solution)/shard_map/ppermute | solution.py:27
  109.8 1.3 collective-permute-start.16
  111.5 2.0 %collective-permute-done.15 = bf16[1024,64]{0,1:T(8,128)(2,1)S(1)} collective-permute-done((bf16[1024,64]{0,1:T(8,128)(2,1)S(1)}, bf16[1024,64]{0,1:T(8,128)(2,1)S(1)}, u32[]{:S(2)}, u32[]{:S(2)}) %collective-permute-start.15) | collective-permute-done | bytes 131104 | tf_op jit(solution)/shard_map/ppermute | solution.py:27
  113.5 4.4 %collective-permute-done.16 = bf16[1024,64]{0,1:T(8,128)(2,1)S(1)} collective-permute-done((bf16[1024,64]{0,1:T(8,128)(2,1)S(1)}, bf16[1024,64]{0,1:T(8,128)(2,1)S(1)}, u32[]{:S(2)}, u32[]{:S(2)}) %collective-permute-start.16) | collective-permute-done | bytes 131104 | tf_op jit(solution)/shard_map/ppermute | solution.py:28
  118.0 0.8 fusion.96
  118.9 0.7 fusion.33
  119.8 1.3 collective-permute-start.18
  121.1 3.0 %collective-permute-start.17 = (bf16[256,256]{0,1:T(8,128)(2,1)S(1)}, bf16[256,256]{0,1:T(8,128)(2,1)S(1)}, u32[]{:S(2)}, u32[]{:S(2)}) collective-permute-start(bf16[256,256]{0,1:T(8,128)(2,1)S(1)} %pad_maximum_fusion.17), channel_id=1, source_target_pairs={{0,8},{8,16},{16,24},{1,9},{9,17},{17,25},{2,10},{10,18},{18,26},{... | collective-permute-start | bytes 393224 | tf_op jit(solution)/shard_map/ppermute | solution.py:84
  124.2 4.0 %collective-permute-start.19 = (bf16[1024,64]{0,1:T(8,128)(2,1)S(1)}, bf16[1024,64]{0,1:T(8,128)(2,1)S(1)}, u32[]{:S(2)}, u32[]{:S(2)}) collective-permute-start(bf16[1024,64]{0,1:T(8,128)(2,1)S(1)} %get-tuple-element.14), channel_id=1, source_target_pairs={{0,1},{1,2},{2,3},{3,4},{4,5},{5,6},{6,7},{8,9},{9,10},{10,11},{11... | collective-permute-start | bytes 393224 | tf_op jit(solution)/shard_map/ppermute | solution.py:27
  128.1 1.3 collective-permute-start.20
  129.8 1.8 %collective-permute-done.19 = bf16[1024,64]{0,1:T(8,128)(2,1)S(1)} collective-permute-done((bf16[1024,64]{0,1:T(8,128)(2,1)S(1)}, bf16[1024,64]{0,1:T(8,128)(2,1)S(1)}, u32[]{:S(2)}, u32[]{:S(2)}) %collective-permute-start.19) | collective-permute-done | bytes 131104 | tf_op jit(solution)/shard_map/ppermute | solution.py:27
  131.6 4.7 %collective-permute-done.20 = bf16[1024,64]{0,1:T(8,128)(2,1)S(1)} collective-permute-done((bf16[1024,64]{0,1:T(8,128)(2,1)S(1)}, bf16[1024,64]{0,1:T(8,128)(2,1)S(1)}, u32[]{:S(2)}, u32[]{:S(2)}) %collective-permute-start.20) | collective-permute-done | bytes 131104 | tf_op jit(solution)/shard_map/ppermute | solution.py:28
  136.3 1.8 %fusion.97 = (bf16[1024,256]{0,1:T(8,128)(2,1)S(1)}, f32[1024,256]{0,1:T(8,128)}) fusion(f32[1024,256]{0,1:T(8,128)S(1)} %get-tuple-element.62, f32[1024,256]{0,1:T(8,128)S(1)} %get-tuple-element.39, f32[1024,256]{0,1:T(8,128)S(1)} %fusion.4, bf16[1024,64]{0,1:T(8,128)(2,1)S(1)} %collective-permute-done.20, bf16[1024,256]{0,1:T(8,128)(2,1)S(1)} %get-tuple-element.61, ...), kind=kOutput, calls=%fused_computation.194 | convolution fusion | flops 140247040 | bytes 7735296 | tf_op jit(solution)/shard_map/dot_general | solution.py:88
  138.2 1.7 %fusion.41 = f32[1024,256]{0,1:T(8,128)} fusion(bf16[1024,256]{0,1:T(8,128)(2,1)S(1)} %get-tuple-element.63, bf16[1024,1536]{1,0:T(8,128)(2,1)S(1)} %bitcast.61), kind=kOutput, calls=%fused_computation.70 | convolution fusion | flops 536870912 | bytes 3670016 | tf_op jit(solution)/shard_map/dot_general | solution.py:86
  140.6 1.3 collective-permute-start.22
  142.5 3.7 %collective-permute-start.21 = (bf16[256,256]{0,1:T(8,128)(2,1)}, bf16[256,256]{0,1:T(8,128)(2,1)}, u32[]{:S(2)}, u32[]{:S(2)}) collective-permute-start(bf16[256,256]{0,1:T(8,128)(2,1)} %pad_maximum_fusion.19), channel_id=1, source_target_pairs={{0,8},{8,16},{16,24},{1,9},{9,17},{17,25},{2,10},{10,18},{18,26},{... | collective-permute-start | bytes 393224 | tf_op jit(solution)/shard_map/ppermute | solution.py:84
  146.2 0.7 fusion.86
  146.9 3.9 %collective-permute-start.23 = (bf16[1024,64]{0,1:T(8,128)(2,1)}, bf16[1024,64]{0,1:T(8,128)(2,1)S(1)}, u32[]{:S(2)}, u32[]{:S(2)}) collective-permute-start(bf16[1024,64]{0,1:T(8,128)(2,1)} %get-tuple-element.12), channel_id=1, source_target_pairs={{0,1},{1,2},{2,3},{3,4},{4,5},{5,6},{6,7},{8,9},{9,10},{10,11},{11... | collective-permute-start | bytes 393224 | tf_op jit(solution)/shard_map/ppermute | solution.py:27
  150.8 1.3 collective-permute-start.24
  152.1 2.5 %copy.38 = f32[1024,256]{1,0:T(8,128)} copy(f32[1024,256]{0,1:T(8,128)} %get-tuple-element.64) | data formatting | bytes 2097152
  154.6 1.8 %convolution_add_fusion.1 = f32[1024,256]{0,1:T(8,128)S(1)} fusion(f32[1024,256]{0,1:T(8,128)} %fusion.41, bf16[256,256]{0,1:T(8,128)(2,1)} %collective-permute-done.21, bf16[1024,1536]{1,0:T(8,128)(2,1)} %bitcast.50), kind=kOutput, calls=%fused_computation.24 | convolution fusion | flops 134479872 | bytes 2752512 | tf_op jit(solution)/shard_map/dot_general | solution.py:87
  156.4 1.5 fusion.32
  157.9 0.8 collective-permute-done.24
  159.1 5.8 %psum.7 = f32[2,256]{1,0:T(2,128)S(1)} all-reduce(f32[2,256]{1,0:T(2,128)S(1)} %pad_maximum_fusion.21), channel_id=1, replica_groups=mesh['space'=4,'tm'=8] {'space'}, use_global_device_ids=true, to_apply=%region_4.5 | all-reduce | flops 512 | bytes 4096 | tf_op jit(solution)/shard_map/psum | solution.py:157
  (76 shorter events, 8.9 us)
Async XLA Ops:
  0.6 15.8 %copy-start = (bf16[8,8,128,128]{3,2,1,0:T(8,128)(2,1)S(1)}, bf16[8,8,128,128]{3,2,1,0:T(8,128)(2,1)}, u32[]{:S(2)}) copy-start(bf16[8,8,128,128]{3,2,1,0:T(8,128)(2,1)} %param.17) | copy-start | bytes 6291460
  0.6 15.7 %copy-start.6 = (s32[8,8]{1,0:T(8,128)S(1)}, s32[8,8]{1,0:T(8,128)}, u32[]{:S(2)}) copy-start(s32[8,8]{1,0:T(8,128)} %param.18) | copy-start | bytes 772
  0.7 32.4 %collective-permute-start.6 = (bf16[1024,256]{1,0:T(8,128)(2,1)}, bf16[1024,256]{1,0:T(8,128)(2,1)}, u32[]{:S(2)}, u32[]{:S(2)}) collective-permute-start(bf16[1024,256]{1,0:T(8,128)(2,1)} %param.23), channel_id=1, source_target_pairs={{0,8},{8,16},{16,24},{24,0},{1,9},{9,17},{17,25},{25,1},{2,10},{10... | collective-permute-start | bytes 1572872 | tf_op jit(solution)/shard_map/ppermute | solution.py:105
  1.2 38.2 %collective-permute-start.7 = (bf16[1024,256]{1,0:T(8,128)(2,1)}, bf16[1024,256]{1,0:T(8,128)(2,1)}, u32[]{:S(2)}, u32[]{:S(2)}) collective-permute-start(bf16[1024,256]{1,0:T(8,128)(2,1)} %param.23), channel_id=1, source_target_pairs={{0,16},{8,24},{16,0},{24,8},{1,17},{9,25},{17,1},{25,9},{2,18},{10... | collective-permute-start | bytes 1572872 | tf_op jit(solution)/shard_map/ppermute | solution.py:105
  3.8 37.1 %collective-permute-start.8 = (bf16[1024,256]{1,0:T(8,128)(2,1)}, bf16[1024,256]{1,0:T(8,128)(2,1)}, u32[]{:S(2)}, u32[]{:S(2)}) collective-permute-start(bf16[1024,256]{1,0:T(8,128)(2,1)} %param.23), channel_id=1, source_target_pairs={{0,24},{8,0},{16,8},{24,16},{1,25},{9,1},{17,9},{25,17},{2,26},{10... | collective-permute-start | bytes 1572872 | tf_op jit(solution)/shard_map/ppermute | solution.py:105
  6.0 17.8 %collective-permute-start = (s32[2]{0:T(128)S(1)}, s32[2]{0:T(128)S(1)}, u32[]{:S(2)}, u32[]{:S(2)}) collective-permute-start(s32[2]{0:T(128)S(1)} %get-tuple-element.54), channel_id=1, source_target_pairs={{8,0},{16,8},{24,16},{9,1},{17,9},{25,17},{10,2},{18,10},{26,18},{... | collective-permute-start | bytes 32 | tf_op jit(solution)/shard_map/ppermute | solution.py:74
  7.3 22.5 %collective-permute-start.2 = (s32[2]{0:T(128)S(1)}, s32[2]{0:T(128)S(1)}, u32[]{:S(2)}, u32[]{:S(2)}) collective-permute-start(s32[2]{0:T(128)S(1)} %get-tuple-element.53), channel_id=1, source_target_pairs={{0,8},{8,16},{16,24},{1,9},{9,17},{17,25},{2,10},{10,18},{18,26},{... | collective-permute-start | bytes 32 | tf_op jit(solution)/shard_map/ppermute | solution.py:75
  20.3 1.7 %copy-start.1 = (bf16[128,8,12,128]{3,1,2,0:T(8,128)(2,1)}, bf16[128,8,12,128]{3,1,2,0:T(8,128)(2,1)S(1)}, u32[]{:S(2)}) copy-start(bf16[128,8,12,128]{3,1,2,0:T(8,128)(2,1)S(1)} %copy.56) | copy-start | bytes 9437188
  20.3 3.4 %copy-start.4 = (s32[2048,1]{0,1:T(1,128)S(1)}, s32[2048,1]{0,1:T(1,128)}, u32[]{:S(2)}) copy-start(s32[2048,1]{0,1:T(1,128)} %param.21) | copy-start | bytes 24580
  20.3 3.5 %copy-start.5 = (s32[2048]{0:T(1024)S(1)}, s32[2048]{0:T(1024)}, u32[]{:S(2)}) copy-start(s32[2048]{0:T(1024)} %param.22) | copy-start | bytes 24580
  23.8 54.6 %collective-permute-start.4 = (bf16[1024,64]{0,1:T(8,128)(2,1)}, bf16[1024,64]{0,1:T(8,128)(2,1)}, u32[]{:S(2)}, u32[]{:S(2)}) collective-permute-start(bf16[1024,64]{0,1:T(8,128)(2,1)} %get-tuple-element.32), channel_id=1, source_target_pairs={{0,1},{1,2},{2,3},{3,4},{4,5},{5,6},{6,7},{8,9},{9,10},{10,11},{11... | collective-permute-start | bytes 393224 | tf_op jit(solution)/shard_map/ppermute | solution.py:27
  29.7 48.6 %collective-permute-start.5 = (bf16[1024,64]{0,1:T(8,128)(2,1)}, bf16[1024,64]{0,1:T(8,128)(2,1)}, u32[]{:S(2)}, u32[]{:S(2)}) collective-permute-start(bf16[1024,64]{0,1:T(8,128)(2,1)} %get-tuple-element.33), channel_id=1, source_target_pairs={{1,0},{2,1},{3,2},{4,3},{5,4},{6,5},{7,6},{9,8},{10,9},{11,10},{12... | collective-permute-start | bytes 393224 | tf_op jit(solution)/shard_map/ppermute | solution.py:28
  33.1 38.4 %collective-permute-start.1 = (bf16[256,256]{0,1:T(8,128)(2,1)S(1)}, bf16[256,256]{0,1:T(8,128)(2,1)}, u32[]{:S(2)}, u32[]{:S(2)}) collective-permute-start(bf16[256,256]{0,1:T(8,128)(2,1)S(1)} %pad_maximum_fusion.11), channel_id=1, source_target_pairs={{0,8},{8,16},{16,24},{1,9},{9,17},{17,25},{2,10},{10,18},{18,26},{... | collective-permute-start | bytes 393224 | tf_op jit(solution)/shard_map/ppermute | solution.py:84
  39.4 39.0 %collective-permute-start.3 = (bf16[256,256]{0,1:T(8,128)(2,1)S(1)}, bf16[256,256]{0,1:T(8,128)(2,1)}, u32[]{:S(2)}, u32[]{:S(2)}) collective-permute-start(bf16[256,256]{0,1:T(8,128)(2,1)S(1)} %pad_maximum_fusion.12), channel_id=1, source_target_pairs={{8,0},{16,8},{24,16},{9,1},{17,9},{25,17},{10,2},{18,10},{26,18},{... | collective-permute-start | bytes 393224 | tf_op jit(solution)/shard_map/ppermute | solution.py:85
  64.1 13.9 %copy-start.3 = (f32[1024]{0:T(1024)S(1)}, f32[1024]{0:T(1024)}, u32[]{:S(2)}) copy-start(f32[1024]{0:T(1024)} %param.13) | copy-start | bytes 12292
  68.0 7.4 %all-to-all-start = ((f32[4,1,4096]{2,1,0:T(1,128)}), f32[4,1,4096]{2,1,0:T(1,128)S(1)}, u32[]{:S(2)}, u32[]{:S(2)}) async-start(f32[4,1,4096]{2,1,0:T(1,128)} %all_to_all.8), calls=%async_computation | async-start | bytes 131072 | tf_op jit(solution)/shard_map/all_to_all | solution.py:131
  78.4 2.8 %copy-start.2 = (bf16[128,8,12,128]{3,1,2,0:T(8,128)(2,1)S(1)}, bf16[128,8,12,128]{3,1,2,0:T(8,128)(2,1)}, u32[]{:S(2)}) copy-start(bf16[128,8,12,128]{3,1,2,0:T(8,128)(2,1)} %copy-done.1) | copy-start | bytes 9437188
  82.1 10.5 %collective-permute-start.10 = (bf16[256,256]{0,1:T(8,128)(2,1)S(1)}, bf16[256,256]{0,1:T(8,128)(2,1)S(1)}, u32[]{:S(2)}, u32[]{:S(2)}) collective-permute-start(bf16[256,256]{0,1:T(8,128)(2,1)S(1)} %pad_maximum_fusion.14), channel_id=1, source_target_pairs={{8,0},{16,8},{24,16},{9,1},{17,9},{25,17},{10,2},{18,10},{26,18},{... | collective-permute-start | bytes 393224 | tf_op jit(solution)/shard_map/ppermute | solution.py:85
  83.4 8.9 %collective-permute-start.9 = (bf16[256,256]{0,1:T(8,128)(2,1)S(1)}, bf16[256,256]{0,1:T(8,128)(2,1)S(1)}, u32[]{:S(2)}, u32[]{:S(2)}) collective-permute-start(bf16[256,256]{0,1:T(8,128)(2,1)S(1)} %pad_maximum_fusion.13), channel_id=1, source_target_pairs={{0,8},{8,16},{16,24},{1,9},{9,17},{17,25},{2,10},{10,18},{18,26},{... | collective-permute-start | bytes 393224 | tf_op jit(solution)/shard_map/ppermute | solution.py:84
  86.5 8.3 %collective-permute-start.11 = (bf16[1024,64]{0,1:T(8,128)(2,1)S(1)}, bf16[1024,64]{0,1:T(8,128)(2,1)S(1)}, u32[]{:S(2)}, u32[]{:S(2)}) collective-permute-start(bf16[1024,64]{0,1:T(8,128)(2,1)S(1)} %get-tuple-element.26), channel_id=1, source_target_pairs={{0,1},{1,2},{2,3},{3,4},{4,5},{5,6},{6,7},{8,9},{9,10},{10,11},{11... | collective-permute-start | bytes 393224 | tf_op jit(solution)/shard_map/ppermute | solution.py:27
  91.0 8.1 %collective-permute-start.12 = (bf16[1024,64]{0,1:T(8,128)(2,1)S(1)}, bf16[1024,64]{0,1:T(8,128)(2,1)S(1)}, u32[]{:S(2)}, u32[]{:S(2)}) collective-permute-start(bf16[1024,64]{0,1:T(8,128)(2,1)S(1)} %get-tuple-element.27), channel_id=1, source_target_pairs={{1,0},{2,1},{3,2},{4,3},{5,4},{6,5},{7,6},{9,8},{10,9},{11,10},{12... | collective-permute-start | bytes 393224 | tf_op jit(solution)/shard_map/ppermute | solution.py:28
  100.9 10.6 %collective-permute-start.14 = (bf16[256,256]{0,1:T(8,128)(2,1)S(1)}, bf16[256,256]{0,1:T(8,128)(2,1)S(1)}, u32[]{:S(2)}, u32[]{:S(2)}) collective-permute-start(bf16[256,256]{0,1:T(8,128)(2,1)S(1)} %pad_maximum_fusion.16), channel_id=1, source_target_pairs={{8,0},{16,8},{24,16},{9,1},{17,9},{25,17},{10,2},{18,10},{26,18},{... | collective-permute-start | bytes 393224 | tf_op jit(solution)/shard_map/ppermute | solution.py:85
  102.2 8.9 %collective-permute-start.13 = (bf16[256,256]{0,1:T(8,128)(2,1)S(1)}, bf16[256,256]{0,1:T(8,128)(2,1)S(1)}, u32[]{:S(2)}, u32[]{:S(2)}) collective-permute-start(bf16[256,256]{0,1:T(8,128)(2,1)S(1)} %pad_maximum_fusion.15), channel_id=1, source_target_pairs={{0,8},{8,16},{16,24},{1,9},{9,17},{17,25},{2,10},{10,18},{18,26},{... | collective-permute-start | bytes 393224 | tf_op jit(solution)/shard_map/ppermute | solution.py:84
  105.3 8.3 %collective-permute-start.15 = (bf16[1024,64]{0,1:T(8,128)(2,1)S(1)}, bf16[1024,64]{0,1:T(8,128)(2,1)S(1)}, u32[]{:S(2)}, u32[]{:S(2)}) collective-permute-start(bf16[1024,64]{0,1:T(8,128)(2,1)S(1)} %get-tuple-element.20), channel_id=1, source_target_pairs={{0,1},{1,2},{2,3},{3,4},{4,5},{5,6},{6,7},{8,9},{9,10},{10,11},{11... | collective-permute-start | bytes 393224 | tf_op jit(solution)/shard_map/ppermute | solution.py:27
  109.8 8.1 %collective-permute-start.16 = (bf16[1024,64]{0,1:T(8,128)(2,1)S(1)}, bf16[1024,64]{0,1:T(8,128)(2,1)S(1)}, u32[]{:S(2)}, u32[]{:S(2)}) collective-permute-start(bf16[1024,64]{0,1:T(8,128)(2,1)S(1)} %get-tuple-element.21), channel_id=1, source_target_pairs={{1,0},{2,1},{3,2},{4,3},{5,4},{6,5},{7,6},{9,8},{10,9},{11,10},{12... | collective-permute-start | bytes 393224 | tf_op jit(solution)/shard_map/ppermute | solution.py:28
  119.8 10.0 %collective-permute-start.18 = (bf16[256,256]{0,1:T(8,128)(2,1)S(1)}, bf16[256,256]{0,1:T(8,128)(2,1)S(1)}, u32[]{:S(2)}, u32[]{:S(2)}) collective-permute-start(bf16[256,256]{0,1:T(8,128)(2,1)S(1)} %pad_maximum_fusion.18), channel_id=1, source_target_pairs={{8,0},{16,8},{24,16},{9,1},{17,9},{25,17},{10,2},{18,10},{26,18},{... | collective-permute-start | bytes 393224 | tf_op jit(solution)/shard_map/ppermute | solution.py:85
  121.1 8.3 %collective-permute-start.17 = (bf16[256,256]{0,1:T(8,128)(2,1)S(1)}, bf16[256,256]{0,1:T(8,128)(2,1)S(1)}, u32[]{:S(2)}, u32[]{:S(2)}) collective-permute-start(bf16[256,256]{0,1:T(8,128)(2,1)S(1)} %pad_maximum_fusion.17), channel_id=1, source_target_pairs={{0,8},{8,16},{16,24},{1,9},{9,17},{17,25},{2,10},{10,18},{18,26},{... | collective-permute-start | bytes 393224 | tf_op jit(solution)/shard_map/ppermute | solution.py:84
  124.2 7.5 %collective-permute-start.19 = (bf16[1024,64]{0,1:T(8,128)(2,1)S(1)}, bf16[1024,64]{0,1:T(8,128)(2,1)S(1)}, u32[]{:S(2)}, u32[]{:S(2)}) collective-permute-start(bf16[1024,64]{0,1:T(8,128)(2,1)S(1)} %get-tuple-element.14), channel_id=1, source_target_pairs={{0,1},{1,2},{2,3},{3,4},{4,5},{5,6},{6,7},{8,9},{9,10},{10,11},{11... | collective-permute-start | bytes 393224 | tf_op jit(solution)/shard_map/ppermute | solution.py:27
  128.1 8.2 %collective-permute-start.20 = (bf16[1024,64]{0,1:T(8,128)(2,1)S(1)}, bf16[1024,64]{0,1:T(8,128)(2,1)S(1)}, u32[]{:S(2)}, u32[]{:S(2)}) collective-permute-start(bf16[1024,64]{0,1:T(8,128)(2,1)S(1)} %get-tuple-element.15), channel_id=1, source_target_pairs={{1,0},{2,1},{3,2},{4,3},{5,4},{6,5},{7,6},{9,8},{10,9},{11,10},{12... | collective-permute-start | bytes 393224 | tf_op jit(solution)/shard_map/ppermute | solution.py:28
  140.6 15.9 %collective-permute-start.22 = (bf16[256,256]{0,1:T(8,128)(2,1)}, bf16[256,256]{0,1:T(8,128)(2,1)S(1)}, u32[]{:S(2)}, u32[]{:S(2)}) collective-permute-start(bf16[256,256]{0,1:T(8,128)(2,1)} %pad_maximum_fusion.20), channel_id=1, source_target_pairs={{8,0},{16,8},{24,16},{9,1},{17,9},{25,17},{10,2},{18,10},{26,18},{... | collective-permute-start | bytes 393224 | tf_op jit(solution)/shard_map/ppermute | solution.py:85
  142.5 12.1 %collective-permute-start.21 = (bf16[256,256]{0,1:T(8,128)(2,1)}, bf16[256,256]{0,1:T(8,128)(2,1)}, u32[]{:S(2)}, u32[]{:S(2)}) collective-permute-start(bf16[256,256]{0,1:T(8,128)(2,1)} %pad_maximum_fusion.19), channel_id=1, source_target_pairs={{0,8},{8,16},{16,24},{1,9},{9,17},{17,25},{2,10},{10,18},{18,26},{... | collective-permute-start | bytes 393224 | tf_op jit(solution)/shard_map/ppermute | solution.py:84
  146.9 11.0 %collective-permute-start.23 = (bf16[1024,64]{0,1:T(8,128)(2,1)}, bf16[1024,64]{0,1:T(8,128)(2,1)S(1)}, u32[]{:S(2)}, u32[]{:S(2)}) collective-permute-start(bf16[1024,64]{0,1:T(8,128)(2,1)} %get-tuple-element.12), channel_id=1, source_target_pairs={{0,1},{1,2},{2,3},{3,4},{4,5},{5,6},{6,7},{8,9},{9,10},{10,11},{11... | collective-permute-start | bytes 393224 | tf_op jit(solution)/shard_map/ppermute | solution.py:27
  150.8 7.9 %collective-permute-start.24 = (bf16[1024,64]{0,1:T(8,128)(2,1)}, bf16[1024,64]{0,1:T(8,128)(2,1)S(1)}, u32[]{:S(2)}, u32[]{:S(2)}) collective-permute-start(bf16[1024,64]{0,1:T(8,128)(2,1)} %get-tuple-element.13), channel_id=1, source_target_pairs={{1,0},{2,1},{3,2},{4,3},{5,4},{6,5},{7,6},{9,8},{10,9},{11,10},{12... | collective-permute-start | bytes 393224 | tf_op jit(solution)/shard_map/ppermute | solution.py:28

commit v8 on v7

--- a/solution.py
+++ b/solution.py
@@ -122,15 +122,14 @@
         [jnp.where(in_step, piece[:, None], 0.0) for piece in (high, middle, low)], axis=1
     ).astype(jnp.bfloat16)
     sums = lax.dot_general(
-        onehot, parts, (((0,), (0,)), ((), ())), preferred_element_type=jnp.float32
+        parts, onehot, (((0,), (0,)), ((), ())), preferred_element_type=jnp.float32
     )
-    local_counts = (sums[:, :T_DEV] + sums[:, T_DEV : 2 * T_DEV] + sums[:, 2 * T_DEV :]).reshape(
-        space_count, nodes_dev * T_DEV
-    )
+    step_counts = sums[:T_DEV] + sums[T_DEV : 2 * T_DEV] + sums[2 * T_DEV :]
+    local_counts = step_counts.reshape(T_DEV, space_count, nodes_dev).transpose(1, 0, 2)
     counted = jnp.sum(
         lax.all_to_all(local_counts, "space", split_axis=0, concat_axis=0, tiled=True), axis=0
     )
-    obs_diag = jnp.repeat(counted.reshape(NODES_DEV, T_DEV), PROBES, axis=1)
+    obs_diag = jnp.repeat(counted, PROBES, axis=0).T
     full_diag = base_diag + obs_diag
     local_diag = kappa[:, None] + obs_diag
     applied = (

time: 167 us -> 159 us (0.952)
  local copies, waits for them, and re-layouts: 30.7 us -> 22.2 us
    all_to_all x1 -> x0, local copies, waits for them, and re-layouts: 3.93 us -> none  [shards(): lax.all_to_all(local_counts, 'space', split_axis=0, concat_axis=0, tiled=...]
    reshape x2 -> x0, local copies, waits for them, and re-layouts: 2.56 us -> none  [shards(): obs_diag = jnp.repeat(counted.reshape(NODES_DEV, T_DEV), PROBES, axis=1)]
    add x1 -> x0, local copies, waits for them, and re-layouts: 1.99 us -> none  [shards(): sums[:, :T_DEV] + sums[:, T_DEV:2 * T_DEV] + sums[:, 2 * T_DEV:]]
  transfers between devices with their start and end apart: 26 -> 26, of which waited for: 8 -> 8; matrix products, arithmetic and copies ran while one was open for 31% -> 30% of each run, Pallas kernels for 0% -> 0%
where the time goes in v8:
time: 159 us; the launch traced here: 158 us
  starting transfers between devices  65.1 us (41%)
  matrix products  27 us (17%)
  local copies, waits for them, and re-layouts  22.2 us (14%)
  waiting for transfers between devices  21.5 us (14%)
  other arithmetic  12 us (8%)
  blocking collectives  5.76 us (4%)
  between operations  3.95 us (2%)
    ppermute x5, starting transfers between devices, with_halo(): before = lax.ppermute(last, axis, up)  20.8 us
    ppermute x5, starting transfers between devices, spatial(): lower = lax.ppermute(pick_blocks(field, upper_wants), 'space', up)  19.1 us
    ppermute x5, waiting for transfers between devices, with_halo(): after = lax.ppermute(initial, axis, down)  14.3 us
    gather x1, local copies, waits for them, and re-layouts, shards(): coef_rows = svc_all[shift * nodes_dev + obs_cell // T_DEV]  10.4 us
    dot_general x5, matrix products, spatial(): jnp.dot(upper.T, upper_t, preferred_element_type=jnp.float32)  7.56 us
    ppermute x5, starting transfers between devices, spatial(): upper = lax.ppermute(pick_blocks(field, lower_wants), 'space', down)  6.62 us
    ppermute x5, starting transfers between devices, with_halo(): after = lax.ppermute(initial, axis, down)  6.46 us
    unnamed x17, local copies, waits for them, and re-layouts  6.38 us
  transfers between devices with their start and end apart: 26, of which 8 were waited for; matrix products, arithmetic and copies ran while one was open for 30% of the time, Pallas kernels for 0%

profile of v8, /device:TPU:0, one launch (start us, length us, event | category | flops | bytes accessed | tf_op | source)
XLA Modules:
  0.0 157.5 jit_solution(4701668646418600024)
XLA Ops:
  1.2 2.6 %collective-permute-start.7 = (bf16[1024,256]{1,0:T(8,128)(2,1)}, bf16[1024,256]{1,0:T(8,128)(2,1)}, u32[]{:S(2)}, u32[]{:S(2)}) collective-permute-start(bf16[1024,256]{1,0:T(8,128)(2,1)} %param.23), channel_id=1, source_target_pairs={{0,16},{8,24},{16,0},{24,8},{1,17},{9,25},{17,1},{25,9},{2,18},{10... | collective-permute-start | bytes 1572872 | tf_op jit(solution)/shard_map/ppermute | solution.py:105
  3.8 1.4 collective-permute-start.8
  5.2 0.8 fusion.92
  6.0 1.3 collective-permute-start
  7.3 3.0 %collective-permute-start.2 = (s32[2]{0:T(128)S(1)}, s32[2]{0:T(128)S(1)}, u32[]{:S(2)}, u32[]{:S(2)}) collective-permute-start(s32[2]{0:T(128)S(1)} %get-tuple-element.53), channel_id=1, source_target_pairs={{0,8},{8,16},{16,24},{1,9},{9,17},{17,25},{2,10},{10,18},{18,26},{... | collective-permute-start | bytes 32 | tf_op jit(solution)/shard_map/ppermute | solution.py:75
  10.3 1.2 copy.27
  11.6 0.7 broadcast_in_dim.67
  12.4 0.7 broadcast_in_dim.64
  13.2 1.0 convert_element_type.83
  14.2 1.1 select_reduce_fusion
  15.3 1.1 fusion.57
  16.4 2.2 %add_convert_fusion = bf16[8,12,128,128]{3,1,2,0:T(8,128)(2,1)S(1)} fusion(f32[8,128,128]{2,1,0:T(8,128)S(1)} %convert_element_type.83, f32[8,12]{1,0:T(8,128)S(1)} %fusion.82, bf16[8,8,128,128]{3,2,1,0:T(8,128)(2,1)S(1)} %copy-done, s32[8,8]{1,0:T(8,128)S(1)} %copy-done.6), kind=kOutput, calls=%fused_computation.4 | convolution fusion | flops 29885184 | bytes 5767808 | tf_op jit(solution)/shard_map/bkm,bkij->bimj/dot_general | solution.py:63
  18.7 1.6 %copy.52 = bf16[128,8,12,128]{3,1,2,0:T(8,128)(2,1)S(1)} copy(bf16[128,8,12,128]{3,2,1,0:T(8,128)(2,1)S(1)} %bitcast.51) | data formatting | bytes 6291456
  20.3 0.7 fusion.90
  21.0 1.0 copy-done.1
  22.0 1.7 %fusion.39 = f32[1024,256]{0,1:T(8,128)} fusion(bf16[1024,256]{0,1:T(8,128)(2,1)S(1)} %fusion.57, bf16[1024,1536]{1,0:T(8,128)(2,1)S(1)} %bitcast.52), kind=kOutput, calls=%fused_computation.68 | convolution fusion | flops 536870912 | bytes 3670016 | tf_op jit(solution)/shard_map/dot_general | solution.py:86
  23.8 4.1 %collective-permute-start.4 = (bf16[1024,64]{0,1:T(8,128)(2,1)}, bf16[1024,64]{0,1:T(8,128)(2,1)}, u32[]{:S(2)}, u32[]{:S(2)}) collective-permute-start(bf16[1024,64]{0,1:T(8,128)(2,1)} %get-tuple-element.32), channel_id=1, source_target_pairs={{0,1},{1,2},{2,3},{3,4},{4,5},{5,6},{6,7},{8,9},{9,10},{10,11},{11... | collective-permute-start | bytes 393224 | tf_op jit(solution)/shard_map/ppermute | solution.py:27
  29.7 1.3 collective-permute-start.5
  33.1 6.3 %collective-permute-start.1 = (bf16[256,256]{0,1:T(8,128)(2,1)S(1)}, bf16[256,256]{0,1:T(8,128)(2,1)}, u32[]{:S(2)}, u32[]{:S(2)}) collective-permute-start(bf16[256,256]{0,1:T(8,128)(2,1)S(1)} %pad_maximum_fusion.11), channel_id=1, source_target_pairs={{0,8},{8,16},{16,24},{1,9},{9,17},{17,25},{2,10},{10,18},{18,26},{... | collective-permute-start | bytes 393224 | tf_op jit(solution)/shard_map/ppermute | solution.py:84
  39.4 1.5 collective-permute-start.3
  40.8 3.0 %pad_maximum_fusion = bf16[4096,256]{1,0:T(8,128)(2,1)} fusion(bf16[1024,256]{1,0:T(8,128)(2,1)} %collective-permute-done.8, bf16[1024,256]{1,0:T(8,128)(2,1)} %collective-permute-done.7, bf16[1024,256]{1,0:T(8,128)(2,1)} %collective-permute-done.6, bf16[1024,256]{1,0:T(8,128)(2,1)} %param.23), kind=kLoop, calls=%fused_computation.13 | loop fusion | flops 8388608 | bytes 4194304 | tf_op jit(solution)/shard_map/concatenate | solution.py:108
  43.8 10.4 %gather_fusion = bf16[2048,256]{1,0:T(8,128)(2,1)} fusion(bf16[4096,256]{1,0:T(8,128)(2,1)} %pad_maximum_fusion, s32[2048]{0:T(1024)S(1)} %get-tuple-element.48), kind=kCustom, calls=%fused_computation | custom fusion | bytes 2105344 | tf_op jit(solution)/shard_map/gather | solution.py:111
  54.2 1.9 %fusion.2 = f32[2048]{0:T(1024)S(1)} fusion(bf16[2048,256]{1,0:T(8,128)(2,1)} %gather_fusion, bf16[2048,256]{1,0:T(8,128)(2,1)} %param.20), kind=kLoop, calls=%fused_computation.15 | loop fusion | flops 2095104 | bytes 2105344 | tf_op jit(solution)/shard_map/rc,rc->r/dot_general | solution.py:112
  56.1 6.0 %fusion = f32[12,4096]{1,0:T(8,128)S(1)} fusion(s32[2048]{0:T(1024)S(1)} %get-tuple-element.47, bf16[2048,4]{0,1:T(4,128)(2,1)S(1)} %get-tuple-element.41, bf16[2048,4]{0,1:T(4,128)(2,1)S(1)} %get-tuple-element.42, bf16[2048,4]{0,1:T(4,128)(2,1)S(1)} %get-tuple-element.40), kind=kOutput, calls=%fused_computation.2 | convolution fusion | flops 209862656 | bytes 253952 | tf_op jit(solution)/shard_map/dot_general | solution.py:124
  62.8 3.3 %all-to-all-start = ((f32[4,4,1024]{2,1,0:T(4,128)}), f32[4,4,1024]{2,1,0:T(4,128)S(1)}, u32[]{:S(2)}, u32[]{:S(2)}) async-start(f32[4,4,1024]{2,1,0:T(4,128)} %bitcast.11), calls=%async_computation | async-start | bytes 131072 | tf_op jit(solution)/shard_map/all_to_all | solution.py:130
  66.1 2.7 %convolution_add_fusion.9 = f32[1024,256]{0,1:T(8,128)} fusion(f32[1024,256]{0,1:T(8,128)} %fusion.39, bf16[256,256]{0,1:T(8,128)(2,1)} %collective-permute-done.1, bf16[1024,1536]{1,0:T(8,128)(2,1)} %bitcast.53), kind=kOutput, calls=%fused_computation.44 | convolution fusion | flops 134479872 | bytes 2752512 | tf_op jit(solution)/shard_map/dot_general | solution.py:87
  68.8 1.3 all-to-all-done
  70.6 2.7 %fusion.94 = (bf16[1024,256]{0,1:T(8,128)(2,1)S(1)}, f32[1024,256]{0,1:T(8,128)S(1)}) fusion(f32[1024,256]{0,1:T(8,128)S(1)} %get-tuple-element.39, f32[1024,256]{0,1:T(8,128)S(1)} %get-tuple-element.38, bf16[1024,64]{0,1:T(8,128)(2,1)} %collective-permute-done.5, bf16[1024,256]{0,1:T(8,128)(2,1)S(1)} %fusion.57, ...), kind=kOutput, calls=%fused_computation.191 | convolution fusion | flops 141557760 | bytes 6695936 | tf_op jit(solution)/shard_map/dot_general | solution.py:88
  73.4 0.7 fusion.37
  74.3 1.3 collective-permute-start.10
  75.6 3.0 %collective-permute-start.9 = (bf16[256,256]{0,1:T(8,128)(2,1)S(1)}, bf16[256,256]{0,1:T(8,128)(2,1)S(1)}, u32[]{:S(2)}, u32[]{:S(2)}) collective-permute-start(bf16[256,256]{0,1:T(8,128)(2,1)S(1)} %pad_maximum_fusion.13), channel_id=1, source_target_pairs={{0,8},{8,16},{16,24},{1,9},{9,17},{17,25},{2,10},{10,18},{18,26},{... | collective-permute-start | bytes 393224 | tf_op jit(solution)/shard_map/ppermute | solution.py:84
  78.7 4.3 %collective-permute-start.11 = (bf16[1024,64]{0,1:T(8,128)(2,1)S(1)}, bf16[1024,64]{0,1:T(8,128)(2,1)S(1)}, u32[]{:S(2)}, u32[]{:S(2)}) collective-permute-start(bf16[1024,64]{0,1:T(8,128)(2,1)S(1)} %get-tuple-element.26), channel_id=1, source_target_pairs={{0,1},{1,2},{2,3},{3,4},{4,5},{5,6},{6,7},{8,9},{9,10},{10,11},{11... | collective-permute-start | bytes 393224 | tf_op jit(solution)/shard_map/ppermute | solution.py:27
  83.0 1.3 collective-permute-start.12
  84.6 2.2 %collective-permute-done.11 = bf16[1024,64]{0,1:T(8,128)(2,1)S(1)} collective-permute-done((bf16[1024,64]{0,1:T(8,128)(2,1)S(1)}, bf16[1024,64]{0,1:T(8,128)(2,1)S(1)}, u32[]{:S(2)}, u32[]{:S(2)}) %collective-permute-start.11) | collective-permute-done | bytes 131104 | tf_op jit(solution)/shard_map/ppermute | solution.py:27
  86.8 4.3 %collective-permute-done.12 = bf16[1024,64]{0,1:T(8,128)(2,1)S(1)} collective-permute-done((bf16[1024,64]{0,1:T(8,128)(2,1)S(1)}, bf16[1024,64]{0,1:T(8,128)(2,1)S(1)}, u32[]{:S(2)}, u32[]{:S(2)}) %collective-permute-start.12) | collective-permute-done | bytes 131104 | tf_op jit(solution)/shard_map/ppermute | solution.py:28
  91.1 0.8 fusion.95
  92.0 0.7 fusion.35
  92.9 1.3 collective-permute-start.14
  94.2 3.0 %collective-permute-start.13 = (bf16[256,256]{0,1:T(8,128)(2,1)S(1)}, bf16[256,256]{0,1:T(8,128)(2,1)S(1)}, u32[]{:S(2)}, u32[]{:S(2)}) collective-permute-start(bf16[256,256]{0,1:T(8,128)(2,1)S(1)} %pad_maximum_fusion.15), channel_id=1, source_target_pairs={{0,8},{8,16},{16,24},{1,9},{9,17},{17,25},{2,10},{10,18},{18,26},{... | collective-permute-start | bytes 393224 | tf_op jit(solution)/shard_map/ppermute | solution.py:84
  97.3 4.8 %collective-permute-start.15 = (bf16[1024,64]{0,1:T(8,128)(2,1)S(1)}, bf16[1024,64]{0,1:T(8,128)(2,1)S(1)}, u32[]{:S(2)}, u32[]{:S(2)}) collective-permute-start(bf16[1024,64]{0,1:T(8,128)(2,1)S(1)} %get-tuple-element.20), channel_id=1, source_target_pairs={{0,1},{1,2},{2,3},{3,4},{4,5},{5,6},{6,7},{8,9},{9,10},{10,11},{11... | collective-permute-start | bytes 393224 | tf_op jit(solution)/shard_map/ppermute | solution.py:27
  102.0 1.3 collective-permute-start.16
  103.7 1.8 %collective-permute-done.15 = bf16[1024,64]{0,1:T(8,128)(2,1)S(1)} collective-permute-done((bf16[1024,64]{0,1:T(8,128)(2,1)S(1)}, bf16[1024,64]{0,1:T(8,128)(2,1)S(1)}, u32[]{:S(2)}, u32[]{:S(2)}) %collective-permute-start.15) | collective-permute-done | bytes 131104 | tf_op jit(solution)/shard_map/ppermute | solution.py:27
  105.5 4.6 %collective-permute-done.16 = bf16[1024,64]{0,1:T(8,128)(2,1)S(1)} collective-permute-done((bf16[1024,64]{0,1:T(8,128)(2,1)S(1)}, bf16[1024,64]{0,1:T(8,128)(2,1)S(1)}, u32[]{:S(2)}, u32[]{:S(2)}) %collective-permute-start.16) | collective-permute-done | bytes 131104 | tf_op jit(solution)/shard_map/ppermute | solution.py:28
  110.1 0.8 fusion.96
  111.0 0.7 fusion.33
  111.9 1.3 collective-permute-start.18
  113.3 3.0 %collective-permute-start.17 = (bf16[256,256]{0,1:T(8,128)(2,1)S(1)}, bf16[256,256]{0,1:T(8,128)(2,1)S(1)}, u32[]{:S(2)}, u32[]{:S(2)}) collective-permute-start(bf16[256,256]{0,1:T(8,128)(2,1)S(1)} %pad_maximum_fusion.17), channel_id=1, source_target_pairs={{0,8},{8,16},{16,24},{1,9},{9,17},{17,25},{2,10},{10,18},{18,26},{... | collective-permute-start | bytes 393224 | tf_op jit(solution)/shard_map/ppermute | solution.py:84
  116.3 4.0 %collective-permute-start.19 = (bf16[1024,64]{0,1:T(8,128)(2,1)S(1)}, bf16[1024,64]{0,1:T(8,128)(2,1)S(1)}, u32[]{:S(2)}, u32[]{:S(2)}) collective-permute-start(bf16[1024,64]{0,1:T(8,128)(2,1)S(1)} %get-tuple-element.14), channel_id=1, source_target_pairs={{0,1},{1,2},{2,3},{3,4},{4,5},{5,6},{6,7},{8,9},{9,10},{10,11},{11... | collective-permute-start | bytes 393224 | tf_op jit(solution)/shard_map/ppermute | solution.py:27
  120.3 1.3 collective-permute-start.20
  122.0 1.8 %collective-permute-done.19 = bf16[1024,64]{0,1:T(8,128)(2,1)S(1)} collective-permute-done((bf16[1024,64]{0,1:T(8,128)(2,1)S(1)}, bf16[1024,64]{0,1:T(8,128)(2,1)S(1)}, u32[]{:S(2)}, u32[]{:S(2)}) %collective-permute-start.19) | collective-permute-done | bytes 131104 | tf_op jit(solution)/shard_map/ppermute | solution.py:27
  123.8 4.7 %collective-permute-done.20 = bf16[1024,64]{0,1:T(8,128)(2,1)S(1)} collective-permute-done((bf16[1024,64]{0,1:T(8,128)(2,1)S(1)}, bf16[1024,64]{0,1:T(8,128)(2,1)S(1)}, u32[]{:S(2)}, u32[]{:S(2)}) %collective-permute-start.20) | collective-permute-done | bytes 131104 | tf_op jit(solution)/shard_map/ppermute | solution.py:28
  128.5 1.8 %fusion.97 = (bf16[1024,256]{0,1:T(8,128)(2,1)S(1)}, f32[1024,256]{0,1:T(8,128)}) fusion(f32[1024,256]{0,1:T(8,128)S(1)} %get-tuple-element.62, f32[1024,256]{0,1:T(8,128)S(1)} %get-tuple-element.39, f32[1024,256]{0,1:T(8,128)S(1)} %fusion.4, bf16[1024,64]{0,1:T(8,128)(2,1)S(1)} %collective-permute-done.20, bf16[1024,256]{0,1:T(8,128)(2,1)S(1)} %get-tuple-element.61, ...), kind=kOutput, calls=%fused_computation.194 | convolution fusion | flops 140247040 | bytes 7735296 | tf_op jit(solution)/shard_map/dot_general | solution.py:88
  130.4 1.7 %fusion.41 = f32[1024,256]{0,1:T(8,128)} fusion(bf16[1024,256]{0,1:T(8,128)(2,1)S(1)} %get-tuple-element.63, bf16[1024,1536]{1,0:T(8,128)(2,1)S(1)} %bitcast.66), kind=kOutput, calls=%fused_computation.70 | convolution fusion | flops 536870912 | bytes 3670016 | tf_op jit(solution)/shard_map/dot_general | solution.py:86
  132.1 0.7 pad_maximum_fusion.20
  132.8 1.3 collective-permute-start.22
  134.7 3.7 %collective-permute-start.21 = (bf16[256,256]{0,1:T(8,128)(2,1)}, bf16[256,256]{0,1:T(8,128)(2,1)}, u32[]{:S(2)}, u32[]{:S(2)}) collective-permute-start(bf16[256,256]{0,1:T(8,128)(2,1)} %pad_maximum_fusion.19), channel_id=1, source_target_pairs={{0,8},{8,16},{16,24},{1,9},{9,17},{17,25},{2,10},{10,18},{18,26},{... | collective-permute-start | bytes 393224 | tf_op jit(solution)/shard_map/ppermute | solution.py:84
  138.4 0.7 fusion.86
  139.1 3.8 %collective-permute-start.23 = (bf16[1024,64]{0,1:T(8,128)(2,1)}, bf16[1024,64]{0,1:T(8,128)(2,1)S(1)}, u32[]{:S(2)}, u32[]{:S(2)}) collective-permute-start(bf16[1024,64]{0,1:T(8,128)(2,1)} %get-tuple-element.12), channel_id=1, source_target_pairs={{0,1},{1,2},{2,3},{3,4},{4,5},{5,6},{6,7},{8,9},{9,10},{10,11},{11... | collective-permute-start | bytes 393224 | tf_op jit(solution)/shard_map/ppermute | solution.py:27
  142.9 1.3 collective-permute-start.24
  144.2 2.5 %copy.34 = f32[1024,256]{1,0:T(8,128)} copy(f32[1024,256]{0,1:T(8,128)} %get-tuple-element.64) | data formatting | bytes 2097152
  146.8 1.8 %convolution_add_fusion.1 = f32[1024,256]{0,1:T(8,128)S(1)} fusion(f32[1024,256]{0,1:T(8,128)} %fusion.41, bf16[256,256]{0,1:T(8,128)(2,1)} %collective-permute-done.21, bf16[1024,1536]{1,0:T(8,128)(2,1)} %bitcast.55), kind=kOutput, calls=%fused_computation.24 | convolution fusion | flops 134479872 | bytes 2752512 | tf_op jit(solution)/shard_map/dot_general | solution.py:87
  148.5 1.5 fusion.32
  150.0 0.8 collective-permute-done.24
  151.2 5.8 %psum.7 = f32[2,256]{1,0:T(2,128)S(1)} all-reduce(f32[2,256]{1,0:T(2,128)S(1)} %pad_maximum_fusion.21), channel_id=1, replica_groups=mesh['space'=4,'tm'=8] {'space'}, use_global_device_ids=true, to_apply=%region_4.5 | all-reduce | flops 512 | bytes 4096 | tf_op jit(solution)/shard_map/psum | solution.py:156
  (72 shorter events, 6.7 us)
Async XLA Ops:
  0.6 15.8 %copy-start = (bf16[8,8,128,128]{3,2,1,0:T(8,128)(2,1)S(1)}, bf16[8,8,128,128]{3,2,1,0:T(8,128)(2,1)}, u32[]{:S(2)}) copy-start(bf16[8,8,128,128]{3,2,1,0:T(8,128)(2,1)} %param.17) | copy-start | bytes 6291460
  0.6 15.7 %copy-start.6 = (s32[8,8]{1,0:T(8,128)S(1)}, s32[8,8]{1,0:T(8,128)}, u32[]{:S(2)}) copy-start(s32[8,8]{1,0:T(8,128)} %param.18) | copy-start | bytes 772
  0.7 32.4 %collective-permute-start.6 = (bf16[1024,256]{1,0:T(8,128)(2,1)}, bf16[1024,256]{1,0:T(8,128)(2,1)}, u32[]{:S(2)}, u32[]{:S(2)}) collective-permute-start(bf16[1024,256]{1,0:T(8,128)(2,1)} %param.23), channel_id=1, source_target_pairs={{0,8},{8,16},{16,24},{24,0},{1,9},{9,17},{17,25},{25,1},{2,10},{10... | collective-permute-start | bytes 1572872 | tf_op jit(solution)/shard_map/ppermute | solution.py:105
  1.2 38.2 %collective-permute-start.7 = (bf16[1024,256]{1,0:T(8,128)(2,1)}, bf16[1024,256]{1,0:T(8,128)(2,1)}, u32[]{:S(2)}, u32[]{:S(2)}) collective-permute-start(bf16[1024,256]{1,0:T(8,128)(2,1)} %param.23), channel_id=1, source_target_pairs={{0,16},{8,24},{16,0},{24,8},{1,17},{9,25},{17,1},{25,9},{2,18},{10... | collective-permute-start | bytes 1572872 | tf_op jit(solution)/shard_map/ppermute | solution.py:105
  3.8 37.1 %collective-permute-start.8 = (bf16[1024,256]{1,0:T(8,128)(2,1)}, bf16[1024,256]{1,0:T(8,128)(2,1)}, u32[]{:S(2)}, u32[]{:S(2)}) collective-permute-start(bf16[1024,256]{1,0:T(8,128)(2,1)} %param.23), channel_id=1, source_target_pairs={{0,24},{8,0},{16,8},{24,16},{1,25},{9,1},{17,9},{25,17},{2,26},{10... | collective-permute-start | bytes 1572872 | tf_op jit(solution)/shard_map/ppermute | solution.py:105
  6.0 17.8 %collective-permute-start = (s32[2]{0:T(128)S(1)}, s32[2]{0:T(128)S(1)}, u32[]{:S(2)}, u32[]{:S(2)}) collective-permute-start(s32[2]{0:T(128)S(1)} %get-tuple-element.54), channel_id=1, source_target_pairs={{8,0},{16,8},{24,16},{9,1},{17,9},{25,17},{10,2},{18,10},{26,18},{... | collective-permute-start | bytes 32 | tf_op jit(solution)/shard_map/ppermute | solution.py:74
  7.3 22.5 %collective-permute-start.2 = (s32[2]{0:T(128)S(1)}, s32[2]{0:T(128)S(1)}, u32[]{:S(2)}, u32[]{:S(2)}) collective-permute-start(s32[2]{0:T(128)S(1)} %get-tuple-element.53), channel_id=1, source_target_pairs={{0,8},{8,16},{16,24},{1,9},{9,17},{17,25},{2,10},{10,18},{18,26},{... | collective-permute-start | bytes 32 | tf_op jit(solution)/shard_map/ppermute | solution.py:75
  20.3 1.7 %copy-start.1 = (bf16[128,8,12,128]{3,1,2,0:T(8,128)(2,1)}, bf16[128,8,12,128]{3,1,2,0:T(8,128)(2,1)S(1)}, u32[]{:S(2)}) copy-start(bf16[128,8,12,128]{3,1,2,0:T(8,128)(2,1)S(1)} %copy.52) | copy-start | bytes 9437188
  20.3 3.4 %copy-start.4 = (s32[2048,1]{0,1:T(1,128)S(1)}, s32[2048,1]{0,1:T(1,128)}, u32[]{:S(2)}) copy-start(s32[2048,1]{0,1:T(1,128)} %param.21) | copy-start | bytes 24580
  20.3 3.5 %copy-start.5 = (s32[2048]{0:T(1024)S(1)}, s32[2048]{0:T(1024)}, u32[]{:S(2)}) copy-start(s32[2048]{0:T(1024)} %param.22) | copy-start | bytes 24580
  23.8 46.8 %collective-permute-start.4 = (bf16[1024,64]{0,1:T(8,128)(2,1)}, bf16[1024,64]{0,1:T(8,128)(2,1)}, u32[]{:S(2)}, u32[]{:S(2)}) collective-permute-start(bf16[1024,64]{0,1:T(8,128)(2,1)} %get-tuple-element.32), channel_id=1, source_target_pairs={{0,1},{1,2},{2,3},{3,4},{4,5},{5,6},{6,7},{8,9},{9,10},{10,11},{11... | collective-permute-start | bytes 393224 | tf_op jit(solution)/shard_map/ppermute | solution.py:27
  29.7 40.8 %collective-permute-start.5 = (bf16[1024,64]{0,1:T(8,128)(2,1)}, bf16[1024,64]{0,1:T(8,128)(2,1)}, u32[]{:S(2)}, u32[]{:S(2)}) collective-permute-start(bf16[1024,64]{0,1:T(8,128)(2,1)} %get-tuple-element.33), channel_id=1, source_target_pairs={{1,0},{2,1},{3,2},{4,3},{5,4},{6,5},{7,6},{9,8},{10,9},{11,10},{12... | collective-permute-start | bytes 393224 | tf_op jit(solution)/shard_map/ppermute | solution.py:28
  33.1 33.0 %collective-permute-start.1 = (bf16[256,256]{0,1:T(8,128)(2,1)S(1)}, bf16[256,256]{0,1:T(8,128)(2,1)}, u32[]{:S(2)}, u32[]{:S(2)}) collective-permute-start(bf16[256,256]{0,1:T(8,128)(2,1)S(1)} %pad_maximum_fusion.11), channel_id=1, source_target_pairs={{0,8},{8,16},{16,24},{1,9},{9,17},{17,25},{2,10},{10,18},{18,26},{... | collective-permute-start | bytes 393224 | tf_op jit(solution)/shard_map/ppermute | solution.py:84
  39.4 31.2 %collective-permute-start.3 = (bf16[256,256]{0,1:T(8,128)(2,1)S(1)}, bf16[256,256]{0,1:T(8,128)(2,1)}, u32[]{:S(2)}, u32[]{:S(2)}) collective-permute-start(bf16[256,256]{0,1:T(8,128)(2,1)S(1)} %pad_maximum_fusion.12), channel_id=1, source_target_pairs={{8,0},{16,8},{24,16},{9,1},{17,9},{25,17},{10,2},{18,10},{26,18},{... | collective-permute-start | bytes 393224 | tf_op jit(solution)/shard_map/ppermute | solution.py:85
  62.1 8.1 %copy-start.3 = (f32[1024]{0:T(1024)S(1)}, f32[1024]{0:T(1024)}, u32[]{:S(2)}) copy-start(f32[1024]{0:T(1024)} %param.13) | copy-start | bytes 12292
  62.8 7.4 %all-to-all-start = ((f32[4,4,1024]{2,1,0:T(4,128)}), f32[4,4,1024]{2,1,0:T(4,128)S(1)}, u32[]{:S(2)}, u32[]{:S(2)}) async-start(f32[4,4,1024]{2,1,0:T(4,128)} %bitcast.11), calls=%async_computation | async-start | bytes 131072 | tf_op jit(solution)/shard_map/all_to_all | solution.py:130
  70.6 2.8 %copy-start.2 = (bf16[128,8,12,128]{3,1,2,0:T(8,128)(2,1)S(1)}, bf16[128,8,12,128]{3,1,2,0:T(8,128)(2,1)}, u32[]{:S(2)}) copy-start(bf16[128,8,12,128]{3,1,2,0:T(8,128)(2,1)} %copy-done.1) | copy-start | bytes 9437188
  74.3 10.4 %collective-permute-start.10 = (bf16[256,256]{0,1:T(8,128)(2,1)S(1)}, bf16[256,256]{0,1:T(8,128)(2,1)S(1)}, u32[]{:S(2)}, u32[]{:S(2)}) collective-permute-start(bf16[256,256]{0,1:T(8,128)(2,1)S(1)} %pad_maximum_fusion.14), channel_id=1, source_target_pairs={{8,0},{16,8},{24,16},{9,1},{17,9},{25,17},{10,2},{18,10},{26,18},{... | collective-permute-start | bytes 393224 | tf_op jit(solution)/shard_map/ppermute | solution.py:85
  75.6 8.7 %collective-permute-start.9 = (bf16[256,256]{0,1:T(8,128)(2,1)S(1)}, bf16[256,256]{0,1:T(8,128)(2,1)S(1)}, u32[]{:S(2)}, u32[]{:S(2)}) collective-permute-start(bf16[256,256]{0,1:T(8,128)(2,1)S(1)} %pad_maximum_fusion.13), channel_id=1, source_target_pairs={{0,8},{8,16},{16,24},{1,9},{9,17},{17,25},{2,10},{10,18},{18,26},{... | collective-permute-start | bytes 393224 | tf_op jit(solution)/shard_map/ppermute | solution.py:84
  78.7 8.1 %collective-permute-start.11 = (bf16[1024,64]{0,1:T(8,128)(2,1)S(1)}, bf16[1024,64]{0,1:T(8,128)(2,1)S(1)}, u32[]{:S(2)}, u32[]{:S(2)}) collective-permute-start(bf16[1024,64]{0,1:T(8,128)(2,1)S(1)} %get-tuple-element.26), channel_id=1, source_target_pairs={{0,1},{1,2},{2,3},{3,4},{4,5},{5,6},{6,7},{8,9},{9,10},{10,11},{11... | collective-permute-start | bytes 393224 | tf_op jit(solution)/shard_map/ppermute | solution.py:27
  83.0 8.1 %collective-permute-start.12 = (bf16[1024,64]{0,1:T(8,128)(2,1)S(1)}, bf16[1024,64]{0,1:T(8,128)(2,1)S(1)}, u32[]{:S(2)}, u32[]{:S(2)}) collective-permute-start(bf16[1024,64]{0,1:T(8,128)(2,1)S(1)} %get-tuple-element.27), channel_id=1, source_target_pairs={{1,0},{2,1},{3,2},{4,3},{5,4},{6,5},{7,6},{9,8},{10,9},{11,10},{12... | collective-permute-start | bytes 393224 | tf_op jit(solution)/shard_map/ppermute | solution.py:28
  92.9 10.8 %collective-permute-start.14 = (bf16[256,256]{0,1:T(8,128)(2,1)S(1)}, bf16[256,256]{0,1:T(8,128)(2,1)S(1)}, u32[]{:S(2)}, u32[]{:S(2)}) collective-permute-start(bf16[256,256]{0,1:T(8,128)(2,1)S(1)} %pad_maximum_fusion.16), channel_id=1, source_target_pairs={{8,0},{16,8},{24,16},{9,1},{17,9},{25,17},{10,2},{18,10},{26,18},{... | collective-permute-start | bytes 393224 | tf_op jit(solution)/shard_map/ppermute | solution.py:85
  94.2 9.1 %collective-permute-start.13 = (bf16[256,256]{0,1:T(8,128)(2,1)S(1)}, bf16[256,256]{0,1:T(8,128)(2,1)S(1)}, u32[]{:S(2)}, u32[]{:S(2)}) collective-permute-start(bf16[256,256]{0,1:T(8,128)(2,1)S(1)} %pad_maximum_fusion.15), channel_id=1, source_target_pairs={{0,8},{8,16},{16,24},{1,9},{9,17},{17,25},{2,10},{10,18},{18,26},{... | collective-permute-start | bytes 393224 | tf_op jit(solution)/shard_map/ppermute | solution.py:84
  97.3 8.3 %collective-permute-start.15 = (bf16[1024,64]{0,1:T(8,128)(2,1)S(1)}, bf16[1024,64]{0,1:T(8,128)(2,1)S(1)}, u32[]{:S(2)}, u32[]{:S(2)}) collective-permute-start(bf16[1024,64]{0,1:T(8,128)(2,1)S(1)} %get-tuple-element.20), channel_id=1, source_target_pairs={{0,1},{1,2},{2,3},{3,4},{4,5},{5,6},{6,7},{8,9},{9,10},{10,11},{11... | collective-permute-start | bytes 393224 | tf_op jit(solution)/shard_map/ppermute | solution.py:27
  102.0 8.1 %collective-permute-start.16 = (bf16[1024,64]{0,1:T(8,128)(2,1)S(1)}, bf16[1024,64]{0,1:T(8,128)(2,1)S(1)}, u32[]{:S(2)}, u32[]{:S(2)}) collective-permute-start(bf16[1024,64]{0,1:T(8,128)(2,1)S(1)} %get-tuple-element.21), channel_id=1, source_target_pairs={{1,0},{2,1},{3,2},{4,3},{5,4},{6,5},{7,6},{9,8},{10,9},{11,10},{12... | collective-permute-start | bytes 393224 | tf_op jit(solution)/shard_map/ppermute | solution.py:28
  111.9 10.0 %collective-permute-start.18 = (bf16[256,256]{0,1:T(8,128)(2,1)S(1)}, bf16[256,256]{0,1:T(8,128)(2,1)S(1)}, u32[]{:S(2)}, u32[]{:S(2)}) collective-permute-start(bf16[256,256]{0,1:T(8,128)(2,1)S(1)} %pad_maximum_fusion.18), channel_id=1, source_target_pairs={{8,0},{16,8},{24,16},{9,1},{17,9},{25,17},{10,2},{18,10},{26,18},{... | collective-permute-start | bytes 393224 | tf_op jit(solution)/shard_map/ppermute | solution.py:85
  113.3 8.4 %collective-permute-start.17 = (bf16[256,256]{0,1:T(8,128)(2,1)S(1)}, bf16[256,256]{0,1:T(8,128)(2,1)S(1)}, u32[]{:S(2)}, u32[]{:S(2)}) collective-permute-start(bf16[256,256]{0,1:T(8,128)(2,1)S(1)} %pad_maximum_fusion.17), channel_id=1, source_target_pairs={{0,8},{8,16},{16,24},{1,9},{9,17},{17,25},{2,10},{10,18},{18,26},{... | collective-permute-start | bytes 393224 | tf_op jit(solution)/shard_map/ppermute | solution.py:84
  116.3 7.5 %collective-permute-start.19 = (bf16[1024,64]{0,1:T(8,128)(2,1)S(1)}, bf16[1024,64]{0,1:T(8,128)(2,1)S(1)}, u32[]{:S(2)}, u32[]{:S(2)}) collective-permute-start(bf16[1024,64]{0,1:T(8,128)(2,1)S(1)} %get-tuple-element.14), channel_id=1, source_target_pairs={{0,1},{1,2},{2,3},{3,4},{4,5},{5,6},{6,7},{8,9},{9,10},{10,11},{11... | collective-permute-start | bytes 393224 | tf_op jit(solution)/shard_map/ppermute | solution.py:27
  120.3 8.2 %collective-permute-start.20 = (bf16[1024,64]{0,1:T(8,128)(2,1)S(1)}, bf16[1024,64]{0,1:T(8,128)(2,1)S(1)}, u32[]{:S(2)}, u32[]{:S(2)}) collective-permute-start(bf16[1024,64]{0,1:T(8,128)(2,1)S(1)} %get-tuple-element.15), channel_id=1, source_target_pairs={{1,0},{2,1},{3,2},{4,3},{5,4},{6,5},{7,6},{9,8},{10,9},{11,10},{12... | collective-permute-start | bytes 393224 | tf_op jit(solution)/shard_map/ppermute | solution.py:28
  132.8 15.8 %collective-permute-start.22 = (bf16[256,256]{0,1:T(8,128)(2,1)}, bf16[256,256]{0,1:T(8,128)(2,1)S(1)}, u32[]{:S(2)}, u32[]{:S(2)}) collective-permute-start(bf16[256,256]{0,1:T(8,128)(2,1)} %pad_maximum_fusion.20), channel_id=1, source_target_pairs={{8,0},{16,8},{24,16},{9,1},{17,9},{25,17},{10,2},{18,10},{26,18},{... | collective-permute-start | bytes 393224 | tf_op jit(solution)/shard_map/ppermute | solution.py:85
  134.7 12.0 %collective-permute-start.21 = (bf16[256,256]{0,1:T(8,128)(2,1)}, bf16[256,256]{0,1:T(8,128)(2,1)}, u32[]{:S(2)}, u32[]{:S(2)}) collective-permute-start(bf16[256,256]{0,1:T(8,128)(2,1)} %pad_maximum_fusion.19), channel_id=1, source_target_pairs={{0,8},{8,16},{16,24},{1,9},{9,17},{17,25},{2,10},{10,18},{18,26},{... | collective-permute-start | bytes 393224 | tf_op jit(solution)/shard_map/ppermute | solution.py:84
  139.1 10.9 %collective-permute-start.23 = (bf16[1024,64]{0,1:T(8,128)(2,1)}, bf16[1024,64]{0,1:T(8,128)(2,1)S(1)}, u32[]{:S(2)}, u32[]{:S(2)}) collective-permute-start(bf16[1024,64]{0,1:T(8,128)(2,1)} %get-tuple-element.12), channel_id=1, source_target_pairs={{0,1},{1,2},{2,3},{3,4},{4,5},{5,6},{6,7},{8,9},{9,10},{10,11},{11... | collective-permute-start | bytes 393224 | tf_op jit(solution)/shard_map/ppermute | solution.py:27
  142.9 7.9 %collective-permute-start.24 = (bf16[1024,64]{0,1:T(8,128)(2,1)}, bf16[1024,64]{0,1:T(8,128)(2,1)S(1)}, u32[]{:S(2)}, u32[]{:S(2)}) collective-permute-start(bf16[1024,64]{0,1:T(8,128)(2,1)} %get-tuple-element.13), channel_id=1, source_target_pairs={{1,0},{2,1},{3,2},{4,3},{5,4},{6,5},{7,6},{9,8},{10,9},{11,10},{12... | collective-permute-start | bytes 393224 | tf_op jit(solution)/shard_map/ppermute | solution.py:28

commit v9 on v8

--- a/solution.py
+++ b/solution.py
@@ -69,10 +69,19 @@
     own_t, lower_t, upper_t = own_part.T, lower_part.T, upper_part.T
 
     space_index = lax.axis_index("space")
+    nodes_dev = svc_coef.shape[0]
     up = [(i, i + 1) for i in range(space_count - 1)]
     down = [(i + 1, i) for i in range(space_count - 1)]
-    upper_wants = lax.ppermute(halo_needs[:HALO_B], "space", down)
-    lower_wants = lax.ppermute(halo_needs[HALO_B:], "space", up)
+    pad_rows = 16
+    needs_rows = jnp.zeros((pad_rows, svc_coef.shape[1]), jnp.bfloat16)
+    needs_rows = needs_rows.at[0, : halo_needs.shape[0]].set(halo_needs.astype(jnp.bfloat16))
+    extended = jnp.concatenate([svc_coef, needs_rows], axis=0)
+    tables = [extended] + [
+        lax.ppermute(extended, "space", [(i, (i + k) % space_count) for i in range(space_count)])
+        for k in range(1, space_count)
+    ]
+    lower_wants = tables[1][nodes_dev, HALO_B : 2 * HALO_B].astype(jnp.int32)
+    upper_wants = tables[space_count - 1][nodes_dev, :HALO_B].astype(jnp.int32)
 
     def pick_blocks(field, wanted):
         return jnp.concatenate(
@@ -100,15 +109,10 @@
     rounded = lax.optimization_barrier(solution.astype(jnp.bfloat16))
     first_space = spatial(rounded)
     first_time = temporal(rounded)
-    nodes_dev = svc_coef.shape[0]
-    tables = [svc_coef] + [
-        lax.ppermute(svc_coef, "space", [(i, (i + k) % space_count) for i in range(space_count)])
-        for k in range(1, space_count)
-    ]
     svc_all = jnp.concatenate(tables, axis=0)
     owner = obs_owner[:, 0]
     shift = (lax.axis_index("space") - owner) % space_count
-    coef_rows = svc_all[shift * nodes_dev + obs_cell // T_DEV]
+    coef_rows = svc_all[shift * (nodes_dev + pad_rows) + obs_cell // T_DEV]
     eta = jnp.einsum("rc,rc->r", covariates, coef_rows, preferred_element_type=jnp.float32)
     obs_weight = jnp.exp(eta)
     node_ids = owner * nodes_dev + obs_cell // T_DEV

time: 159 us -> 161 us (1.013)
  starting transfers between devices: 65.1 us -> 54.3 us
  local copies, waits for them, and re-layouts: 22.2 us -> 29.7 us
  waiting for transfers between devices: 21.5 us -> 26.3 us
  blocking collectives: 5.76 us -> 8.98 us
    unnamed x17 -> x22, local copies, waits for them, and re-layouts: 6.38 us -> 12.7 us
    ppermute x5, starting transfers between devices: 19.1 us -> 13.4 us  [spatial(): lower = lax.ppermute(pick_blocks(field, upper_wants), 'space', up)]
    ppermute x5 -> x3, starting transfers between devices: 8.82 us -> 4.74 us  [shards(): lax.ppermute(extended, 'space', [(i, (i + k) % space_count) for i in rang...]
    psum x1, blocking collectives: 5.76 us -> 8.98 us  [shards(): totals = lax.psum(partial_sums, 'space')]
    ppermute x5, waiting for transfers between devices: 14.3 us -> 17.4 us  [with_halo(): after = lax.ppermute(initial, axis, down)]
    ppermute x5 -> x3, waiting for transfers between devices: 0.01 us -> 2.65 us  [shards(): lax.ppermute(extended, 'space', [(i, (i + k) % space_count) for i in rang...]
    concatenate x0 -> x1, local copies, waits for them, and re-layouts: none -> 1.89 us  [shards(): svc_all = jnp.concatenate(tables, axis=0)]
    ppermute x5, waiting for transfers between devices: 5.83 us -> 4.11 us  [with_halo(): before = lax.ppermute(last, axis, up)]
  transfers between devices with their start and end apart: 26 -> 24, of which waited for: 8 -> 9; matrix products, arithmetic and copies ran while one was open for 30% -> 28% of each run, Pallas kernels for 0% -> 0%
where the time goes in v9:
time: 161 us; the launch traced here: 160 us
  starting transfers between devices  54.3 us (34%)
  local copies, waits for them, and re-layouts  29.7 us (18%)
  matrix products  26.4 us (16%)
  waiting for transfers between devices  26.3 us (16%)
  other arithmetic  10.6 us (7%)
  blocking collectives  8.98 us (6%)
  between operations  3.84 us (2%)
    ppermute x5, starting transfers between devices, with_halo(): before = lax.ppermute(last, axis, up)  19.8 us
    ppermute x5, waiting for transfers between devices, with_halo(): after = lax.ppermute(initial, axis, down)  17.4 us
    ppermute x5, starting transfers between devices, spatial(): lower = lax.ppermute(pick_blocks(field, upper_wants), 'space', up)  13.4 us
    unnamed x22, local copies, waits for them, and re-layouts  12.7 us
    gather x1, local copies, waits for them, and re-layouts, shards(): coef_rows = svc_all[shift * (nodes_dev + pad_rows) + obs_cell // T_DEV]  10.4 us
    psum x1, blocking collectives, shards(): totals = lax.psum(partial_sums, 'space')  8.98 us
    dot_general x5, matrix products, spatial(): jnp.dot(upper.T, upper_t, preferred_element_type=jnp.float32)  6.83 us
    ppermute x5, starting transfers between devices, with_halo(): after = lax.ppermute(initial, axis, down)  6.67 us
  transfers between devices with their start and end apart: 24, of which 9 were waited for; matrix products, arithmetic and copies ran while one was open for 28% of the time, Pallas kernels for 0%

profile of v9, /device:TPU:0, one launch (start us, length us, event | category | flops | bytes accessed | tf_op | source)
XLA Modules:
  0.0 160.0 jit_solution(14373837845738644708)
XLA Ops:
  0.7 0.8 convert_bitcast_fusion
  1.5 1.9 %constant_dynamic-update-slice_fusion.4 = bf16[4160,256]{1,0:T(8,128)(2,1)} fusion(bf16[1024,256]{1,0:T(8,128)(2,1)} %param.25), kind=kLoop, calls=%fused_computation.147 | loop fusion | bytes 1048576
  4.0 1.9 %pad_maximum_fusion = bf16[1040,256]{1,0:T(8,128)(2,1)} fusion(bf16[16,256]{1,0:T(8,128)(2,1)S(1)} %get-tuple-element.67, bf16[1024,256]{1,0:T(8,128)(2,1)} %param.25), kind=kLoop, calls=%fused_computation.87 | loop fusion | flops 1064960 | bytes 1064960 | tf_op jit(solution)/shard_map/concatenate | solution.py:78
  5.8 3.0 %collective-permute-start.6 = (bf16[1040,256]{1,0:T(8,128)(2,1)}, bf16[1040,256]{1,0:T(8,128)(2,1)}, u32[]{:S(2)}, u32[]{:S(2)}) collective-permute-start(bf16[1040,256]{1,0:T(8,128)(2,1)} %pad_maximum_fusion), channel_id=1, source_target_pairs={{0,16},{8,24},{16,0},{24,8},{1,17},{9,25},{17,1},{25,9},{2,18},{10... | collective-permute-start | bytes 1597448 | tf_op jit(solution)/shard_map/ppermute | solution.py:80
  8.8 1.7 %collective-permute-start = (bf16[1040,256]{1,0:T(8,128)(2,1)}, bf16[1040,256]{1,0:T(8,128)(2,1)}, u32[]{:S(2)}, u32[]{:S(2)}) collective-permute-start(bf16[1040,256]{1,0:T(8,128)(2,1)} %pad_maximum_fusion), channel_id=1, source_target_pairs={{0,24},{8,0},{16,8},{24,16},{1,25},{9,1},{17,9},{25,17},{2,26},{10... | collective-permute-start | bytes 1597448 | tf_op jit(solution)/shard_map/ppermute | solution.py:80
  10.6 0.7 broadcast_in_dim.65
  11.4 0.7 broadcast_in_dim.68
  12.2 1.2 copy.27
  14.0 0.8 fusion.90
  14.8 4.0 %collective-permute-start.4 = (bf16[1024,64]{0,1:T(8,128)(2,1)}, bf16[1024,64]{0,1:T(8,128)(2,1)}, u32[]{:S(2)}, u32[]{:S(2)}) collective-permute-start(bf16[1024,64]{0,1:T(8,128)(2,1)} %get-tuple-element.44), channel_id=1, source_target_pairs={{0,1},{1,2},{2,3},{3,4},{4,5},{5,6},{6,7},{8,9},{9,10},{10,11},{11... | collective-permute-start | bytes 393224 | tf_op jit(solution)/shard_map/ppermute | solution.py:27
  18.8 1.3 collective-permute-start.5
  20.1 0.8 convert_element_type.94
  21.0 3.1 %add_convert_fusion = bf16[8,12,128,128]{3,1,2,0:T(8,128)(2,1)S(1)} fusion(f32[8,128,128]{2,1,0:T(8,128)} %convert_element_type.94, f32[8,12]{1,0:T(8,128)S(1)} %fusion.82, bf16[8,8,128,128]{3,2,1,0:T(8,128)(2,1)S(1)} %copy-done, s32[8,8]{1,0:T(8,128)S(1)} %copy-done.7), kind=kOutput, calls=%fused_computation.4 | convolution fusion | flops 29885184 | bytes 5767808 | tf_op jit(solution)/shard_map/bkm,bkij->bimj/dot_general | solution.py:63
  24.1 1.6 copy.52
  25.8 1.6 copy-done.1
  27.4 1.8 %fusion.39 = f32[1024,256]{0,1:T(8,128)} fusion(bf16[1024,256]{0,1:T(8,128)(2,1)S(1)} %fusion.57, bf16[1024,1536]{1,0:T(8,128)(2,1)S(1)} %bitcast.54), kind=kOutput, calls=%fused_computation.67 | convolution fusion | flops 536870912 | bytes 3670016 | tf_op jit(solution)/shard_map/dot_general | solution.py:95
  29.1 2.6 %collective-permute-done.2 = bf16[1040,256]{1,0:T(8,128)(2,1)} collective-permute-done((bf16[1040,256]{1,0:T(8,128)(2,1)}, bf16[1040,256]{1,0:T(8,128)(2,1)}, u32[]{:S(2)}, u32[]{:S(2)}) %collective-permute-start.2) | collective-permute-done | bytes 532512 | tf_op jit(solution)/shard_map/ppermute | solution.py:80
  31.8 0.7 slice_convert_fusion
  37.0 1.9 %constant_dynamic-update-slice_fusion.2 = bf16[4160,256]{1,0:T(8,128)(2,1)} fusion(bf16[4160,256]{1,0:T(8,128)(2,1)} %get-tuple-element.68, bf16[1040,256]{1,0:T(8,128)(2,1)} %collective-permute-done.2), kind=kLoop, calls=%fused_computation.145 | loop fusion | bytes 1064960
  38.9 1.9 %constant_dynamic-update-slice_fusion.1 = bf16[4160,256]{1,0:T(8,128)(2,1)} fusion(bf16[4160,256]{1,0:T(8,128)(2,1)} %constant_dynamic-update-slice_fusion.2, bf16[1040,256]{1,0:T(8,128)(2,1)} %collective-permute-done.6), kind=kLoop, calls=%fused_computation.144 | loop fusion | bytes 1064960
  40.8 1.9 %constant_dynamic-update-slice_fusion = bf16[4160,256]{1,0:T(8,128)(2,1)} fusion(bf16[4160,256]{1,0:T(8,128)(2,1)} %constant_dynamic-update-slice_fusion.1, bf16[1040,256]{1,0:T(8,128)(2,1)} %collective-permute-done), kind=kLoop, calls=%fused_computation.143 | loop fusion | bytes 1064960 | tf_op jit(solution)/shard_map/concatenate | solution.py:112
  42.7 10.4 %gather_fusion = bf16[2048,256]{1,0:T(8,128)(2,1)} fusion(bf16[4160,256]{1,0:T(8,128)(2,1)} %constant_dynamic-update-slice_fusion, s32[2048]{0:T(1024)S(1)} %get-tuple-element.60), kind=kCustom, calls=%fused_computation | custom fusion | bytes 2105344 | tf_op jit(solution)/shard_map/gather | solution.py:115
  53.0 1.9 %fusion.2 = f32[2048]{0:T(1024)S(1)} fusion(bf16[2048,256]{1,0:T(8,128)(2,1)} %gather_fusion, bf16[2048,256]{1,0:T(8,128)(2,1)} %param.22), kind=kLoop, calls=%fused_computation.14 | loop fusion | flops 2095104 | bytes 2105344 | tf_op jit(solution)/shard_map/rc,rc->r/dot_general | solution.py:116
  55.1 1.9 %collective-permute-start.1 = (bf16[256,256]{0,1:T(8,128)(2,1)S(1)}, bf16[256,256]{0,1:T(8,128)(2,1)}, u32[]{:S(2)}, u32[]{:S(2)}) collective-permute-start(bf16[256,256]{0,1:T(8,128)(2,1)S(1)} %pad_maximum_fusion.11), channel_id=1, source_target_pairs={{0,8},{8,16},{16,24},{1,9},{9,17},{17,25},{2,10},{10,18},{18,26},{... | collective-permute-start | bytes 393224 | tf_op jit(solution)/shard_map/ppermute | solution.py:93
  57.1 6.0 %fusion = f32[12,4096]{1,0:T(8,128)S(1)} fusion(s32[2048]{0:T(1024)S(1)} %get-tuple-element.59, bf16[2048,4]{0,1:T(4,128)(2,1)S(1)} %get-tuple-element.53, bf16[2048,4]{0,1:T(4,128)(2,1)S(1)} %get-tuple-element.54, bf16[2048,4]{0,1:T(4,128)(2,1)S(1)} %get-tuple-element.52), kind=kOutput, calls=%fused_computation.2 | convolution fusion | flops 209862656 | bytes 253952 | tf_op jit(solution)/shard_map/dot_general | solution.py:128
  63.7 3.3 %all-to-all-start = ((f32[4,4,1024]{2,1,0:T(4,128)}), f32[4,4,1024]{2,1,0:T(4,128)S(1)}, u32[]{:S(2)}, u32[]{:S(2)}) async-start(f32[4,4,1024]{2,1,0:T(4,128)} %bitcast.12), calls=%async_computation | async-start | bytes 131072 | tf_op jit(solution)/shard_map/all_to_all | solution.py:134
  67.7 1.3 collective-permute-start.3
  69.0 2.1 %all-to-all-done = f32[4,4,1024]{2,1,0:T(4,128)S(1)} async-done(((f32[4,4,1024]{2,1,0:T(4,128)}), f32[4,4,1024]{2,1,0:T(4,128)S(1)}, u32[]{:S(2)}, u32[]{:S(2)}) %all-to-all-start) | async-done | bytes 65568 | tf_op jit(solution)/shard_map/all_to_all | solution.py:134
  71.5 1.9 %convolution_add_fusion.9 = f32[1024,256]{0,1:T(8,128)S(1)} fusion(f32[1024,256]{0,1:T(8,128)} %fusion.39, bf16[256,256]{0,1:T(8,128)(2,1)} %collective-permute-done.1, bf16[1024,1536]{1,0:T(8,128)(2,1)} %bitcast.55), kind=kOutput, calls=%fused_computation.43 | convolution fusion | flops 134479872 | bytes 2752512 | tf_op jit(solution)/shard_map/dot_general | solution.py:96
  73.5 2.0 %fusion.94 = (bf16[1024,256]{0,1:T(8,128)(2,1)S(1)}, f32[1024,256]{0,1:T(8,128)S(1)}) fusion(f32[1024,256]{0,1:T(8,128)S(1)} %get-tuple-element.51, f32[1024,256]{0,1:T(8,128)S(1)} %get-tuple-element.50, bf16[1024,64]{0,1:T(8,128)(2,1)} %collective-permute-done.5, bf16[1024,256]{0,1:T(8,128)(2,1)S(1)} %fusion.57, ...), kind=kOutput, calls=%fused_computation.199 | convolution fusion | flops 141557760 | bytes 6695936 | tf_op jit(solution)/shard_map/dot_general | solution.py:97
  75.7 0.7 fusion.37
  76.5 4.3 %collective-permute-start.7 = (bf16[256,256]{0,1:T(8,128)(2,1)S(1)}, bf16[256,256]{0,1:T(8,128)(2,1)S(1)}, u32[]{:S(2)}, u32[]{:S(2)}) collective-permute-start(bf16[256,256]{0,1:T(8,128)(2,1)S(1)} %pad_maximum_fusion.13), channel_id=1, source_target_pairs={{0,8},{8,16},{16,24},{1,9},{9,17},{17,25},{2,10},{10,18},{18,26},{... | collective-permute-start | bytes 393224 | tf_op jit(solution)/shard_map/ppermute | solution.py:93
  80.8 1.3 collective-permute-start.8
  82.1 3.4 %collective-permute-start.9 = (bf16[1024,64]{0,1:T(8,128)(2,1)S(1)}, bf16[1024,64]{0,1:T(8,128)(2,1)S(1)}, u32[]{:S(2)}, u32[]{:S(2)}) collective-permute-start(bf16[1024,64]{0,1:T(8,128)(2,1)S(1)} %get-tuple-element.38), channel_id=1, source_target_pairs={{0,1},{1,2},{2,3},{3,4},{4,5},{5,6},{6,7},{8,9},{9,10},{10,11},{11... | collective-permute-start | bytes 393224 | tf_op jit(solution)/shard_map/ppermute | solution.py:27
  85.5 1.3 collective-permute-start.10
  87.2 2.0 %collective-permute-done.9 = bf16[1024,64]{0,1:T(8,128)(2,1)S(1)} collective-permute-done((bf16[1024,64]{0,1:T(8,128)(2,1)S(1)}, bf16[1024,64]{0,1:T(8,128)(2,1)S(1)}, u32[]{:S(2)}, u32[]{:S(2)}) %collective-permute-start.9) | collective-permute-done | bytes 131104 | tf_op jit(solution)/shard_map/ppermute | solution.py:27
  89.2 4.4 %collective-permute-done.10 = bf16[1024,64]{0,1:T(8,128)(2,1)S(1)} collective-permute-done((bf16[1024,64]{0,1:T(8,128)(2,1)S(1)}, bf16[1024,64]{0,1:T(8,128)(2,1)S(1)}, u32[]{:S(2)}, u32[]{:S(2)}) %collective-permute-start.10) | collective-permute-done | bytes 131104 | tf_op jit(solution)/shard_map/ppermute | solution.py:28
  93.7 0.8 fusion.95
  94.7 0.7 fusion.35
  95.5 1.9 %collective-permute-start.11 = (bf16[256,256]{0,1:T(8,128)(2,1)S(1)}, bf16[256,256]{0,1:T(8,128)(2,1)S(1)}, u32[]{:S(2)}, u32[]{:S(2)}) collective-permute-start(bf16[256,256]{0,1:T(8,128)(2,1)S(1)} %pad_maximum_fusion.15), channel_id=1, source_target_pairs={{0,8},{8,16},{16,24},{1,9},{9,17},{17,25},{2,10},{10,18},{18,26},{... | collective-permute-start | bytes 393224 | tf_op jit(solution)/shard_map/ppermute | solution.py:93
  97.4 1.3 collective-permute-start.12
  98.7 4.4 %collective-permute-start.13 = (bf16[1024,64]{0,1:T(8,128)(2,1)S(1)}, bf16[1024,64]{0,1:T(8,128)(2,1)S(1)}, u32[]{:S(2)}, u32[]{:S(2)}) collective-permute-start(bf16[1024,64]{0,1:T(8,128)(2,1)S(1)} %get-tuple-element.32), channel_id=1, source_target_pairs={{0,1},{1,2},{2,3},{3,4},{4,5},{5,6},{6,7},{8,9},{9,10},{10,11},{11... | collective-permute-start | bytes 393224 | tf_op jit(solution)/shard_map/ppermute | solution.py:27
  103.1 1.5 collective-permute-start.14
  105.0 1.2 collective-permute-done.13
  106.2 4.7 %collective-permute-done.14 = bf16[1024,64]{0,1:T(8,128)(2,1)S(1)} collective-permute-done((bf16[1024,64]{0,1:T(8,128)(2,1)S(1)}, bf16[1024,64]{0,1:T(8,128)(2,1)S(1)}, u32[]{:S(2)}, u32[]{:S(2)}) %collective-permute-start.14) | collective-permute-done | bytes 131104 | tf_op jit(solution)/shard_map/ppermute | solution.py:28
  110.9 0.8 fusion.96
  111.9 0.7 fusion.33
  112.7 2.2 %collective-permute-start.15 = (bf16[256,256]{0,1:T(8,128)(2,1)S(1)}, bf16[256,256]{0,1:T(8,128)(2,1)S(1)}, u32[]{:S(2)}, u32[]{:S(2)}) collective-permute-start(bf16[256,256]{0,1:T(8,128)(2,1)S(1)} %pad_maximum_fusion.17), channel_id=1, source_target_pairs={{0,8},{8,16},{16,24},{1,9},{9,17},{17,25},{2,10},{10,18},{18,26},{... | collective-permute-start | bytes 393224 | tf_op jit(solution)/shard_map/ppermute | solution.py:93
  114.9 1.3 collective-permute-start.16
  116.2 4.0 %collective-permute-start.17 = (bf16[1024,64]{0,1:T(8,128)(2,1)S(1)}, bf16[1024,64]{0,1:T(8,128)(2,1)S(1)}, u32[]{:S(2)}, u32[]{:S(2)}) collective-permute-start(bf16[1024,64]{0,1:T(8,128)(2,1)S(1)} %get-tuple-element.26), channel_id=1, source_target_pairs={{0,1},{1,2},{2,3},{3,4},{4,5},{5,6},{6,7},{8,9},{9,10},{10,11},{11... | collective-permute-start | bytes 393224 | tf_op jit(solution)/shard_map/ppermute | solution.py:27
  120.2 1.3 collective-permute-start.18
  121.9 0.8 collective-permute-done.17
  122.7 4.5 %collective-permute-done.18 = bf16[1024,64]{0,1:T(8,128)(2,1)S(1)} collective-permute-done((bf16[1024,64]{0,1:T(8,128)(2,1)S(1)}, bf16[1024,64]{0,1:T(8,128)(2,1)S(1)}, u32[]{:S(2)}, u32[]{:S(2)}) %collective-permute-start.18) | collective-permute-done | bytes 131104 | tf_op jit(solution)/shard_map/ppermute | solution.py:28
  127.2 1.8 %fusion.97 = (bf16[1024,256]{0,1:T(8,128)(2,1)S(1)}, f32[1024,256]{0,1:T(8,128)}) fusion(f32[1024,256]{0,1:T(8,128)S(1)} %get-tuple-element.74, f32[1024,256]{0,1:T(8,128)S(1)} %get-tuple-element.51, f32[1024,256]{0,1:T(8,128)S(1)} %fusion.4, bf16[1024,64]{0,1:T(8,128)(2,1)S(1)} %collective-permute-done.18, bf16[1024,256]{0,1:T(8,128)(2,1)S(1)} %get-tuple-element.73, ...), kind=kOutput, calls=%fused_computation.202 | convolution fusion | flops 140247040 | bytes 7735296 | tf_op jit(solution)/shard_map/dot_general | solution.py:97
  129.1 1.8 %fusion.41 = f32[1024,256]{0,1:T(8,128)} fusion(bf16[1024,256]{0,1:T(8,128)(2,1)S(1)} %get-tuple-element.75, bf16[1024,1536]{1,0:T(8,128)(2,1)S(1)} %bitcast.68), kind=kOutput, calls=%fused_computation.69 | convolution fusion | flops 536870912 | bytes 3670016 | tf_op jit(solution)/shard_map/dot_general | solution.py:95
  130.8 2.5 %copy.34 = f32[1024,256]{1,0:T(8,128)} copy(f32[1024,256]{0,1:T(8,128)} %get-tuple-element.76) | data formatting | bytes 2097152
  133.4 3.0 %collective-permute-start.19 = (bf16[256,256]{0,1:T(8,128)(2,1)S(1)}, bf16[256,256]{0,1:T(8,128)(2,1)S(1)}, u32[]{:S(2)}, u32[]{:S(2)}) collective-permute-start(bf16[256,256]{0,1:T(8,128)(2,1)S(1)} %pad_maximum_fusion.19), channel_id=1, source_target_pairs={{0,8},{8,16},{16,24},{1,9},{9,17},{17,25},{2,10},{10,18},{18,26},{... | collective-permute-start | bytes 393224 | tf_op jit(solution)/shard_map/ppermute | solution.py:93
  136.4 1.3 collective-permute-start.20
  137.8 4.0 %collective-permute-start.21 = (bf16[1024,64]{0,1:T(8,128)(2,1)S(1)}, bf16[1024,64]{0,1:T(8,128)(2,1)S(1)}, u32[]{:S(2)}, u32[]{:S(2)}) collective-permute-start(bf16[1024,64]{0,1:T(8,128)(2,1)S(1)} %get-tuple-element.24), channel_id=1, source_target_pairs={{0,1},{1,2},{2,3},{3,4},{4,5},{5,6},{6,7},{8,9},{9,10},{10,11},{11... | collective-permute-start | bytes 393224 | tf_op jit(solution)/shard_map/ppermute | solution.py:27
  141.7 1.3 collective-permute-start.22
  143.1 1.7 %convolution_add_fusion.1 = f32[1024,256]{0,1:T(8,128)S(1)} fusion(f32[1024,256]{0,1:T(8,128)} %fusion.41, bf16[256,256]{0,1:T(8,128)(2,1)S(1)} %collective-permute-done.19, bf16[1024,1536]{1,0:T(8,128)(2,1)} %bitcast.56), kind=kOutput, calls=%fused_computation.23 | convolution fusion | flops 134479872 | bytes 2752512 | tf_op jit(solution)/shard_map/dot_general | solution.py:96
  144.8 3.8 %collective-permute-done.22 = bf16[1024,64]{0,1:T(8,128)(2,1)S(1)} collective-permute-done((bf16[1024,64]{0,1:T(8,128)(2,1)S(1)}, bf16[1024,64]{0,1:T(8,128)(2,1)S(1)}, u32[]{:S(2)}, u32[]{:S(2)}) %collective-permute-start.22) | collective-permute-done | bytes 131104 | tf_op jit(solution)/shard_map/ppermute | solution.py:28
  149.0 1.5 fusion.32
  150.5 9.0 %psum.7 = f32[2,256]{1,0:T(2,128)S(1)} all-reduce(f32[2,256]{1,0:T(2,128)S(1)} %pad_maximum_fusion.21), channel_id=1, replica_groups=mesh['space'=4,'tm'=8] {'space'}, use_global_device_ids=true, to_apply=%region_4.5 | all-reduce | flops 512 | bytes 4096 | tf_op jit(solution)/shard_map/psum | solution.py:160
  (77 shorter events, 8.1 us)
Async XLA Ops:
  0.6 20.3 %copy-start = (bf16[8,8,128,128]{3,2,1,0:T(8,128)(2,1)S(1)}, bf16[8,8,128,128]{3,2,1,0:T(8,128)(2,1)}, u32[]{:S(2)}) copy-start(bf16[8,8,128,128]{3,2,1,0:T(8,128)(2,1)} %param.19) | copy-start | bytes 6291460
  0.6 12.8 %copy-start.3 = (bf16[8,128,128]{2,1,0:T(8,128)(2,1)S(1)}, bf16[8,128,128]{2,1,0:T(8,128)(2,1)}, u32[]{:S(2)}) copy-start(bf16[8,128,128]{2,1,0:T(8,128)(2,1)} %param.18) | copy-start | bytes 786436
  0.7 13.0 %copy-start.4 = (f32[1024]{0:T(1024)S(1)}, f32[1024]{0:T(1024)}, u32[]{:S(2)}) copy-start(f32[1024]{0:T(1024)} %param.15) | copy-start | bytes 12292
  0.7 20.3 %copy-start.7 = (s32[8,8]{1,0:T(8,128)S(1)}, s32[8,8]{1,0:T(8,128)}, u32[]{:S(2)}) copy-start(s32[8,8]{1,0:T(8,128)} %param.20) | copy-start | bytes 772
  5.8 33.1 %collective-permute-start.6 = (bf16[1040,256]{1,0:T(8,128)(2,1)}, bf16[1040,256]{1,0:T(8,128)(2,1)}, u32[]{:S(2)}, u32[]{:S(2)}) collective-permute-start(bf16[1040,256]{1,0:T(8,128)(2,1)} %pad_maximum_fusion), channel_id=1, source_target_pairs={{0,16},{8,24},{16,0},{24,8},{1,17},{9,25},{17,1},{25,9},{2,18},{10... | collective-permute-start | bytes 1597448 | tf_op jit(solution)/shard_map/ppermute | solution.py:80
  8.8 23.0 %collective-permute-start.2 = (bf16[1040,256]{1,0:T(8,128)(2,1)}, bf16[1040,256]{1,0:T(8,128)(2,1)}, u32[]{:S(2)}, u32[]{:S(2)}) collective-permute-start(bf16[1040,256]{1,0:T(8,128)(2,1)} %pad_maximum_fusion), channel_id=1, source_target_pairs={{0,8},{8,16},{16,24},{24,0},{1,9},{9,17},{17,25},{25,1},{2,10},{10... | collective-permute-start | bytes 1597448 | tf_op jit(solution)/shard_map/ppermute | solution.py:80
  8.8 25.7 %collective-permute-start = (bf16[1040,256]{1,0:T(8,128)(2,1)}, bf16[1040,256]{1,0:T(8,128)(2,1)}, u32[]{:S(2)}, u32[]{:S(2)}) collective-permute-start(bf16[1040,256]{1,0:T(8,128)(2,1)} %pad_maximum_fusion), channel_id=1, source_target_pairs={{0,24},{8,0},{16,8},{24,16},{1,25},{9,1},{17,9},{25,17},{2,26},{10... | collective-permute-start | bytes 1597448 | tf_op jit(solution)/shard_map/ppermute | solution.py:80
  14.8 58.6 %collective-permute-start.4 = (bf16[1024,64]{0,1:T(8,128)(2,1)}, bf16[1024,64]{0,1:T(8,128)(2,1)}, u32[]{:S(2)}, u32[]{:S(2)}) collective-permute-start(bf16[1024,64]{0,1:T(8,128)(2,1)} %get-tuple-element.44), channel_id=1, source_target_pairs={{0,1},{1,2},{2,3},{3,4},{4,5},{5,6},{6,7},{8,9},{9,10},{10,11},{11... | collective-permute-start | bytes 393224 | tf_op jit(solution)/shard_map/ppermute | solution.py:27
  18.8 54.6 %collective-permute-start.5 = (bf16[1024,64]{0,1:T(8,128)(2,1)}, bf16[1024,64]{0,1:T(8,128)(2,1)}, u32[]{:S(2)}, u32[]{:S(2)}) collective-permute-start(bf16[1024,64]{0,1:T(8,128)(2,1)} %get-tuple-element.45), channel_id=1, source_target_pairs={{1,0},{2,1},{3,2},{4,3},{5,4},{6,5},{7,6},{9,8},{10,9},{11,10},{12... | collective-permute-start | bytes 393224 | tf_op jit(solution)/shard_map/ppermute | solution.py:28
  24.1 1.6 %copy-start.5 = (s32[2048,1]{0,1:T(1,128)S(1)}, s32[2048,1]{0,1:T(1,128)}, u32[]{:S(2)}) copy-start(s32[2048,1]{0,1:T(1,128)} %param.23) | copy-start | bytes 24580
  25.7 1.6 %copy-start.1 = (bf16[128,8,12,128]{3,1,2,0:T(8,128)(2,1)}, bf16[128,8,12,128]{3,1,2,0:T(8,128)(2,1)S(1)}, u32[]{:S(2)}) copy-start(bf16[128,8,12,128]{3,1,2,0:T(8,128)(2,1)S(1)} %copy.52) | copy-start | bytes 9437188
  25.7 3.4 %copy-start.6 = (s32[2048]{0:T(1024)S(1)}, s32[2048]{0:T(1024)}, u32[]{:S(2)}) copy-start(s32[2048]{0:T(1024)} %param.24) | copy-start | bytes 24580
  55.1 16.4 %collective-permute-start.1 = (bf16[256,256]{0,1:T(8,128)(2,1)S(1)}, bf16[256,256]{0,1:T(8,128)(2,1)}, u32[]{:S(2)}, u32[]{:S(2)}) collective-permute-start(bf16[256,256]{0,1:T(8,128)(2,1)S(1)} %pad_maximum_fusion.11), channel_id=1, source_target_pairs={{0,8},{8,16},{16,24},{1,9},{9,17},{17,25},{2,10},{10,18},{18,26},{... | collective-permute-start | bytes 393224 | tf_op jit(solution)/shard_map/ppermute | solution.py:93
  63.7 7.4 %all-to-all-start = ((f32[4,4,1024]{2,1,0:T(4,128)}), f32[4,4,1024]{2,1,0:T(4,128)S(1)}, u32[]{:S(2)}, u32[]{:S(2)}) async-start(f32[4,4,1024]{2,1,0:T(4,128)} %bitcast.12), calls=%async_computation | async-start | bytes 131072 | tf_op jit(solution)/shard_map/all_to_all | solution.py:134
  67.7 5.8 %collective-permute-start.3 = (bf16[256,256]{0,1:T(8,128)(2,1)}, bf16[256,256]{0,1:T(8,128)(2,1)S(1)}, u32[]{:S(2)}, u32[]{:S(2)}) collective-permute-start(bf16[256,256]{0,1:T(8,128)(2,1)} %pad_maximum_fusion.12), channel_id=1, source_target_pairs={{8,0},{16,8},{24,16},{9,1},{17,9},{25,17},{10,2},{18,10},{26,18},{... | collective-permute-start | bytes 393224 | tf_op jit(solution)/shard_map/ppermute | solution.py:94
  71.1 2.4 %copy-start.2 = (bf16[128,8,12,128]{3,1,2,0:T(8,128)(2,1)S(1)}, bf16[128,8,12,128]{3,1,2,0:T(8,128)(2,1)}, u32[]{:S(2)}) copy-start(bf16[128,8,12,128]{3,1,2,0:T(8,128)(2,1)} %copy-done.1) | copy-start | bytes 9437188
  76.5 10.3 %collective-permute-start.7 = (bf16[256,256]{0,1:T(8,128)(2,1)S(1)}, bf16[256,256]{0,1:T(8,128)(2,1)S(1)}, u32[]{:S(2)}, u32[]{:S(2)}) collective-permute-start(bf16[256,256]{0,1:T(8,128)(2,1)S(1)} %pad_maximum_fusion.13), channel_id=1, source_target_pairs={{0,8},{8,16},{16,24},{1,9},{9,17},{17,25},{2,10},{10,18},{18,26},{... | collective-permute-start | bytes 393224 | tf_op jit(solution)/shard_map/ppermute | solution.py:93
  80.8 6.4 %collective-permute-start.8 = (bf16[256,256]{0,1:T(8,128)(2,1)S(1)}, bf16[256,256]{0,1:T(8,128)(2,1)S(1)}, u32[]{:S(2)}, u32[]{:S(2)}) collective-permute-start(bf16[256,256]{0,1:T(8,128)(2,1)S(1)} %pad_maximum_fusion.14), channel_id=1, source_target_pairs={{8,0},{16,8},{24,16},{9,1},{17,9},{25,17},{10,2},{18,10},{26,18},{... | collective-permute-start | bytes 393224 | tf_op jit(solution)/shard_map/ppermute | solution.py:94
  82.1 7.1 %collective-permute-start.9 = (bf16[1024,64]{0,1:T(8,128)(2,1)S(1)}, bf16[1024,64]{0,1:T(8,128)(2,1)S(1)}, u32[]{:S(2)}, u32[]{:S(2)}) collective-permute-start(bf16[1024,64]{0,1:T(8,128)(2,1)S(1)} %get-tuple-element.38), channel_id=1, source_target_pairs={{0,1},{1,2},{2,3},{3,4},{4,5},{5,6},{6,7},{8,9},{9,10},{10,11},{11... | collective-permute-start | bytes 393224 | tf_op jit(solution)/shard_map/ppermute | solution.py:27
  85.5 8.1 %collective-permute-start.10 = (bf16[1024,64]{0,1:T(8,128)(2,1)S(1)}, bf16[1024,64]{0,1:T(8,128)(2,1)S(1)}, u32[]{:S(2)}, u32[]{:S(2)}) collective-permute-start(bf16[1024,64]{0,1:T(8,128)(2,1)S(1)} %get-tuple-element.39), channel_id=1, source_target_pairs={{1,0},{2,1},{3,2},{4,3},{5,4},{6,5},{7,6},{9,8},{10,9},{11,10},{12... | collective-permute-start | bytes 393224 | tf_op jit(solution)/shard_map/ppermute | solution.py:28
  95.5 9.2 %collective-permute-start.11 = (bf16[256,256]{0,1:T(8,128)(2,1)S(1)}, bf16[256,256]{0,1:T(8,128)(2,1)S(1)}, u32[]{:S(2)}, u32[]{:S(2)}) collective-permute-start(bf16[256,256]{0,1:T(8,128)(2,1)S(1)} %pad_maximum_fusion.15), channel_id=1, source_target_pairs={{0,8},{8,16},{16,24},{1,9},{9,17},{17,25},{2,10},{10,18},{18,26},{... | collective-permute-start | bytes 393224 | tf_op jit(solution)/shard_map/ppermute | solution.py:93
  97.4 7.6 %collective-permute-start.12 = (bf16[256,256]{0,1:T(8,128)(2,1)S(1)}, bf16[256,256]{0,1:T(8,128)(2,1)S(1)}, u32[]{:S(2)}, u32[]{:S(2)}) collective-permute-start(bf16[256,256]{0,1:T(8,128)(2,1)S(1)} %pad_maximum_fusion.16), channel_id=1, source_target_pairs={{8,0},{16,8},{24,16},{9,1},{17,9},{25,17},{10,2},{18,10},{26,18},{... | collective-permute-start | bytes 393224 | tf_op jit(solution)/shard_map/ppermute | solution.py:94
  98.7 7.5 %collective-permute-start.13 = (bf16[1024,64]{0,1:T(8,128)(2,1)S(1)}, bf16[1024,64]{0,1:T(8,128)(2,1)S(1)}, u32[]{:S(2)}, u32[]{:S(2)}) collective-permute-start(bf16[1024,64]{0,1:T(8,128)(2,1)S(1)} %get-tuple-element.32), channel_id=1, source_target_pairs={{0,1},{1,2},{2,3},{3,4},{4,5},{5,6},{6,7},{8,9},{9,10},{10,11},{11... | collective-permute-start | bytes 393224 | tf_op jit(solution)/shard_map/ppermute | solution.py:27
  103.1 7.8 %collective-permute-start.14 = (bf16[1024,64]{0,1:T(8,128)(2,1)S(1)}, bf16[1024,64]{0,1:T(8,128)(2,1)S(1)}, u32[]{:S(2)}, u32[]{:S(2)}) collective-permute-start(bf16[1024,64]{0,1:T(8,128)(2,1)S(1)} %get-tuple-element.33), channel_id=1, source_target_pairs={{1,0},{2,1},{3,2},{4,3},{5,4},{6,5},{7,6},{9,8},{10,9},{11,10},{12... | collective-permute-start | bytes 393224 | tf_op jit(solution)/shard_map/ppermute | solution.py:28
  112.7 8.9 %collective-permute-start.15 = (bf16[256,256]{0,1:T(8,128)(2,1)S(1)}, bf16[256,256]{0,1:T(8,128)(2,1)S(1)}, u32[]{:S(2)}, u32[]{:S(2)}) collective-permute-start(bf16[256,256]{0,1:T(8,128)(2,1)S(1)} %pad_maximum_fusion.17), channel_id=1, source_target_pairs={{0,8},{8,16},{16,24},{1,9},{9,17},{17,25},{2,10},{10,18},{18,26},{... | collective-permute-start | bytes 393224 | tf_op jit(solution)/shard_map/ppermute | solution.py:93
  114.9 7.0 %collective-permute-start.16 = (bf16[256,256]{0,1:T(8,128)(2,1)S(1)}, bf16[256,256]{0,1:T(8,128)(2,1)S(1)}, u32[]{:S(2)}, u32[]{:S(2)}) collective-permute-start(bf16[256,256]{0,1:T(8,128)(2,1)S(1)} %pad_maximum_fusion.18), channel_id=1, source_target_pairs={{8,0},{16,8},{24,16},{9,1},{17,9},{25,17},{10,2},{18,10},{26,18},{... | collective-permute-start | bytes 393224 | tf_op jit(solution)/shard_map/ppermute | solution.py:94
  116.2 6.5 %collective-permute-start.17 = (bf16[1024,64]{0,1:T(8,128)(2,1)S(1)}, bf16[1024,64]{0,1:T(8,128)(2,1)S(1)}, u32[]{:S(2)}, u32[]{:S(2)}) collective-permute-start(bf16[1024,64]{0,1:T(8,128)(2,1)S(1)} %get-tuple-element.26), channel_id=1, source_target_pairs={{0,1},{1,2},{2,3},{3,4},{4,5},{5,6},{6,7},{8,9},{9,10},{10,11},{11... | collective-permute-start | bytes 393224 | tf_op jit(solution)/shard_map/ppermute | solution.py:27
  120.2 6.9 %collective-permute-start.18 = (bf16[1024,64]{0,1:T(8,128)(2,1)S(1)}, bf16[1024,64]{0,1:T(8,128)(2,1)S(1)}, u32[]{:S(2)}, u32[]{:S(2)}) collective-permute-start(bf16[1024,64]{0,1:T(8,128)(2,1)S(1)} %get-tuple-element.27), channel_id=1, source_target_pairs={{1,0},{2,1},{3,2},{4,3},{5,4},{6,5},{7,6},{9,8},{10,9},{11,10},{12... | collective-permute-start | bytes 393224 | tf_op jit(solution)/shard_map/ppermute | solution.py:28
  133.4 9.7 %collective-permute-start.19 = (bf16[256,256]{0,1:T(8,128)(2,1)S(1)}, bf16[256,256]{0,1:T(8,128)(2,1)S(1)}, u32[]{:S(2)}, u32[]{:S(2)}) collective-permute-start(bf16[256,256]{0,1:T(8,128)(2,1)S(1)} %pad_maximum_fusion.19), channel_id=1, source_target_pairs={{0,8},{8,16},{16,24},{1,9},{9,17},{17,25},{2,10},{10,18},{18,26},{... | collective-permute-start | bytes 393224 | tf_op jit(solution)/shard_map/ppermute | solution.py:93
  136.4 12.5 %collective-permute-start.20 = (bf16[256,256]{0,1:T(8,128)(2,1)S(1)}, bf16[256,256]{0,1:T(8,128)(2,1)S(1)}, u32[]{:S(2)}, u32[]{:S(2)}) collective-permute-start(bf16[256,256]{0,1:T(8,128)(2,1)S(1)} %pad_maximum_fusion.20), channel_id=1, source_target_pairs={{8,0},{16,8},{24,16},{9,1},{17,9},{25,17},{10,2},{18,10},{26,18},{... | collective-permute-start | bytes 393224 | tf_op jit(solution)/shard_map/ppermute | solution.py:94
  137.8 7.0 %collective-permute-start.21 = (bf16[1024,64]{0,1:T(8,128)(2,1)S(1)}, bf16[1024,64]{0,1:T(8,128)(2,1)S(1)}, u32[]{:S(2)}, u32[]{:S(2)}) collective-permute-start(bf16[1024,64]{0,1:T(8,128)(2,1)S(1)} %get-tuple-element.24), channel_id=1, source_target_pairs={{0,1},{1,2},{2,3},{3,4},{4,5},{5,6},{6,7},{8,9},{9,10},{10,11},{11... | collective-permute-start | bytes 393224 | tf_op jit(solution)/shard_map/ppermute | solution.py:27
  141.7 6.9 %collective-permute-start.22 = (bf16[1024,64]{0,1:T(8,128)(2,1)S(1)}, bf16[1024,64]{0,1:T(8,128)(2,1)S(1)}, u32[]{:S(2)}, u32[]{:S(2)}) collective-permute-start(bf16[1024,64]{0,1:T(8,128)(2,1)S(1)} %get-tuple-element.25), channel_id=1, source_target_pairs={{1,0},{2,1},{3,2},{4,3},{5,4},{6,5},{7,6},{9,8},{10,9},{11,10},{12... | collective-permute-start | bytes 393224 | tf_op jit(solution)/shard_map/ppermute | solution.py:28

commit v10 on v8

--- a/solution.py
+++ b/solution.py
@@ -111,21 +111,20 @@
     coef_rows = svc_all[shift * nodes_dev + obs_cell // T_DEV]
     eta = jnp.einsum("rc,rc->r", covariates, coef_rows, preferred_element_type=jnp.float32)
     obs_weight = jnp.exp(eta)
-    node_ids = owner * nodes_dev + obs_cell // T_DEV
-    onehot = (node_ids[:, None] == jnp.arange(space_count * nodes_dev)[None, :]).astype(jnp.bfloat16)
+    onehot = (obs_cell[:, None] // T_DEV == jnp.arange(nodes_dev)[None, :]).astype(jnp.bfloat16)
     high = lax.reduce_precision(obs_weight, exponent_bits=8, mantissa_bits=7)
     rest = obs_weight - high
     middle = lax.reduce_precision(rest, exponent_bits=8, mantissa_bits=7)
     low = rest - middle
-    in_step = obs_cell[:, None] % T_DEV == jnp.arange(T_DEV)[None, :]
+    slot = owner * T_DEV + obs_cell % T_DEV
+    in_slot = slot[:, None] == jnp.arange(space_count * T_DEV)[None, :]
     parts = jnp.concatenate(
-        [jnp.where(in_step, piece[:, None], 0.0) for piece in (high, middle, low)], axis=1
+        [jnp.where(in_slot, piece[:, None], 0.0) for piece in (high, middle, low)], axis=1
     ).astype(jnp.bfloat16)
     sums = lax.dot_general(
         parts, onehot, (((0,), (0,)), ((), ())), preferred_element_type=jnp.float32
-    )
-    step_counts = sums[:T_DEV] + sums[T_DEV : 2 * T_DEV] + sums[2 * T_DEV :]
-    local_counts = step_counts.reshape(T_DEV, space_count, nodes_dev).transpose(1, 0, 2)
+    ).reshape(3, space_count, T_DEV, nodes_dev)
+    local_counts = sums[0] + sums[1] + sums[2]
     counted = jnp.sum(
         lax.all_to_all(local_counts, "space", split_axis=0, concat_axis=0, tiled=True), axis=0
     )

time: 159 us -> 154 us (0.969)
  matrix products: 27 us -> 22.7 us
    dot_general x1, matrix products: 6 us -> 1.71 us  [shards(): lax.dot_general(parts, onehot, (((0,), (0,)), ((), ())), preferred_elemen...]
  transfers between devices with their start and end apart: 26 -> 26, of which waited for: 8 -> 8; matrix products, arithmetic and copies ran while one was open for 30% -> 28% of each run, Pallas kernels for 0% -> 0%
where the time goes in v10:
time: 154 us; the launch traced here: 153 us
  starting transfers between devices  65 us (42%)
  local copies, waits for them, and re-layouts  22.9 us (15%)
  matrix products  22.7 us (15%)
  waiting for transfers between devices  21.4 us (14%)
  other arithmetic  11.3 us (7%)
  blocking collectives  5.76 us (4%)
  between operations  3.97 us (3%)
    ppermute x5, starting transfers between devices, with_halo(): before = lax.ppermute(last, axis, up)  20.8 us
    ppermute x5, starting transfers between devices, spatial(): lower = lax.ppermute(pick_blocks(field, upper_wants), 'space', up)  19.1 us
    ppermute x5, waiting for transfers between devices, with_halo(): after = lax.ppermute(initial, axis, down)  14.1 us
    gather x1, local copies, waits for them, and re-layouts, shards(): coef_rows = svc_all[shift * nodes_dev + obs_cell // T_DEV]  10.4 us
    dot_general x5, matrix products, spatial(): jnp.dot(upper.T, upper_t, preferred_element_type=jnp.float32)  7.54 us
    ppermute x5, starting transfers between devices, with_halo(): after = lax.ppermute(initial, axis, down)  6.64 us
    ppermute x5, starting transfers between devices, spatial(): upper = lax.ppermute(pick_blocks(field, lower_wants), 'space', down)  6.44 us
    unnamed x17, local copies, waits for them, and re-layouts  6.38 us
  transfers between devices with their start and end apart: 26, of which 8 were waited for; matrix products, arithmetic and copies ran while one was open for 28% of the time, Pallas kernels for 0%

profile of v10, /device:TPU:0, one launch (start us, length us, event | category | flops | bytes accessed | tf_op | source)
XLA Modules:
  0.0 153.0 jit_solution(14893584213222322028)
XLA Ops:
  1.2 2.6 %collective-permute-start.7 = (bf16[1024,256]{1,0:T(8,128)(2,1)}, bf16[1024,256]{1,0:T(8,128)(2,1)}, u32[]{:S(2)}, u32[]{:S(2)}) collective-permute-start(bf16[1024,256]{1,0:T(8,128)(2,1)} %param.23), channel_id=1, source_target_pairs={{0,16},{8,24},{16,0},{24,8},{1,17},{9,25},{17,1},{25,9},{2,18},{10... | collective-permute-start | bytes 1572872 | tf_op jit(solution)/shard_map/ppermute | solution.py:105
  3.8 1.4 collective-permute-start.8
  5.2 0.8 fusion.92
  6.0 1.3 collective-permute-start
  7.3 3.0 %collective-permute-start.2 = (s32[2]{0:T(128)S(1)}, s32[2]{0:T(128)S(1)}, u32[]{:S(2)}, u32[]{:S(2)}) collective-permute-start(s32[2]{0:T(128)S(1)} %get-tuple-element.53), channel_id=1, source_target_pairs={{0,8},{8,16},{16,24},{1,9},{9,17},{17,25},{2,10},{10,18},{18,26},{... | collective-permute-start | bytes 32 | tf_op jit(solution)/shard_map/ppermute | solution.py:75
  10.3 1.2 copy.27
  11.6 0.7 broadcast_in_dim.67
  12.4 0.7 broadcast_in_dim.64
  13.2 1.0 convert_element_type.83
  14.2 1.1 select_reduce_fusion
  15.3 1.1 fusion.57
  16.4 2.2 %add_convert_fusion = bf16[8,12,128,128]{3,1,2,0:T(8,128)(2,1)S(1)} fusion(f32[8,128,128]{2,1,0:T(8,128)S(1)} %convert_element_type.83, f32[8,12]{1,0:T(8,128)S(1)} %fusion.83, bf16[8,8,128,128]{3,2,1,0:T(8,128)(2,1)S(1)} %copy-done, s32[8,8]{1,0:T(8,128)S(1)} %copy-done.6), kind=kOutput, calls=%fused_computation.2 | convolution fusion | flops 29885184 | bytes 5767808 | tf_op jit(solution)/shard_map/bkm,bkij->bimj/dot_general | solution.py:63
  18.7 1.6 %copy.51 = bf16[128,8,12,128]{3,1,2,0:T(8,128)(2,1)S(1)} copy(bf16[128,8,12,128]{3,2,1,0:T(8,128)(2,1)S(1)} %bitcast.48) | data formatting | bytes 6291456
  20.3 0.7 fusion.90
  21.0 1.0 copy-done.1
  22.0 1.7 %fusion.39 = f32[1024,256]{0,1:T(8,128)} fusion(bf16[1024,256]{0,1:T(8,128)(2,1)S(1)} %fusion.57, bf16[1024,1536]{1,0:T(8,128)(2,1)S(1)} %bitcast.49), kind=kOutput, calls=%fused_computation.68 | convolution fusion | flops 536870912 | bytes 3670016 | tf_op jit(solution)/shard_map/dot_general | solution.py:86
  23.8 4.1 %collective-permute-start.4 = (bf16[1024,64]{0,1:T(8,128)(2,1)}, bf16[1024,64]{0,1:T(8,128)(2,1)}, u32[]{:S(2)}, u32[]{:S(2)}) collective-permute-start(bf16[1024,64]{0,1:T(8,128)(2,1)} %get-tuple-element.32), channel_id=1, source_target_pairs={{0,1},{1,2},{2,3},{3,4},{4,5},{5,6},{6,7},{8,9},{9,10},{10,11},{11... | collective-permute-start | bytes 393224 | tf_op jit(solution)/shard_map/ppermute | solution.py:27
  29.7 1.3 collective-permute-start.5
  33.1 6.3 %collective-permute-start.1 = (bf16[256,256]{0,1:T(8,128)(2,1)S(1)}, bf16[256,256]{0,1:T(8,128)(2,1)}, u32[]{:S(2)}, u32[]{:S(2)}) collective-permute-start(bf16[256,256]{0,1:T(8,128)(2,1)S(1)} %pad_maximum_fusion.11), channel_id=1, source_target_pairs={{0,8},{8,16},{16,24},{1,9},{9,17},{17,25},{2,10},{10,18},{18,26},{... | collective-permute-start | bytes 393224 | tf_op jit(solution)/shard_map/ppermute | solution.py:84
  39.4 1.3 collective-permute-start.3
  40.7 3.0 %pad_maximum_fusion = bf16[4096,256]{1,0:T(8,128)(2,1)} fusion(bf16[1024,256]{1,0:T(8,128)(2,1)} %collective-permute-done.8, bf16[1024,256]{1,0:T(8,128)(2,1)} %collective-permute-done.7, bf16[1024,256]{1,0:T(8,128)(2,1)} %collective-permute-done.6, bf16[1024,256]{1,0:T(8,128)(2,1)} %param.23), kind=kLoop, calls=%fused_computation.13 | loop fusion | flops 8388608 | bytes 4194304 | tf_op jit(solution)/shard_map/concatenate | solution.py:108
  43.7 10.4 %gather_fusion = bf16[2048,256]{1,0:T(8,128)(2,1)} fusion(bf16[4096,256]{1,0:T(8,128)(2,1)} %pad_maximum_fusion, s32[2048]{0:T(1024)S(1)} %get-tuple-element.47), kind=kCustom, calls=%fused_computation | custom fusion | bytes 2105344 | tf_op jit(solution)/shard_map/gather | solution.py:111
  54.0 1.9 %fusion.2 = f32[2048]{0:T(1024)S(1)} fusion(bf16[2048,256]{1,0:T(8,128)(2,1)} %gather_fusion, bf16[2048,256]{1,0:T(8,128)(2,1)} %param.20), kind=kLoop, calls=%fused_computation.15 | loop fusion | flops 2095104 | bytes 2105344 | tf_op jit(solution)/shard_map/rc,rc->r/dot_general | solution.py:112
  56.0 1.7 %fusion = f32[48,1024]{1,0:T(8,128)S(1)} fusion(s32[2048]{0:T(1024)S(1)} %get-tuple-element.48, bf16[2048,16]{0,1:T(8,128)(2,1)S(1)} %get-tuple-element.41, bf16[2048,16]{0,1:T(8,128)(2,1)S(1)} %get-tuple-element.42, bf16[2048,16]{0,1:T(8,128)(2,1)S(1)} %get-tuple-element.40), kind=kOutput, calls=%fused_computation.3 | convolution fusion | flops 204013568 | bytes 401408 | tf_op jit(solution)/shard_map/dot_general | solution.py:124
  58.4 3.3 %all-to-all-start = ((f32[4,4,1024]{2,1,0:T(4,128)}), f32[4,4,1024]{2,1,0:T(4,128)S(1)}, u32[]{:S(2)}, u32[]{:S(2)}) async-start(f32[4,4,1024]{2,1,0:T(4,128)} %add.190), calls=%async_computation | async-start | bytes 131072 | tf_op jit(solution)/shard_map/all_to_all | solution.py:129
  61.7 2.7 %convolution_add_fusion.9 = f32[1024,256]{0,1:T(8,128)} fusion(f32[1024,256]{0,1:T(8,128)} %fusion.39, bf16[256,256]{0,1:T(8,128)(2,1)} %collective-permute-done.1, bf16[1024,1536]{1,0:T(8,128)(2,1)} %bitcast.50), kind=kOutput, calls=%fused_computation.44 | convolution fusion | flops 134479872 | bytes 2752512 | tf_op jit(solution)/shard_map/dot_general | solution.py:87
  64.4 1.3 all-to-all-done
  66.2 2.7 %fusion.94 = (bf16[1024,256]{0,1:T(8,128)(2,1)S(1)}, f32[1024,256]{0,1:T(8,128)S(1)}) fusion(f32[1024,256]{0,1:T(8,128)S(1)} %get-tuple-element.39, f32[1024,256]{0,1:T(8,128)S(1)} %get-tuple-element.38, bf16[1024,64]{0,1:T(8,128)(2,1)} %collective-permute-done.5, bf16[1024,256]{0,1:T(8,128)(2,1)S(1)} %fusion.57, ...), kind=kOutput, calls=%fused_computation.191 | convolution fusion | flops 141557760 | bytes 6695936 | tf_op jit(solution)/shard_map/dot_general | solution.py:88
  69.0 0.7 fusion.37
  69.9 1.3 collective-permute-start.10
  71.2 3.0 %collective-permute-start.9 = (bf16[256,256]{0,1:T(8,128)(2,1)S(1)}, bf16[256,256]{0,1:T(8,128)(2,1)S(1)}, u32[]{:S(2)}, u32[]{:S(2)}) collective-permute-start(bf16[256,256]{0,1:T(8,128)(2,1)S(1)} %pad_maximum_fusion.13), channel_id=1, source_target_pairs={{0,8},{8,16},{16,24},{1,9},{9,17},{17,25},{2,10},{10,18},{18,26},{... | collective-permute-start | bytes 393224 | tf_op jit(solution)/shard_map/ppermute | solution.py:84
  74.3 4.3 %collective-permute-start.11 = (bf16[1024,64]{0,1:T(8,128)(2,1)S(1)}, bf16[1024,64]{0,1:T(8,128)(2,1)S(1)}, u32[]{:S(2)}, u32[]{:S(2)}) collective-permute-start(bf16[1024,64]{0,1:T(8,128)(2,1)S(1)} %get-tuple-element.26), channel_id=1, source_target_pairs={{0,1},{1,2},{2,3},{3,4},{4,5},{5,6},{6,7},{8,9},{9,10},{10,11},{11... | collective-permute-start | bytes 393224 | tf_op jit(solution)/shard_map/ppermute | solution.py:27
  78.6 1.5 collective-permute-start.12
  80.4 2.0 %collective-permute-done.11 = bf16[1024,64]{0,1:T(8,128)(2,1)S(1)} collective-permute-done((bf16[1024,64]{0,1:T(8,128)(2,1)S(1)}, bf16[1024,64]{0,1:T(8,128)(2,1)S(1)}, u32[]{:S(2)}, u32[]{:S(2)}) %collective-permute-start.11) | collective-permute-done | bytes 131104 | tf_op jit(solution)/shard_map/ppermute | solution.py:27
  82.4 4.3 %collective-permute-done.12 = bf16[1024,64]{0,1:T(8,128)(2,1)S(1)} collective-permute-done((bf16[1024,64]{0,1:T(8,128)(2,1)S(1)}, bf16[1024,64]{0,1:T(8,128)(2,1)S(1)}, u32[]{:S(2)}, u32[]{:S(2)}) %collective-permute-start.12) | collective-permute-done | bytes 131104 | tf_op jit(solution)/shard_map/ppermute | solution.py:28
  86.6 0.8 fusion.95
  87.5 0.7 fusion.35
  88.4 1.3 collective-permute-start.14
  89.8 3.0 %collective-permute-start.13 = (bf16[256,256]{0,1:T(8,128)(2,1)S(1)}, bf16[256,256]{0,1:T(8,128)(2,1)S(1)}, u32[]{:S(2)}, u32[]{:S(2)}) collective-permute-start(bf16[256,256]{0,1:T(8,128)(2,1)S(1)} %pad_maximum_fusion.15), channel_id=1, source_target_pairs={{0,8},{8,16},{16,24},{1,9},{9,17},{17,25},{2,10},{10,18},{18,26},{... | collective-permute-start | bytes 393224 | tf_op jit(solution)/shard_map/ppermute | solution.py:84
  92.8 4.5 %collective-permute-start.15 = (bf16[1024,64]{0,1:T(8,128)(2,1)S(1)}, bf16[1024,64]{0,1:T(8,128)(2,1)S(1)}, u32[]{:S(2)}, u32[]{:S(2)}) collective-permute-start(bf16[1024,64]{0,1:T(8,128)(2,1)S(1)} %get-tuple-element.20), channel_id=1, source_target_pairs={{0,1},{1,2},{2,3},{3,4},{4,5},{5,6},{6,7},{8,9},{9,10},{10,11},{11... | collective-permute-start | bytes 393224 | tf_op jit(solution)/shard_map/ppermute | solution.py:27
  97.4 1.3 collective-permute-start.16
  99.0 2.1 %collective-permute-done.15 = bf16[1024,64]{0,1:T(8,128)(2,1)S(1)} collective-permute-done((bf16[1024,64]{0,1:T(8,128)(2,1)S(1)}, bf16[1024,64]{0,1:T(8,128)(2,1)S(1)}, u32[]{:S(2)}, u32[]{:S(2)}) %collective-permute-start.15) | collective-permute-done | bytes 131104 | tf_op jit(solution)/shard_map/ppermute | solution.py:27
  101.1 4.4 %collective-permute-done.16 = bf16[1024,64]{0,1:T(8,128)(2,1)S(1)} collective-permute-done((bf16[1024,64]{0,1:T(8,128)(2,1)S(1)}, bf16[1024,64]{0,1:T(8,128)(2,1)S(1)}, u32[]{:S(2)}, u32[]{:S(2)}) %collective-permute-start.16) | collective-permute-done | bytes 131104 | tf_op jit(solution)/shard_map/ppermute | solution.py:28
  105.5 0.8 fusion.96
  106.4 0.7 fusion.33
  107.3 1.3 collective-permute-start.18
  108.6 3.0 %collective-permute-start.17 = (bf16[256,256]{0,1:T(8,128)(2,1)S(1)}, bf16[256,256]{0,1:T(8,128)(2,1)S(1)}, u32[]{:S(2)}, u32[]{:S(2)}) collective-permute-start(bf16[256,256]{0,1:T(8,128)(2,1)S(1)} %pad_maximum_fusion.17), channel_id=1, source_target_pairs={{0,8},{8,16},{16,24},{1,9},{9,17},{17,25},{2,10},{10,18},{18,26},{... | collective-permute-start | bytes 393224 | tf_op jit(solution)/shard_map/ppermute | solution.py:84
  111.7 4.0 %collective-permute-start.19 = (bf16[1024,64]{0,1:T(8,128)(2,1)S(1)}, bf16[1024,64]{0,1:T(8,128)(2,1)S(1)}, u32[]{:S(2)}, u32[]{:S(2)}) collective-permute-start(bf16[1024,64]{0,1:T(8,128)(2,1)S(1)} %get-tuple-element.14), channel_id=1, source_target_pairs={{0,1},{1,2},{2,3},{3,4},{4,5},{5,6},{6,7},{8,9},{9,10},{10,11},{11... | collective-permute-start | bytes 393224 | tf_op jit(solution)/shard_map/ppermute | solution.py:27
  115.7 1.3 collective-permute-start.20
  117.3 1.8 %collective-permute-done.19 = bf16[1024,64]{0,1:T(8,128)(2,1)S(1)} collective-permute-done((bf16[1024,64]{0,1:T(8,128)(2,1)S(1)}, bf16[1024,64]{0,1:T(8,128)(2,1)S(1)}, u32[]{:S(2)}, u32[]{:S(2)}) %collective-permute-start.19) | collective-permute-done | bytes 131104 | tf_op jit(solution)/shard_map/ppermute | solution.py:27
  119.1 4.7 %collective-permute-done.20 = bf16[1024,64]{0,1:T(8,128)(2,1)S(1)} collective-permute-done((bf16[1024,64]{0,1:T(8,128)(2,1)S(1)}, bf16[1024,64]{0,1:T(8,128)(2,1)S(1)}, u32[]{:S(2)}, u32[]{:S(2)}) %collective-permute-start.20) | collective-permute-done | bytes 131104 | tf_op jit(solution)/shard_map/ppermute | solution.py:28
  123.8 1.8 %fusion.97 = (bf16[1024,256]{0,1:T(8,128)(2,1)S(1)}, f32[1024,256]{0,1:T(8,128)}) fusion(f32[1024,256]{0,1:T(8,128)S(1)} %get-tuple-element.62, f32[1024,256]{0,1:T(8,128)S(1)} %get-tuple-element.39, f32[1024,256]{0,1:T(8,128)S(1)} %fusion.4, bf16[1024,64]{0,1:T(8,128)(2,1)S(1)} %collective-permute-done.20, bf16[1024,256]{0,1:T(8,128)(2,1)S(1)} %get-tuple-element.61, ...), kind=kOutput, calls=%fused_computation.194 | convolution fusion | flops 140247040 | bytes 7735296 | tf_op jit(solution)/shard_map/dot_general | solution.py:88
  125.7 1.7 %fusion.41 = f32[1024,256]{0,1:T(8,128)} fusion(bf16[1024,256]{0,1:T(8,128)(2,1)S(1)} %get-tuple-element.63, bf16[1024,1536]{1,0:T(8,128)(2,1)S(1)} %bitcast.63), kind=kOutput, calls=%fused_computation.70 | convolution fusion | flops 536870912 | bytes 3670016 | tf_op jit(solution)/shard_map/dot_general | solution.py:86
  127.4 0.7 pad_maximum_fusion.20
  128.1 1.3 collective-permute-start.22
  130.1 3.7 %collective-permute-start.21 = (bf16[256,256]{0,1:T(8,128)(2,1)}, bf16[256,256]{0,1:T(8,128)(2,1)}, u32[]{:S(2)}, u32[]{:S(2)}) collective-permute-start(bf16[256,256]{0,1:T(8,128)(2,1)} %pad_maximum_fusion.19), channel_id=1, source_target_pairs={{0,8},{8,16},{16,24},{1,9},{9,17},{17,25},{2,10},{10,18},{18,26},{... | collective-permute-start | bytes 393224 | tf_op jit(solution)/shard_map/ppermute | solution.py:84
  133.8 0.7 fusion.86
  134.5 3.9 %collective-permute-start.23 = (bf16[1024,64]{0,1:T(8,128)(2,1)}, bf16[1024,64]{0,1:T(8,128)(2,1)S(1)}, u32[]{:S(2)}, u32[]{:S(2)}) collective-permute-start(bf16[1024,64]{0,1:T(8,128)(2,1)} %get-tuple-element.12), channel_id=1, source_target_pairs={{0,1},{1,2},{2,3},{3,4},{4,5},{5,6},{6,7},{8,9},{9,10},{10,11},{11... | collective-permute-start | bytes 393224 | tf_op jit(solution)/shard_map/ppermute | solution.py:27
  138.4 1.3 collective-permute-start.24
  139.7 2.5 %copy.33 = f32[1024,256]{1,0:T(8,128)} copy(f32[1024,256]{0,1:T(8,128)} %get-tuple-element.64) | data formatting | bytes 2097152
  142.2 1.8 %convolution_add_fusion.1 = f32[1024,256]{0,1:T(8,128)S(1)} fusion(f32[1024,256]{0,1:T(8,128)} %fusion.41, bf16[256,256]{0,1:T(8,128)(2,1)} %collective-permute-done.21, bf16[1024,1536]{1,0:T(8,128)(2,1)} %bitcast.52), kind=kOutput, calls=%fused_computation.24 | convolution fusion | flops 134479872 | bytes 2752512 | tf_op jit(solution)/shard_map/dot_general | solution.py:87
  144.0 1.5 fusion.32
  145.5 0.8 collective-permute-done.24
  146.7 5.8 %psum.7 = f32[2,256]{1,0:T(2,128)S(1)} all-reduce(f32[2,256]{1,0:T(2,128)S(1)} %pad_maximum_fusion.21), channel_id=1, replica_groups=mesh['space'=4,'tm'=8] {'space'}, use_global_device_ids=true, to_apply=%region_4.5 | all-reduce | flops 512 | bytes 4096 | tf_op jit(solution)/shard_map/psum | solution.py:155
  (73 shorter events, 6.7 us)
Async XLA Ops:
  0.6 15.8 %copy-start = (bf16[8,8,128,128]{3,2,1,0:T(8,128)(2,1)S(1)}, bf16[8,8,128,128]{3,2,1,0:T(8,128)(2,1)}, u32[]{:S(2)}) copy-start(bf16[8,8,128,128]{3,2,1,0:T(8,128)(2,1)} %param.17) | copy-start | bytes 6291460
  0.6 15.7 %copy-start.6 = (s32[8,8]{1,0:T(8,128)S(1)}, s32[8,8]{1,0:T(8,128)}, u32[]{:S(2)}) copy-start(s32[8,8]{1,0:T(8,128)} %param.18) | copy-start | bytes 772
  0.7 32.4 %collective-permute-start.6 = (bf16[1024,256]{1,0:T(8,128)(2,1)}, bf16[1024,256]{1,0:T(8,128)(2,1)}, u32[]{:S(2)}, u32[]{:S(2)}) collective-permute-start(bf16[1024,256]{1,0:T(8,128)(2,1)} %param.23), channel_id=1, source_target_pairs={{0,8},{8,16},{16,24},{24,0},{1,9},{9,17},{17,25},{25,1},{2,10},{10... | collective-permute-start | bytes 1572872 | tf_op jit(solution)/shard_map/ppermute | solution.py:105
  1.2 38.2 %collective-permute-start.7 = (bf16[1024,256]{1,0:T(8,128)(2,1)}, bf16[1024,256]{1,0:T(8,128)(2,1)}, u32[]{:S(2)}, u32[]{:S(2)}) collective-permute-start(bf16[1024,256]{1,0:T(8,128)(2,1)} %param.23), channel_id=1, source_target_pairs={{0,16},{8,24},{16,0},{24,8},{1,17},{9,25},{17,1},{25,9},{2,18},{10... | collective-permute-start | bytes 1572872 | tf_op jit(solution)/shard_map/ppermute | solution.py:105
  3.8 36.9 %collective-permute-start.8 = (bf16[1024,256]{1,0:T(8,128)(2,1)}, bf16[1024,256]{1,0:T(8,128)(2,1)}, u32[]{:S(2)}, u32[]{:S(2)}) collective-permute-start(bf16[1024,256]{1,0:T(8,128)(2,1)} %param.23), channel_id=1, source_target_pairs={{0,24},{8,0},{16,8},{24,16},{1,25},{9,1},{17,9},{25,17},{2,26},{10... | collective-permute-start | bytes 1572872 | tf_op jit(solution)/shard_map/ppermute | solution.py:105
  6.0 17.8 %collective-permute-start = (s32[2]{0:T(128)S(1)}, s32[2]{0:T(128)S(1)}, u32[]{:S(2)}, u32[]{:S(2)}) collective-permute-start(s32[2]{0:T(128)S(1)} %get-tuple-element.54), channel_id=1, source_target_pairs={{8,0},{16,8},{24,16},{9,1},{17,9},{25,17},{10,2},{18,10},{26,18},{... | collective-permute-start | bytes 32 | tf_op jit(solution)/shard_map/ppermute | solution.py:74
  7.3 22.5 %collective-permute-start.2 = (s32[2]{0:T(128)S(1)}, s32[2]{0:T(128)S(1)}, u32[]{:S(2)}, u32[]{:S(2)}) collective-permute-start(s32[2]{0:T(128)S(1)} %get-tuple-element.53), channel_id=1, source_target_pairs={{0,8},{8,16},{16,24},{1,9},{9,17},{17,25},{2,10},{10,18},{18,26},{... | collective-permute-start | bytes 32 | tf_op jit(solution)/shard_map/ppermute | solution.py:75
  20.3 1.7 %copy-start.1 = (bf16[128,8,12,128]{3,1,2,0:T(8,128)(2,1)}, bf16[128,8,12,128]{3,1,2,0:T(8,128)(2,1)S(1)}, u32[]{:S(2)}) copy-start(bf16[128,8,12,128]{3,1,2,0:T(8,128)(2,1)S(1)} %copy.51) | copy-start | bytes 9437188
  20.3 3.4 %copy-start.4 = (s32[2048,1]{0,1:T(1,128)S(1)}, s32[2048,1]{0,1:T(1,128)}, u32[]{:S(2)}) copy-start(s32[2048,1]{0,1:T(1,128)} %param.21) | copy-start | bytes 24580
  20.3 3.5 %copy-start.5 = (s32[2048]{0:T(1024)S(1)}, s32[2048]{0:T(1024)}, u32[]{:S(2)}) copy-start(s32[2048]{0:T(1024)} %param.22) | copy-start | bytes 24580
  23.8 42.4 %collective-permute-start.4 = (bf16[1024,64]{0,1:T(8,128)(2,1)}, bf16[1024,64]{0,1:T(8,128)(2,1)}, u32[]{:S(2)}, u32[]{:S(2)}) collective-permute-start(bf16[1024,64]{0,1:T(8,128)(2,1)} %get-tuple-element.32), channel_id=1, source_target_pairs={{0,1},{1,2},{2,3},{3,4},{4,5},{5,6},{6,7},{8,9},{9,10},{10,11},{11... | collective-permute-start | bytes 393224 | tf_op jit(solution)/shard_map/ppermute | solution.py:27
  29.7 36.4 %collective-permute-start.5 = (bf16[1024,64]{0,1:T(8,128)(2,1)}, bf16[1024,64]{0,1:T(8,128)(2,1)}, u32[]{:S(2)}, u32[]{:S(2)}) collective-permute-start(bf16[1024,64]{0,1:T(8,128)(2,1)} %get-tuple-element.33), channel_id=1, source_target_pairs={{1,0},{2,1},{3,2},{4,3},{5,4},{6,5},{7,6},{9,8},{10,9},{11,10},{12... | collective-permute-start | bytes 393224 | tf_op jit(solution)/shard_map/ppermute | solution.py:28
  33.1 28.6 %collective-permute-start.1 = (bf16[256,256]{0,1:T(8,128)(2,1)S(1)}, bf16[256,256]{0,1:T(8,128)(2,1)}, u32[]{:S(2)}, u32[]{:S(2)}) collective-permute-start(bf16[256,256]{0,1:T(8,128)(2,1)S(1)} %pad_maximum_fusion.11), channel_id=1, source_target_pairs={{0,8},{8,16},{16,24},{1,9},{9,17},{17,25},{2,10},{10,18},{18,26},{... | collective-permute-start | bytes 393224 | tf_op jit(solution)/shard_map/ppermute | solution.py:84
  39.4 26.8 %collective-permute-start.3 = (bf16[256,256]{0,1:T(8,128)(2,1)S(1)}, bf16[256,256]{0,1:T(8,128)(2,1)}, u32[]{:S(2)}, u32[]{:S(2)}) collective-permute-start(bf16[256,256]{0,1:T(8,128)(2,1)S(1)} %pad_maximum_fusion.12), channel_id=1, source_target_pairs={{8,0},{16,8},{24,16},{9,1},{17,9},{25,17},{10,2},{18,10},{26,18},{... | collective-permute-start | bytes 393224 | tf_op jit(solution)/shard_map/ppermute | solution.py:85
  56.0 9.8 %copy-start.3 = (f32[1024]{0:T(1024)S(1)}, f32[1024]{0:T(1024)}, u32[]{:S(2)}) copy-start(f32[1024]{0:T(1024)} %param.13) | copy-start | bytes 12292
  58.4 7.4 %all-to-all-start = ((f32[4,4,1024]{2,1,0:T(4,128)}), f32[4,4,1024]{2,1,0:T(4,128)S(1)}, u32[]{:S(2)}, u32[]{:S(2)}) async-start(f32[4,4,1024]{2,1,0:T(4,128)} %add.190), calls=%async_computation | async-start | bytes 131072 | tf_op jit(solution)/shard_map/all_to_all | solution.py:129
  66.2 2.8 %copy-start.2 = (bf16[128,8,12,128]{3,1,2,0:T(8,128)(2,1)S(1)}, bf16[128,8,12,128]{3,1,2,0:T(8,128)(2,1)}, u32[]{:S(2)}) copy-start(bf16[128,8,12,128]{3,1,2,0:T(8,128)(2,1)} %copy-done.1) | copy-start | bytes 9437188
  69.9 10.5 %collective-permute-start.10 = (bf16[256,256]{0,1:T(8,128)(2,1)S(1)}, bf16[256,256]{0,1:T(8,128)(2,1)S(1)}, u32[]{:S(2)}, u32[]{:S(2)}) collective-permute-start(bf16[256,256]{0,1:T(8,128)(2,1)S(1)} %pad_maximum_fusion.14), channel_id=1, source_target_pairs={{8,0},{16,8},{24,16},{9,1},{17,9},{25,17},{10,2},{18,10},{26,18},{... | collective-permute-start | bytes 393224 | tf_op jit(solution)/shard_map/ppermute | solution.py:85
  71.2 8.9 %collective-permute-start.9 = (bf16[256,256]{0,1:T(8,128)(2,1)S(1)}, bf16[256,256]{0,1:T(8,128)(2,1)S(1)}, u32[]{:S(2)}, u32[]{:S(2)}) collective-permute-start(bf16[256,256]{0,1:T(8,128)(2,1)S(1)} %pad_maximum_fusion.13), channel_id=1, source_target_pairs={{0,8},{8,16},{16,24},{1,9},{9,17},{17,25},{2,10},{10,18},{18,26},{... | collective-permute-start | bytes 393224 | tf_op jit(solution)/shard_map/ppermute | solution.py:84
  74.3 8.1 %collective-permute-start.11 = (bf16[1024,64]{0,1:T(8,128)(2,1)S(1)}, bf16[1024,64]{0,1:T(8,128)(2,1)S(1)}, u32[]{:S(2)}, u32[]{:S(2)}) collective-permute-start(bf16[1024,64]{0,1:T(8,128)(2,1)S(1)} %get-tuple-element.26), channel_id=1, source_target_pairs={{0,1},{1,2},{2,3},{3,4},{4,5},{5,6},{6,7},{8,9},{9,10},{10,11},{11... | collective-permute-start | bytes 393224 | tf_op jit(solution)/shard_map/ppermute | solution.py:27
  78.6 8.1 %collective-permute-start.12 = (bf16[1024,64]{0,1:T(8,128)(2,1)S(1)}, bf16[1024,64]{0,1:T(8,128)(2,1)S(1)}, u32[]{:S(2)}, u32[]{:S(2)}) collective-permute-start(bf16[1024,64]{0,1:T(8,128)(2,1)S(1)} %get-tuple-element.27), channel_id=1, source_target_pairs={{1,0},{2,1},{3,2},{4,3},{5,4},{6,5},{7,6},{9,8},{10,9},{11,10},{12... | collective-permute-start | bytes 393224 | tf_op jit(solution)/shard_map/ppermute | solution.py:28
  88.4 10.6 %collective-permute-start.14 = (bf16[256,256]{0,1:T(8,128)(2,1)S(1)}, bf16[256,256]{0,1:T(8,128)(2,1)S(1)}, u32[]{:S(2)}, u32[]{:S(2)}) collective-permute-start(bf16[256,256]{0,1:T(8,128)(2,1)S(1)} %pad_maximum_fusion.16), channel_id=1, source_target_pairs={{8,0},{16,8},{24,16},{9,1},{17,9},{25,17},{10,2},{18,10},{26,18},{... | collective-permute-start | bytes 393224 | tf_op jit(solution)/shard_map/ppermute | solution.py:85
  89.8 8.9 %collective-permute-start.13 = (bf16[256,256]{0,1:T(8,128)(2,1)S(1)}, bf16[256,256]{0,1:T(8,128)(2,1)S(1)}, u32[]{:S(2)}, u32[]{:S(2)}) collective-permute-start(bf16[256,256]{0,1:T(8,128)(2,1)S(1)} %pad_maximum_fusion.15), channel_id=1, source_target_pairs={{0,8},{8,16},{16,24},{1,9},{9,17},{17,25},{2,10},{10,18},{18,26},{... | collective-permute-start | bytes 393224 | tf_op jit(solution)/shard_map/ppermute | solution.py:84
  92.8 8.3 %collective-permute-start.15 = (bf16[1024,64]{0,1:T(8,128)(2,1)S(1)}, bf16[1024,64]{0,1:T(8,128)(2,1)S(1)}, u32[]{:S(2)}, u32[]{:S(2)}) collective-permute-start(bf16[1024,64]{0,1:T(8,128)(2,1)S(1)} %get-tuple-element.20), channel_id=1, source_target_pairs={{0,1},{1,2},{2,3},{3,4},{4,5},{5,6},{6,7},{8,9},{9,10},{10,11},{11... | collective-permute-start | bytes 393224 | tf_op jit(solution)/shard_map/ppermute | solution.py:27
  97.4 8.1 %collective-permute-start.16 = (bf16[1024,64]{0,1:T(8,128)(2,1)S(1)}, bf16[1024,64]{0,1:T(8,128)(2,1)S(1)}, u32[]{:S(2)}, u32[]{:S(2)}) collective-permute-start(bf16[1024,64]{0,1:T(8,128)(2,1)S(1)} %get-tuple-element.21), channel_id=1, source_target_pairs={{1,0},{2,1},{3,2},{4,3},{5,4},{6,5},{7,6},{9,8},{10,9},{11,10},{12... | collective-permute-start | bytes 393224 | tf_op jit(solution)/shard_map/ppermute | solution.py:28
  107.3 10.1 %collective-permute-start.18 = (bf16[256,256]{0,1:T(8,128)(2,1)S(1)}, bf16[256,256]{0,1:T(8,128)(2,1)S(1)}, u32[]{:S(2)}, u32[]{:S(2)}) collective-permute-start(bf16[256,256]{0,1:T(8,128)(2,1)S(1)} %pad_maximum_fusion.18), channel_id=1, source_target_pairs={{8,0},{16,8},{24,16},{9,1},{17,9},{25,17},{10,2},{18,10},{26,18},{... | collective-permute-start | bytes 393224 | tf_op jit(solution)/shard_map/ppermute | solution.py:85
  108.6 8.4 %collective-permute-start.17 = (bf16[256,256]{0,1:T(8,128)(2,1)S(1)}, bf16[256,256]{0,1:T(8,128)(2,1)S(1)}, u32[]{:S(2)}, u32[]{:S(2)}) collective-permute-start(bf16[256,256]{0,1:T(8,128)(2,1)S(1)} %pad_maximum_fusion.17), channel_id=1, source_target_pairs={{0,8},{8,16},{16,24},{1,9},{9,17},{17,25},{2,10},{10,18},{18,26},{... | collective-permute-start | bytes 393224 | tf_op jit(solution)/shard_map/ppermute | solution.py:84
  111.7 7.5 %collective-permute-start.19 = (bf16[1024,64]{0,1:T(8,128)(2,1)S(1)}, bf16[1024,64]{0,1:T(8,128)(2,1)S(1)}, u32[]{:S(2)}, u32[]{:S(2)}) collective-permute-start(bf16[1024,64]{0,1:T(8,128)(2,1)S(1)} %get-tuple-element.14), channel_id=1, source_target_pairs={{0,1},{1,2},{2,3},{3,4},{4,5},{5,6},{6,7},{8,9},{9,10},{10,11},{11... | collective-permute-start | bytes 393224 | tf_op jit(solution)/shard_map/ppermute | solution.py:27
  115.7 8.2 %collective-permute-start.20 = (bf16[1024,64]{0,1:T(8,128)(2,1)S(1)}, bf16[1024,64]{0,1:T(8,128)(2,1)S(1)}, u32[]{:S(2)}, u32[]{:S(2)}) collective-permute-start(bf16[1024,64]{0,1:T(8,128)(2,1)S(1)} %get-tuple-element.15), channel_id=1, source_target_pairs={{1,0},{2,1},{3,2},{4,3},{5,4},{6,5},{7,6},{9,8},{10,9},{11,10},{12... | collective-permute-start | bytes 393224 | tf_op jit(solution)/shard_map/ppermute | solution.py:28
  128.1 15.9 %collective-permute-start.22 = (bf16[256,256]{0,1:T(8,128)(2,1)}, bf16[256,256]{0,1:T(8,128)(2,1)S(1)}, u32[]{:S(2)}, u32[]{:S(2)}) collective-permute-start(bf16[256,256]{0,1:T(8,128)(2,1)} %pad_maximum_fusion.20), channel_id=1, source_target_pairs={{8,0},{16,8},{24,16},{9,1},{17,9},{25,17},{10,2},{18,10},{26,18},{... | collective-permute-start | bytes 393224 | tf_op jit(solution)/shard_map/ppermute | solution.py:85
  130.1 12.1 %collective-permute-start.21 = (bf16[256,256]{0,1:T(8,128)(2,1)}, bf16[256,256]{0,1:T(8,128)(2,1)}, u32[]{:S(2)}, u32[]{:S(2)}) collective-permute-start(bf16[256,256]{0,1:T(8,128)(2,1)} %pad_maximum_fusion.19), channel_id=1, source_target_pairs={{0,8},{8,16},{16,24},{1,9},{9,17},{17,25},{2,10},{10,18},{18,26},{... | collective-permute-start | bytes 393224 | tf_op jit(solution)/shard_map/ppermute | solution.py:84
  134.5 11.0 %collective-permute-start.23 = (bf16[1024,64]{0,1:T(8,128)(2,1)}, bf16[1024,64]{0,1:T(8,128)(2,1)S(1)}, u32[]{:S(2)}, u32[]{:S(2)}) collective-permute-start(bf16[1024,64]{0,1:T(8,128)(2,1)} %get-tuple-element.12), channel_id=1, source_target_pairs={{0,1},{1,2},{2,3},{3,4},{4,5},{5,6},{6,7},{8,9},{9,10},{10,11},{11... | collective-permute-start | bytes 393224 | tf_op jit(solution)/shard_map/ppermute | solution.py:27
  138.4 7.9 %collective-permute-start.24 = (bf16[1024,64]{0,1:T(8,128)(2,1)}, bf16[1024,64]{0,1:T(8,128)(2,1)S(1)}, u32[]{:S(2)}, u32[]{:S(2)}) collective-permute-start(bf16[1024,64]{0,1:T(8,128)(2,1)} %get-tuple-element.13), channel_id=1, source_target_pairs={{1,0},{2,1},{3,2},{4,3},{5,4},{6,5},{7,6},{9,8},{10,9},{11,10},{12... | collective-permute-start | bytes 393224 | tf_op jit(solution)/shard_map/ppermute | solution.py:28

commit v11 on v10

--- a/solution.py
+++ b/solution.py
@@ -96,6 +96,21 @@
             - arrived[:, 2 * PROBES :].astype(jnp.float32)
         )
 
+    def add_block(whole, part, block):
+        start = block * BLOCK
+        current = lax.dynamic_slice_in_dim(whole, start, BLOCK, axis=0)
+        return lax.dynamic_update_slice_in_dim(whole, current + part, start, axis=0)
+
+    probe_space = jnp.dot(own_part.T, probe_field, preferred_element_type=jnp.float32)
+    to_lower = jnp.dot(lower_part.T, probe_field, preferred_element_type=jnp.float32)
+    to_upper = jnp.dot(upper_part.T, probe_field, preferred_element_type=jnp.float32)
+    from_upper = lax.ppermute(to_lower, "space", down)
+    from_lower = lax.ppermute(to_upper, "space", up)
+    for j in range(HALO_B):
+        rows = slice(j * BLOCK, (j + 1) * BLOCK)
+        probe_space = add_block(probe_space, from_upper[rows], upper_wants[j])
+        probe_space = add_block(probe_space, from_lower[rows], lower_wants[j])
+
     solution = relaxation * probe_vals / base_diag
     rounded = lax.optimization_barrier(solution.astype(jnp.bfloat16))
     first_space = spatial(rounded)
@@ -148,7 +163,7 @@
     rounded = solution.astype(jnp.bfloat16)
     partial_sums = jnp.stack(
         [
-            jnp.sum(probe_vals * spatial(rounded), axis=0),
+            jnp.sum(probe_space * rounded.astype(jnp.float32), axis=0),
             jnp.sum(probe_vals * temporal(rounded), axis=0),
         ]
     )

time: 154 us -> 163 us (1.058)
  other arithmetic: 11.3 us -> 18.3 us
  waiting for transfers between devices: 21.4 us -> 23.9 us
  starting transfers between devices: 65 us -> 66.8 us
    ppermute x5 -> x4, starting transfers between devices: 19.1 us -> 12.3 us  [spatial(): lower = lax.ppermute(pick_blocks(field, upper_wants), 'space', up)]
    dynamic_update_slice x0 -> x4, other arithmetic: none -> 6.44 us  [add_block(): return lax.dynamic_update_slice_in_dim(whole, current + part, start, axis=0)]
    ppermute x0 -> x2, starting transfers between devices: none -> 5.83 us  [the longest x1 4.54 us: shards(): from_lower = lax.ppermute(to_upper, 'space', up)]
    dot_general x0 -> x3, matrix products: none -> 3.81 us  [the longest x1 1.74 us: shards(): jnp.dot(own_part.T, probe_field, preferred_element_type=jnp.float32)]
    all_to_all x1, starting transfers between devices: 3.28 us -> 5.69 us  [shards(): lax.all_to_all(local_counts, 'space', split_axis=0, concat_axis=0, tiled=...]
    dot_general x5 -> x4, matrix products: 5.5 us -> 3.73 us  [spatial(): jnp.dot(lower.T, lower_t, preferred_element_type=jnp.float32)]
    dot_general x5 -> x4, matrix products: 5.66 us -> 3.91 us  [spatial(): total = jnp.dot(field.T, own_t, preferred_element_type=jnp.float32)]
    dot_general x5 -> x4, matrix products: 7.54 us -> 6.02 us  [spatial(): jnp.dot(upper.T, upper_t, preferred_element_type=jnp.float32)]
  transfers between devices with their start and end apart: 26 -> 26, of which waited for: 8 -> 9; matrix products, arithmetic and copies ran while one was open for 28% -> 31% of each run, Pallas kernels for 0% -> 0%
where the time goes in v11:
time: 163 us; the launch traced here: 162 us
  starting transfers between devices  66.8 us (41%)
  waiting for transfers between devices  23.9 us (15%)
  local copies, waits for them, and re-layouts  21.9 us (13%)
  matrix products  21.4 us (13%)
  other arithmetic  18.3 us (11%)
  blocking collectives  5.76 us (4%)
  between operations  3.89 us (2%)
    ppermute x5, starting transfers between devices, with_halo(): before = lax.ppermute(last, axis, up)  22.4 us
    ppermute x5, waiting for transfers between devices, with_halo(): after = lax.ppermute(initial, axis, down)  15 us
    ppermute x4, starting transfers between devices, spatial(): lower = lax.ppermute(pick_blocks(field, upper_wants), 'space', up)  12.3 us
    gather x1, local copies, waits for them, and re-layouts, shards(): coef_rows = svc_all[shift * nodes_dev + obs_cell // T_DEV]  10.4 us
    dynamic_update_slice x4, other arithmetic, add_block(): return lax.dynamic_update_slice_in_dim(whole, current + part, start, axis=0)  6.44 us
    ppermute x5, starting transfers between devices, with_halo(): after = lax.ppermute(initial, axis, down)  6.44 us
    ppermute x5, waiting for transfers between devices, with_halo(): before = lax.ppermute(last, axis, up)  6.15 us
    dot_general x4, matrix products, spatial(): jnp.dot(upper.T, upper_t, preferred_element_type=jnp.float32)  6.02 us
  transfers between devices with their start and end apart: 26, of which 9 were waited for; matrix products, arithmetic and copies ran while one was open for 31% of the time, Pallas kernels for 0%

profile of v11, /device:TPU:0, one launch (start us, length us, event | category | flops | bytes accessed | tf_op | source)
XLA Modules:
  0.0 161.9 jit_solution(7853178274254043012)
XLA Ops:
  1.2 2.6 %collective-permute-start.7 = (bf16[1024,256]{1,0:T(8,128)(2,1)}, bf16[1024,256]{1,0:T(8,128)(2,1)}, u32[]{:S(2)}, u32[]{:S(2)}) collective-permute-start(bf16[1024,256]{1,0:T(8,128)(2,1)} %param.23), channel_id=1, source_target_pairs={{0,16},{8,24},{16,0},{24,8},{1,17},{9,25},{17,1},{25,9},{2,18},{10... | collective-permute-start | bytes 1572872 | tf_op jit(solution)/shard_map/ppermute | solution.py:120
  3.8 1.4 collective-permute-start.8
  5.2 0.8 fusion.100
  6.0 1.3 collective-permute-start
  7.3 3.0 %collective-permute-start.2 = (s32[2]{0:T(128)S(1)}, s32[2]{0:T(128)S(1)}, u32[]{:S(2)}, u32[]{:S(2)}) collective-permute-start(s32[2]{0:T(128)S(1)} %get-tuple-element.51), channel_id=1, source_target_pairs={{0,8},{8,16},{16,24},{1,9},{9,17},{17,25},{2,10},{10,18},{18,26},{... | collective-permute-start | bytes 32 | tf_op jit(solution)/shard_map/ppermute | solution.py:75
  10.3 0.7 broadcast_in_dim.67
  11.2 1.2 copy.29
  13.2 1.0 convert_element_type.84
  14.2 1.1 select_reduce_fusion
  15.3 1.1 fusion.59
  16.4 2.2 %add_convert_fusion = bf16[8,12,128,128]{3,1,2,0:T(8,128)(2,1)S(1)} fusion(f32[8,128,128]{2,1,0:T(8,128)S(1)} %convert_element_type.84, f32[8,12]{1,0:T(8,128)S(1)} %fusion.91, bf16[8,8,128,128]{3,2,1,0:T(8,128)(2,1)S(1)} %copy-done, s32[8,8]{1,0:T(8,128)S(1)} %copy-done.8), kind=kOutput, calls=%fused_computation.2 | convolution fusion | flops 29885184 | bytes 5767808 | tf_op jit(solution)/shard_map/bkm,bkij->bimj/dot_general | solution.py:63
  18.7 1.6 copy.54
  21.0 1.7 %fusion.38 = f32[1024,256]{0,1:T(8,128)} fusion(bf16[1024,256]{0,1:T(8,128)(2,1)S(1)} %fusion.59, bf16[1024,1536]{1,0:T(8,128)(2,1)S(1)} %bitcast.49), kind=kOutput, calls=%fused_computation.66 | convolution fusion | flops 536870912 | bytes 3670016 | tf_op jit(solution)/shard_map/dot_general | solution.py:86
  22.7 1.0 fusion.70
  23.7 1.7 %fusion.40 = f32[1024,256]{0,1:T(8,128)} fusion(bf16[1024,256]{1,0:T(8,128)(2,1)S(1)} %copy-done.3, bf16[1024,1536]{1,0:T(8,128)(2,1)S(1)} %bitcast.51), kind=kOutput, calls=%fused_computation.68 | convolution fusion | flops 536870912 | bytes 3670016 | tf_op jit(solution)/shard_map/dot_general | solution.py:104
  25.5 1.0 fusion.64
  26.6 1.3 collective-permute-start.21
  31.8 3.2 %collective-permute-start.1 = (bf16[256,256]{0,1:T(8,128)(2,1)S(1)}, bf16[256,256]{0,1:T(8,128)(2,1)S(1)}, u32[]{:S(2)}, u32[]{:S(2)}) collective-permute-start(bf16[256,256]{0,1:T(8,128)(2,1)S(1)} %pad_maximum_fusion.11), channel_id=1, source_target_pairs={{0,8},{8,16},{16,24},{1,9},{9,17},{17,25},{2,10},{10,18},{18,26},{... | collective-permute-start | bytes 393224 | tf_op jit(solution)/shard_map/ppermute | solution.py:84
  35.9 4.5 %collective-permute-start.22 = (f32[256,256]{0,1:T(8,128)}, f32[256,256]{0,1:T(8,128)S(1)}, u32[]{:S(2)}, u32[]{:S(2)}) collective-permute-start(f32[256,256]{0,1:T(8,128)} %fusion.64), channel_id=1, source_target_pairs={{0,8},{8,16},{16,24},{1,9},{9,17},{17,25},{2,10},{10,18},{18,26},{... | collective-permute-start | bytes 786440 | tf_op jit(solution)/shard_map/ppermute | solution.py:108
  40.5 2.7 %convolution_add_fusion.7 = f32[1024,256]{0,1:T(8,128)} fusion(f32[1024,256]{0,1:T(8,128)} %fusion.38, bf16[256,256]{0,1:T(8,128)(2,1)S(1)} %collective-permute-done.1, bf16[1024,1536]{1,0:T(8,128)(2,1)} %bitcast.53), kind=kOutput, calls=%fused_computation.41 | convolution fusion | flops 134479872 | bytes 2752512 | tf_op jit(solution)/shard_map/dot_general | solution.py:87
  43.2 4.8 %collective-permute-start.4 = (bf16[1024,64]{0,1:T(8,128)(2,1)}, bf16[1024,64]{0,1:T(8,128)(2,1)}, u32[]{:S(2)}, u32[]{:S(2)}) collective-permute-start(bf16[1024,64]{0,1:T(8,128)(2,1)} %get-tuple-element.30), channel_id=1, source_target_pairs={{0,1},{1,2},{2,3},{3,4},{4,5},{5,6},{6,7},{8,9},{9,10},{10,11},{11... | collective-permute-start | bytes 393224 | tf_op jit(solution)/shard_map/ppermute | solution.py:27
  48.1 1.6 %fusion.80 = f32[1024,256]{0,1:T(8,128)} fusion(f32[1024,256]{0,1:T(8,128)} %fusion.40, s32[]{:T(128)S(6)} %select_n.70, f32[256,256]{0,1:T(8,128)} %collective-permute-done.21), kind=kLoop, calls=%fused_computation.124 | loop fusion | flops 32768 | bytes 393220 | tf_op jit(solution)/shard_map/dynamic_update_slice | solution.py:102
  49.7 1.3 collective-permute-start.5
  51.0 1.6 fusion.79
  52.6 1.3 collective-permute-start.3
  53.9 2.8 %pad_maximum_fusion = bf16[4096,256]{1,0:T(8,128)(2,1)} fusion(bf16[1024,256]{1,0:T(8,128)(2,1)} %collective-permute-done.8, bf16[1024,256]{1,0:T(8,128)(2,1)} %collective-permute-done.7, bf16[1024,256]{1,0:T(8,128)(2,1)} %collective-permute-done.6, bf16[1024,256]{1,0:T(8,128)(2,1)S(1)} %copy-done.4), kind=kLoop, calls=%fused_computation.12 | loop fusion | flops 8388608 | bytes 4194304 | tf_op jit(solution)/shard_map/concatenate | solution.py:123
  56.7 10.4 %gather_fusion = bf16[2048,256]{1,0:T(8,128)(2,1)} fusion(bf16[4096,256]{1,0:T(8,128)(2,1)} %pad_maximum_fusion, s32[2048]{0:T(1024)S(1)} %get-tuple-element.45), kind=kCustom, calls=%fused_computation | custom fusion | bytes 2105344 | tf_op jit(solution)/shard_map/gather | solution.py:126
  67.1 1.9 %fusion.2 = f32[2048]{0:T(1024)S(1)} fusion(bf16[2048,256]{1,0:T(8,128)(2,1)} %gather_fusion, bf16[2048,256]{1,0:T(8,128)(2,1)} %param.20), kind=kLoop, calls=%fused_computation.14 | loop fusion | flops 2095104 | bytes 2105344 | tf_op jit(solution)/shard_map/rc,rc->r/dot_general | solution.py:127
  69.0 1.7 %fusion = f32[48,1024]{1,0:T(8,128)S(1)} fusion(s32[2048]{0:T(1024)S(1)} %get-tuple-element.46, bf16[2048,16]{0,1:T(8,128)(2,1)S(1)} %get-tuple-element.39, bf16[2048,16]{0,1:T(8,128)(2,1)S(1)} %get-tuple-element.40, bf16[2048,16]{0,1:T(8,128)(2,1)S(1)} %get-tuple-element.38), kind=kOutput, calls=%fused_computation.3 | convolution fusion | flops 204013568 | bytes 401408 | tf_op jit(solution)/shard_map/dot_general | solution.py:139
  71.4 5.7 %all-to-all-start = ((f32[4,4,1024]{2,1,0:T(4,128)}), f32[4,4,1024]{2,1,0:T(4,128)S(1)}, u32[]{:S(2)}, u32[]{:S(2)}) async-start(f32[4,4,1024]{2,1,0:T(4,128)} %add.198), calls=%async_computation | async-start | bytes 131072 | tf_op jit(solution)/shard_map/all_to_all | solution.py:144
  77.1 1.6 %fusion.78 = f32[1024,256]{0,1:T(8,128)} fusion(f32[1024,256]{0,1:T(8,128)} %fusion.79, s32[]{:T(128)S(6)} %select_n.71, f32[256,256]{0,1:T(8,128)} %collective-permute-done.21), kind=kLoop, calls=%fused_computation.120 | loop fusion | flops 32768 | bytes 393220 | tf_op jit(solution)/shard_map/dynamic_update_slice | solution.py:102
  78.8 2.5 %all-to-all-done = f32[4,4,1024]{2,1,0:T(4,128)S(1)} async-done(((f32[4,4,1024]{2,1,0:T(4,128)}), f32[4,4,1024]{2,1,0:T(4,128)S(1)}, u32[]{:S(2)}, u32[]{:S(2)}) %all-to-all-start) | async-done | bytes 65568 | tf_op jit(solution)/shard_map/all_to_all | solution.py:144
  81.7 2.7 %fusion.102 = (bf16[1024,256]{0,1:T(8,128)(2,1)S(1)}, f32[1024,256]{0,1:T(8,128)S(1)}) fusion(f32[1024,256]{0,1:T(8,128)S(1)} %get-tuple-element.37, f32[1024,256]{0,1:T(8,128)S(1)} %get-tuple-element.36, bf16[1024,64]{0,1:T(8,128)(2,1)} %collective-permute-done.5, bf16[1024,256]{0,1:T(8,128)(2,1)S(1)} %fusion.59, ...), kind=kOutput, calls=%fused_computation.196 | convolution fusion | flops 141557760 | bytes 6695936 | tf_op jit(solution)/shard_map/dot_general | solution.py:88
  84.5 0.7 fusion.36
  85.4 1.5 collective-permute-start.10
  86.9 3.0 %collective-permute-start.9 = (bf16[256,256]{0,1:T(8,128)(2,1)S(1)}, bf16[256,256]{0,1:T(8,128)(2,1)S(1)}, u32[]{:S(2)}, u32[]{:S(2)}) collective-permute-start(bf16[256,256]{0,1:T(8,128)(2,1)S(1)} %pad_maximum_fusion.13), channel_id=1, source_target_pairs={{0,8},{8,16},{16,24},{1,9},{9,17},{17,25},{2,10},{10,18},{18,26},{... | collective-permute-start | bytes 393224 | tf_op jit(solution)/shard_map/ppermute | solution.py:84
  89.9 4.3 %collective-permute-start.11 = (bf16[1024,64]{0,1:T(8,128)(2,1)S(1)}, bf16[1024,64]{0,1:T(8,128)(2,1)S(1)}, u32[]{:S(2)}, u32[]{:S(2)}) collective-permute-start(bf16[1024,64]{0,1:T(8,128)(2,1)S(1)} %get-tuple-element.24), channel_id=1, source_target_pairs={{0,1},{1,2},{2,3},{3,4},{4,5},{5,6},{6,7},{8,9},{9,10},{10,11},{11... | collective-permute-start | bytes 393224 | tf_op jit(solution)/shard_map/ppermute | solution.py:27
  94.2 1.3 collective-permute-start.12
  95.9 2.1 %collective-permute-done.11 = bf16[1024,64]{0,1:T(8,128)(2,1)S(1)} collective-permute-done((bf16[1024,64]{0,1:T(8,128)(2,1)S(1)}, bf16[1024,64]{0,1:T(8,128)(2,1)S(1)}, u32[]{:S(2)}, u32[]{:S(2)}) %collective-permute-start.11) | collective-permute-done | bytes 131104 | tf_op jit(solution)/shard_map/ppermute | solution.py:27
  98.0 4.2 %collective-permute-done.12 = bf16[1024,64]{0,1:T(8,128)(2,1)S(1)} collective-permute-done((bf16[1024,64]{0,1:T(8,128)(2,1)S(1)}, bf16[1024,64]{0,1:T(8,128)(2,1)S(1)}, u32[]{:S(2)}, u32[]{:S(2)}) %collective-permute-start.12) | collective-permute-done | bytes 131104 | tf_op jit(solution)/shard_map/ppermute | solution.py:28
  102.2 0.8 fusion.103
  103.1 0.7 fusion.34
  103.9 1.3 collective-permute-start.14
  105.3 3.0 %collective-permute-start.13 = (bf16[256,256]{0,1:T(8,128)(2,1)S(1)}, bf16[256,256]{0,1:T(8,128)(2,1)S(1)}, u32[]{:S(2)}, u32[]{:S(2)}) collective-permute-start(bf16[256,256]{0,1:T(8,128)(2,1)S(1)} %pad_maximum_fusion.15), channel_id=1, source_target_pairs={{0,8},{8,16},{16,24},{1,9},{9,17},{17,25},{2,10},{10,18},{18,26},{... | collective-permute-start | bytes 393224 | tf_op jit(solution)/shard_map/ppermute | solution.py:84
  108.3 4.5 %collective-permute-start.15 = (bf16[1024,64]{0,1:T(8,128)(2,1)S(1)}, bf16[1024,64]{0,1:T(8,128)(2,1)S(1)}, u32[]{:S(2)}, u32[]{:S(2)}) collective-permute-start(bf16[1024,64]{0,1:T(8,128)(2,1)S(1)} %get-tuple-element.18), channel_id=1, source_target_pairs={{0,1},{1,2},{2,3},{3,4},{4,5},{5,6},{6,7},{8,9},{9,10},{10,11},{11... | collective-permute-start | bytes 393224 | tf_op jit(solution)/shard_map/ppermute | solution.py:27
  112.9 1.3 collective-permute-start.16
  114.6 2.2 %collective-permute-done.15 = bf16[1024,64]{0,1:T(8,128)(2,1)S(1)} collective-permute-done((bf16[1024,64]{0,1:T(8,128)(2,1)S(1)}, bf16[1024,64]{0,1:T(8,128)(2,1)S(1)}, u32[]{:S(2)}, u32[]{:S(2)}) %collective-permute-start.15) | collective-permute-done | bytes 131104 | tf_op jit(solution)/shard_map/ppermute | solution.py:27
  116.8 4.1 %collective-permute-done.16 = bf16[1024,64]{0,1:T(8,128)(2,1)S(1)} collective-permute-done((bf16[1024,64]{0,1:T(8,128)(2,1)S(1)}, bf16[1024,64]{0,1:T(8,128)(2,1)S(1)}, u32[]{:S(2)}, u32[]{:S(2)}) %collective-permute-start.16) | collective-permute-done | bytes 131104 | tf_op jit(solution)/shard_map/ppermute | solution.py:28
  120.9 0.8 fusion.104
  121.8 0.7 fusion.32
  122.7 1.3 collective-permute-start.18
  124.0 3.0 %collective-permute-start.17 = (bf16[256,256]{0,1:T(8,128)(2,1)S(1)}, bf16[256,256]{0,1:T(8,128)(2,1)S(1)}, u32[]{:S(2)}, u32[]{:S(2)}) collective-permute-start(bf16[256,256]{0,1:T(8,128)(2,1)S(1)} %pad_maximum_fusion.17), channel_id=1, source_target_pairs={{0,8},{8,16},{16,24},{1,9},{9,17},{17,25},{2,10},{10,18},{18,26},{... | collective-permute-start | bytes 393224 | tf_op jit(solution)/shard_map/ppermute | solution.py:84
  127.1 4.2 %collective-permute-start.19 = (bf16[1024,64]{0,1:T(8,128)(2,1)S(1)}, bf16[1024,64]{0,1:T(8,128)(2,1)S(1)}, u32[]{:S(2)}, u32[]{:S(2)}) collective-permute-start(bf16[1024,64]{0,1:T(8,128)(2,1)S(1)} %get-tuple-element.12), channel_id=1, source_target_pairs={{0,1},{1,2},{2,3},{3,4},{4,5},{5,6},{6,7},{8,9},{9,10},{10,11},{11... | collective-permute-start | bytes 393224 | tf_op jit(solution)/shard_map/ppermute | solution.py:27
  131.3 1.3 collective-permute-start.20
  132.9 1.8 %collective-permute-done.19 = bf16[1024,64]{0,1:T(8,128)(2,1)S(1)} collective-permute-done((bf16[1024,64]{0,1:T(8,128)(2,1)S(1)}, bf16[1024,64]{0,1:T(8,128)(2,1)S(1)}, u32[]{:S(2)}, u32[]{:S(2)}) %collective-permute-start.19) | collective-permute-done | bytes 131104 | tf_op jit(solution)/shard_map/ppermute | solution.py:27
  134.7 4.7 %collective-permute-done.20 = bf16[1024,64]{0,1:T(8,128)(2,1)S(1)} collective-permute-done((bf16[1024,64]{0,1:T(8,128)(2,1)S(1)}, bf16[1024,64]{0,1:T(8,128)(2,1)S(1)}, u32[]{:S(2)}, u32[]{:S(2)}) %collective-permute-start.20) | collective-permute-done | bytes 131104 | tf_op jit(solution)/shard_map/ppermute | solution.py:28
  139.4 1.8 %fusion.105 = (bf16[1024,256]{0,1:T(8,128)(2,1)S(1)}, f32[1024,256]{0,1:T(8,128)}) fusion(f32[1024,256]{0,1:T(8,128)S(1)} %get-tuple-element.60, f32[1024,256]{0,1:T(8,128)S(1)} %get-tuple-element.37, f32[1024,256]{0,1:T(8,128)S(1)} %fusion.4, bf16[1024,64]{0,1:T(8,128)(2,1)S(1)} %collective-permute-done.20, bf16[1024,256]{0,1:T(8,128)(2,1)S(1)} %get-tuple-element.59, ...), kind=kOutput, calls=%fused_computation.199 | convolution fusion | flops 140247040 | bytes 7735296 | tf_op jit(solution)/shard_map/dot_general | solution.py:88
  141.9 4.5 %collective-permute-start.23 = (bf16[1024,64]{0,1:T(8,128)(2,1)}, bf16[1024,64]{0,1:T(8,128)(2,1)}, u32[]{:S(2)}, u32[]{:S(2)}) collective-permute-start(bf16[1024,64]{0,1:T(8,128)(2,1)} %get-tuple-element.10), channel_id=1, source_target_pairs={{0,1},{1,2},{2,3},{3,4},{4,5},{5,6},{6,7},{8,9},{9,10},{10,11},{11... | collective-permute-start | bytes 393224 | tf_op jit(solution)/shard_map/ppermute | solution.py:27
  146.4 1.3 collective-permute-start.24
  147.7 1.6 fusion.77
  149.3 2.5 %copy.36 = f32[1024,256]{1,0:T(8,128)} copy(f32[1024,256]{0,1:T(8,128)} %get-tuple-element.62) | data formatting | bytes 2097152
  151.8 2.0 %collective-permute-done.24 = bf16[1024,64]{0,1:T(8,128)(2,1)} collective-permute-done((bf16[1024,64]{0,1:T(8,128)(2,1)}, bf16[1024,64]{0,1:T(8,128)(2,1)}, u32[]{:S(2)}, u32[]{:S(2)}) %collective-permute-start.24) | collective-permute-done | bytes 131104 | tf_op jit(solution)/shard_map/ppermute | solution.py:28
  153.9 1.7 %fusion.54 = (f32[256]{0:T(256)S(1)}, f32[256]{0:T(256)S(1)}) fusion(f32[1024,256]{0,1:T(8,128)} %fusion.77, bf16[1024,256]{0,1:T(8,128)(2,1)S(1)} %get-tuple-element.61, bf16[1024,64]{0,1:T(8,128)(2,1)} %collective-permute-done.24, bf16[1024,64]{0,1:T(8,128)(2,1)} %collective-permute-done.23, bf16[1024,256]{0,1:T(8,128)(2,1)S(1)} %copy.29), kind=kLoop, calls=%fused_computation.82 | loop fusion | flops 4455936 | bytes 2361344 | tf_op jit(solution)/shard_map/reduce_sum | solution.py:166
  155.6 5.8 %psum.7 = f32[2,256]{1,0:T(2,128)S(1)} all-reduce(f32[2,256]{1,0:T(2,128)S(1)} %pad_maximum_fusion.19), channel_id=1, replica_groups=mesh['space'=4,'tm'=8] {'space'}, use_global_device_ids=true, to_apply=%region_4.5 | all-reduce | flops 512 | bytes 4096 | tf_op jit(solution)/shard_map/psum | solution.py:170
  (78 shorter events, 8.7 us)
Async XLA Ops:
  0.6 15.8 %copy-start = (bf16[8,8,128,128]{3,2,1,0:T(8,128)(2,1)S(1)}, bf16[8,8,128,128]{3,2,1,0:T(8,128)(2,1)}, u32[]{:S(2)}) copy-start(bf16[8,8,128,128]{3,2,1,0:T(8,128)(2,1)} %param.17) | copy-start | bytes 6291460
  0.6 15.7 %copy-start.8 = (s32[8,8]{1,0:T(8,128)S(1)}, s32[8,8]{1,0:T(8,128)}, u32[]{:S(2)}) copy-start(s32[8,8]{1,0:T(8,128)} %param.18) | copy-start | bytes 772
  0.7 51.9 %collective-permute-start.6 = (bf16[1024,256]{1,0:T(8,128)(2,1)}, bf16[1024,256]{1,0:T(8,128)(2,1)}, u32[]{:S(2)}, u32[]{:S(2)}) collective-permute-start(bf16[1024,256]{1,0:T(8,128)(2,1)} %param.23), channel_id=1, source_target_pairs={{0,8},{8,16},{16,24},{24,0},{1,9},{9,17},{17,25},{25,1},{2,10},{10... | collective-permute-start | bytes 1572872 | tf_op jit(solution)/shard_map/ppermute | solution.py:120
  1.2 52.7 %collective-permute-start.7 = (bf16[1024,256]{1,0:T(8,128)(2,1)}, bf16[1024,256]{1,0:T(8,128)(2,1)}, u32[]{:S(2)}, u32[]{:S(2)}) collective-permute-start(bf16[1024,256]{1,0:T(8,128)(2,1)} %param.23), channel_id=1, source_target_pairs={{0,16},{8,24},{16,0},{24,8},{1,17},{9,25},{17,1},{25,9},{2,18},{10... | collective-permute-start | bytes 1572872 | tf_op jit(solution)/shard_map/ppermute | solution.py:120
  3.8 50.1 %collective-permute-start.8 = (bf16[1024,256]{1,0:T(8,128)(2,1)}, bf16[1024,256]{1,0:T(8,128)(2,1)}, u32[]{:S(2)}, u32[]{:S(2)}) collective-permute-start(bf16[1024,256]{1,0:T(8,128)(2,1)} %param.23), channel_id=1, source_target_pairs={{0,24},{8,0},{16,8},{24,16},{1,25},{9,1},{17,9},{25,17},{2,26},{10... | collective-permute-start | bytes 1572872 | tf_op jit(solution)/shard_map/ppermute | solution.py:120
  6.0 20.6 %collective-permute-start = (s32[2]{0:T(128)S(1)}, s32[2]{0:T(128)S(1)}, u32[]{:S(2)}, u32[]{:S(2)}) collective-permute-start(s32[2]{0:T(128)S(1)} %get-tuple-element.52), channel_id=1, source_target_pairs={{8,0},{16,8},{24,16},{9,1},{17,9},{25,17},{10,2},{18,10},{26,18},{... | collective-permute-start | bytes 32 | tf_op jit(solution)/shard_map/ppermute | solution.py:74
  7.3 22.6 %collective-permute-start.2 = (s32[2]{0:T(128)S(1)}, s32[2]{0:T(128)S(1)}, u32[]{:S(2)}, u32[]{:S(2)}) collective-permute-start(s32[2]{0:T(128)S(1)} %get-tuple-element.51), channel_id=1, source_target_pairs={{0,8},{8,16},{16,24},{1,9},{9,17},{17,25},{2,10},{10,18},{18,26},{... | collective-permute-start | bytes 32 | tf_op jit(solution)/shard_map/ppermute | solution.py:75
  20.3 5.2 %copy-start.1 = (bf16[128,8,12,128]{3,1,2,0:T(8,128)(2,1)}, bf16[128,8,12,128]{3,1,2,0:T(8,128)(2,1)S(1)}, u32[]{:S(2)}) copy-start(bf16[128,8,12,128]{3,1,2,0:T(8,128)(2,1)S(1)} %copy.54) | copy-start | bytes 9437188
  20.3 2.4 %copy-start.3 = (bf16[1024,256]{1,0:T(8,128)(2,1)S(1)}, bf16[1024,256]{1,0:T(8,128)(2,1)}, u32[]{:S(2)}) copy-start(bf16[1024,256]{1,0:T(8,128)(2,1)} %param.12) | copy-start | bytes 1572868
  23.7 2.8 %copy-start.6 = (s32[2048,1]{0,1:T(1,128)S(1)}, s32[2048,1]{0,1:T(1,128)}, u32[]{:S(2)}) copy-start(s32[2048,1]{0,1:T(1,128)} %param.21) | copy-start | bytes 24580
  23.7 11.2 %copy-start.7 = (s32[2048]{0:T(1024)S(1)}, s32[2048]{0:T(1024)}, u32[]{:S(2)}) copy-start(s32[2048]{0:T(1024)} %param.22) | copy-start | bytes 24580
  26.6 16.7 %collective-permute-start.21 = (f32[256,256]{0,1:T(8,128)}, f32[256,256]{0,1:T(8,128)}, u32[]{:S(2)}, u32[]{:S(2)}) collective-permute-start(f32[256,256]{0,1:T(8,128)} %fusion.70), channel_id=1, source_target_pairs={{8,0},{16,8},{24,16},{9,1},{17,9},{25,17},{10,2},{18,10},{26,18},{... | collective-permute-start | bytes 786440 | tf_op jit(solution)/shard_map/ppermute | solution.py:107
  31.7 22.2 %copy-start.4 = (bf16[1024,256]{1,0:T(8,128)(2,1)S(1)}, bf16[1024,256]{1,0:T(8,128)(2,1)}, u32[]{:S(2)}) copy-start(bf16[1024,256]{1,0:T(8,128)(2,1)} %param.23) | copy-start | bytes 1572868
  31.8 4.1 %collective-permute-start.1 = (bf16[256,256]{0,1:T(8,128)(2,1)S(1)}, bf16[256,256]{0,1:T(8,128)(2,1)S(1)}, u32[]{:S(2)}, u32[]{:S(2)}) collective-permute-start(bf16[256,256]{0,1:T(8,128)(2,1)S(1)} %pad_maximum_fusion.11), channel_id=1, source_target_pairs={{0,8},{8,16},{16,24},{1,9},{9,17},{17,25},{2,10},{10,18},{18,26},{... | collective-permute-start | bytes 393224 | tf_op jit(solution)/shard_map/ppermute | solution.py:84
  35.9 13.8 %collective-permute-start.22 = (f32[256,256]{0,1:T(8,128)}, f32[256,256]{0,1:T(8,128)S(1)}, u32[]{:S(2)}, u32[]{:S(2)}) collective-permute-start(f32[256,256]{0,1:T(8,128)} %fusion.64), channel_id=1, source_target_pairs={{0,8},{8,16},{16,24},{1,9},{9,17},{17,25},{2,10},{10,18},{18,26},{... | collective-permute-start | bytes 786440 | tf_op jit(solution)/shard_map/ppermute | solution.py:108
  43.2 38.4 %collective-permute-start.4 = (bf16[1024,64]{0,1:T(8,128)(2,1)}, bf16[1024,64]{0,1:T(8,128)(2,1)}, u32[]{:S(2)}, u32[]{:S(2)}) collective-permute-start(bf16[1024,64]{0,1:T(8,128)(2,1)} %get-tuple-element.30), channel_id=1, source_target_pairs={{0,1},{1,2},{2,3},{3,4},{4,5},{5,6},{6,7},{8,9},{9,10},{10,11},{11... | collective-permute-start | bytes 393224 | tf_op jit(solution)/shard_map/ppermute | solution.py:27
  49.7 31.9 %collective-permute-start.5 = (bf16[1024,64]{0,1:T(8,128)(2,1)}, bf16[1024,64]{0,1:T(8,128)(2,1)}, u32[]{:S(2)}, u32[]{:S(2)}) collective-permute-start(bf16[1024,64]{0,1:T(8,128)(2,1)} %get-tuple-element.31), channel_id=1, source_target_pairs={{1,0},{2,1},{3,2},{4,3},{5,4},{6,5},{7,6},{9,8},{10,9},{11,10},{12... | collective-permute-start | bytes 393224 | tf_op jit(solution)/shard_map/ppermute | solution.py:28
  52.6 29.1 %collective-permute-start.3 = (bf16[256,256]{0,1:T(8,128)(2,1)}, bf16[256,256]{0,1:T(8,128)(2,1)}, u32[]{:S(2)}, u32[]{:S(2)}) collective-permute-start(bf16[256,256]{0,1:T(8,128)(2,1)} %pad_maximum_fusion.12), channel_id=1, source_target_pairs={{8,0},{16,8},{24,16},{9,1},{17,9},{25,17},{10,2},{18,10},{26,18},{... | collective-permute-start | bytes 393224 | tf_op jit(solution)/shard_map/ppermute | solution.py:85
  67.1 14.2 %copy-start.5 = (f32[1024]{0:T(1024)S(1)}, f32[1024]{0:T(1024)}, u32[]{:S(2)}) copy-start(f32[1024]{0:T(1024)} %param.13) | copy-start | bytes 12292
  71.4 9.8 %all-to-all-start = ((f32[4,4,1024]{2,1,0:T(4,128)}), f32[4,4,1024]{2,1,0:T(4,128)S(1)}, u32[]{:S(2)}, u32[]{:S(2)}) async-start(f32[4,4,1024]{2,1,0:T(4,128)} %add.198), calls=%async_computation | async-start | bytes 131072 | tf_op jit(solution)/shard_map/all_to_all | solution.py:144
  81.7 2.8 %copy-start.2 = (bf16[128,8,12,128]{3,1,2,0:T(8,128)(2,1)S(1)}, bf16[128,8,12,128]{3,1,2,0:T(8,128)(2,1)}, u32[]{:S(2)}) copy-start(bf16[128,8,12,128]{3,1,2,0:T(8,128)(2,1)} %copy-done.1) | copy-start | bytes 9437188
  85.4 10.5 %collective-permute-start.10 = (bf16[256,256]{0,1:T(8,128)(2,1)S(1)}, bf16[256,256]{0,1:T(8,128)(2,1)S(1)}, u32[]{:S(2)}, u32[]{:S(2)}) collective-permute-start(bf16[256,256]{0,1:T(8,128)(2,1)S(1)} %pad_maximum_fusion.14), channel_id=1, source_target_pairs={{8,0},{16,8},{24,16},{9,1},{17,9},{25,17},{10,2},{18,10},{26,18},{... | collective-permute-start | bytes 393224 | tf_op jit(solution)/shard_map/ppermute | solution.py:85
  86.9 8.6 %collective-permute-start.9 = (bf16[256,256]{0,1:T(8,128)(2,1)S(1)}, bf16[256,256]{0,1:T(8,128)(2,1)S(1)}, u32[]{:S(2)}, u32[]{:S(2)}) collective-permute-start(bf16[256,256]{0,1:T(8,128)(2,1)S(1)} %pad_maximum_fusion.13), channel_id=1, source_target_pairs={{0,8},{8,16},{16,24},{1,9},{9,17},{17,25},{2,10},{10,18},{18,26},{... | collective-permute-start | bytes 393224 | tf_op jit(solution)/shard_map/ppermute | solution.py:84
  89.9 8.0 %collective-permute-start.11 = (bf16[1024,64]{0,1:T(8,128)(2,1)S(1)}, bf16[1024,64]{0,1:T(8,128)(2,1)S(1)}, u32[]{:S(2)}, u32[]{:S(2)}) collective-permute-start(bf16[1024,64]{0,1:T(8,128)(2,1)S(1)} %get-tuple-element.24), channel_id=1, source_target_pairs={{0,1},{1,2},{2,3},{3,4},{4,5},{5,6},{6,7},{8,9},{9,10},{10,11},{11... | collective-permute-start | bytes 393224 | tf_op jit(solution)/shard_map/ppermute | solution.py:27
  94.2 8.0 %collective-permute-start.12 = (bf16[1024,64]{0,1:T(8,128)(2,1)S(1)}, bf16[1024,64]{0,1:T(8,128)(2,1)S(1)}, u32[]{:S(2)}, u32[]{:S(2)}) collective-permute-start(bf16[1024,64]{0,1:T(8,128)(2,1)S(1)} %get-tuple-element.25), channel_id=1, source_target_pairs={{1,0},{2,1},{3,2},{4,3},{5,4},{6,5},{7,6},{9,8},{10,9},{11,10},{12... | collective-permute-start | bytes 393224 | tf_op jit(solution)/shard_map/ppermute | solution.py:28
  103.9 10.6 %collective-permute-start.14 = (bf16[256,256]{0,1:T(8,128)(2,1)S(1)}, bf16[256,256]{0,1:T(8,128)(2,1)S(1)}, u32[]{:S(2)}, u32[]{:S(2)}) collective-permute-start(bf16[256,256]{0,1:T(8,128)(2,1)S(1)} %pad_maximum_fusion.16), channel_id=1, source_target_pairs={{8,0},{16,8},{24,16},{9,1},{17,9},{25,17},{10,2},{18,10},{26,18},{... | collective-permute-start | bytes 393224 | tf_op jit(solution)/shard_map/ppermute | solution.py:85
  105.3 8.9 %collective-permute-start.13 = (bf16[256,256]{0,1:T(8,128)(2,1)S(1)}, bf16[256,256]{0,1:T(8,128)(2,1)S(1)}, u32[]{:S(2)}, u32[]{:S(2)}) collective-permute-start(bf16[256,256]{0,1:T(8,128)(2,1)S(1)} %pad_maximum_fusion.15), channel_id=1, source_target_pairs={{0,8},{8,16},{16,24},{1,9},{9,17},{17,25},{2,10},{10,18},{18,26},{... | collective-permute-start | bytes 393224 | tf_op jit(solution)/shard_map/ppermute | solution.py:84
  108.3 8.4 %collective-permute-start.15 = (bf16[1024,64]{0,1:T(8,128)(2,1)S(1)}, bf16[1024,64]{0,1:T(8,128)(2,1)S(1)}, u32[]{:S(2)}, u32[]{:S(2)}) collective-permute-start(bf16[1024,64]{0,1:T(8,128)(2,1)S(1)} %get-tuple-element.18), channel_id=1, source_target_pairs={{0,1},{1,2},{2,3},{3,4},{4,5},{5,6},{6,7},{8,9},{9,10},{10,11},{11... | collective-permute-start | bytes 393224 | tf_op jit(solution)/shard_map/ppermute | solution.py:27
  112.9 8.0 %collective-permute-start.16 = (bf16[1024,64]{0,1:T(8,128)(2,1)S(1)}, bf16[1024,64]{0,1:T(8,128)(2,1)S(1)}, u32[]{:S(2)}, u32[]{:S(2)}) collective-permute-start(bf16[1024,64]{0,1:T(8,128)(2,1)S(1)} %get-tuple-element.19), channel_id=1, source_target_pairs={{1,0},{2,1},{3,2},{4,3},{5,4},{6,5},{7,6},{9,8},{10,9},{11,10},{12... | collective-permute-start | bytes 393224 | tf_op jit(solution)/shard_map/ppermute | solution.py:28
  122.7 10.2 %collective-permute-start.18 = (bf16[256,256]{0,1:T(8,128)(2,1)S(1)}, bf16[256,256]{0,1:T(8,128)(2,1)S(1)}, u32[]{:S(2)}, u32[]{:S(2)}) collective-permute-start(bf16[256,256]{0,1:T(8,128)(2,1)S(1)} %pad_maximum_fusion.18), channel_id=1, source_target_pairs={{8,0},{16,8},{24,16},{9,1},{17,9},{25,17},{10,2},{18,10},{26,18},{... | collective-permute-start | bytes 393224 | tf_op jit(solution)/shard_map/ppermute | solution.py:85
  124.0 8.6 %collective-permute-start.17 = (bf16[256,256]{0,1:T(8,128)(2,1)S(1)}, bf16[256,256]{0,1:T(8,128)(2,1)S(1)}, u32[]{:S(2)}, u32[]{:S(2)}) collective-permute-start(bf16[256,256]{0,1:T(8,128)(2,1)S(1)} %pad_maximum_fusion.17), channel_id=1, source_target_pairs={{0,8},{8,16},{16,24},{1,9},{9,17},{17,25},{2,10},{10,18},{18,26},{... | collective-permute-start | bytes 393224 | tf_op jit(solution)/shard_map/ppermute | solution.py:84
  127.1 7.7 %collective-permute-start.19 = (bf16[1024,64]{0,1:T(8,128)(2,1)S(1)}, bf16[1024,64]{0,1:T(8,128)(2,1)S(1)}, u32[]{:S(2)}, u32[]{:S(2)}) collective-permute-start(bf16[1024,64]{0,1:T(8,128)(2,1)S(1)} %get-tuple-element.12), channel_id=1, source_target_pairs={{0,1},{1,2},{2,3},{3,4},{4,5},{5,6},{6,7},{8,9},{9,10},{10,11},{11... | collective-permute-start | bytes 393224 | tf_op jit(solution)/shard_map/ppermute | solution.py:27
  131.3 8.2 %collective-permute-start.20 = (bf16[1024,64]{0,1:T(8,128)(2,1)S(1)}, bf16[1024,64]{0,1:T(8,128)(2,1)S(1)}, u32[]{:S(2)}, u32[]{:S(2)}) collective-permute-start(bf16[1024,64]{0,1:T(8,128)(2,1)S(1)} %get-tuple-element.13), channel_id=1, source_target_pairs={{1,0},{2,1},{3,2},{4,3},{5,4},{6,5},{7,6},{9,8},{10,9},{11,10},{12... | collective-permute-start | bytes 393224 | tf_op jit(solution)/shard_map/ppermute | solution.py:28
  141.9 9.9 %collective-permute-start.23 = (bf16[1024,64]{0,1:T(8,128)(2,1)}, bf16[1024,64]{0,1:T(8,128)(2,1)}, u32[]{:S(2)}, u32[]{:S(2)}) collective-permute-start(bf16[1024,64]{0,1:T(8,128)(2,1)} %get-tuple-element.10), channel_id=1, source_target_pairs={{0,1},{1,2},{2,3},{3,4},{4,5},{5,6},{6,7},{8,9},{9,10},{10,11},{11... | collective-permute-start | bytes 393224 | tf_op jit(solution)/shard_map/ppermute | solution.py:27
  146.4 7.4 %collective-permute-start.24 = (bf16[1024,64]{0,1:T(8,128)(2,1)}, bf16[1024,64]{0,1:T(8,128)(2,1)}, u32[]{:S(2)}, u32[]{:S(2)}) collective-permute-start(bf16[1024,64]{0,1:T(8,128)(2,1)} %get-tuple-element.11), channel_id=1, source_target_pairs={{1,0},{2,1},{3,2},{4,3},{5,4},{6,5},{7,6},{9,8},{10,9},{11,10},{12... | collective-permute-start | bytes 393224 | tf_op jit(solution)/shard_map/ppermute | solution.py:28

commit v12 on v10

--- a/solution.py
+++ b/solution.py
@@ -105,11 +105,11 @@
         lax.ppermute(svc_coef, "space", [(i, (i + k) % space_count) for i in range(space_count)])
         for k in range(1, space_count)
     ]
-    svc_all = jnp.concatenate(tables, axis=0)
+    svc_all = jnp.concatenate(tables, axis=0).astype(jnp.float32)
     owner = obs_owner[:, 0]
     shift = (lax.axis_index("space") - owner) % space_count
     coef_rows = svc_all[shift * nodes_dev + obs_cell // T_DEV]
-    eta = jnp.einsum("rc,rc->r", covariates, coef_rows, preferred_element_type=jnp.float32)
+    eta = jnp.sum(covariates.astype(jnp.float32) * coef_rows, axis=1)
     obs_weight = jnp.exp(eta)
     onehot = (obs_cell[:, None] // T_DEV == jnp.arange(nodes_dev)[None, :]).astype(jnp.bfloat16)
     high = lax.reduce_precision(obs_weight, exponent_bits=8, mantissa_bits=7)

time: 154 us -> 150 us (0.974)
  waiting for transfers between devices: 21.4 us -> 12.4 us
  starting transfers between devices: 65 us -> 66.7 us
    ppermute x5, waiting for transfers between devices: 14.1 us -> 0.45 us  [with_halo(): after = lax.ppermute(initial, axis, down)]
    convert_element_type x0 -> x1, other arithmetic: none -> 3.82 us  [shards(): svc_all = jnp.concatenate(tables, axis=0).astype(jnp.float32)]
    ppermute x5, waiting for transfers between devices: 5.89 us -> 9.16 us  [with_halo(): before = lax.ppermute(last, axis, up)]
    concatenate x1 -> x0, other arithmetic: 2.99 us -> none  [shards(): svc_all = jnp.concatenate(tables, axis=0)]
    ppermute x5, starting transfers between devices: 20.8 us -> 23.5 us  [with_halo(): before = lax.ppermute(last, axis, up)]
    reduce_sum x0 -> x1, other arithmetic: none -> 2.2 us  [shards(): eta = jnp.sum(covariates.astype(jnp.float32) * coef_rows, axis=1)]
    dot_general x1 -> x0, other arithmetic: 1.89 us -> none  [shards(): jnp.einsum('rc,rc->r', covariates, coef_rows, preferred_element_type=jnp....]
  transfers between devices with their start and end apart: 26 -> 26, of which waited for: 8 -> 7; matrix products, arithmetic and copies ran while one was open for 28% -> 30% of each run, Pallas kernels for 0% -> 0%
where the time goes in v12:
time: 150 us; the launch traced here: 149 us
  starting transfers between devices  66.7 us (44%)
  local copies, waits for them, and re-layouts  24 us (16%)
  matrix products  23.5 us (16%)
  waiting for transfers between devices  12.4 us (8%)
  other arithmetic  11.9 us (8%)
  blocking collectives  6.43 us (4%)
  between operations  3.93 us (3%)
    ppermute x5, starting transfers between devices, with_halo(): before = lax.ppermute(last, axis, up)  23.5 us
    ppermute x5, starting transfers between devices, spatial(): lower = lax.ppermute(pick_blocks(field, upper_wants), 'space', up)  18.3 us
    gather x1, local copies, waits for them, and re-layouts, shards(): coef_rows = svc_all[shift * nodes_dev + obs_cell // T_DEV]  10.8 us
    ppermute x5, waiting for transfers between devices, with_halo(): before = lax.ppermute(last, axis, up)  9.16 us
    dot_general x5, matrix products, spatial(): jnp.dot(upper.T, upper_t, preferred_element_type=jnp.float32)  7.51 us
    unnamed x17, local copies, waits for them, and re-layouts  7.03 us
    ppermute x5, starting transfers between devices, spatial(): upper = lax.ppermute(pick_blocks(field, lower_wants), 'space', down)  6.63 us
    ppermute x5, starting transfers between devices, with_halo(): after = lax.ppermute(initial, axis, down)  6.44 us
  transfers between devices with their start and end apart: 26, of which 7 were waited for; matrix products, arithmetic and copies ran while one was open for 30% of the time, Pallas kernels for 0%

profile of v12, /device:TPU:0, one launch (start us, length us, event | category | flops | bytes accessed | tf_op | source)
XLA Modules:
  0.0 148.9 jit_solution(1164004478116782376)
XLA Ops:
  0.7 2.5 %collective-permute-start.8 = (bf16[1024,256]{1,0:T(8,128)(2,1)}, bf16[1024,256]{1,0:T(8,128)(2,1)}, u32[]{:S(2)}, u32[]{:S(2)}) collective-permute-start(bf16[1024,256]{1,0:T(8,128)(2,1)} %param.23), channel_id=1, source_target_pairs={{0,24},{8,0},{16,8},{24,16},{1,25},{9,1},{17,9},{25,17},{2,26},{10... | collective-permute-start | bytes 1572872 | tf_op jit(solution)/shard_map/ppermute | solution.py:105
  3.1 0.6 collective-permute-start.7
  4.0 1.2 copy.27
  5.2 0.7 broadcast_in_dim.67
  6.0 0.7 broadcast_in_dim.64
  6.8 1.1 select_reduce_fusion
  7.9 1.1 fusion.56
  9.0 0.7 fusion.89
  9.7 1.3 collective-permute-start.5
  11.0 0.8 fusion.91
  11.8 3.2 %collective-permute-start.2 = (s32[2]{0:T(128)S(1)}, s32[2]{0:T(128)S(1)}, u32[]{:S(2)}, u32[]{:S(2)}) collective-permute-start(s32[2]{0:T(128)S(1)} %get-tuple-element.53), channel_id=1, source_target_pairs={{0,8},{8,16},{16,24},{1,9},{9,17},{17,25},{2,10},{10,18},{18,26},{... | collective-permute-start | bytes 32 | tf_op jit(solution)/shard_map/ppermute | solution.py:75
  15.1 1.8 %convert_element_type.89 = f32[8,128,128]{2,1,0:T(8,128)} convert(bf16[8,128,128]{2,1,0:T(8,128)(2,1)} %param.16) | non-fusion elementwise | flops 131072 | bytes 786432 | tf_op jit(solution)/shard_map/convert_element_type | solution.py:52
  16.9 3.1 %add_convert_fusion = bf16[8,12,128,128]{3,1,2,0:T(8,128)(2,1)S(1)} fusion(f32[8,128,128]{2,1,0:T(8,128)} %convert_element_type.89, f32[8,12]{1,0:T(8,128)S(1)} %fusion.82, bf16[8,8,128,128]{3,2,1,0:T(8,128)(2,1)S(1)} %copy-done, s32[8,8]{1,0:T(8,128)S(1)} %copy-done.6), kind=kOutput, calls=%fused_computation.2 | convolution fusion | flops 29885184 | bytes 5767808 | tf_op jit(solution)/shard_map/bkm,bkij->bimj/dot_general | solution.py:63
  20.0 1.6 %copy.46 = bf16[128,8,12,128]{3,1,2,0:T(8,128)(2,1)S(1)} copy(bf16[128,8,12,128]{3,2,1,0:T(8,128)(2,1)S(1)} %bitcast.48) | data formatting | bytes 6291456
  21.6 1.6 %copy-done.1 = bf16[128,8,12,128]{3,1,2,0:T(8,128)(2,1)} copy-done((bf16[128,8,12,128]{3,1,2,0:T(8,128)(2,1)}, bf16[128,8,12,128]{3,1,2,0:T(8,128)(2,1)S(1)}, u32[]{:S(2)}) %copy-start.1) | copy-done | bytes 3145752
  23.3 1.7 %fusion.38 = f32[1024,256]{0,1:T(8,128)} fusion(bf16[1024,256]{0,1:T(8,128)(2,1)S(1)} %fusion.56, bf16[1024,1536]{1,0:T(8,128)(2,1)S(1)} %bitcast.49), kind=kOutput, calls=%fused_computation.67 | convolution fusion | flops 536870912 | bytes 3670016 | tf_op jit(solution)/shard_map/dot_general | solution.py:86
  25.0 1.3 collective-permute-start
  26.3 0.7 fusion.90
  28.3 1.3 collective-permute-done
  29.7 4.1 %collective-permute-start.4 = (bf16[1024,64]{0,1:T(8,128)(2,1)}, bf16[1024,64]{0,1:T(8,128)(2,1)}, u32[]{:S(2)}, u32[]{:S(2)}) collective-permute-start(bf16[1024,64]{0,1:T(8,128)(2,1)} %get-tuple-element.32), channel_id=1, source_target_pairs={{0,1},{1,2},{2,3},{3,4},{4,5},{5,6},{6,7},{8,9},{9,10},{10,11},{11... | collective-permute-start | bytes 393224 | tf_op jit(solution)/shard_map/ppermute | solution.py:27
  33.7 0.6 fusion.92
  35.7 5.4 %collective-permute-start.1 = (bf16[256,256]{0,1:T(8,128)(2,1)S(1)}, bf16[256,256]{0,1:T(8,128)(2,1)}, u32[]{:S(2)}, u32[]{:S(2)}) collective-permute-start(bf16[256,256]{0,1:T(8,128)(2,1)S(1)} %pad_maximum_fusion.10), channel_id=1, source_target_pairs={{0,8},{8,16},{16,24},{1,9},{9,17},{17,25},{2,10},{10,18},{18,26},{... | collective-permute-start | bytes 393224 | tf_op jit(solution)/shard_map/ppermute | solution.py:84
  41.1 1.3 collective-permute-start.3
  42.4 3.8 %maximum_convert_fusion = f32[4096,256]{1,0:T(8,128)} fusion(bf16[1024,256]{1,0:T(8,128)(2,1)} %collective-permute-done.8, bf16[1024,256]{1,0:T(8,128)(2,1)} %collective-permute-done.7, bf16[1024,256]{1,0:T(8,128)(2,1)} %collective-permute-done.6, bf16[1024,256]{1,0:T(8,128)(2,1)} %param.23), kind=kLoop, calls=%fused_computation.13 | loop fusion | flops 8388608 | bytes 6291456 | tf_op jit(solution)/shard_map/convert_element_type | solution.py:108
  46.2 10.8 %gather_fusion = f32[2048,256]{1,0:T(8,128)} fusion(f32[4096,256]{1,0:T(8,128)} %maximum_convert_fusion, s32[2048]{0:T(1024)S(1)} %get-tuple-element.47), kind=kCustom, calls=%fused_computation | custom fusion | bytes 4202496 | tf_op jit(solution)/shard_map/gather | solution.py:111
  57.0 2.2 %multiply_reduce_fusion = f32[2048]{0:T(1024)S(1)} fusion(f32[2048,256]{1,0:T(8,128)} %gather_fusion, bf16[2048,256]{1,0:T(8,128)(2,1)} %param.20), kind=kLoop, calls=%fused_computation.15 | loop fusion | flops 1570816 | bytes 3153920 | tf_op jit(solution)/shard_map/reduce_sum | solution.py:112
  59.3 1.7 %fusion = f32[48,1024]{1,0:T(8,128)S(1)} fusion(s32[2048]{0:T(1024)S(1)} %get-tuple-element.48, bf16[2048,16]{0,1:T(8,128)(2,1)S(1)} %get-tuple-element.41, bf16[2048,16]{0,1:T(8,128)(2,1)S(1)} %get-tuple-element.42, bf16[2048,16]{0,1:T(8,128)(2,1)S(1)} %get-tuple-element.40), kind=kOutput, calls=%fused_computation.3 | convolution fusion | flops 204013568 | bytes 401408 | tf_op jit(solution)/shard_map/dot_general | solution.py:124
  61.1 0.7 add.190
  61.7 4.0 %all-to-all-start = ((f32[4,4,1024]{2,1,0:T(4,128)}), f32[4,4,1024]{2,1,0:T(4,128)S(1)}, u32[]{:S(2)}, u32[]{:S(2)}) async-start(f32[4,4,1024]{2,1,0:T(4,128)} %add.190), calls=%async_computation | async-start | bytes 131072 | tf_op jit(solution)/shard_map/all_to_all | solution.py:129
  65.7 2.7 %convolution_add_fusion.9 = f32[1024,256]{0,1:T(8,128)} fusion(f32[1024,256]{0,1:T(8,128)} %fusion.38, bf16[256,256]{0,1:T(8,128)(2,1)} %collective-permute-done.1, bf16[1024,1536]{1,0:T(8,128)(2,1)} %bitcast.50), kind=kOutput, calls=%fused_computation.43 | convolution fusion | flops 134479872 | bytes 2752512 | tf_op jit(solution)/shard_map/dot_general | solution.py:87
  68.4 1.4 all-to-all-done
  70.2 2.7 %fusion.93 = (bf16[1024,256]{0,1:T(8,128)(2,1)S(1)}, f32[1024,256]{0,1:T(8,128)S(1)}) fusion(f32[1024,256]{0,1:T(8,128)S(1)} %get-tuple-element.39, f32[1024,256]{0,1:T(8,128)S(1)} %get-tuple-element.38, bf16[1024,64]{0,1:T(8,128)(2,1)} %collective-permute-done.5, bf16[1024,256]{0,1:T(8,128)(2,1)S(1)} %fusion.56, ...), kind=kOutput, calls=%fused_computation.190 | convolution fusion | flops 141557760 | bytes 6695936 | tf_op jit(solution)/shard_map/dot_general | solution.py:88
  72.9 0.7 fusion.36
  73.8 1.6 %collective-permute-start.9 = (bf16[256,256]{0,1:T(8,128)(2,1)S(1)}, bf16[256,256]{0,1:T(8,128)(2,1)S(1)}, u32[]{:S(2)}, u32[]{:S(2)}) collective-permute-start(bf16[256,256]{0,1:T(8,128)(2,1)S(1)} %pad_maximum_fusion.12), channel_id=1, source_target_pairs={{0,8},{8,16},{16,24},{1,9},{9,17},{17,25},{2,10},{10,18},{18,26},{... | collective-permute-start | bytes 393224 | tf_op jit(solution)/shard_map/ppermute | solution.py:84
  75.5 1.3 collective-permute-start.12
  76.8 4.6 %collective-permute-start.11 = (bf16[1024,64]{0,1:T(8,128)(2,1)S(1)}, bf16[1024,64]{0,1:T(8,128)(2,1)S(1)}, u32[]{:S(2)}, u32[]{:S(2)}) collective-permute-start(bf16[1024,64]{0,1:T(8,128)(2,1)S(1)} %get-tuple-element.26), channel_id=1, source_target_pairs={{0,1},{1,2},{2,3},{3,4},{4,5},{5,6},{6,7},{8,9},{9,10},{10,11},{11... | collective-permute-start | bytes 393224 | tf_op jit(solution)/shard_map/ppermute | solution.py:27
  81.4 1.5 collective-permute-start.10
  83.6 2.3 %collective-permute-done.11 = bf16[1024,64]{0,1:T(8,128)(2,1)S(1)} collective-permute-done((bf16[1024,64]{0,1:T(8,128)(2,1)S(1)}, bf16[1024,64]{0,1:T(8,128)(2,1)S(1)}, u32[]{:S(2)}, u32[]{:S(2)}) %collective-permute-start.11) | collective-permute-done | bytes 131104 | tf_op jit(solution)/shard_map/ppermute | solution.py:27
  85.9 0.8 fusion.94
  86.7 0.7 fusion.34
  87.6 4.2 %collective-permute-start.13 = (bf16[256,256]{0,1:T(8,128)(2,1)S(1)}, bf16[256,256]{0,1:T(8,128)(2,1)S(1)}, u32[]{:S(2)}, u32[]{:S(2)}) collective-permute-start(bf16[256,256]{0,1:T(8,128)(2,1)S(1)} %pad_maximum_fusion.14), channel_id=1, source_target_pairs={{0,8},{8,16},{16,24},{1,9},{9,17},{17,25},{2,10},{10,18},{18,26},{... | collective-permute-start | bytes 393224 | tf_op jit(solution)/shard_map/ppermute | solution.py:84
  92.0 1.3 collective-permute-start.16
  93.3 4.6 %collective-permute-start.15 = (bf16[1024,64]{0,1:T(8,128)(2,1)S(1)}, bf16[1024,64]{0,1:T(8,128)(2,1)S(1)}, u32[]{:S(2)}, u32[]{:S(2)}) collective-permute-start(bf16[1024,64]{0,1:T(8,128)(2,1)S(1)} %get-tuple-element.20), channel_id=1, source_target_pairs={{0,1},{1,2},{2,3},{3,4},{4,5},{5,6},{6,7},{8,9},{9,10},{10,11},{11... | collective-permute-start | bytes 393224 | tf_op jit(solution)/shard_map/ppermute | solution.py:27
  97.9 1.3 collective-permute-start.14
  99.5 2.8 %collective-permute-done.15 = bf16[1024,64]{0,1:T(8,128)(2,1)S(1)} collective-permute-done((bf16[1024,64]{0,1:T(8,128)(2,1)S(1)}, bf16[1024,64]{0,1:T(8,128)(2,1)S(1)}, u32[]{:S(2)}, u32[]{:S(2)}) %collective-permute-start.15) | collective-permute-done | bytes 131104 | tf_op jit(solution)/shard_map/ppermute | solution.py:27
  102.3 0.8 fusion.95
  103.1 0.7 fusion.32
  104.0 3.3 %collective-permute-start.17 = (bf16[256,256]{0,1:T(8,128)(2,1)S(1)}, bf16[256,256]{0,1:T(8,128)(2,1)S(1)}, u32[]{:S(2)}, u32[]{:S(2)}) collective-permute-start(bf16[256,256]{0,1:T(8,128)(2,1)S(1)} %pad_maximum_fusion.16), channel_id=1, source_target_pairs={{0,8},{8,16},{16,24},{1,9},{9,17},{17,25},{2,10},{10,18},{18,26},{... | collective-permute-start | bytes 393224 | tf_op jit(solution)/shard_map/ppermute | solution.py:84
  107.4 1.3 collective-permute-start.20
  108.7 5.2 %collective-permute-start.19 = (bf16[1024,64]{0,1:T(8,128)(2,1)S(1)}, bf16[1024,64]{0,1:T(8,128)(2,1)S(1)}, u32[]{:S(2)}, u32[]{:S(2)}) collective-permute-start(bf16[1024,64]{0,1:T(8,128)(2,1)S(1)} %get-tuple-element.14), channel_id=1, source_target_pairs={{0,1},{1,2},{2,3},{3,4},{4,5},{5,6},{6,7},{8,9},{9,10},{10,11},{11... | collective-permute-start | bytes 393224 | tf_op jit(solution)/shard_map/ppermute | solution.py:27
  113.9 1.3 collective-permute-start.18
  115.6 3.0 %collective-permute-done.19 = bf16[1024,64]{0,1:T(8,128)(2,1)S(1)} collective-permute-done((bf16[1024,64]{0,1:T(8,128)(2,1)S(1)}, bf16[1024,64]{0,1:T(8,128)(2,1)S(1)}, u32[]{:S(2)}, u32[]{:S(2)}) %collective-permute-start.19) | collective-permute-done | bytes 131104 | tf_op jit(solution)/shard_map/ppermute | solution.py:27
  118.6 1.8 %fusion.96 = (bf16[1024,256]{0,1:T(8,128)(2,1)S(1)}, f32[1024,256]{0,1:T(8,128)}) fusion(f32[1024,256]{0,1:T(8,128)S(1)} %get-tuple-element.62, f32[1024,256]{0,1:T(8,128)S(1)} %get-tuple-element.39, f32[1024,256]{0,1:T(8,128)S(1)} %fusion.3, bf16[1024,64]{0,1:T(8,128)(2,1)S(1)} %collective-permute-done.20, bf16[1024,256]{0,1:T(8,128)(2,1)S(1)} %get-tuple-element.61, ...), kind=kOutput, calls=%fused_computation.193 | convolution fusion | flops 140247040 | bytes 7735296 | tf_op jit(solution)/shard_map/dot_general | solution.py:88
  120.3 1.7 %fusion.40 = f32[1024,256]{0,1:T(8,128)} fusion(bf16[1024,256]{0,1:T(8,128)(2,1)S(1)} %get-tuple-element.63, bf16[1024,1536]{1,0:T(8,128)(2,1)S(1)} %bitcast.63), kind=kOutput, calls=%fused_computation.69 | convolution fusion | flops 536870912 | bytes 3670016 | tf_op jit(solution)/shard_map/dot_general | solution.py:86
  122.1 3.9 %collective-permute-start.21 = (bf16[256,256]{0,1:T(8,128)(2,1)S(1)}, bf16[256,256]{0,1:T(8,128)(2,1)}, u32[]{:S(2)}, u32[]{:S(2)}) collective-permute-start(bf16[256,256]{0,1:T(8,128)(2,1)S(1)} %pad_maximum_fusion.18), channel_id=1, source_target_pairs={{0,8},{8,16},{16,24},{1,9},{9,17},{17,25},{2,10},{10,18},{18,26},{... | collective-permute-start | bytes 393224 | tf_op jit(solution)/shard_map/ppermute | solution.py:84
  126.1 0.7 fusion.85
  126.7 2.5 %copy.33 = f32[1024,256]{1,0:T(8,128)} copy(f32[1024,256]{0,1:T(8,128)} %get-tuple-element.64) | data formatting | bytes 2097152
  129.3 1.3 collective-permute-start.24
  130.6 5.2 %collective-permute-start.23 = (bf16[1024,64]{0,1:T(8,128)(2,1)S(1)}, bf16[1024,64]{0,1:T(8,128)(2,1)S(1)}, u32[]{:S(2)}, u32[]{:S(2)}) collective-permute-start(bf16[1024,64]{0,1:T(8,128)(2,1)S(1)} %get-tuple-element.12), channel_id=1, source_target_pairs={{0,1},{1,2},{2,3},{3,4},{4,5},{5,6},{6,7},{8,9},{9,10},{10,11},{11... | collective-permute-start | bytes 393224 | tf_op jit(solution)/shard_map/ppermute | solution.py:27
  135.7 1.3 collective-permute-start.22
  137.1 1.8 %convolution_add_fusion.1 = f32[1024,256]{0,1:T(8,128)S(1)} fusion(f32[1024,256]{0,1:T(8,128)} %fusion.40, bf16[256,256]{0,1:T(8,128)(2,1)} %collective-permute-done.21, bf16[1024,1536]{1,0:T(8,128)(2,1)} %bitcast.52), kind=kOutput, calls=%fused_computation.23 | convolution fusion | flops 134479872 | bytes 2752512 | tf_op jit(solution)/shard_map/dot_general | solution.py:87
  138.8 1.1 collective-permute-done.23
  140.4 1.5 fusion.31
  141.8 6.4 %psum.7 = f32[2,256]{1,0:T(2,128)S(1)} all-reduce(f32[2,256]{1,0:T(2,128)S(1)} %pad_maximum_fusion.20), channel_id=1, replica_groups=mesh['space'=4,'tm'=8] {'space'}, use_global_device_ids=true, to_apply=%region_5.6 | all-reduce | flops 512 | bytes 4096 | tf_op jit(solution)/shard_map/psum | solution.py:155
  (73 shorter events, 4.3 us)
Async XLA Ops:
  0.6 16.2 %copy-start = (bf16[8,8,128,128]{3,2,1,0:T(8,128)(2,1)S(1)}, bf16[8,8,128,128]{3,2,1,0:T(8,128)(2,1)}, u32[]{:S(2)}) copy-start(bf16[8,8,128,128]{3,2,1,0:T(8,128)(2,1)} %param.17) | copy-start | bytes 6291460
  0.6 16.2 %copy-start.6 = (s32[8,8]{1,0:T(8,128)S(1)}, s32[8,8]{1,0:T(8,128)}, u32[]{:S(2)}) copy-start(s32[8,8]{1,0:T(8,128)} %param.18) | copy-start | bytes 772
  0.7 35.1 %collective-permute-start.8 = (bf16[1024,256]{1,0:T(8,128)(2,1)}, bf16[1024,256]{1,0:T(8,128)(2,1)}, u32[]{:S(2)}, u32[]{:S(2)}) collective-permute-start(bf16[1024,256]{1,0:T(8,128)(2,1)} %param.23), channel_id=1, source_target_pairs={{0,24},{8,0},{16,8},{24,16},{1,25},{9,1},{17,9},{25,17},{2,26},{10... | collective-permute-start | bytes 1572872 | tf_op jit(solution)/shard_map/ppermute | solution.py:105
  3.1 38.0 %collective-permute-start.7 = (bf16[1024,256]{1,0:T(8,128)(2,1)}, bf16[1024,256]{1,0:T(8,128)(2,1)}, u32[]{:S(2)}, u32[]{:S(2)}) collective-permute-start(bf16[1024,256]{1,0:T(8,128)(2,1)} %param.23), channel_id=1, source_target_pairs={{0,16},{8,24},{16,0},{24,8},{1,17},{9,25},{17,1},{25,9},{2,18},{10... | collective-permute-start | bytes 1572872 | tf_op jit(solution)/shard_map/ppermute | solution.py:105
  3.8 38.6 %collective-permute-start.6 = (bf16[1024,256]{1,0:T(8,128)(2,1)}, bf16[1024,256]{1,0:T(8,128)(2,1)}, u32[]{:S(2)}, u32[]{:S(2)}) collective-permute-start(bf16[1024,256]{1,0:T(8,128)(2,1)} %param.23), channel_id=1, source_target_pairs={{0,8},{8,16},{16,24},{24,0},{1,9},{9,17},{17,25},{25,1},{2,10},{10... | collective-permute-start | bytes 1572872 | tf_op jit(solution)/shard_map/ppermute | solution.py:105
  9.7 60.5 %collective-permute-start.5 = (bf16[1024,64]{0,1:T(8,128)(2,1)}, bf16[1024,64]{0,1:T(8,128)(2,1)}, u32[]{:S(2)}, u32[]{:S(2)}) collective-permute-start(bf16[1024,64]{0,1:T(8,128)(2,1)} %get-tuple-element.33), channel_id=1, source_target_pairs={{1,0},{2,1},{3,2},{4,3},{5,4},{6,5},{7,6},{9,8},{10,9},{11,10},{12... | collective-permute-start | bytes 393224 | tf_op jit(solution)/shard_map/ppermute | solution.py:28
  11.8 13.2 %collective-permute-start.2 = (s32[2]{0:T(128)S(1)}, s32[2]{0:T(128)S(1)}, u32[]{:S(2)}, u32[]{:S(2)}) collective-permute-start(s32[2]{0:T(128)S(1)} %get-tuple-element.53), channel_id=1, source_target_pairs={{0,8},{8,16},{16,24},{1,9},{9,17},{17,25},{2,10},{10,18},{18,26},{... | collective-permute-start | bytes 32 | tf_op jit(solution)/shard_map/ppermute | solution.py:75
  21.6 1.6 %copy-start.1 = (bf16[128,8,12,128]{3,1,2,0:T(8,128)(2,1)}, bf16[128,8,12,128]{3,1,2,0:T(8,128)(2,1)S(1)}, u32[]{:S(2)}) copy-start(bf16[128,8,12,128]{3,1,2,0:T(8,128)(2,1)S(1)} %copy.46) | copy-start | bytes 9437188
  21.6 3.3 %copy-start.4 = (s32[2048,1]{0,1:T(1,128)S(1)}, s32[2048,1]{0,1:T(1,128)}, u32[]{:S(2)}) copy-start(s32[2048,1]{0,1:T(1,128)} %param.21) | copy-start | bytes 24580
  21.6 3.4 %copy-start.5 = (s32[2048]{0:T(1024)S(1)}, s32[2048]{0:T(1024)}, u32[]{:S(2)}) copy-start(s32[2048]{0:T(1024)} %param.22) | copy-start | bytes 24580
  25.0 4.6 %collective-permute-start = (s32[2]{0:T(128)S(1)}, s32[2]{0:T(128)S(1)}, u32[]{:S(2)}, u32[]{:S(2)}) collective-permute-start(s32[2]{0:T(128)S(1)} %get-tuple-element.54), channel_id=1, source_target_pairs={{8,0},{16,8},{24,16},{9,1},{17,9},{25,17},{10,2},{18,10},{26,18},{... | collective-permute-start | bytes 32 | tf_op jit(solution)/shard_map/ppermute | solution.py:74
  29.7 40.5 %collective-permute-start.4 = (bf16[1024,64]{0,1:T(8,128)(2,1)}, bf16[1024,64]{0,1:T(8,128)(2,1)}, u32[]{:S(2)}, u32[]{:S(2)}) collective-permute-start(bf16[1024,64]{0,1:T(8,128)(2,1)} %get-tuple-element.32), channel_id=1, source_target_pairs={{0,1},{1,2},{2,3},{3,4},{4,5},{5,6},{6,7},{8,9},{9,10},{10,11},{11... | collective-permute-start | bytes 393224 | tf_op jit(solution)/shard_map/ppermute | solution.py:27
  35.7 30.0 %collective-permute-start.1 = (bf16[256,256]{0,1:T(8,128)(2,1)S(1)}, bf16[256,256]{0,1:T(8,128)(2,1)}, u32[]{:S(2)}, u32[]{:S(2)}) collective-permute-start(bf16[256,256]{0,1:T(8,128)(2,1)S(1)} %pad_maximum_fusion.10), channel_id=1, source_target_pairs={{0,8},{8,16},{16,24},{1,9},{9,17},{17,25},{2,10},{10,18},{18,26},{... | collective-permute-start | bytes 393224 | tf_op jit(solution)/shard_map/ppermute | solution.py:84
  41.1 29.1 %collective-permute-start.3 = (bf16[256,256]{0,1:T(8,128)(2,1)S(1)}, bf16[256,256]{0,1:T(8,128)(2,1)}, u32[]{:S(2)}, u32[]{:S(2)}) collective-permute-start(bf16[256,256]{0,1:T(8,128)(2,1)S(1)} %pad_maximum_fusion.11), channel_id=1, source_target_pairs={{8,0},{16,8},{24,16},{9,1},{17,9},{25,17},{10,2},{18,10},{26,18},{... | collective-permute-start | bytes 393224 | tf_op jit(solution)/shard_map/ppermute | solution.py:85
  59.3 10.5 %copy-start.3 = (f32[1024]{0:T(1024)S(1)}, f32[1024]{0:T(1024)}, u32[]{:S(2)}) copy-start(f32[1024]{0:T(1024)} %param.13) | copy-start | bytes 12292
  61.7 8.1 %all-to-all-start = ((f32[4,4,1024]{2,1,0:T(4,128)}), f32[4,4,1024]{2,1,0:T(4,128)S(1)}, u32[]{:S(2)}, u32[]{:S(2)}) async-start(f32[4,4,1024]{2,1,0:T(4,128)} %add.190), calls=%async_computation | async-start | bytes 131072 | tf_op jit(solution)/shard_map/all_to_all | solution.py:129
  70.2 2.7 %copy-start.2 = (bf16[128,8,12,128]{3,1,2,0:T(8,128)(2,1)S(1)}, bf16[128,8,12,128]{3,1,2,0:T(8,128)(2,1)}, u32[]{:S(2)}) copy-start(bf16[128,8,12,128]{3,1,2,0:T(8,128)(2,1)} %copy-done.1) | copy-start | bytes 9437188
  73.8 9.1 %collective-permute-start.9 = (bf16[256,256]{0,1:T(8,128)(2,1)S(1)}, bf16[256,256]{0,1:T(8,128)(2,1)S(1)}, u32[]{:S(2)}, u32[]{:S(2)}) collective-permute-start(bf16[256,256]{0,1:T(8,128)(2,1)S(1)} %pad_maximum_fusion.12), channel_id=1, source_target_pairs={{0,8},{8,16},{16,24},{1,9},{9,17},{17,25},{2,10},{10,18},{18,26},{... | collective-permute-start | bytes 393224 | tf_op jit(solution)/shard_map/ppermute | solution.py:84
  75.5 8.1 %collective-permute-start.12 = (bf16[1024,64]{0,1:T(8,128)(2,1)S(1)}, bf16[1024,64]{0,1:T(8,128)(2,1)S(1)}, u32[]{:S(2)}, u32[]{:S(2)}) collective-permute-start(bf16[1024,64]{0,1:T(8,128)(2,1)S(1)} %get-tuple-element.27), channel_id=1, source_target_pairs={{1,0},{2,1},{3,2},{4,3},{5,4},{6,5},{7,6},{9,8},{10,9},{11,10},{12... | collective-permute-start | bytes 393224 | tf_op jit(solution)/shard_map/ppermute | solution.py:28
  76.8 9.1 %collective-permute-start.11 = (bf16[1024,64]{0,1:T(8,128)(2,1)S(1)}, bf16[1024,64]{0,1:T(8,128)(2,1)S(1)}, u32[]{:S(2)}, u32[]{:S(2)}) collective-permute-start(bf16[1024,64]{0,1:T(8,128)(2,1)S(1)} %get-tuple-element.26), channel_id=1, source_target_pairs={{0,1},{1,2},{2,3},{3,4},{4,5},{5,6},{6,7},{8,9},{9,10},{10,11},{11... | collective-permute-start | bytes 393224 | tf_op jit(solution)/shard_map/ppermute | solution.py:27
  81.4 4.5 %collective-permute-start.10 = (bf16[256,256]{0,1:T(8,128)(2,1)S(1)}, bf16[256,256]{0,1:T(8,128)(2,1)S(1)}, u32[]{:S(2)}, u32[]{:S(2)}) collective-permute-start(bf16[256,256]{0,1:T(8,128)(2,1)S(1)} %pad_maximum_fusion.13), channel_id=1, source_target_pairs={{8,0},{16,8},{24,16},{9,1},{17,9},{25,17},{10,2},{18,10},{26,18},{... | collective-permute-start | bytes 393224 | tf_op jit(solution)/shard_map/ppermute | solution.py:85
  87.6 11.6 %collective-permute-start.13 = (bf16[256,256]{0,1:T(8,128)(2,1)S(1)}, bf16[256,256]{0,1:T(8,128)(2,1)S(1)}, u32[]{:S(2)}, u32[]{:S(2)}) collective-permute-start(bf16[256,256]{0,1:T(8,128)(2,1)S(1)} %pad_maximum_fusion.14), channel_id=1, source_target_pairs={{0,8},{8,16},{16,24},{1,9},{9,17},{17,25},{2,10},{10,18},{18,26},{... | collective-permute-start | bytes 393224 | tf_op jit(solution)/shard_map/ppermute | solution.py:84
  92.0 7.5 %collective-permute-start.16 = (bf16[1024,64]{0,1:T(8,128)(2,1)S(1)}, bf16[1024,64]{0,1:T(8,128)(2,1)S(1)}, u32[]{:S(2)}, u32[]{:S(2)}) collective-permute-start(bf16[1024,64]{0,1:T(8,128)(2,1)S(1)} %get-tuple-element.21), channel_id=1, source_target_pairs={{1,0},{2,1},{3,2},{4,3},{5,4},{6,5},{7,6},{9,8},{10,9},{11,10},{12... | collective-permute-start | bytes 393224 | tf_op jit(solution)/shard_map/ppermute | solution.py:28
  93.3 9.0 %collective-permute-start.15 = (bf16[1024,64]{0,1:T(8,128)(2,1)S(1)}, bf16[1024,64]{0,1:T(8,128)(2,1)S(1)}, u32[]{:S(2)}, u32[]{:S(2)}) collective-permute-start(bf16[1024,64]{0,1:T(8,128)(2,1)S(1)} %get-tuple-element.20), channel_id=1, source_target_pairs={{0,1},{1,2},{2,3},{3,4},{4,5},{5,6},{6,7},{8,9},{9,10},{10,11},{11... | collective-permute-start | bytes 393224 | tf_op jit(solution)/shard_map/ppermute | solution.py:27
  97.9 4.4 %collective-permute-start.14 = (bf16[256,256]{0,1:T(8,128)(2,1)S(1)}, bf16[256,256]{0,1:T(8,128)(2,1)S(1)}, u32[]{:S(2)}, u32[]{:S(2)}) collective-permute-start(bf16[256,256]{0,1:T(8,128)(2,1)S(1)} %pad_maximum_fusion.15), channel_id=1, source_target_pairs={{8,0},{16,8},{24,16},{9,1},{17,9},{25,17},{10,2},{18,10},{26,18},{... | collective-permute-start | bytes 393224 | tf_op jit(solution)/shard_map/ppermute | solution.py:85
  104.0 11.2 %collective-permute-start.17 = (bf16[256,256]{0,1:T(8,128)(2,1)S(1)}, bf16[256,256]{0,1:T(8,128)(2,1)S(1)}, u32[]{:S(2)}, u32[]{:S(2)}) collective-permute-start(bf16[256,256]{0,1:T(8,128)(2,1)S(1)} %pad_maximum_fusion.16), channel_id=1, source_target_pairs={{0,8},{8,16},{16,24},{1,9},{9,17},{17,25},{2,10},{10,18},{18,26},{... | collective-permute-start | bytes 393224 | tf_op jit(solution)/shard_map/ppermute | solution.py:84
  107.4 8.2 %collective-permute-start.20 = (bf16[1024,64]{0,1:T(8,128)(2,1)S(1)}, bf16[1024,64]{0,1:T(8,128)(2,1)S(1)}, u32[]{:S(2)}, u32[]{:S(2)}) collective-permute-start(bf16[1024,64]{0,1:T(8,128)(2,1)S(1)} %get-tuple-element.15), channel_id=1, source_target_pairs={{1,0},{2,1},{3,2},{4,3},{5,4},{6,5},{7,6},{9,8},{10,9},{11,10},{12... | collective-permute-start | bytes 393224 | tf_op jit(solution)/shard_map/ppermute | solution.py:28
  108.7 9.9 %collective-permute-start.19 = (bf16[1024,64]{0,1:T(8,128)(2,1)S(1)}, bf16[1024,64]{0,1:T(8,128)(2,1)S(1)}, u32[]{:S(2)}, u32[]{:S(2)}) collective-permute-start(bf16[1024,64]{0,1:T(8,128)(2,1)S(1)} %get-tuple-element.14), channel_id=1, source_target_pairs={{0,1},{1,2},{2,3},{3,4},{4,5},{5,6},{6,7},{8,9},{9,10},{10,11},{11... | collective-permute-start | bytes 393224 | tf_op jit(solution)/shard_map/ppermute | solution.py:27
  113.9 4.7 %collective-permute-start.18 = (bf16[256,256]{0,1:T(8,128)(2,1)S(1)}, bf16[256,256]{0,1:T(8,128)(2,1)S(1)}, u32[]{:S(2)}, u32[]{:S(2)}) collective-permute-start(bf16[256,256]{0,1:T(8,128)(2,1)S(1)} %pad_maximum_fusion.17), channel_id=1, source_target_pairs={{8,0},{16,8},{24,16},{9,1},{17,9},{25,17},{10,2},{18,10},{26,18},{... | collective-permute-start | bytes 393224 | tf_op jit(solution)/shard_map/ppermute | solution.py:85
  122.1 14.9 %collective-permute-start.21 = (bf16[256,256]{0,1:T(8,128)(2,1)S(1)}, bf16[256,256]{0,1:T(8,128)(2,1)}, u32[]{:S(2)}, u32[]{:S(2)}) collective-permute-start(bf16[256,256]{0,1:T(8,128)(2,1)S(1)} %pad_maximum_fusion.18), channel_id=1, source_target_pairs={{0,8},{8,16},{16,24},{1,9},{9,17},{17,25},{2,10},{10,18},{18,26},{... | collective-permute-start | bytes 393224 | tf_op jit(solution)/shard_map/ppermute | solution.py:84
  129.3 9.6 %collective-permute-start.24 = (bf16[1024,64]{0,1:T(8,128)(2,1)}, bf16[1024,64]{0,1:T(8,128)(2,1)S(1)}, u32[]{:S(2)}, u32[]{:S(2)}) collective-permute-start(bf16[1024,64]{0,1:T(8,128)(2,1)} %get-tuple-element.13), channel_id=1, source_target_pairs={{1,0},{2,1},{3,2},{4,3},{5,4},{6,5},{7,6},{9,8},{10,9},{11,10},{12... | collective-permute-start | bytes 393224 | tf_op jit(solution)/shard_map/ppermute | solution.py:28
  130.6 9.4 %collective-permute-start.23 = (bf16[1024,64]{0,1:T(8,128)(2,1)S(1)}, bf16[1024,64]{0,1:T(8,128)(2,1)S(1)}, u32[]{:S(2)}, u32[]{:S(2)}) collective-permute-start(bf16[1024,64]{0,1:T(8,128)(2,1)S(1)} %get-tuple-element.12), channel_id=1, source_target_pairs={{0,1},{1,2},{2,3},{3,4},{4,5},{5,6},{6,7},{8,9},{9,10},{10,11},{11... | collective-permute-start | bytes 393224 | tf_op jit(solution)/shard_map/ppermute | solution.py:27
  135.7 4.6 %collective-permute-start.22 = (bf16[256,256]{0,1:T(8,128)(2,1)S(1)}, bf16[256,256]{0,1:T(8,128)(2,1)S(1)}, u32[]{:S(2)}, u32[]{:S(2)}) collective-permute-start(bf16[256,256]{0,1:T(8,128)(2,1)S(1)} %pad_maximum_fusion.19), channel_id=1, source_target_pairs={{8,0},{16,8},{24,16},{9,1},{17,9},{25,17},{10,2},{18,10},{26,18},{... | collective-permute-start | bytes 393224 | tf_op jit(solution)/shard_map/ppermute | solution.py:85

commit v13 on v12

--- a/solution.py
+++ b/solution.py
@@ -152,7 +152,13 @@
             jnp.sum(probe_vals * temporal(rounded), axis=0),
         ]
     )
-    totals = lax.psum(partial_sums, "space")
+    totals = jnp.sum(
+        lax.all_to_all(
+            jnp.broadcast_to(partial_sums[None], (space_count,) + partial_sums.shape),
+            "space", split_axis=0, concat_axis=0, tiled=True,
+        ),
+        axis=0,
+    )
     grads = totals / (NODES_DEV * space_count)
     return (solution, grads)
 

time: 150 us -> 146 us (0.973)
  blocking collectives: 6.43 us -> 0 us
  matrix products: 23.5 us -> 20 us
  waiting for transfers between devices: 12.4 us -> 15.6 us
  starting transfers between devices: 66.7 us -> 69.2 us
    psum x1 -> x0, blocking collectives: 6.43 us -> none  [shards(): totals = lax.psum(partial_sums, 'space')]
    all_to_all x0 -> x1, starting transfers between devices: none -> 3.23 us  [shards(): lax.all_to_all(jnp.broadcast_to(partial_sums[None], (space_count,) + part...]
    ppermute x5, waiting for transfers between devices: 9.16 us -> 11 us  [with_halo(): before = lax.ppermute(last, axis, up)]
  transfers between devices with their start and end apart: 26 -> 27, of which waited for: 7 -> 8; matrix products, arithmetic and copies ran while one was open for 30% -> 30% of each run, Pallas kernels for 0% -> 0%
where the time goes in v13:
time: 146 us; the launch traced here: 145 us
  starting transfers between devices  69.2 us (47%)
  local copies, waits for them, and re-layouts  24 us (16%)
  matrix products  20 us (14%)
  waiting for transfers between devices  15.6 us (11%)
  other arithmetic  12 us (8%)
  between operations  3.88 us (3%)
    ppermute x5, starting transfers between devices, with_halo(): before = lax.ppermute(last, axis, up)  23.5 us
    ppermute x5, starting transfers between devices, spatial(): lower = lax.ppermute(pick_blocks(field, upper_wants), 'space', up)  17.7 us
    ppermute x5, waiting for transfers between devices, with_halo(): before = lax.ppermute(last, axis, up)  11 us
    gather x1, local copies, waits for them, and re-layouts, shards(): coef_rows = svc_all[shift * nodes_dev + obs_cell // T_DEV]  10.8 us
    unnamed x17, local copies, waits for them, and re-layouts  7.02 us
    ppermute x5, starting transfers between devices, spatial(): upper = lax.ppermute(pick_blocks(field, lower_wants), 'space', down)  6.63 us
    dot_general x5, matrix products, spatial(): jnp.dot(upper.T, upper_t, preferred_element_type=jnp.float32)  6.46 us
    ppermute x5, starting transfers between devices, with_halo(): after = lax.ppermute(initial, axis, down)  6.45 us
  transfers between devices with their start and end apart: 27, of which 8 were waited for; matrix products, arithmetic and copies ran while one was open for 30% of the time, Pallas kernels for 0%

profile of v13, /device:TPU:0, one launch (start us, length us, event | category | flops | bytes accessed | tf_op | source)
XLA Modules:
  0.0 144.6 jit_solution(2602311455721596753)
XLA Ops:
  0.7 2.5 %collective-permute-start.8 = (bf16[1024,256]{1,0:T(8,128)(2,1)}, bf16[1024,256]{1,0:T(8,128)(2,1)}, u32[]{:S(2)}, u32[]{:S(2)}) collective-permute-start(bf16[1024,256]{1,0:T(8,128)(2,1)} %param.23), channel_id=1, source_target_pairs={{0,24},{8,0},{16,8},{24,16},{1,25},{9,1},{17,9},{25,17},{2,26},{10... | collective-permute-start | bytes 1572872 | tf_op jit(solution)/shard_map/ppermute | solution.py:105
  3.1 0.6 collective-permute-start.7
  4.0 1.2 copy.41
  5.2 0.7 broadcast_in_dim.73
  6.0 0.7 broadcast_in_dim.70
  6.8 1.1 select_reduce_fusion
  7.9 1.1 fusion.56
  9.0 0.7 fusion.89
  9.7 1.3 collective-permute-start.5
  11.0 0.8 fusion.91
  11.8 3.2 %collective-permute-start.2 = (s32[2]{0:T(128)S(1)}, s32[2]{0:T(128)S(1)}, u32[]{:S(2)}, u32[]{:S(2)}) collective-permute-start(s32[2]{0:T(128)S(1)} %get-tuple-element.57), channel_id=1, source_target_pairs={{0,8},{8,16},{16,24},{1,9},{9,17},{17,25},{2,10},{10,18},{18,26},{... | collective-permute-start | bytes 32 | tf_op jit(solution)/shard_map/ppermute | solution.py:75
  15.1 1.8 %convert_element_type.89 = f32[8,128,128]{2,1,0:T(8,128)} convert(bf16[8,128,128]{2,1,0:T(8,128)(2,1)} %param.16) | non-fusion elementwise | flops 131072 | bytes 786432 | tf_op jit(solution)/shard_map/convert_element_type | solution.py:52
  16.9 3.1 %add_convert_fusion = bf16[8,12,128,128]{3,1,2,0:T(8,128)(2,1)S(1)} fusion(f32[8,128,128]{2,1,0:T(8,128)} %convert_element_type.89, f32[8,12]{1,0:T(8,128)S(1)} %fusion.82, bf16[8,8,128,128]{3,2,1,0:T(8,128)(2,1)S(1)} %copy-done, s32[8,8]{1,0:T(8,128)S(1)} %copy-done.6), kind=kOutput, calls=%fused_computation.2 | convolution fusion | flops 29885184 | bytes 5767808 | tf_op jit(solution)/shard_map/bkm,bkij->bimj/dot_general | solution.py:63
  20.0 1.6 %copy.62 = bf16[128,8,12,128]{3,1,2,0:T(8,128)(2,1)S(1)} copy(bf16[128,8,12,128]{3,2,1,0:T(8,128)(2,1)S(1)} %bitcast.48) | data formatting | bytes 6291456
  21.6 1.6 %copy-done.1 = bf16[128,8,12,128]{3,1,2,0:T(8,128)(2,1)} copy-done((bf16[128,8,12,128]{3,1,2,0:T(8,128)(2,1)}, bf16[128,8,12,128]{3,1,2,0:T(8,128)(2,1)S(1)}, u32[]{:S(2)}) %copy-start.1) | copy-done | bytes 3145752
  23.3 1.7 %fusion.38 = f32[1024,256]{0,1:T(8,128)} fusion(bf16[1024,256]{0,1:T(8,128)(2,1)S(1)} %fusion.56, bf16[1024,1536]{1,0:T(8,128)(2,1)S(1)} %bitcast.49), kind=kOutput, calls=%fused_computation.67 | convolution fusion | flops 536870912 | bytes 3670016 | tf_op jit(solution)/shard_map/dot_general | solution.py:86
  25.0 1.3 collective-permute-start
  26.3 0.6 fusion.90
  28.2 1.5 %collective-permute-done = s32[2]{0:T(128)S(1)} collective-permute-done((s32[2]{0:T(128)S(1)}, s32[2]{0:T(128)S(1)}, u32[]{:S(2)}, u32[]{:S(2)}) %collective-permute-start) | collective-permute-done | bytes 40 | tf_op jit(solution)/shard_map/ppermute | solution.py:74
  29.7 4.1 %collective-permute-start.4 = (bf16[1024,64]{0,1:T(8,128)(2,1)}, bf16[1024,64]{0,1:T(8,128)(2,1)}, u32[]{:S(2)}, u32[]{:S(2)}) collective-permute-start(bf16[1024,64]{0,1:T(8,128)(2,1)} %get-tuple-element.36), channel_id=1, source_target_pairs={{0,1},{1,2},{2,3},{3,4},{4,5},{5,6},{6,7},{8,9},{9,10},{10,11},{11... | collective-permute-start | bytes 393224 | tf_op jit(solution)/shard_map/ppermute | solution.py:27
  33.7 0.6 fusion.92
  35.8 5.4 %collective-permute-start.1 = (bf16[256,256]{0,1:T(8,128)(2,1)S(1)}, bf16[256,256]{0,1:T(8,128)(2,1)}, u32[]{:S(2)}, u32[]{:S(2)}) collective-permute-start(bf16[256,256]{0,1:T(8,128)(2,1)S(1)} %pad_maximum_fusion.10), channel_id=1, source_target_pairs={{0,8},{8,16},{16,24},{1,9},{9,17},{17,25},{2,10},{10,18},{18,26},{... | collective-permute-start | bytes 393224 | tf_op jit(solution)/shard_map/ppermute | solution.py:84
  41.2 1.3 collective-permute-start.3
  42.5 3.8 %maximum_convert_fusion = f32[4096,256]{1,0:T(8,128)} fusion(bf16[1024,256]{1,0:T(8,128)(2,1)} %collective-permute-done.8, bf16[1024,256]{1,0:T(8,128)(2,1)} %collective-permute-done.7, bf16[1024,256]{1,0:T(8,128)(2,1)} %collective-permute-done.6, bf16[1024,256]{1,0:T(8,128)(2,1)} %param.23), kind=kLoop, calls=%fused_computation.13 | loop fusion | flops 8388608 | bytes 6291456 | tf_op jit(solution)/shard_map/convert_element_type | solution.py:108
  46.3 10.8 %gather_fusion = f32[2048,256]{1,0:T(8,128)} fusion(f32[4096,256]{1,0:T(8,128)} %maximum_convert_fusion, s32[2048]{0:T(1024)S(1)} %get-tuple-element.51), kind=kCustom, calls=%fused_computation | custom fusion | bytes 4202496 | tf_op jit(solution)/shard_map/gather | solution.py:111
  57.1 2.2 %multiply_reduce_fusion = f32[2048]{0:T(1024)S(1)} fusion(f32[2048,256]{1,0:T(8,128)} %gather_fusion, bf16[2048,256]{1,0:T(8,128)(2,1)} %param.20), kind=kLoop, calls=%fused_computation.15 | loop fusion | flops 1570816 | bytes 3153920 | tf_op jit(solution)/shard_map/reduce_sum | solution.py:112
  59.4 1.7 %fusion = f32[48,1024]{1,0:T(8,128)S(1)} fusion(s32[2048]{0:T(1024)S(1)} %get-tuple-element.52, bf16[2048,16]{0,1:T(8,128)(2,1)S(1)} %get-tuple-element.45, bf16[2048,16]{0,1:T(8,128)(2,1)S(1)} %get-tuple-element.46, bf16[2048,16]{0,1:T(8,128)(2,1)S(1)} %get-tuple-element.44), kind=kOutput, calls=%fused_computation.3 | convolution fusion | flops 204013568 | bytes 401408 | tf_op jit(solution)/shard_map/dot_general | solution.py:124
  61.1 0.6 add.188
  61.8 3.8 %all-to-all-start = ((f32[4,4,1024]{2,1,0:T(4,128)}), f32[4,4,1024]{2,1,0:T(4,128)S(1)}, u32[]{:S(2)}, u32[]{:S(2)}) async-start(f32[4,4,1024]{2,1,0:T(4,128)} %add.188), calls=%async_computation | async-start | bytes 131072 | tf_op jit(solution)/shard_map/all_to_all | solution.py:129
  65.6 2.7 %convolution_add_fusion.9 = f32[1024,256]{0,1:T(8,128)} fusion(f32[1024,256]{0,1:T(8,128)} %fusion.38, bf16[256,256]{0,1:T(8,128)(2,1)} %collective-permute-done.1, bf16[1024,1536]{1,0:T(8,128)(2,1)} %bitcast.50), kind=kOutput, calls=%fused_computation.43 | convolution fusion | flops 134479872 | bytes 2752512 | tf_op jit(solution)/shard_map/dot_general | solution.py:87
  68.3 1.4 all-to-all-done
  70.1 2.7 %fusion.93 = (bf16[1024,256]{0,1:T(8,128)(2,1)S(1)}, f32[1024,256]{0,1:T(8,128)S(1)}) fusion(f32[1024,256]{0,1:T(8,128)S(1)} %get-tuple-element.43, f32[1024,256]{0,1:T(8,128)S(1)} %get-tuple-element.42, bf16[1024,64]{0,1:T(8,128)(2,1)} %collective-permute-done.5, bf16[1024,256]{0,1:T(8,128)(2,1)S(1)} %fusion.56, ...), kind=kOutput, calls=%fused_computation.190 | convolution fusion | flops 141557760 | bytes 6695936 | tf_op jit(solution)/shard_map/dot_general | solution.py:88
  72.8 0.7 fusion.36
  73.7 1.6 %collective-permute-start.9 = (bf16[256,256]{0,1:T(8,128)(2,1)S(1)}, bf16[256,256]{0,1:T(8,128)(2,1)S(1)}, u32[]{:S(2)}, u32[]{:S(2)}) collective-permute-start(bf16[256,256]{0,1:T(8,128)(2,1)S(1)} %pad_maximum_fusion.12), channel_id=1, source_target_pairs={{0,8},{8,16},{16,24},{1,9},{9,17},{17,25},{2,10},{10,18},{18,26},{... | collective-permute-start | bytes 393224 | tf_op jit(solution)/shard_map/ppermute | solution.py:84
  75.4 1.3 collective-permute-start.12
  76.7 4.6 %collective-permute-start.11 = (bf16[1024,64]{0,1:T(8,128)(2,1)S(1)}, bf16[1024,64]{0,1:T(8,128)(2,1)S(1)}, u32[]{:S(2)}, u32[]{:S(2)}) collective-permute-start(bf16[1024,64]{0,1:T(8,128)(2,1)S(1)} %get-tuple-element.30), channel_id=1, source_target_pairs={{0,1},{1,2},{2,3},{3,4},{4,5},{5,6},{6,7},{8,9},{9,10},{10,11},{11... | collective-permute-start | bytes 393224 | tf_op jit(solution)/shard_map/ppermute | solution.py:27
  81.3 1.5 %collective-permute-start.10 = (bf16[256,256]{0,1:T(8,128)(2,1)S(1)}, bf16[256,256]{0,1:T(8,128)(2,1)S(1)}, u32[]{:S(2)}, u32[]{:S(2)}) collective-permute-start(bf16[256,256]{0,1:T(8,128)(2,1)S(1)} %pad_maximum_fusion.13), channel_id=1, source_target_pairs={{8,0},{16,8},{24,16},{9,1},{17,9},{25,17},{10,2},{18,10},{26,18},{... | collective-permute-start | bytes 393224 | tf_op jit(solution)/shard_map/ppermute | solution.py:85
  83.5 2.3 %collective-permute-done.11 = bf16[1024,64]{0,1:T(8,128)(2,1)S(1)} collective-permute-done((bf16[1024,64]{0,1:T(8,128)(2,1)S(1)}, bf16[1024,64]{0,1:T(8,128)(2,1)S(1)}, u32[]{:S(2)}, u32[]{:S(2)}) %collective-permute-start.11) | collective-permute-done | bytes 131104 | tf_op jit(solution)/shard_map/ppermute | solution.py:27
  85.8 0.8 fusion.94
  86.6 0.7 fusion.34
  87.5 4.3 %collective-permute-start.13 = (bf16[256,256]{0,1:T(8,128)(2,1)S(1)}, bf16[256,256]{0,1:T(8,128)(2,1)S(1)}, u32[]{:S(2)}, u32[]{:S(2)}) collective-permute-start(bf16[256,256]{0,1:T(8,128)(2,1)S(1)} %pad_maximum_fusion.14), channel_id=1, source_target_pairs={{0,8},{8,16},{16,24},{1,9},{9,17},{17,25},{2,10},{10,18},{18,26},{... | collective-permute-start | bytes 393224 | tf_op jit(solution)/shard_map/ppermute | solution.py:84
  91.9 1.3 collective-permute-start.16
  93.2 4.6 %collective-permute-start.15 = (bf16[1024,64]{0,1:T(8,128)(2,1)S(1)}, bf16[1024,64]{0,1:T(8,128)(2,1)S(1)}, u32[]{:S(2)}, u32[]{:S(2)}) collective-permute-start(bf16[1024,64]{0,1:T(8,128)(2,1)S(1)} %get-tuple-element.24), channel_id=1, source_target_pairs={{0,1},{1,2},{2,3},{3,4},{4,5},{5,6},{6,7},{8,9},{9,10},{10,11},{11... | collective-permute-start | bytes 393224 | tf_op jit(solution)/shard_map/ppermute | solution.py:27
  97.8 1.3 collective-permute-start.14
  99.4 2.8 %collective-permute-done.15 = bf16[1024,64]{0,1:T(8,128)(2,1)S(1)} collective-permute-done((bf16[1024,64]{0,1:T(8,128)(2,1)S(1)}, bf16[1024,64]{0,1:T(8,128)(2,1)S(1)}, u32[]{:S(2)}, u32[]{:S(2)}) %collective-permute-start.15) | collective-permute-done | bytes 131104 | tf_op jit(solution)/shard_map/ppermute | solution.py:27
  102.2 0.8 fusion.95
  103.0 0.7 fusion.32
  103.9 3.3 %collective-permute-start.17 = (bf16[256,256]{0,1:T(8,128)(2,1)S(1)}, bf16[256,256]{0,1:T(8,128)(2,1)S(1)}, u32[]{:S(2)}, u32[]{:S(2)}) collective-permute-start(bf16[256,256]{0,1:T(8,128)(2,1)S(1)} %pad_maximum_fusion.16), channel_id=1, source_target_pairs={{0,8},{8,16},{16,24},{1,9},{9,17},{17,25},{2,10},{10,18},{18,26},{... | collective-permute-start | bytes 393224 | tf_op jit(solution)/shard_map/ppermute | solution.py:84
  107.3 1.3 collective-permute-start.20
  108.6 5.2 %collective-permute-start.19 = (bf16[1024,64]{0,1:T(8,128)(2,1)S(1)}, bf16[1024,64]{0,1:T(8,128)(2,1)S(1)}, u32[]{:S(2)}, u32[]{:S(2)}) collective-permute-start(bf16[1024,64]{0,1:T(8,128)(2,1)S(1)} %get-tuple-element.18), channel_id=1, source_target_pairs={{0,1},{1,2},{2,3},{3,4},{4,5},{5,6},{6,7},{8,9},{9,10},{10,11},{11... | collective-permute-start | bytes 393224 | tf_op jit(solution)/shard_map/ppermute | solution.py:27
  113.8 1.3 collective-permute-start.18
  115.5 3.0 %collective-permute-done.19 = bf16[1024,64]{0,1:T(8,128)(2,1)S(1)} collective-permute-done((bf16[1024,64]{0,1:T(8,128)(2,1)S(1)}, bf16[1024,64]{0,1:T(8,128)(2,1)S(1)}, u32[]{:S(2)}, u32[]{:S(2)}) %collective-permute-start.19) | collective-permute-done | bytes 131104 | tf_op jit(solution)/shard_map/ppermute | solution.py:27
  118.5 1.8 %fusion.96 = (bf16[1024,256]{0,1:T(8,128)(2,1)S(1)}, f32[1024,256]{0,1:T(8,128)}) fusion(f32[1024,256]{0,1:T(8,128)S(1)} %get-tuple-element.66, f32[1024,256]{0,1:T(8,128)S(1)} %get-tuple-element.43, f32[1024,256]{0,1:T(8,128)S(1)} %fusion.3, bf16[1024,64]{0,1:T(8,128)(2,1)S(1)} %collective-permute-done.20, bf16[1024,256]{0,1:T(8,128)(2,1)S(1)} %get-tuple-element.65, ...), kind=kOutput, calls=%fused_computation.193 | convolution fusion | flops 140247040 | bytes 7735296 | tf_op jit(solution)/shard_map/dot_general | solution.py:88
  120.2 0.7 fusion.40
  121.1 3.3 %collective-permute-start.21 = (bf16[256,256]{0,1:T(8,128)(2,1)S(1)}, bf16[256,256]{0,1:T(8,128)(2,1)S(1)}, u32[]{:S(2)}, u32[]{:S(2)}) collective-permute-start(bf16[256,256]{0,1:T(8,128)(2,1)S(1)} %pad_maximum_fusion.18), channel_id=1, source_target_pairs={{0,8},{8,16},{16,24},{1,9},{9,17},{17,25},{2,10},{10,18},{18,26},{... | collective-permute-start | bytes 393224 | tf_op jit(solution)/shard_map/ppermute | solution.py:84
  124.4 1.3 collective-permute-start.24
  125.7 5.2 %collective-permute-start.23 = (bf16[1024,64]{0,1:T(8,128)(2,1)S(1)}, bf16[1024,64]{0,1:T(8,128)(2,1)S(1)}, u32[]{:S(2)}, u32[]{:S(2)}) collective-permute-start(bf16[1024,64]{0,1:T(8,128)(2,1)S(1)} %get-tuple-element.16), channel_id=1, source_target_pairs={{0,1},{1,2},{2,3},{3,4},{4,5},{5,6},{6,7},{8,9},{9,10},{10,11},{11... | collective-permute-start | bytes 393224 | tf_op jit(solution)/shard_map/ppermute | solution.py:27
  130.9 1.3 collective-permute-start.22
  132.6 3.0 %collective-permute-done.23 = bf16[1024,64]{0,1:T(8,128)(2,1)S(1)} collective-permute-done((bf16[1024,64]{0,1:T(8,128)(2,1)S(1)}, bf16[1024,64]{0,1:T(8,128)(2,1)S(1)}, u32[]{:S(2)}, u32[]{:S(2)}) %collective-permute-start.23) | collective-permute-done | bytes 131104 | tf_op jit(solution)/shard_map/ppermute | solution.py:27
  136.4 0.6 broadcast_in_dim.80
  137.0 3.2 %all-to-all-start.1 = ((f32[4,2,256]{2,1,0:T(2,128)}), f32[4,2,256]{2,1,0:T(2,128)S(1)}, u32[]{:S(2)}, u32[]{:S(2)}) async-start(f32[4,2,256]{2,1,0:T(2,128)} %broadcast_in_dim.80), calls=%async_computation.1 | async-start | bytes 16384 | tf_op jit(solution)/shard_map/all_to_all | solution.py:156
  140.2 2.5 %copy.48 = f32[1024,256]{1,0:T(8,128)} copy(f32[1024,256]{0,1:T(8,128)} %get-tuple-element.68) | data formatting | bytes 2097152
  142.7 1.2 all-to-all-done.1
  144.0 0.6 broadcast_multiply_fusion.1
  (76 shorter events, 4.5 us)
Async XLA Ops:
  0.6 16.2 %copy-start = (bf16[8,8,128,128]{3,2,1,0:T(8,128)(2,1)S(1)}, bf16[8,8,128,128]{3,2,1,0:T(8,128)(2,1)}, u32[]{:S(2)}) copy-start(bf16[8,8,128,128]{3,2,1,0:T(8,128)(2,1)} %param.17) | copy-start | bytes 6291460
  0.6 16.2 %copy-start.6 = (s32[8,8]{1,0:T(8,128)S(1)}, s32[8,8]{1,0:T(8,128)}, u32[]{:S(2)}) copy-start(s32[8,8]{1,0:T(8,128)} %param.18) | copy-start | bytes 772
  0.7 35.1 %collective-permute-start.8 = (bf16[1024,256]{1,0:T(8,128)(2,1)}, bf16[1024,256]{1,0:T(8,128)(2,1)}, u32[]{:S(2)}, u32[]{:S(2)}) collective-permute-start(bf16[1024,256]{1,0:T(8,128)(2,1)} %param.23), channel_id=1, source_target_pairs={{0,24},{8,0},{16,8},{24,16},{1,25},{9,1},{17,9},{25,17},{2,26},{10... | collective-permute-start | bytes 1572872 | tf_op jit(solution)/shard_map/ppermute | solution.py:105
  3.1 38.0 %collective-permute-start.7 = (bf16[1024,256]{1,0:T(8,128)(2,1)}, bf16[1024,256]{1,0:T(8,128)(2,1)}, u32[]{:S(2)}, u32[]{:S(2)}) collective-permute-start(bf16[1024,256]{1,0:T(8,128)(2,1)} %param.23), channel_id=1, source_target_pairs={{0,16},{8,24},{16,0},{24,8},{1,17},{9,25},{17,1},{25,9},{2,18},{10... | collective-permute-start | bytes 1572872 | tf_op jit(solution)/shard_map/ppermute | solution.py:105
  3.8 38.7 %collective-permute-start.6 = (bf16[1024,256]{1,0:T(8,128)(2,1)}, bf16[1024,256]{1,0:T(8,128)(2,1)}, u32[]{:S(2)}, u32[]{:S(2)}) collective-permute-start(bf16[1024,256]{1,0:T(8,128)(2,1)} %param.23), channel_id=1, source_target_pairs={{0,8},{8,16},{16,24},{24,0},{1,9},{9,17},{17,25},{25,1},{2,10},{10... | collective-permute-start | bytes 1572872 | tf_op jit(solution)/shard_map/ppermute | solution.py:105
  9.7 60.4 %collective-permute-start.5 = (bf16[1024,64]{0,1:T(8,128)(2,1)}, bf16[1024,64]{0,1:T(8,128)(2,1)}, u32[]{:S(2)}, u32[]{:S(2)}) collective-permute-start(bf16[1024,64]{0,1:T(8,128)(2,1)} %get-tuple-element.37), channel_id=1, source_target_pairs={{1,0},{2,1},{3,2},{4,3},{5,4},{6,5},{7,6},{9,8},{10,9},{11,10},{12... | collective-permute-start | bytes 393224 | tf_op jit(solution)/shard_map/ppermute | solution.py:28
  11.8 13.2 %collective-permute-start.2 = (s32[2]{0:T(128)S(1)}, s32[2]{0:T(128)S(1)}, u32[]{:S(2)}, u32[]{:S(2)}) collective-permute-start(s32[2]{0:T(128)S(1)} %get-tuple-element.57), channel_id=1, source_target_pairs={{0,8},{8,16},{16,24},{1,9},{9,17},{17,25},{2,10},{10,18},{18,26},{... | collective-permute-start | bytes 32 | tf_op jit(solution)/shard_map/ppermute | solution.py:75
  21.6 1.6 %copy-start.1 = (bf16[128,8,12,128]{3,1,2,0:T(8,128)(2,1)}, bf16[128,8,12,128]{3,1,2,0:T(8,128)(2,1)S(1)}, u32[]{:S(2)}) copy-start(bf16[128,8,12,128]{3,1,2,0:T(8,128)(2,1)S(1)} %copy.62) | copy-start | bytes 9437188
  21.6 3.3 %copy-start.4 = (s32[2048,1]{0,1:T(1,128)S(1)}, s32[2048,1]{0,1:T(1,128)}, u32[]{:S(2)}) copy-start(s32[2048,1]{0,1:T(1,128)} %param.21) | copy-start | bytes 24580
  21.6 3.3 %copy-start.5 = (s32[2048]{0:T(1024)S(1)}, s32[2048]{0:T(1024)}, u32[]{:S(2)}) copy-start(s32[2048]{0:T(1024)} %param.22) | copy-start | bytes 24580
  25.0 4.6 %collective-permute-start = (s32[2]{0:T(128)S(1)}, s32[2]{0:T(128)S(1)}, u32[]{:S(2)}, u32[]{:S(2)}) collective-permute-start(s32[2]{0:T(128)S(1)} %get-tuple-element.58), channel_id=1, source_target_pairs={{8,0},{16,8},{24,16},{9,1},{17,9},{25,17},{10,2},{18,10},{26,18},{... | collective-permute-start | bytes 32 | tf_op jit(solution)/shard_map/ppermute | solution.py:74
  29.7 40.4 %collective-permute-start.4 = (bf16[1024,64]{0,1:T(8,128)(2,1)}, bf16[1024,64]{0,1:T(8,128)(2,1)}, u32[]{:S(2)}, u32[]{:S(2)}) collective-permute-start(bf16[1024,64]{0,1:T(8,128)(2,1)} %get-tuple-element.36), channel_id=1, source_target_pairs={{0,1},{1,2},{2,3},{3,4},{4,5},{5,6},{6,7},{8,9},{9,10},{10,11},{11... | collective-permute-start | bytes 393224 | tf_op jit(solution)/shard_map/ppermute | solution.py:27
  35.8 29.8 %collective-permute-start.1 = (bf16[256,256]{0,1:T(8,128)(2,1)S(1)}, bf16[256,256]{0,1:T(8,128)(2,1)}, u32[]{:S(2)}, u32[]{:S(2)}) collective-permute-start(bf16[256,256]{0,1:T(8,128)(2,1)S(1)} %pad_maximum_fusion.10), channel_id=1, source_target_pairs={{0,8},{8,16},{16,24},{1,9},{9,17},{17,25},{2,10},{10,18},{18,26},{... | collective-permute-start | bytes 393224 | tf_op jit(solution)/shard_map/ppermute | solution.py:84
  41.2 29.0 %collective-permute-start.3 = (bf16[256,256]{0,1:T(8,128)(2,1)S(1)}, bf16[256,256]{0,1:T(8,128)(2,1)}, u32[]{:S(2)}, u32[]{:S(2)}) collective-permute-start(bf16[256,256]{0,1:T(8,128)(2,1)S(1)} %pad_maximum_fusion.11), channel_id=1, source_target_pairs={{8,0},{16,8},{24,16},{9,1},{17,9},{25,17},{10,2},{18,10},{26,18},{... | collective-permute-start | bytes 393224 | tf_op jit(solution)/shard_map/ppermute | solution.py:85
  59.4 10.4 %copy-start.3 = (f32[1024]{0:T(1024)S(1)}, f32[1024]{0:T(1024)}, u32[]{:S(2)}) copy-start(f32[1024]{0:T(1024)} %param.13) | copy-start | bytes 12292
  61.8 8.0 %all-to-all-start = ((f32[4,4,1024]{2,1,0:T(4,128)}), f32[4,4,1024]{2,1,0:T(4,128)S(1)}, u32[]{:S(2)}, u32[]{:S(2)}) async-start(f32[4,4,1024]{2,1,0:T(4,128)} %add.188), calls=%async_computation | async-start | bytes 131072 | tf_op jit(solution)/shard_map/all_to_all | solution.py:129
  70.1 2.7 %copy-start.2 = (bf16[128,8,12,128]{3,1,2,0:T(8,128)(2,1)S(1)}, bf16[128,8,12,128]{3,1,2,0:T(8,128)(2,1)}, u32[]{:S(2)}) copy-start(bf16[128,8,12,128]{3,1,2,0:T(8,128)(2,1)} %copy-done.1) | copy-start | bytes 9437188
  73.7 9.1 %collective-permute-start.9 = (bf16[256,256]{0,1:T(8,128)(2,1)S(1)}, bf16[256,256]{0,1:T(8,128)(2,1)S(1)}, u32[]{:S(2)}, u32[]{:S(2)}) collective-permute-start(bf16[256,256]{0,1:T(8,128)(2,1)S(1)} %pad_maximum_fusion.12), channel_id=1, source_target_pairs={{0,8},{8,16},{16,24},{1,9},{9,17},{17,25},{2,10},{10,18},{18,26},{... | collective-permute-start | bytes 393224 | tf_op jit(solution)/shard_map/ppermute | solution.py:84
  75.4 8.1 %collective-permute-start.12 = (bf16[1024,64]{0,1:T(8,128)(2,1)S(1)}, bf16[1024,64]{0,1:T(8,128)(2,1)S(1)}, u32[]{:S(2)}, u32[]{:S(2)}) collective-permute-start(bf16[1024,64]{0,1:T(8,128)(2,1)S(1)} %get-tuple-element.31), channel_id=1, source_target_pairs={{1,0},{2,1},{3,2},{4,3},{5,4},{6,5},{7,6},{9,8},{10,9},{11,10},{12... | collective-permute-start | bytes 393224 | tf_op jit(solution)/shard_map/ppermute | solution.py:28
  76.7 9.1 %collective-permute-start.11 = (bf16[1024,64]{0,1:T(8,128)(2,1)S(1)}, bf16[1024,64]{0,1:T(8,128)(2,1)S(1)}, u32[]{:S(2)}, u32[]{:S(2)}) collective-permute-start(bf16[1024,64]{0,1:T(8,128)(2,1)S(1)} %get-tuple-element.30), channel_id=1, source_target_pairs={{0,1},{1,2},{2,3},{3,4},{4,5},{5,6},{6,7},{8,9},{9,10},{10,11},{11... | collective-permute-start | bytes 393224 | tf_op jit(solution)/shard_map/ppermute | solution.py:27
  81.3 4.5 %collective-permute-start.10 = (bf16[256,256]{0,1:T(8,128)(2,1)S(1)}, bf16[256,256]{0,1:T(8,128)(2,1)S(1)}, u32[]{:S(2)}, u32[]{:S(2)}) collective-permute-start(bf16[256,256]{0,1:T(8,128)(2,1)S(1)} %pad_maximum_fusion.13), channel_id=1, source_target_pairs={{8,0},{16,8},{24,16},{9,1},{17,9},{25,17},{10,2},{18,10},{26,18},{... | collective-permute-start | bytes 393224 | tf_op jit(solution)/shard_map/ppermute | solution.py:85
  87.5 11.6 %collective-permute-start.13 = (bf16[256,256]{0,1:T(8,128)(2,1)S(1)}, bf16[256,256]{0,1:T(8,128)(2,1)S(1)}, u32[]{:S(2)}, u32[]{:S(2)}) collective-permute-start(bf16[256,256]{0,1:T(8,128)(2,1)S(1)} %pad_maximum_fusion.14), channel_id=1, source_target_pairs={{0,8},{8,16},{16,24},{1,9},{9,17},{17,25},{2,10},{10,18},{18,26},{... | collective-permute-start | bytes 393224 | tf_op jit(solution)/shard_map/ppermute | solution.py:84
  91.9 7.5 %collective-permute-start.16 = (bf16[1024,64]{0,1:T(8,128)(2,1)S(1)}, bf16[1024,64]{0,1:T(8,128)(2,1)S(1)}, u32[]{:S(2)}, u32[]{:S(2)}) collective-permute-start(bf16[1024,64]{0,1:T(8,128)(2,1)S(1)} %get-tuple-element.25), channel_id=1, source_target_pairs={{1,0},{2,1},{3,2},{4,3},{5,4},{6,5},{7,6},{9,8},{10,9},{11,10},{12... | collective-permute-start | bytes 393224 | tf_op jit(solution)/shard_map/ppermute | solution.py:28
  93.2 9.0 %collective-permute-start.15 = (bf16[1024,64]{0,1:T(8,128)(2,1)S(1)}, bf16[1024,64]{0,1:T(8,128)(2,1)S(1)}, u32[]{:S(2)}, u32[]{:S(2)}) collective-permute-start(bf16[1024,64]{0,1:T(8,128)(2,1)S(1)} %get-tuple-element.24), channel_id=1, source_target_pairs={{0,1},{1,2},{2,3},{3,4},{4,5},{5,6},{6,7},{8,9},{9,10},{10,11},{11... | collective-permute-start | bytes 393224 | tf_op jit(solution)/shard_map/ppermute | solution.py:27
  97.8 4.4 %collective-permute-start.14 = (bf16[256,256]{0,1:T(8,128)(2,1)S(1)}, bf16[256,256]{0,1:T(8,128)(2,1)S(1)}, u32[]{:S(2)}, u32[]{:S(2)}) collective-permute-start(bf16[256,256]{0,1:T(8,128)(2,1)S(1)} %pad_maximum_fusion.15), channel_id=1, source_target_pairs={{8,0},{16,8},{24,16},{9,1},{17,9},{25,17},{10,2},{18,10},{26,18},{... | collective-permute-start | bytes 393224 | tf_op jit(solution)/shard_map/ppermute | solution.py:85
  103.9 11.2 %collective-permute-start.17 = (bf16[256,256]{0,1:T(8,128)(2,1)S(1)}, bf16[256,256]{0,1:T(8,128)(2,1)S(1)}, u32[]{:S(2)}, u32[]{:S(2)}) collective-permute-start(bf16[256,256]{0,1:T(8,128)(2,1)S(1)} %pad_maximum_fusion.16), channel_id=1, source_target_pairs={{0,8},{8,16},{16,24},{1,9},{9,17},{17,25},{2,10},{10,18},{18,26},{... | collective-permute-start | bytes 393224 | tf_op jit(solution)/shard_map/ppermute | solution.py:84
  107.3 8.2 %collective-permute-start.20 = (bf16[1024,64]{0,1:T(8,128)(2,1)S(1)}, bf16[1024,64]{0,1:T(8,128)(2,1)S(1)}, u32[]{:S(2)}, u32[]{:S(2)}) collective-permute-start(bf16[1024,64]{0,1:T(8,128)(2,1)S(1)} %get-tuple-element.19), channel_id=1, source_target_pairs={{1,0},{2,1},{3,2},{4,3},{5,4},{6,5},{7,6},{9,8},{10,9},{11,10},{12... | collective-permute-start | bytes 393224 | tf_op jit(solution)/shard_map/ppermute | solution.py:28
  108.6 9.9 %collective-permute-start.19 = (bf16[1024,64]{0,1:T(8,128)(2,1)S(1)}, bf16[1024,64]{0,1:T(8,128)(2,1)S(1)}, u32[]{:S(2)}, u32[]{:S(2)}) collective-permute-start(bf16[1024,64]{0,1:T(8,128)(2,1)S(1)} %get-tuple-element.18), channel_id=1, source_target_pairs={{0,1},{1,2},{2,3},{3,4},{4,5},{5,6},{6,7},{8,9},{9,10},{10,11},{11... | collective-permute-start | bytes 393224 | tf_op jit(solution)/shard_map/ppermute | solution.py:27
  113.8 4.7 %collective-permute-start.18 = (bf16[256,256]{0,1:T(8,128)(2,1)S(1)}, bf16[256,256]{0,1:T(8,128)(2,1)S(1)}, u32[]{:S(2)}, u32[]{:S(2)}) collective-permute-start(bf16[256,256]{0,1:T(8,128)(2,1)S(1)} %pad_maximum_fusion.17), channel_id=1, source_target_pairs={{8,0},{16,8},{24,16},{9,1},{17,9},{25,17},{10,2},{18,10},{26,18},{... | collective-permute-start | bytes 393224 | tf_op jit(solution)/shard_map/ppermute | solution.py:85
  121.1 11.1 %collective-permute-start.21 = (bf16[256,256]{0,1:T(8,128)(2,1)S(1)}, bf16[256,256]{0,1:T(8,128)(2,1)S(1)}, u32[]{:S(2)}, u32[]{:S(2)}) collective-permute-start(bf16[256,256]{0,1:T(8,128)(2,1)S(1)} %pad_maximum_fusion.18), channel_id=1, source_target_pairs={{0,8},{8,16},{16,24},{1,9},{9,17},{17,25},{2,10},{10,18},{18,26},{... | collective-permute-start | bytes 393224 | tf_op jit(solution)/shard_map/ppermute | solution.py:84
  124.4 8.2 %collective-permute-start.24 = (bf16[1024,64]{0,1:T(8,128)(2,1)S(1)}, bf16[1024,64]{0,1:T(8,128)(2,1)S(1)}, u32[]{:S(2)}, u32[]{:S(2)}) collective-permute-start(bf16[1024,64]{0,1:T(8,128)(2,1)S(1)} %get-tuple-element.17), channel_id=1, source_target_pairs={{1,0},{2,1},{3,2},{4,3},{5,4},{6,5},{7,6},{9,8},{10,9},{11,10},{12... | collective-permute-start | bytes 393224 | tf_op jit(solution)/shard_map/ppermute | solution.py:28
  125.7 9.8 %collective-permute-start.23 = (bf16[1024,64]{0,1:T(8,128)(2,1)S(1)}, bf16[1024,64]{0,1:T(8,128)(2,1)S(1)}, u32[]{:S(2)}, u32[]{:S(2)}) collective-permute-start(bf16[1024,64]{0,1:T(8,128)(2,1)S(1)} %get-tuple-element.16), channel_id=1, source_target_pairs={{0,1},{1,2},{2,3},{3,4},{4,5},{5,6},{6,7},{8,9},{9,10},{10,11},{11... | collective-permute-start | bytes 393224 | tf_op jit(solution)/shard_map/ppermute | solution.py:27
  130.9 5.0 %collective-permute-start.22 = (bf16[256,256]{0,1:T(8,128)(2,1)S(1)}, bf16[256,256]{0,1:T(8,128)(2,1)S(1)}, u32[]{:S(2)}, u32[]{:S(2)}) collective-permute-start(bf16[256,256]{0,1:T(8,128)(2,1)S(1)} %pad_maximum_fusion.19), channel_id=1, source_target_pairs={{8,0},{16,8},{24,16},{9,1},{17,9},{25,17},{10,2},{18,10},{26,18},{... | collective-permute-start | bytes 393224 | tf_op jit(solution)/shard_map/ppermute | solution.py:85
  137.0 7.0 %all-to-all-start.1 = ((f32[4,2,256]{2,1,0:T(2,128)}), f32[4,2,256]{2,1,0:T(2,128)S(1)}, u32[]{:S(2)}, u32[]{:S(2)}) async-start(f32[4,2,256]{2,1,0:T(2,128)} %broadcast_in_dim.80), calls=%async_computation.1 | async-start | bytes 16384 | tf_op jit(solution)/shard_map/all_to_all | solution.py:156

commit v14 on v13

--- a/solution.py
+++ b/solution.py
@@ -71,8 +71,13 @@
     space_index = lax.axis_index("space")
     up = [(i, i + 1) for i in range(space_count - 1)]
     down = [(i + 1, i) for i in range(space_count - 1)]
-    upper_wants = lax.ppermute(halo_needs[:HALO_B], "space", down)
-    lower_wants = lax.ppermute(halo_needs[HALO_B:], "space", up)
+    every_needs = lax.all_to_all(
+        jnp.broadcast_to(halo_needs[None], (space_count,) + halo_needs.shape),
+        "space", split_axis=0, concat_axis=0, tiled=True,
+    )
+    space_index = lax.axis_index("space")
+    upper_wants = every_needs[jnp.minimum(space_index + 1, space_count - 1), :HALO_B]
+    lower_wants = every_needs[jnp.maximum(space_index - 1, 0), HALO_B:]
 
     def pick_blocks(field, wanted):
         return jnp.concatenate(

time: 146 us -> 143 us (0.979)
  starting transfers between devices: 69.2 us -> 67.1 us
    ppermute x2 -> x0, starting transfers between devices: 4.53 us -> none  [the longest x1 3.24 us: shards(): lower_wants = lax.ppermute(halo_needs[HALO_B:], 'space', up)]
    all_to_all x0 -> x1, starting transfers between devices: none -> 3.22 us  [shards(): lax.all_to_all(jnp.broadcast_to(halo_needs[None], (space_count,) + halo_n...]
    ppermute x5, starting transfers between devices: 17.7 us -> 14.8 us  [spatial(): lower = lax.ppermute(pick_blocks(field, upper_wants), 'space', up)]
    ppermute x5, starting transfers between devices: 23.5 us -> 25.3 us  [with_halo(): before = lax.ppermute(last, axis, up)]
    ppermute x2 -> x0, waiting for transfers between devices: 1.47 us -> none  [the longest x1 1.47 us: shards(): upper_wants = lax.ppermute(halo_needs[:HALO_B], 'space', down)]
  transfers between devices with their start and end apart: 27 -> 26, of which waited for: 8 -> 7; matrix products, arithmetic and copies ran while one was open for 30% -> 30% of each run, Pallas kernels for 0% -> 0%
where the time goes in v14:
time: 143 us; the launch traced here: 142 us
  starting transfers between devices  67.1 us (47%)
  local copies, waits for them, and re-layouts  23.7 us (17%)
  matrix products  20 us (14%)
  waiting for transfers between devices  15.2 us (11%)
  other arithmetic  12 us (8%)
  between operations  3.87 us (3%)
    ppermute x5, starting transfers between devices, with_halo(): before = lax.ppermute(last, axis, up)  25.3 us
    ppermute x5, starting transfers between devices, spatial(): lower = lax.ppermute(pick_blocks(field, upper_wants), 'space', up)  14.8 us
    ppermute x5, waiting for transfers between devices, with_halo(): before = lax.ppermute(last, axis, up)  12 us
    gather x1, local copies, waits for them, and re-layouts, shards(): coef_rows = svc_all[shift * nodes_dev + obs_cell // T_DEV]  10.7 us
    unnamed x17, local copies, waits for them, and re-layouts  7.02 us
    ppermute x5, starting transfers between devices, spatial(): upper = lax.ppermute(pick_blocks(field, lower_wants), 'space', down)  6.63 us
    dot_general x5, matrix products, spatial(): jnp.dot(upper.T, upper_t, preferred_element_type=jnp.float32)  6.48 us
    ppermute x5, starting transfers between devices, with_halo(): after = lax.ppermute(initial, axis, down)  6.45 us
  transfers between devices with their start and end apart: 26, of which 7 were waited for; matrix products, arithmetic and copies ran while one was open for 30% of the time, Pallas kernels for 0%

profile of v14, /device:TPU:0, one launch (start us, length us, event | category | flops | bytes accessed | tf_op | source)
XLA Modules:
  0.0 141.9 jit_solution(7467076967392889436)
XLA Ops:
  0.7 2.5 %collective-permute-start.6 = (bf16[1024,256]{1,0:T(8,128)(2,1)}, bf16[1024,256]{1,0:T(8,128)(2,1)}, u32[]{:S(2)}, u32[]{:S(2)}) collective-permute-start(bf16[1024,256]{1,0:T(8,128)(2,1)} %param.23), channel_id=1, source_target_pairs={{0,24},{8,0},{16,8},{24,16},{1,25},{9,1},{17,9},{25,17},{2,26},{10... | collective-permute-start | bytes 1572872 | tf_op jit(solution)/shard_map/ppermute | solution.py:110
  3.1 0.6 collective-permute-start.5
  4.0 1.2 copy.41
  5.2 0.7 broadcast_in_dim.79
  6.0 0.7 broadcast_in_dim.76
  6.8 1.1 select_reduce_fusion
  7.9 1.1 fusion.56
  9.0 0.7 fusion.91
  9.7 1.3 collective-permute-start.3
  11.0 5.2 %collective-permute-start.2 = (bf16[1024,64]{0,1:T(8,128)(2,1)}, bf16[1024,64]{0,1:T(8,128)(2,1)}, u32[]{:S(2)}, u32[]{:S(2)}) collective-permute-start(bf16[1024,64]{0,1:T(8,128)(2,1)} %get-tuple-element.36), channel_id=1, source_target_pairs={{0,1},{1,2},{2,3},{3,4},{4,5},{5,6},{6,7},{8,9},{9,10},{10,11},{11... | collective-permute-start | bytes 393224 | tf_op jit(solution)/shard_map/ppermute | solution.py:27
  16.2 1.2 broadcast_in_dim.80
  17.4 3.2 %all-to-all-start = ((s32[4,1,4]{2,1,0:T(1,128)}), s32[4,1,4]{2,1,0:T(1,128)S(1)}, u32[]{:S(2)}, u32[]{:S(2)}) async-start(s32[4,1,4]{2,1,0:T(1,128)} %broadcast_in_dim.80), calls=%async_computation | async-start | bytes 4096 | tf_op jit(solution)/shard_map/all_to_all | solution.py:74
  20.7 1.8 %convert_element_type.89 = f32[8,128,128]{2,1,0:T(8,128)} convert(bf16[8,128,128]{2,1,0:T(8,128)(2,1)} %param.16) | non-fusion elementwise | flops 131072 | bytes 786432 | tf_op jit(solution)/shard_map/convert_element_type | solution.py:52
  22.5 3.1 %add_convert_fusion = bf16[8,12,128,128]{3,1,2,0:T(8,128)(2,1)S(1)} fusion(f32[8,128,128]{2,1,0:T(8,128)} %convert_element_type.89, f32[8,12]{1,0:T(8,128)S(1)} %fusion.82, bf16[8,8,128,128]{3,2,1,0:T(8,128)(2,1)S(1)} %copy-done, s32[8,8]{1,0:T(8,128)S(1)} %copy-done.6), kind=kOutput, calls=%fused_computation.2 | convolution fusion | flops 29885184 | bytes 5767808 | tf_op jit(solution)/shard_map/bkm,bkij->bimj/dot_general | solution.py:63
  25.6 1.6 %copy.62 = bf16[128,8,12,128]{3,1,2,0:T(8,128)(2,1)S(1)} copy(bf16[128,8,12,128]{3,2,1,0:T(8,128)(2,1)S(1)} %bitcast.52) | data formatting | bytes 6291456
  27.2 1.6 %copy-done.1 = bf16[128,8,12,128]{3,1,2,0:T(8,128)(2,1)} copy-done((bf16[128,8,12,128]{3,1,2,0:T(8,128)(2,1)}, bf16[128,8,12,128]{3,1,2,0:T(8,128)(2,1)S(1)}, u32[]{:S(2)}) %copy-start.1) | copy-done | bytes 3145752
  28.9 1.7 %fusion.38 = f32[1024,256]{0,1:T(8,128)} fusion(bf16[1024,256]{0,1:T(8,128)(2,1)S(1)} %fusion.56, bf16[1024,1536]{1,0:T(8,128)(2,1)S(1)} %bitcast.53), kind=kOutput, calls=%fused_computation.67 | convolution fusion | flops 536870912 | bytes 3670016 | tf_op jit(solution)/shard_map/dot_general | solution.py:91
  30.7 0.6 fusion.92
  34.0 3.3 %collective-permute-start = (bf16[256,256]{0,1:T(8,128)(2,1)S(1)}, bf16[256,256]{0,1:T(8,128)(2,1)}, u32[]{:S(2)}, u32[]{:S(2)}) collective-permute-start(bf16[256,256]{0,1:T(8,128)(2,1)S(1)} %pad_maximum_fusion.10), channel_id=1, source_target_pairs={{0,8},{8,16},{16,24},{1,9},{9,17},{17,25},{2,10},{10,18},{18,26},{... | collective-permute-start | bytes 393224 | tf_op jit(solution)/shard_map/ppermute | solution.py:89
  37.4 1.3 collective-permute-start.1
  38.7 3.8 %maximum_convert_fusion = f32[4096,256]{1,0:T(8,128)} fusion(bf16[1024,256]{1,0:T(8,128)(2,1)} %collective-permute-done.6, bf16[1024,256]{1,0:T(8,128)(2,1)} %collective-permute-done.5, bf16[1024,256]{1,0:T(8,128)(2,1)} %collective-permute-done.4, bf16[1024,256]{1,0:T(8,128)(2,1)} %param.23), kind=kLoop, calls=%fused_computation.13 | loop fusion | flops 8388608 | bytes 6291456 | tf_op jit(solution)/shard_map/convert_element_type | solution.py:113
  42.5 10.7 %gather_fusion = f32[2048,256]{1,0:T(8,128)} fusion(f32[4096,256]{1,0:T(8,128)} %maximum_convert_fusion, s32[2048]{0:T(1024)S(1)} %get-tuple-element.51), kind=kCustom, calls=%fused_computation | custom fusion | bytes 4202496 | tf_op jit(solution)/shard_map/gather | solution.py:116
  53.2 2.2 %multiply_reduce_fusion = f32[2048]{0:T(1024)S(1)} fusion(f32[2048,256]{1,0:T(8,128)} %gather_fusion, bf16[2048,256]{1,0:T(8,128)(2,1)} %param.20), kind=kLoop, calls=%fused_computation.15 | loop fusion | flops 1570816 | bytes 3153920 | tf_op jit(solution)/shard_map/reduce_sum | solution.py:117
  55.5 1.7 %fusion = f32[48,1024]{1,0:T(8,128)S(1)} fusion(s32[2048]{0:T(1024)S(1)} %get-tuple-element.52, bf16[2048,16]{0,1:T(8,128)(2,1)S(1)} %get-tuple-element.45, bf16[2048,16]{0,1:T(8,128)(2,1)S(1)} %get-tuple-element.46, bf16[2048,16]{0,1:T(8,128)(2,1)S(1)} %get-tuple-element.44), kind=kOutput, calls=%fused_computation.3 | convolution fusion | flops 204013568 | bytes 401408 | tf_op jit(solution)/shard_map/dot_general | solution.py:129
  57.3 0.6 add.198
  57.9 4.2 %all-to-all-start.1 = ((f32[4,4,1024]{2,1,0:T(4,128)}), f32[4,4,1024]{2,1,0:T(4,128)S(1)}, u32[]{:S(2)}, u32[]{:S(2)}) async-start(f32[4,4,1024]{2,1,0:T(4,128)} %add.198), calls=%async_computation.1 | async-start | bytes 131072 | tf_op jit(solution)/shard_map/all_to_all | solution.py:134
  62.1 2.7 %convolution_add_fusion.9 = f32[1024,256]{0,1:T(8,128)} fusion(f32[1024,256]{0,1:T(8,128)} %fusion.38, bf16[256,256]{0,1:T(8,128)(2,1)} %collective-permute-done, bf16[1024,1536]{1,0:T(8,128)(2,1)} %bitcast.54), kind=kOutput, calls=%fused_computation.43 | convolution fusion | flops 134479872 | bytes 2752512 | tf_op jit(solution)/shard_map/dot_general | solution.py:92
  64.8 1.4 all-to-all-done.1
  66.6 2.7 %fusion.94 = (bf16[1024,256]{0,1:T(8,128)(2,1)S(1)}, f32[1024,256]{0,1:T(8,128)S(1)}) fusion(f32[1024,256]{0,1:T(8,128)S(1)} %get-tuple-element.43, f32[1024,256]{0,1:T(8,128)S(1)} %get-tuple-element.42, bf16[1024,64]{0,1:T(8,128)(2,1)} %collective-permute-done.3, bf16[1024,256]{0,1:T(8,128)(2,1)S(1)} %fusion.56, ...), kind=kOutput, calls=%fused_computation.193 | convolution fusion | flops 141557760 | bytes 6695936 | tf_op jit(solution)/shard_map/dot_general | solution.py:93
  69.3 0.7 fusion.36
  70.2 1.6 %collective-permute-start.7 = (bf16[256,256]{0,1:T(8,128)(2,1)S(1)}, bf16[256,256]{0,1:T(8,128)(2,1)S(1)}, u32[]{:S(2)}, u32[]{:S(2)}) collective-permute-start(bf16[256,256]{0,1:T(8,128)(2,1)S(1)} %pad_maximum_fusion.12), channel_id=1, source_target_pairs={{0,8},{8,16},{16,24},{1,9},{9,17},{17,25},{2,10},{10,18},{18,26},{... | collective-permute-start | bytes 393224 | tf_op jit(solution)/shard_map/ppermute | solution.py:89
  71.9 1.3 collective-permute-start.10
  73.2 4.6 %collective-permute-start.9 = (bf16[1024,64]{0,1:T(8,128)(2,1)S(1)}, bf16[1024,64]{0,1:T(8,128)(2,1)S(1)}, u32[]{:S(2)}, u32[]{:S(2)}) collective-permute-start(bf16[1024,64]{0,1:T(8,128)(2,1)S(1)} %get-tuple-element.30), channel_id=1, source_target_pairs={{0,1},{1,2},{2,3},{3,4},{4,5},{5,6},{6,7},{8,9},{9,10},{10,11},{11... | collective-permute-start | bytes 393224 | tf_op jit(solution)/shard_map/ppermute | solution.py:27
  77.8 1.5 %collective-permute-start.8 = (bf16[256,256]{0,1:T(8,128)(2,1)S(1)}, bf16[256,256]{0,1:T(8,128)(2,1)S(1)}, u32[]{:S(2)}, u32[]{:S(2)}) collective-permute-start(bf16[256,256]{0,1:T(8,128)(2,1)S(1)} %pad_maximum_fusion.13), channel_id=1, source_target_pairs={{8,0},{16,8},{24,16},{9,1},{17,9},{25,17},{10,2},{18,10},{26,18},{... | collective-permute-start | bytes 393224 | tf_op jit(solution)/shard_map/ppermute | solution.py:90
  79.6 0.4 collective-permute-done.10
  80.0 3.1 %collective-permute-done.9 = bf16[1024,64]{0,1:T(8,128)(2,1)S(1)} collective-permute-done((bf16[1024,64]{0,1:T(8,128)(2,1)S(1)}, bf16[1024,64]{0,1:T(8,128)(2,1)S(1)}, u32[]{:S(2)}, u32[]{:S(2)}) %collective-permute-start.9) | collective-permute-done | bytes 131104 | tf_op jit(solution)/shard_map/ppermute | solution.py:27
  83.2 0.8 fusion.95
  84.0 0.7 fusion.34
  84.8 3.4 %collective-permute-start.11 = (bf16[256,256]{0,1:T(8,128)(2,1)S(1)}, bf16[256,256]{0,1:T(8,128)(2,1)S(1)}, u32[]{:S(2)}, u32[]{:S(2)}) collective-permute-start(bf16[256,256]{0,1:T(8,128)(2,1)S(1)} %pad_maximum_fusion.14), channel_id=1, source_target_pairs={{0,8},{8,16},{16,24},{1,9},{9,17},{17,25},{2,10},{10,18},{18,26},{... | collective-permute-start | bytes 393224 | tf_op jit(solution)/shard_map/ppermute | solution.py:89
  88.4 1.3 collective-permute-start.14
  89.7 5.2 %collective-permute-start.13 = (bf16[1024,64]{0,1:T(8,128)(2,1)S(1)}, bf16[1024,64]{0,1:T(8,128)(2,1)S(1)}, u32[]{:S(2)}, u32[]{:S(2)}) collective-permute-start(bf16[1024,64]{0,1:T(8,128)(2,1)S(1)} %get-tuple-element.24), channel_id=1, source_target_pairs={{0,1},{1,2},{2,3},{3,4},{4,5},{5,6},{6,7},{8,9},{9,10},{10,11},{11... | collective-permute-start | bytes 393224 | tf_op jit(solution)/shard_map/ppermute | solution.py:27
  94.9 1.3 collective-permute-start.12
  96.6 3.0 %collective-permute-done.13 = bf16[1024,64]{0,1:T(8,128)(2,1)S(1)} collective-permute-done((bf16[1024,64]{0,1:T(8,128)(2,1)S(1)}, bf16[1024,64]{0,1:T(8,128)(2,1)S(1)}, u32[]{:S(2)}, u32[]{:S(2)}) %collective-permute-start.13) | collective-permute-done | bytes 131104 | tf_op jit(solution)/shard_map/ppermute | solution.py:27
  99.6 0.8 fusion.96
  100.4 0.7 fusion.32
  101.2 3.3 %collective-permute-start.15 = (bf16[256,256]{0,1:T(8,128)(2,1)S(1)}, bf16[256,256]{0,1:T(8,128)(2,1)S(1)}, u32[]{:S(2)}, u32[]{:S(2)}) collective-permute-start(bf16[256,256]{0,1:T(8,128)(2,1)S(1)} %pad_maximum_fusion.16), channel_id=1, source_target_pairs={{0,8},{8,16},{16,24},{1,9},{9,17},{17,25},{2,10},{10,18},{18,26},{... | collective-permute-start | bytes 393224 | tf_op jit(solution)/shard_map/ppermute | solution.py:89
  104.6 1.3 collective-permute-start.18
  105.9 5.2 %collective-permute-start.17 = (bf16[1024,64]{0,1:T(8,128)(2,1)S(1)}, bf16[1024,64]{0,1:T(8,128)(2,1)S(1)}, u32[]{:S(2)}, u32[]{:S(2)}) collective-permute-start(bf16[1024,64]{0,1:T(8,128)(2,1)S(1)} %get-tuple-element.18), channel_id=1, source_target_pairs={{0,1},{1,2},{2,3},{3,4},{4,5},{5,6},{6,7},{8,9},{9,10},{10,11},{11... | collective-permute-start | bytes 393224 | tf_op jit(solution)/shard_map/ppermute | solution.py:27
  111.1 1.3 collective-permute-start.16
  112.8 3.0 %collective-permute-done.17 = bf16[1024,64]{0,1:T(8,128)(2,1)S(1)} collective-permute-done((bf16[1024,64]{0,1:T(8,128)(2,1)S(1)}, bf16[1024,64]{0,1:T(8,128)(2,1)S(1)}, u32[]{:S(2)}, u32[]{:S(2)}) %collective-permute-start.17) | collective-permute-done | bytes 131104 | tf_op jit(solution)/shard_map/ppermute | solution.py:27
  115.8 1.8 %fusion.97 = (bf16[1024,256]{0,1:T(8,128)(2,1)S(1)}, f32[1024,256]{0,1:T(8,128)}) fusion(f32[1024,256]{0,1:T(8,128)S(1)} %get-tuple-element.66, f32[1024,256]{0,1:T(8,128)S(1)} %get-tuple-element.43, f32[1024,256]{0,1:T(8,128)S(1)} %fusion.3, bf16[1024,64]{0,1:T(8,128)(2,1)S(1)} %collective-permute-done.18, bf16[1024,256]{0,1:T(8,128)(2,1)S(1)} %get-tuple-element.65, ...), kind=kOutput, calls=%fused_computation.196 | convolution fusion | flops 140247040 | bytes 7735296 | tf_op jit(solution)/shard_map/dot_general | solution.py:93
  117.6 0.7 fusion.40
  118.4 3.3 %collective-permute-start.19 = (bf16[256,256]{0,1:T(8,128)(2,1)S(1)}, bf16[256,256]{0,1:T(8,128)(2,1)S(1)}, u32[]{:S(2)}, u32[]{:S(2)}) collective-permute-start(bf16[256,256]{0,1:T(8,128)(2,1)S(1)} %pad_maximum_fusion.18), channel_id=1, source_target_pairs={{0,8},{8,16},{16,24},{1,9},{9,17},{17,25},{2,10},{10,18},{18,26},{... | collective-permute-start | bytes 393224 | tf_op jit(solution)/shard_map/ppermute | solution.py:89
  121.7 1.3 collective-permute-start.22
  123.0 5.2 %collective-permute-start.21 = (bf16[1024,64]{0,1:T(8,128)(2,1)S(1)}, bf16[1024,64]{0,1:T(8,128)(2,1)S(1)}, u32[]{:S(2)}, u32[]{:S(2)}) collective-permute-start(bf16[1024,64]{0,1:T(8,128)(2,1)S(1)} %get-tuple-element.16), channel_id=1, source_target_pairs={{0,1},{1,2},{2,3},{3,4},{4,5},{5,6},{6,7},{8,9},{9,10},{10,11},{11... | collective-permute-start | bytes 393224 | tf_op jit(solution)/shard_map/ppermute | solution.py:27
  128.2 1.3 collective-permute-start.20
  129.9 3.0 %collective-permute-done.21 = bf16[1024,64]{0,1:T(8,128)(2,1)S(1)} collective-permute-done((bf16[1024,64]{0,1:T(8,128)(2,1)S(1)}, bf16[1024,64]{0,1:T(8,128)(2,1)S(1)}, u32[]{:S(2)}, u32[]{:S(2)}) %collective-permute-start.21) | collective-permute-done | bytes 131104 | tf_op jit(solution)/shard_map/ppermute | solution.py:27
  132.9 0.4 fusion.55
  133.3 0.4 fusion.31
  133.7 0.6 broadcast_in_dim.87
  134.3 3.2 %all-to-all-start.2 = ((f32[4,2,256]{2,1,0:T(2,128)}), f32[4,2,256]{2,1,0:T(2,128)S(1)}, u32[]{:S(2)}, u32[]{:S(2)}) async-start(f32[4,2,256]{2,1,0:T(2,128)} %broadcast_in_dim.87), calls=%async_computation.2 | async-start | bytes 16384 | tf_op jit(solution)/shard_map/all_to_all | solution.py:161
  137.6 2.5 %copy.48 = f32[1024,256]{1,0:T(8,128)} copy(f32[1024,256]{0,1:T(8,128)} %get-tuple-element.68) | data formatting | bytes 2097152
  140.1 1.2 all-to-all-done.2
  141.4 0.6 broadcast_multiply_fusion.1
  (74 shorter events, 3.5 us)
Async XLA Ops:
  0.6 21.8 %copy-start = (bf16[8,8,128,128]{3,2,1,0:T(8,128)(2,1)S(1)}, bf16[8,8,128,128]{3,2,1,0:T(8,128)(2,1)}, u32[]{:S(2)}) copy-start(bf16[8,8,128,128]{3,2,1,0:T(8,128)(2,1)} %param.17) | copy-start | bytes 6291460
  0.6 21.8 %copy-start.6 = (s32[8,8]{1,0:T(8,128)S(1)}, s32[8,8]{1,0:T(8,128)}, u32[]{:S(2)}) copy-start(s32[8,8]{1,0:T(8,128)} %param.18) | copy-start | bytes 772
  0.7 33.4 %collective-permute-start.6 = (bf16[1024,256]{1,0:T(8,128)(2,1)}, bf16[1024,256]{1,0:T(8,128)(2,1)}, u32[]{:S(2)}, u32[]{:S(2)}) collective-permute-start(bf16[1024,256]{1,0:T(8,128)(2,1)} %param.23), channel_id=1, source_target_pairs={{0,24},{8,0},{16,8},{24,16},{1,25},{9,1},{17,9},{25,17},{2,26},{10... | collective-permute-start | bytes 1572872 | tf_op jit(solution)/shard_map/ppermute | solution.py:110
  3.1 34.2 %collective-permute-start.5 = (bf16[1024,256]{1,0:T(8,128)(2,1)}, bf16[1024,256]{1,0:T(8,128)(2,1)}, u32[]{:S(2)}, u32[]{:S(2)}) collective-permute-start(bf16[1024,256]{1,0:T(8,128)(2,1)} %param.23), channel_id=1, source_target_pairs={{0,16},{8,24},{16,0},{24,8},{1,17},{9,25},{17,1},{25,9},{2,18},{10... | collective-permute-start | bytes 1572872 | tf_op jit(solution)/shard_map/ppermute | solution.py:110
  3.8 34.9 %collective-permute-start.4 = (bf16[1024,256]{1,0:T(8,128)(2,1)}, bf16[1024,256]{1,0:T(8,128)(2,1)}, u32[]{:S(2)}, u32[]{:S(2)}) collective-permute-start(bf16[1024,256]{1,0:T(8,128)(2,1)} %param.23), channel_id=1, source_target_pairs={{0,8},{8,16},{16,24},{24,0},{1,9},{9,17},{17,25},{25,1},{2,10},{10... | collective-permute-start | bytes 1572872 | tf_op jit(solution)/shard_map/ppermute | solution.py:110
  9.7 56.9 %collective-permute-start.3 = (bf16[1024,64]{0,1:T(8,128)(2,1)}, bf16[1024,64]{0,1:T(8,128)(2,1)}, u32[]{:S(2)}, u32[]{:S(2)}) collective-permute-start(bf16[1024,64]{0,1:T(8,128)(2,1)} %get-tuple-element.37), channel_id=1, source_target_pairs={{1,0},{2,1},{3,2},{4,3},{5,4},{6,5},{7,6},{9,8},{10,9},{11,10},{12... | collective-permute-start | bytes 393224 | tf_op jit(solution)/shard_map/ppermute | solution.py:28
  11.0 55.6 %collective-permute-start.2 = (bf16[1024,64]{0,1:T(8,128)(2,1)}, bf16[1024,64]{0,1:T(8,128)(2,1)}, u32[]{:S(2)}, u32[]{:S(2)}) collective-permute-start(bf16[1024,64]{0,1:T(8,128)(2,1)} %get-tuple-element.36), channel_id=1, source_target_pairs={{0,1},{1,2},{2,3},{3,4},{4,5},{5,6},{6,7},{8,9},{9,10},{10,11},{11... | collective-permute-start | bytes 393224 | tf_op jit(solution)/shard_map/ppermute | solution.py:27
  17.4 13.2 %all-to-all-start = ((s32[4,1,4]{2,1,0:T(1,128)}), s32[4,1,4]{2,1,0:T(1,128)S(1)}, u32[]{:S(2)}, u32[]{:S(2)}) async-start(s32[4,1,4]{2,1,0:T(1,128)} %broadcast_in_dim.80), calls=%async_computation | async-start | bytes 4096 | tf_op jit(solution)/shard_map/all_to_all | solution.py:74
  27.2 1.6 %copy-start.1 = (bf16[128,8,12,128]{3,1,2,0:T(8,128)(2,1)}, bf16[128,8,12,128]{3,1,2,0:T(8,128)(2,1)S(1)}, u32[]{:S(2)}) copy-start(bf16[128,8,12,128]{3,1,2,0:T(8,128)(2,1)S(1)} %copy.62) | copy-start | bytes 9437188
  27.2 3.3 %copy-start.4 = (s32[2048,1]{0,1:T(1,128)S(1)}, s32[2048,1]{0,1:T(1,128)}, u32[]{:S(2)}) copy-start(s32[2048,1]{0,1:T(1,128)} %param.21) | copy-start | bytes 24580
  27.2 3.4 %copy-start.5 = (s32[2048]{0:T(1024)S(1)}, s32[2048]{0:T(1024)}, u32[]{:S(2)}) copy-start(s32[2048]{0:T(1024)} %param.22) | copy-start | bytes 24580
  34.0 28.1 %collective-permute-start = (bf16[256,256]{0,1:T(8,128)(2,1)S(1)}, bf16[256,256]{0,1:T(8,128)(2,1)}, u32[]{:S(2)}, u32[]{:S(2)}) collective-permute-start(bf16[256,256]{0,1:T(8,128)(2,1)S(1)} %pad_maximum_fusion.10), channel_id=1, source_target_pairs={{0,8},{8,16},{16,24},{1,9},{9,17},{17,25},{2,10},{10,18},{18,26},{... | collective-permute-start | bytes 393224 | tf_op jit(solution)/shard_map/ppermute | solution.py:89
  37.4 29.3 %collective-permute-start.1 = (bf16[256,256]{0,1:T(8,128)(2,1)S(1)}, bf16[256,256]{0,1:T(8,128)(2,1)}, u32[]{:S(2)}, u32[]{:S(2)}) collective-permute-start(bf16[256,256]{0,1:T(8,128)(2,1)S(1)} %pad_maximum_fusion.11), channel_id=1, source_target_pairs={{8,0},{16,8},{24,16},{9,1},{17,9},{25,17},{10,2},{18,10},{26,18},{... | collective-permute-start | bytes 393224 | tf_op jit(solution)/shard_map/ppermute | solution.py:90
  55.5 10.7 %copy-start.3 = (f32[1024]{0:T(1024)S(1)}, f32[1024]{0:T(1024)}, u32[]{:S(2)}) copy-start(f32[1024]{0:T(1024)} %param.13) | copy-start | bytes 12292
  57.9 8.3 %all-to-all-start.1 = ((f32[4,4,1024]{2,1,0:T(4,128)}), f32[4,4,1024]{2,1,0:T(4,128)S(1)}, u32[]{:S(2)}, u32[]{:S(2)}) async-start(f32[4,4,1024]{2,1,0:T(4,128)} %add.198), calls=%async_computation.1 | async-start | bytes 131072 | tf_op jit(solution)/shard_map/all_to_all | solution.py:134
  66.6 2.7 %copy-start.2 = (bf16[128,8,12,128]{3,1,2,0:T(8,128)(2,1)S(1)}, bf16[128,8,12,128]{3,1,2,0:T(8,128)(2,1)}, u32[]{:S(2)}) copy-start(bf16[128,8,12,128]{3,1,2,0:T(8,128)(2,1)} %copy-done.1) | copy-start | bytes 9437188
  70.2 9.1 %collective-permute-start.7 = (bf16[256,256]{0,1:T(8,128)(2,1)S(1)}, bf16[256,256]{0,1:T(8,128)(2,1)S(1)}, u32[]{:S(2)}, u32[]{:S(2)}) collective-permute-start(bf16[256,256]{0,1:T(8,128)(2,1)S(1)} %pad_maximum_fusion.12), channel_id=1, source_target_pairs={{0,8},{8,16},{16,24},{1,9},{9,17},{17,25},{2,10},{10,18},{18,26},{... | collective-permute-start | bytes 393224 | tf_op jit(solution)/shard_map/ppermute | solution.py:89
  71.9 8.1 %collective-permute-start.10 = (bf16[1024,64]{0,1:T(8,128)(2,1)S(1)}, bf16[1024,64]{0,1:T(8,128)(2,1)S(1)}, u32[]{:S(2)}, u32[]{:S(2)}) collective-permute-start(bf16[1024,64]{0,1:T(8,128)(2,1)S(1)} %get-tuple-element.31), channel_id=1, source_target_pairs={{1,0},{2,1},{3,2},{4,3},{5,4},{6,5},{7,6},{9,8},{10,9},{11,10},{12... | collective-permute-start | bytes 393224 | tf_op jit(solution)/shard_map/ppermute | solution.py:28
  73.2 9.9 %collective-permute-start.9 = (bf16[1024,64]{0,1:T(8,128)(2,1)S(1)}, bf16[1024,64]{0,1:T(8,128)(2,1)S(1)}, u32[]{:S(2)}, u32[]{:S(2)}) collective-permute-start(bf16[1024,64]{0,1:T(8,128)(2,1)S(1)} %get-tuple-element.30), channel_id=1, source_target_pairs={{0,1},{1,2},{2,3},{3,4},{4,5},{5,6},{6,7},{8,9},{9,10},{10,11},{11... | collective-permute-start | bytes 393224 | tf_op jit(solution)/shard_map/ppermute | solution.py:27
  77.8 5.4 %collective-permute-start.8 = (bf16[256,256]{0,1:T(8,128)(2,1)S(1)}, bf16[256,256]{0,1:T(8,128)(2,1)S(1)}, u32[]{:S(2)}, u32[]{:S(2)}) collective-permute-start(bf16[256,256]{0,1:T(8,128)(2,1)S(1)} %pad_maximum_fusion.13), channel_id=1, source_target_pairs={{8,0},{16,8},{24,16},{9,1},{17,9},{25,17},{10,2},{18,10},{26,18},{... | collective-permute-start | bytes 393224 | tf_op jit(solution)/shard_map/ppermute | solution.py:90
  84.8 11.4 %collective-permute-start.11 = (bf16[256,256]{0,1:T(8,128)(2,1)S(1)}, bf16[256,256]{0,1:T(8,128)(2,1)S(1)}, u32[]{:S(2)}, u32[]{:S(2)}) collective-permute-start(bf16[256,256]{0,1:T(8,128)(2,1)S(1)} %pad_maximum_fusion.14), channel_id=1, source_target_pairs={{0,8},{8,16},{16,24},{1,9},{9,17},{17,25},{2,10},{10,18},{18,26},{... | collective-permute-start | bytes 393224 | tf_op jit(solution)/shard_map/ppermute | solution.py:89
  88.4 8.2 %collective-permute-start.14 = (bf16[1024,64]{0,1:T(8,128)(2,1)S(1)}, bf16[1024,64]{0,1:T(8,128)(2,1)S(1)}, u32[]{:S(2)}, u32[]{:S(2)}) collective-permute-start(bf16[1024,64]{0,1:T(8,128)(2,1)S(1)} %get-tuple-element.25), channel_id=1, source_target_pairs={{1,0},{2,1},{3,2},{4,3},{5,4},{6,5},{7,6},{9,8},{10,9},{11,10},{12... | collective-permute-start | bytes 393224 | tf_op jit(solution)/shard_map/ppermute | solution.py:28
  89.7 9.9 %collective-permute-start.13 = (bf16[1024,64]{0,1:T(8,128)(2,1)S(1)}, bf16[1024,64]{0,1:T(8,128)(2,1)S(1)}, u32[]{:S(2)}, u32[]{:S(2)}) collective-permute-start(bf16[1024,64]{0,1:T(8,128)(2,1)S(1)} %get-tuple-element.24), channel_id=1, source_target_pairs={{0,1},{1,2},{2,3},{3,4},{4,5},{5,6},{6,7},{8,9},{9,10},{10,11},{11... | collective-permute-start | bytes 393224 | tf_op jit(solution)/shard_map/ppermute | solution.py:27
  94.9 4.7 %collective-permute-start.12 = (bf16[256,256]{0,1:T(8,128)(2,1)S(1)}, bf16[256,256]{0,1:T(8,128)(2,1)S(1)}, u32[]{:S(2)}, u32[]{:S(2)}) collective-permute-start(bf16[256,256]{0,1:T(8,128)(2,1)S(1)} %pad_maximum_fusion.15), channel_id=1, source_target_pairs={{8,0},{16,8},{24,16},{9,1},{17,9},{25,17},{10,2},{18,10},{26,18},{... | collective-permute-start | bytes 393224 | tf_op jit(solution)/shard_map/ppermute | solution.py:90
  101.2 11.2 %collective-permute-start.15 = (bf16[256,256]{0,1:T(8,128)(2,1)S(1)}, bf16[256,256]{0,1:T(8,128)(2,1)S(1)}, u32[]{:S(2)}, u32[]{:S(2)}) collective-permute-start(bf16[256,256]{0,1:T(8,128)(2,1)S(1)} %pad_maximum_fusion.16), channel_id=1, source_target_pairs={{0,8},{8,16},{16,24},{1,9},{9,17},{17,25},{2,10},{10,18},{18,26},{... | collective-permute-start | bytes 393224 | tf_op jit(solution)/shard_map/ppermute | solution.py:89
  104.6 8.2 %collective-permute-start.18 = (bf16[1024,64]{0,1:T(8,128)(2,1)S(1)}, bf16[1024,64]{0,1:T(8,128)(2,1)S(1)}, u32[]{:S(2)}, u32[]{:S(2)}) collective-permute-start(bf16[1024,64]{0,1:T(8,128)(2,1)S(1)} %get-tuple-element.19), channel_id=1, source_target_pairs={{1,0},{2,1},{3,2},{4,3},{5,4},{6,5},{7,6},{9,8},{10,9},{11,10},{12... | collective-permute-start | bytes 393224 | tf_op jit(solution)/shard_map/ppermute | solution.py:28
  105.9 9.9 %collective-permute-start.17 = (bf16[1024,64]{0,1:T(8,128)(2,1)S(1)}, bf16[1024,64]{0,1:T(8,128)(2,1)S(1)}, u32[]{:S(2)}, u32[]{:S(2)}) collective-permute-start(bf16[1024,64]{0,1:T(8,128)(2,1)S(1)} %get-tuple-element.18), channel_id=1, source_target_pairs={{0,1},{1,2},{2,3},{3,4},{4,5},{5,6},{6,7},{8,9},{9,10},{10,11},{11... | collective-permute-start | bytes 393224 | tf_op jit(solution)/shard_map/ppermute | solution.py:27
  111.1 4.7 %collective-permute-start.16 = (bf16[256,256]{0,1:T(8,128)(2,1)S(1)}, bf16[256,256]{0,1:T(8,128)(2,1)S(1)}, u32[]{:S(2)}, u32[]{:S(2)}) collective-permute-start(bf16[256,256]{0,1:T(8,128)(2,1)S(1)} %pad_maximum_fusion.17), channel_id=1, source_target_pairs={{8,0},{16,8},{24,16},{9,1},{17,9},{25,17},{10,2},{18,10},{26,18},{... | collective-permute-start | bytes 393224 | tf_op jit(solution)/shard_map/ppermute | solution.py:90
  118.4 11.1 %collective-permute-start.19 = (bf16[256,256]{0,1:T(8,128)(2,1)S(1)}, bf16[256,256]{0,1:T(8,128)(2,1)S(1)}, u32[]{:S(2)}, u32[]{:S(2)}) collective-permute-start(bf16[256,256]{0,1:T(8,128)(2,1)S(1)} %pad_maximum_fusion.18), channel_id=1, source_target_pairs={{0,8},{8,16},{16,24},{1,9},{9,17},{17,25},{2,10},{10,18},{18,26},{... | collective-permute-start | bytes 393224 | tf_op jit(solution)/shard_map/ppermute | solution.py:89
  121.7 8.2 %collective-permute-start.22 = (bf16[1024,64]{0,1:T(8,128)(2,1)S(1)}, bf16[1024,64]{0,1:T(8,128)(2,1)S(1)}, u32[]{:S(2)}, u32[]{:S(2)}) collective-permute-start(bf16[1024,64]{0,1:T(8,128)(2,1)S(1)} %get-tuple-element.17), channel_id=1, source_target_pairs={{1,0},{2,1},{3,2},{4,3},{5,4},{6,5},{7,6},{9,8},{10,9},{11,10},{12... | collective-permute-start | bytes 393224 | tf_op jit(solution)/shard_map/ppermute | solution.py:28
  123.0 9.9 %collective-permute-start.21 = (bf16[1024,64]{0,1:T(8,128)(2,1)S(1)}, bf16[1024,64]{0,1:T(8,128)(2,1)S(1)}, u32[]{:S(2)}, u32[]{:S(2)}) collective-permute-start(bf16[1024,64]{0,1:T(8,128)(2,1)S(1)} %get-tuple-element.16), channel_id=1, source_target_pairs={{0,1},{1,2},{2,3},{3,4},{4,5},{5,6},{6,7},{8,9},{9,10},{10,11},{11... | collective-permute-start | bytes 393224 | tf_op jit(solution)/shard_map/ppermute | solution.py:27
  128.2 5.0 %collective-permute-start.20 = (bf16[256,256]{0,1:T(8,128)(2,1)S(1)}, bf16[256,256]{0,1:T(8,128)(2,1)S(1)}, u32[]{:S(2)}, u32[]{:S(2)}) collective-permute-start(bf16[256,256]{0,1:T(8,128)(2,1)S(1)} %pad_maximum_fusion.19), channel_id=1, source_target_pairs={{8,0},{16,8},{24,16},{9,1},{17,9},{25,17},{10,2},{18,10},{26,18},{... | collective-permute-start | bytes 393224 | tf_op jit(solution)/shard_map/ppermute | solution.py:90
  134.3 7.0 %all-to-all-start.2 = ((f32[4,2,256]{2,1,0:T(2,128)}), f32[4,2,256]{2,1,0:T(2,128)S(1)}, u32[]{:S(2)}, u32[]{:S(2)}) async-start(f32[4,2,256]{2,1,0:T(2,128)} %broadcast_in_dim.87), calls=%async_computation.2 | async-start | bytes 16384 | tf_op jit(solution)/shard_map/all_to_all | solution.py:161

commit v15 on v14

--- a/solution.py
+++ b/solution.py
@@ -86,8 +86,27 @@
         )
 
     def spatial(field):
-        lower = lax.ppermute(pick_blocks(field, upper_wants), "space", up)
-        upper = lax.ppermute(pick_blocks(field, lower_wants), "space", down)
+        to_upper = pick_blocks(field, upper_wants)
+        to_lower = pick_blocks(field, lower_wants)
+        targets = jnp.arange(space_count)[:, None, None]
+        outgoing = jnp.where(
+            targets == space_index + 1,
+            to_upper[None],
+            jnp.where(targets == space_index - 1, to_lower[None], jnp.zeros_like(to_upper)[None]),
+        )
+        incoming = lax.all_to_all(outgoing, "space", split_axis=0, concat_axis=0, tiled=True)
+        lower = jnp.where(
+            space_index > 0,
+            lax.dynamic_index_in_dim(incoming, jnp.maximum(space_index - 1, 0), keepdims=False),
+            jnp.zeros_like(to_upper),
+        )
+        upper = jnp.where(
+            space_index < space_count - 1,
+            lax.dynamic_index_in_dim(
+                incoming, jnp.minimum(space_index + 1, space_count - 1), keepdims=False
+            ),
+            jnp.zeros_like(to_upper),
+        )
         total = jnp.dot(field.T, own_t, preferred_element_type=jnp.float32)
         total = total + jnp.dot(lower.T, lower_t, preferred_element_type=jnp.float32)
         total = total + jnp.dot(upper.T, upper_t, preferred_element_type=jnp.float32)

time: 143 us -> 172 us (1.20)
  matrix products: 20 us -> 40.2 us
  other arithmetic: 12 us -> 24.9 us
  waiting for transfers between devices: 15.2 us -> 6.7 us
  local copies, waits for them, and re-layouts: 23.7 us -> 27.9 us
    ppermute x10 -> x0, starting transfers between devices: 21.5 us -> none  [the longest x5 14.8 us: spatial(): lower = lax.ppermute(pick_blocks(field, upper_wants), 'space', up)]
    all_to_all x0 -> x5, starting transfers between devices: none -> 20 us  [spatial(): lax.all_to_all(outgoing, 'space', split_axis=0, concat_axis=0, tiled=True)]
    ppermute x5, waiting for transfers between devices: 12 us -> 0.01 us  [with_halo(): before = lax.ppermute(last, axis, up)]
    dot_general x5, matrix products: 4.64 us -> 15.3 us  [spatial(): total = jnp.dot(field.T, own_t, preferred_element_type=jnp.float32)]
    select_n x0 -> x5, other arithmetic: none -> 7.17 us  [spatial(): jnp.where(targets == space_index + 1, to_upper[None], jnp.where(targets =...]
    dot_general x5, matrix products: 4.07 us -> 10.3 us  [spatial(): jnp.dot(lower.T, lower_t, preferred_element_type=jnp.float32)]
    all_to_all x0 -> x5, waiting for transfers between devices: none -> 4.05 us  [spatial(): lax.all_to_all(outgoing, 'space', split_axis=0, concat_axis=0, tiled=True)]
    convert_element_type x1 -> x3, other arithmetic: 1.07 us -> 4.68 us  [shards(): rounded = lax.optimization_barrier(solution.astype(jnp.bfloat16))]
  transfers between devices with their start and end apart: 26 -> 21, of which waited for: 7 -> 3; matrix products, arithmetic and copies ran while one was open for 30% -> 42% of each run, Pallas kernels for 0% -> 0%
where the time goes in v15:
time: 172 us; the launch traced here: 170 us
  starting transfers between devices  66.1 us (38%)
  matrix products  40.2 us (23%)
  local copies, waits for them, and re-layouts  27.9 us (16%)
  other arithmetic  24.9 us (14%)
  waiting for transfers between devices  6.7 us (4%)
  between operations  4.21 us (2%)
    ppermute x5, starting transfers between devices, with_halo(): before = lax.ppermute(last, axis, up)  26.7 us
    all_to_all x5, starting transfers between devices, spatial(): lax.all_to_all(outgoing, 'space', split_axis=0, concat_axis=0, tiled=True)  20 us
    dot_general x5, matrix products, spatial(): total = jnp.dot(field.T, own_t, preferred_element_type=jnp.float32)  15.3 us
    gather x1, local copies, waits for them, and re-layouts, shards(): coef_rows = svc_all[shift * nodes_dev + obs_cell // T_DEV]  10.8 us
    dot_general x5, matrix products, spatial(): jnp.dot(lower.T, lower_t, preferred_element_type=jnp.float32)  10.3 us
    dot_general x5, matrix products, spatial(): jnp.dot(upper.T, upper_t, preferred_element_type=jnp.float32)  9.8 us
    unnamed x79, local copies, waits for them, and re-layouts  7.31 us
    select_n x5, other arithmetic, spatial(): jnp.where(targets == space_index + 1, to_upper[None], jnp.where(targets =...  7.17 us
  transfers between devices with their start and end apart: 21, of which 3 were waited for; matrix products, arithmetic and copies ran while one was open for 42% of the time, Pallas kernels for 0%

profile of v15, /device:TPU:0, one launch (start us, length us, event | category | flops | bytes accessed | tf_op | source)
XLA Modules:
  0.0 170.0 jit_solution(13934663667920734816)
XLA Ops:
  0.7 2.5 %collective-permute-start.4 = (bf16[1024,256]{1,0:T(8,128)(2,1)}, bf16[1024,256]{1,0:T(8,128)(2,1)}, u32[]{:S(2)}, u32[]{:S(2)}) collective-permute-start(bf16[1024,256]{1,0:T(8,128)(2,1)} %param.23), channel_id=1, source_target_pairs={{0,24},{8,0},{16,8},{24,16},{1,25},{9,1},{17,9},{25,17},{2,26},{10... | collective-permute-start | bytes 1572872 | tf_op jit(solution)/shard_map/ppermute | solution.py:129
  4.0 1.2 copy.81
  5.2 0.7 broadcast_in_dim.210
  6.0 0.7 broadcast_in_dim.207
  6.8 1.1 select_reduce_fusion
  8.0 1.1 fusion.56
  9.8 1.3 collective-permute-start.1
  11.1 5.2 %collective-permute-start = (bf16[1024,64]{0,1:T(8,128)(2,1)S(1)}, bf16[1024,64]{0,1:T(8,128)(2,1)}, u32[]{:S(2)}, u32[]{:S(2)}) collective-permute-start(bf16[1024,64]{0,1:T(8,128)(2,1)S(1)} %get-tuple-element.44), channel_id=1, source_target_pairs={{0,1},{1,2},{2,3},{3,4},{4,5},{5,6},{6,7},{8,9},{9,10},{10,11},{11... | collective-permute-start | bytes 393224 | tf_op jit(solution)/shard_map/ppermute | solution.py:27
  16.3 1.2 broadcast_in_dim.212
  17.5 3.2 %all-to-all-start = ((s32[4,1,4]{2,1,0:T(1,128)}), s32[4,1,4]{2,1,0:T(1,128)S(1)}, u32[]{:S(2)}, u32[]{:S(2)}) async-start(s32[4,1,4]{2,1,0:T(1,128)} %broadcast_in_dim.212), calls=%async_computation | async-start | bytes 4096 | tf_op jit(solution)/shard_map/all_to_all | solution.py:74
  20.7 1.8 %convert_element_type.89 = f32[8,128,128]{2,1,0:T(8,128)} convert(bf16[8,128,128]{2,1,0:T(8,128)(2,1)} %param.16) | non-fusion elementwise | flops 131072 | bytes 786432 | tf_op jit(solution)/shard_map/convert_element_type | solution.py:52
  22.6 3.1 %add_convert_fusion = bf16[8,12,128,128]{3,1,2,0:T(8,128)(2,1)S(1)} fusion(f32[8,128,128]{2,1,0:T(8,128)} %convert_element_type.89, f32[8,12]{1,0:T(8,128)S(1)} %fusion.142, bf16[8,8,128,128]{3,2,1,0:T(8,128)(2,1)S(1)} %copy-done, s32[8,8]{1,0:T(8,128)S(1)} %copy-done.37), kind=kOutput, calls=%fused_computation.2 | convolution fusion | flops 29885184 | bytes 5767808 | tf_op jit(solution)/shard_map/bkm,bkij->bimj/dot_general | solution.py:63
  25.8 1.6 copy.112
  27.4 1.6 copy-done.1
  29.0 1.7 %fusion.18 = f32[1024,256]{0,1:T(8,128)} fusion(bf16[1024,256]{0,1:T(8,128)(2,1)S(1)} %fusion.56, bf16[1024,1536]{1,0:T(8,128)(2,1)S(1)} %bitcast.118), kind=kOutput, calls=%fused_computation.47 | convolution fusion | flops 536870912 | bytes 3670016 | tf_op jit(solution)/shard_map/dot_general | solution.py:110
  34.4 0.9 select_select_fusion.4
  35.3 3.5 %all-to-all-start.1 = ((bf16[4,256,256]{2,1,0:T(8,128)(2,1)}), bf16[4,256,256]{2,1,0:T(8,128)(2,1)S(1)}, u32[]{:S(2)}, u32[]{:S(2)}) async-start(bf16[4,256,256]{2,1,0:T(8,128)(2,1)} %select_select_fusion.4), calls=%async_computation.1 | async-start | bytes 1048576 | tf_op jit(solution)/shard_map/all_to_all | solution.py:97
  38.8 3.8 %maximum_convert_fusion = f32[4096,256]{1,0:T(8,128)} fusion(bf16[1024,256]{1,0:T(8,128)(2,1)} %collective-permute-done.4, bf16[1024,256]{1,0:T(8,128)(2,1)} %collective-permute-done.3, bf16[1024,256]{1,0:T(8,128)(2,1)} %collective-permute-done.2, bf16[1024,256]{1,0:T(8,128)(2,1)} %param.23), kind=kLoop, calls=%fused_computation.13 | loop fusion | flops 8388608 | bytes 6291456 | tf_op jit(solution)/shard_map/convert_element_type | solution.py:132
  42.6 10.8 %gather_fusion = f32[2048,256]{1,0:T(8,128)} fusion(f32[4096,256]{1,0:T(8,128)} %maximum_convert_fusion, s32[2048]{0:T(1024)S(1)} %get-tuple-element.57), kind=kCustom, calls=%fused_computation | custom fusion | bytes 4202496 | tf_op jit(solution)/shard_map/gather | solution.py:135
  53.4 2.2 %multiply_reduce_fusion = f32[2048]{0:T(1024)S(1)} fusion(f32[2048,256]{1,0:T(8,128)} %gather_fusion, bf16[2048,256]{1,0:T(8,128)(2,1)} %param.20), kind=kLoop, calls=%fused_computation.15 | loop fusion | flops 1570816 | bytes 3153920 | tf_op jit(solution)/shard_map/reduce_sum | solution.py:136
  55.7 1.7 %fusion = f32[48,1024]{1,0:T(8,128)S(1)} fusion(s32[2048]{0:T(1024)S(1)} %get-tuple-element.58, bf16[2048,16]{0,1:T(8,128)(2,1)S(1)} %get-tuple-element.51, bf16[2048,16]{0,1:T(8,128)(2,1)S(1)} %get-tuple-element.52, bf16[2048,16]{0,1:T(8,128)(2,1)S(1)} %get-tuple-element.50), kind=kOutput, calls=%fused_computation.3 | convolution fusion | flops 204013568 | bytes 401408 | tf_op jit(solution)/shard_map/dot_general | solution.py:148
  58.1 3.3 %all-to-all-start.2 = ((f32[4,4,1024]{2,1,0:T(4,128)}), f32[4,4,1024]{2,1,0:T(4,128)S(1)}, u32[]{:S(2)}, u32[]{:S(2)}) async-start(f32[4,4,1024]{2,1,0:T(4,128)} %add.219), calls=%async_computation.2 | async-start | bytes 131072 | tf_op jit(solution)/shard_map/all_to_all | solution.py:153
  61.4 2.7 %convolution_add_fusion.9 = f32[1024,256]{0,1:T(8,128)} fusion(f32[1024,256]{0,1:T(8,128)} %fusion.18, bf16[1024,1536]{1,0:T(8,128)(2,1)} %bitcast.119, bf16[4,256,256]{2,1,0:T(8,128)(2,1)S(1)} %all-to-all-done.1, s32[]{:T(128)S(6)} %max.2, pred[]{:T(512)S(6)} %gt.2), kind=kOutput, calls=%fused_computation.35 | convolution fusion | flops 134545408 | bytes 2752517 | tf_op jit(solution)/shard_map/dot_general | solution.py:111
  64.1 1.4 all-to-all-done.2
  65.6 4.0 %fusion.163 = (bf16[1024,256]{0,1:T(8,128)(2,1)S(1)}, f32[1024,256]{0,1:T(8,128)}) fusion(f32[4,1024]{1,0:T(4,128)S(1)} %reduce_sum.56, bf16[1024,64]{0,1:T(8,128)(2,1)} %collective-permute-done.1, bf16[1024,256]{0,1:T(8,128)(2,1)} %copy-done.8, bf16[1024,64]{0,1:T(8,128)(2,1)} %collective-permute-done, f32[256]{0:T(256)S(1)} %broadcast_in_dim_reshape.2, ...), kind=kOutput, calls=%fused_computation.266 | convolution fusion | flops 142409728 | bytes 4615173 | tf_op jit(solution)/shard_map/dot_general | solution.py:112
  69.9 1.5 select_select_fusion.3
  71.5 4.2 %all-to-all-start.3 = ((bf16[4,256,256]{2,1,0:T(8,128)(2,1)}), bf16[4,256,256]{2,1,0:T(8,128)(2,1)}, u32[]{:S(2)}, u32[]{:S(2)}) async-start(bf16[4,256,256]{2,1,0:T(8,128)(2,1)} %select_select_fusion.3), calls=%async_computation.3 | async-start | bytes 1048576 | tf_op jit(solution)/shard_map/all_to_all | solution.py:97
  75.6 0.7 fusion.168
  76.4 1.3 collective-permute-start.6
  77.7 4.7 %collective-permute-start.5 = (bf16[1024,64]{0,1:T(8,128)(2,1)}, bf16[1024,64]{0,1:T(8,128)(2,1)S(1)}, u32[]{:S(2)}, u32[]{:S(2)}) collective-permute-start(bf16[1024,64]{0,1:T(8,128)(2,1)} %get-tuple-element.38), channel_id=1, source_target_pairs={{0,1},{1,2},{2,3},{3,4},{4,5},{5,6},{6,7},{8,9},{9,10},{10,11},{11... | collective-permute-start | bytes 393224 | tf_op jit(solution)/shard_map/ppermute | solution.py:27
  82.4 3.4 %fusion.16 = f32[1024,256]{0,1:T(8,128)} fusion(bf16[1024,256]{0,1:T(8,128)(2,1)S(1)} %get-tuple-element.18, bf16[1024,1536]{1,0:T(8,128)(2,1)} %bitcast.121), kind=kOutput, calls=%fused_computation.45 | convolution fusion | flops 536870912 | bytes 3670016 | tf_op jit(solution)/shard_map/dot_general | solution.py:110
  85.8 1.9 %convolution_add_fusion.7 = f32[1024,256]{0,1:T(8,128)S(1)} fusion(f32[1024,256]{0,1:T(8,128)} %fusion.16, bf16[1024,1536]{1,0:T(8,128)(2,1)} %bitcast.122, bf16[4,256,256]{2,1,0:T(8,128)(2,1)} %all-to-all-done.3, s32[]{:T(128)S(6)} %max.2, pred[]{:T(512)S(6)} %gt.2), kind=kOutput, calls=%fused_computation.32 | convolution fusion | flops 134545408 | bytes 2752517 | tf_op jit(solution)/shard_map/dot_general | solution.py:111
  87.8 1.4 fusion.9
  89.3 1.8 %fusion.161 = (bf16[1024,256]{0,1:T(8,128)(2,1)S(1)}, f32[1024,256]{0,1:T(8,128)}) fusion(f32[1024,256]{0,1:T(8,128)S(1)} %copy-done.11, f32[256]{0:T(256)S(1)} %copy-done.30, f32[1024]{0:T(1024)S(1)} %bitcast.136, f32[256]{0:T(256)S(1)} %copy-done.22, f32[4,1024]{1,0:T(4,128)S(1)} %reduce_sum.56, f32[1024]{0:T(1024)S(1)} %copy-done.18, ...), kind=kLoop, calls=%fused_computation.265 | loop fusion | flops 7077888 | bytes 5008384 | tf_op jit(solution)/shard_map/convert_element_type | solution.py:165
  91.4 1.5 select_select_fusion.2
  93.0 4.2 %all-to-all-start.4 = ((bf16[4,256,256]{2,1,0:T(8,128)(2,1)}), bf16[4,256,256]{2,1,0:T(8,128)(2,1)}, u32[]{:S(2)}, u32[]{:S(2)}) async-start(bf16[4,256,256]{2,1,0:T(8,128)(2,1)} %select_select_fusion.2), calls=%async_computation.4 | async-start | bytes 1048576 | tf_op jit(solution)/shard_map/all_to_all | solution.py:97
  97.1 0.7 fusion.167
  97.8 1.3 collective-permute-start.8
  99.1 5.2 %collective-permute-start.7 = (bf16[1024,64]{0,1:T(8,128)(2,1)}, bf16[1024,64]{0,1:T(8,128)(2,1)S(1)}, u32[]{:S(2)}, u32[]{:S(2)}) collective-permute-start(bf16[1024,64]{0,1:T(8,128)(2,1)} %get-tuple-element.32), channel_id=1, source_target_pairs={{0,1},{1,2},{2,3},{3,4},{4,5},{5,6},{6,7},{8,9},{9,10},{10,11},{11... | collective-permute-start | bytes 393224 | tf_op jit(solution)/shard_map/ppermute | solution.py:27
  104.3 3.4 %fusion.14 = f32[1024,256]{0,1:T(8,128)} fusion(bf16[1024,256]{0,1:T(8,128)(2,1)S(1)} %get-tuple-element.16, bf16[1024,1536]{1,0:T(8,128)(2,1)} %bitcast.124), kind=kOutput, calls=%fused_computation.43 | convolution fusion | flops 536870912 | bytes 3670016 | tf_op jit(solution)/shard_map/dot_general | solution.py:110
  107.8 1.9 %convolution_add_fusion.5 = f32[1024,256]{0,1:T(8,128)S(1)} fusion(f32[1024,256]{0,1:T(8,128)} %fusion.14, bf16[1024,1536]{1,0:T(8,128)(2,1)} %bitcast.125, bf16[4,256,256]{2,1,0:T(8,128)(2,1)} %all-to-all-done.4, s32[]{:T(128)S(6)} %max.2, pred[]{:T(512)S(6)} %gt.2), kind=kOutput, calls=%fused_computation.29 | convolution fusion | flops 134545408 | bytes 2752517 | tf_op jit(solution)/shard_map/dot_general | solution.py:111
  109.7 1.4 fusion.8
  111.2 1.8 %fusion.159 = (bf16[1024,256]{0,1:T(8,128)(2,1)S(1)}, f32[1024,256]{0,1:T(8,128)}) fusion(f32[1024,256]{0,1:T(8,128)S(1)} %copy-done.10, f32[256]{0:T(256)S(1)} %copy-done.31, f32[1024]{0:T(1024)S(1)} %bitcast.137, f32[256]{0:T(256)S(1)} %copy-done.23, f32[4,1024]{1,0:T(4,128)S(1)} %reduce_sum.56, f32[1024]{0:T(1024)S(1)} %copy-done.19, ...), kind=kLoop, calls=%fused_computation.264 | loop fusion | flops 7077888 | bytes 5008384 | tf_op jit(solution)/shard_map/convert_element_type | solution.py:165
  113.4 1.6 select_select_fusion.1
  114.9 4.1 %all-to-all-start.5 = ((bf16[4,256,256]{2,1,0:T(8,128)(2,1)}), bf16[4,256,256]{2,1,0:T(8,128)(2,1)}, u32[]{:S(2)}, u32[]{:S(2)}) async-start(bf16[4,256,256]{2,1,0:T(8,128)(2,1)} %select_select_fusion.1), calls=%async_computation.5 | async-start | bytes 1048576 | tf_op jit(solution)/shard_map/all_to_all | solution.py:97
  119.8 1.3 collective-permute-start.10
  121.1 5.5 %collective-permute-start.9 = (bf16[1024,64]{0,1:T(8,128)(2,1)}, bf16[1024,64]{0,1:T(8,128)(2,1)S(1)}, u32[]{:S(2)}, u32[]{:S(2)}) collective-permute-start(bf16[1024,64]{0,1:T(8,128)(2,1)} %get-tuple-element.26), channel_id=1, source_target_pairs={{0,1},{1,2},{2,3},{3,4},{4,5},{5,6},{6,7},{8,9},{9,10},{10,11},{11... | collective-permute-start | bytes 393224 | tf_op jit(solution)/shard_map/ppermute | solution.py:27
  126.5 3.4 %fusion.12 = f32[1024,256]{0,1:T(8,128)} fusion(bf16[1024,256]{0,1:T(8,128)(2,1)S(1)} %get-tuple-element.14, bf16[1024,1536]{1,0:T(8,128)(2,1)} %bitcast.127), kind=kOutput, calls=%fused_computation.41 | convolution fusion | flops 536870912 | bytes 3670016 | tf_op jit(solution)/shard_map/dot_general | solution.py:110
  129.9 1.9 %convolution_add_fusion.3 = f32[1024,256]{0,1:T(8,128)S(1)} fusion(f32[1024,256]{0,1:T(8,128)} %fusion.12, bf16[1024,1536]{1,0:T(8,128)(2,1)} %bitcast.128, bf16[4,256,256]{2,1,0:T(8,128)(2,1)} %all-to-all-done.5, s32[]{:T(128)S(6)} %max.2, pred[]{:T(512)S(6)} %gt.2), kind=kOutput, calls=%fused_computation.26 | convolution fusion | flops 134545408 | bytes 2752517 | tf_op jit(solution)/shard_map/dot_general | solution.py:111
  131.9 1.4 fusion.7
  133.4 1.9 %fusion.157 = (bf16[1024,256]{0,1:T(8,128)(2,1)S(1)}, f32[1024,256]{0,1:T(8,128)}) fusion(f32[1024,256]{0,1:T(8,128)S(1)} %copy-done.9, f32[256]{0:T(256)S(1)} %copy-done.32, f32[1024]{0:T(1024)S(1)} %bitcast.138, f32[256]{0:T(256)S(1)} %copy-done.24, f32[4,1024]{1,0:T(4,128)S(1)} %reduce_sum.56, f32[1024]{0:T(1024)S(1)} %copy-done.20, ...), kind=kLoop, calls=%fused_computation.263 | loop fusion | flops 7077888 | bytes 5008384 | tf_op jit(solution)/shard_map/convert_element_type | solution.py:172
  135.2 0.8 fusion.165
  136.2 1.3 collective-permute-start.12
  137.5 6.1 %collective-permute-start.11 = (bf16[1024,64]{0,1:T(8,128)(2,1)}, bf16[1024,64]{0,1:T(8,128)(2,1)}, u32[]{:S(2)}, u32[]{:S(2)}) collective-permute-start(bf16[1024,64]{0,1:T(8,128)(2,1)} %get-tuple-element.24), channel_id=1, source_target_pairs={{0,1},{1,2},{2,3},{3,4},{4,5},{5,6},{6,7},{8,9},{9,10},{10,11},{11... | collective-permute-start | bytes 393224 | tf_op jit(solution)/shard_map/ppermute | solution.py:27
  143.9 1.6 select_select_fusion
  145.5 4.1 %all-to-all-start.6 = ((bf16[4,256,256]{2,1,0:T(8,128)(2,1)}), bf16[4,256,256]{2,1,0:T(8,128)(2,1)}, u32[]{:S(2)}, u32[]{:S(2)}) async-start(bf16[4,256,256]{2,1,0:T(8,128)(2,1)} %select_select_fusion), calls=%async_computation.6 | async-start | bytes 1048576 | tf_op jit(solution)/shard_map/all_to_all | solution.py:97
  149.6 3.5 %fusion.20 = f32[1024,256]{0,1:T(8,128)} fusion(bf16[1024,256]{0,1:T(8,128)(2,1)} %copy-done.4, bf16[1024,1536]{1,0:T(8,128)(2,1)} %bitcast.130), kind=kOutput, calls=%fused_computation.49 | convolution fusion | flops 536870912 | bytes 3670016 | tf_op jit(solution)/shard_map/dot_general | solution.py:110
  153.1 1.3 fusion.55
  154.4 4.0 %all-to-all-done.6 = bf16[4,256,256]{2,1,0:T(8,128)(2,1)} async-done(((bf16[4,256,256]{2,1,0:T(8,128)(2,1)}), bf16[4,256,256]{2,1,0:T(8,128)(2,1)}, u32[]{:S(2)}, u32[]{:S(2)}) %all-to-all-start.6) | async-done | bytes 524320 | tf_op jit(solution)/shard_map/all_to_all | solution.py:97
  158.5 1.8 %convolution_add_fusion.1 = f32[1024,256]{0,1:T(8,128)S(1)} fusion(f32[1024,256]{0,1:T(8,128)} %fusion.20, bf16[1024,1536]{1,0:T(8,128)(2,1)} %bitcast.131, bf16[4,256,256]{2,1,0:T(8,128)(2,1)} %all-to-all-done.6, s32[]{:T(128)S(6)} %max.2, pred[]{:T(512)S(6)} %gt.2), kind=kOutput, calls=%fused_computation.23 | convolution fusion | flops 134545408 | bytes 2752517 | tf_op jit(solution)/shard_map/dot_general | solution.py:111
  160.3 1.5 fusion.11
  162.4 3.2 %all-to-all-start.7 = ((f32[4,2,256]{2,1,0:T(2,128)}), f32[4,2,256]{2,1,0:T(2,128)S(1)}, u32[]{:S(2)}, u32[]{:S(2)}) async-start(f32[4,2,256]{2,1,0:T(2,128)} %broadcast_in_dim.231), calls=%async_computation.7 | async-start | bytes 16384 | tf_op jit(solution)/shard_map/all_to_all | solution.py:180
  165.7 2.5 %copy.98 = f32[1024,256]{1,0:T(8,128)} copy(f32[1024,256]{0,1:T(8,128)} %get-tuple-element.13) | data formatting | bytes 2097152
  168.2 1.2 all-to-all-done.7
  (141 shorter events, 6.9 us)
Async XLA Ops:
  0.6 22.0 %copy-start = (bf16[8,8,128,128]{3,2,1,0:T(8,128)(2,1)S(1)}, bf16[8,8,128,128]{3,2,1,0:T(8,128)(2,1)}, u32[]{:S(2)}) copy-start(bf16[8,8,128,128]{3,2,1,0:T(8,128)(2,1)} %param.17) | copy-start | bytes 6291460
  0.6 21.9 %copy-start.35 = (s32[2048,1]{0,1:T(1,128)S(1)}, s32[2048,1]{0,1:T(1,128)}, u32[]{:S(2)}) copy-start(s32[2048,1]{0,1:T(1,128)} %param.21) | copy-start | bytes 24580
  0.7 21.9 %copy-start.37 = (s32[8,8]{1,0:T(8,128)S(1)}, s32[8,8]{1,0:T(8,128)}, u32[]{:S(2)}) copy-start(s32[8,8]{1,0:T(8,128)} %param.18) | copy-start | bytes 772
  0.7 38.1 %collective-permute-start.4 = (bf16[1024,256]{1,0:T(8,128)(2,1)}, bf16[1024,256]{1,0:T(8,128)(2,1)}, u32[]{:S(2)}, u32[]{:S(2)}) collective-permute-start(bf16[1024,256]{1,0:T(8,128)(2,1)} %param.23), channel_id=1, source_target_pairs={{0,24},{8,0},{16,8},{24,16},{1,25},{9,1},{17,9},{25,17},{2,26},{10... | collective-permute-start | bytes 1572872 | tf_op jit(solution)/shard_map/ppermute | solution.py:129
  3.2 35.6 %collective-permute-start.3 = (bf16[1024,256]{1,0:T(8,128)(2,1)}, bf16[1024,256]{1,0:T(8,128)(2,1)}, u32[]{:S(2)}, u32[]{:S(2)}) collective-permute-start(bf16[1024,256]{1,0:T(8,128)(2,1)} %param.23), channel_id=1, source_target_pairs={{0,16},{8,24},{16,0},{24,8},{1,17},{9,25},{17,1},{25,9},{2,18},{10... | collective-permute-start | bytes 1572872 | tf_op jit(solution)/shard_map/ppermute | solution.py:129
  3.8 35.0 %collective-permute-start.2 = (bf16[1024,256]{1,0:T(8,128)(2,1)}, bf16[1024,256]{1,0:T(8,128)(2,1)}, u32[]{:S(2)}, u32[]{:S(2)}) collective-permute-start(bf16[1024,256]{1,0:T(8,128)(2,1)} %param.23), channel_id=1, source_target_pairs={{0,8},{8,16},{16,24},{24,0},{1,9},{9,17},{17,25},{25,1},{2,10},{10... | collective-permute-start | bytes 1572872 | tf_op jit(solution)/shard_map/ppermute | solution.py:129
  6.0 59.5 %copy-start.25 = (f32[256]{0:T(256)}, f32[256]{0:T(256)S(1)}, u32[]{:S(2)}) copy-start(f32[256]{0:T(256)S(1)} %broadcast_in_dim_reshape.2) | copy-start | bytes 3076
  6.0 59.5 %copy-start.29 = (f32[256]{0:T(256)}, f32[256]{0:T(256)S(1)}, u32[]{:S(2)}) copy-start(f32[256]{0:T(256)S(1)} %broadcast_multiply_fusion.2) | copy-start | bytes 3076
  6.8 58.7 %copy-start.21 = (f32[256]{0:T(256)}, f32[256]{0:T(256)S(1)}, u32[]{:S(2)}) copy-start(f32[256]{0:T(256)S(1)} %mul.187) | copy-start | bytes 3076
  7.9 57.6 %copy-start.13 = (f32[8,128]{1,0:T(8,128)}, f32[8,128]{1,0:T(8,128)S(1)}, u32[]{:S(2)}) copy-start(f32[8,128]{1,0:T(8,128)S(1)} %select_reduce_fusion) | copy-start | bytes 12292
  9.0 25.0 %copy-start.8 = (bf16[1024,256]{0,1:T(8,128)(2,1)}, bf16[1024,256]{0,1:T(8,128)(2,1)S(1)}, u32[]{:S(2)}) copy-start(bf16[1024,256]{0,1:T(8,128)(2,1)S(1)} %fusion.56) | copy-start | bytes 1572868
  9.8 55.7 %collective-permute-start.1 = (bf16[1024,64]{0,1:T(8,128)(2,1)}, bf16[1024,64]{0,1:T(8,128)(2,1)}, u32[]{:S(2)}, u32[]{:S(2)}) collective-permute-start(bf16[1024,64]{0,1:T(8,128)(2,1)} %get-tuple-element.45), channel_id=1, source_target_pairs={{1,0},{2,1},{3,2},{4,3},{5,4},{6,5},{7,6},{9,8},{10,9},{11,10},{12... | collective-permute-start | bytes 393224 | tf_op jit(solution)/shard_map/ppermute | solution.py:28
  11.1 54.5 %collective-permute-start = (bf16[1024,64]{0,1:T(8,128)(2,1)S(1)}, bf16[1024,64]{0,1:T(8,128)(2,1)}, u32[]{:S(2)}, u32[]{:S(2)}) collective-permute-start(bf16[1024,64]{0,1:T(8,128)(2,1)S(1)} %get-tuple-element.44), channel_id=1, source_target_pairs={{0,1},{1,2},{2,3},{3,4},{4,5},{5,6},{6,7},{8,9},{9,10},{10,11},{11... | collective-permute-start | bytes 393224 | tf_op jit(solution)/shard_map/ppermute | solution.py:27
  17.5 13.3 %all-to-all-start = ((s32[4,1,4]{2,1,0:T(1,128)}), s32[4,1,4]{2,1,0:T(1,128)S(1)}, u32[]{:S(2)}, u32[]{:S(2)}) async-start(s32[4,1,4]{2,1,0:T(1,128)} %broadcast_in_dim.212), calls=%async_computation | async-start | bytes 4096 | tf_op jit(solution)/shard_map/all_to_all | solution.py:74
  22.5 11.9 %copy-start.33 = (pred[4]{0:T(512)(128)(4,1)}, pred[4]{0:T(512)(128)(4,1)S(1)}, u32[]{:S(2)}) copy-start(pred[4]{0:T(512)(128)(4,1)S(1)} %get-tuple-element.69) | copy-start | bytes 16
  22.5 11.9 %copy-start.34 = (pred[4]{0:T(512)(128)(4,1)}, pred[4]{0:T(512)(128)(4,1)S(1)}, u32[]{:S(2)}) copy-start(pred[4]{0:T(512)(128)(4,1)S(1)} %get-tuple-element.70) | copy-start | bytes 16
  27.4 1.7 copy-start.1
  27.4 3.4 %copy-start.36 = (s32[2048]{0:T(1024)S(1)}, s32[2048]{0:T(1024)}, u32[]{:S(2)}) copy-start(s32[2048]{0:T(1024)} %param.22) | copy-start | bytes 24580
  35.3 22.8 %all-to-all-start.1 = ((bf16[4,256,256]{2,1,0:T(8,128)(2,1)}), bf16[4,256,256]{2,1,0:T(8,128)(2,1)S(1)}, u32[]{:S(2)}, u32[]{:S(2)}) async-start(bf16[4,256,256]{2,1,0:T(8,128)(2,1)} %select_select_fusion.4), calls=%async_computation.1 | async-start | bytes 1048576 | tf_op jit(solution)/shard_map/all_to_all | solution.py:97
  55.7 9.9 %copy-start.17 = (f32[1024]{0:T(1024)S(1)}, f32[1024]{0:T(1024)}, u32[]{:S(2)}) copy-start(f32[1024]{0:T(1024)} %param.13) | copy-start | bytes 12292
  58.1 7.4 %copy-start.12 = (bf16[4,256,256]{2,1,0:T(8,128)(2,1)}, bf16[4,256,256]{2,1,0:T(8,128)(2,1)S(1)}, u32[]{:S(2)}) copy-start(bf16[4,256,256]{2,1,0:T(8,128)(2,1)S(1)} %all-to-all-done.1) | copy-start | bytes 1572868
  58.1 7.4 %all-to-all-start.2 = ((f32[4,4,1024]{2,1,0:T(4,128)}), f32[4,4,1024]{2,1,0:T(4,128)S(1)}, u32[]{:S(2)}, u32[]{:S(2)}) async-start(f32[4,4,1024]{2,1,0:T(4,128)} %add.219), calls=%async_computation.2 | async-start | bytes 131072 | tf_op jit(solution)/shard_map/all_to_all | solution.py:153
  69.6 16.2 %copy-start.6 = (bf16[1024,256]{0,1:T(8,128)(2,1)}, bf16[1024,256]{0,1:T(8,128)(2,1)S(1)}, u32[]{:S(2)}) copy-start(bf16[1024,256]{0,1:T(8,128)(2,1)S(1)} %get-tuple-element.18) | copy-start | bytes 1572868
  71.5 14.3 %all-to-all-start.3 = ((bf16[4,256,256]{2,1,0:T(8,128)(2,1)}), bf16[4,256,256]{2,1,0:T(8,128)(2,1)}, u32[]{:S(2)}, u32[]{:S(2)}) async-start(bf16[4,256,256]{2,1,0:T(8,128)(2,1)} %select_select_fusion.3), calls=%async_computation.3 | async-start | bytes 1048576 | tf_op jit(solution)/shard_map/all_to_all | solution.py:97
  76.4 12.8 %collective-permute-start.6 = (bf16[1024,64]{0,1:T(8,128)(2,1)}, bf16[1024,64]{0,1:T(8,128)(2,1)S(1)}, u32[]{:S(2)}, u32[]{:S(2)}) collective-permute-start(bf16[1024,64]{0,1:T(8,128)(2,1)} %get-tuple-element.39), channel_id=1, source_target_pairs={{1,0},{2,1},{3,2},{4,3},{5,4},{6,5},{7,6},{9,8},{10,9},{11,10},{12... | collective-permute-start | bytes 393224 | tf_op jit(solution)/shard_map/ppermute | solution.py:28
  77.6 10.1 %copy-start.22 = (f32[256]{0:T(256)S(1)}, f32[256]{0:T(256)}, u32[]{:S(2)}) copy-start(f32[256]{0:T(256)} %copy-done.21) | copy-start | bytes 3076
  77.7 11.6 %collective-permute-start.5 = (bf16[1024,64]{0,1:T(8,128)(2,1)}, bf16[1024,64]{0,1:T(8,128)(2,1)S(1)}, u32[]{:S(2)}, u32[]{:S(2)}) collective-permute-start(bf16[1024,64]{0,1:T(8,128)(2,1)} %get-tuple-element.38), channel_id=1, source_target_pairs={{0,1},{1,2},{2,3},{3,4},{4,5},{5,6},{6,7},{8,9},{9,10},{10,11},{11... | collective-permute-start | bytes 393224 | tf_op jit(solution)/shard_map/ppermute | solution.py:27
  85.8 3.4 %copy-start.14 = (f32[8,128]{1,0:T(8,128)S(1)}, f32[8,128]{1,0:T(8,128)}, u32[]{:S(2)}) copy-start(f32[8,128]{1,0:T(8,128)} %copy-done.13) | copy-start | bytes 12292
  85.8 3.5 %copy-start.18 = (f32[1024]{0:T(1024)S(1)}, f32[1024]{0:T(1024)}, u32[]{:S(2)}) copy-start(f32[1024]{0:T(1024)} %param.13) | copy-start | bytes 12292
  85.8 3.5 %copy-start.26 = (f32[256]{0:T(256)S(1)}, f32[256]{0:T(256)}, u32[]{:S(2)}) copy-start(f32[256]{0:T(256)} %copy-done.25) | copy-start | bytes 3076
  85.8 3.5 %copy-start.30 = (f32[256]{0:T(256)S(1)}, f32[256]{0:T(256)}, u32[]{:S(2)}) copy-start(f32[256]{0:T(256)} %copy-done.29) | copy-start | bytes 3076
  85.8 3.5 %copy-start.7 = (bf16[1024,256]{0,1:T(8,128)(2,1)S(1)}, bf16[1024,256]{0,1:T(8,128)(2,1)}, u32[]{:S(2)}) copy-start(bf16[1024,256]{0,1:T(8,128)(2,1)} %copy-done.6) | copy-start | bytes 1572868
  85.8 3.5 %copy-start.11 = (f32[1024,256]{0,1:T(8,128)S(1)}, f32[1024,256]{0,1:T(8,128)}, u32[]{:S(2)}) copy-start(f32[1024,256]{0,1:T(8,128)} %get-tuple-element.19) | copy-start | bytes 3145732
  91.1 16.6 %copy-start.2 = (bf16[1024,256]{0,1:T(8,128)(2,1)}, bf16[1024,256]{0,1:T(8,128)(2,1)S(1)}, u32[]{:S(2)}) copy-start(bf16[1024,256]{0,1:T(8,128)(2,1)S(1)} %get-tuple-element.16) | copy-start | bytes 1572868
  93.0 14.8 %all-to-all-start.4 = ((bf16[4,256,256]{2,1,0:T(8,128)(2,1)}), bf16[4,256,256]{2,1,0:T(8,128)(2,1)}, u32[]{:S(2)}, u32[]{:S(2)}) async-start(bf16[4,256,256]{2,1,0:T(8,128)(2,1)} %select_select_fusion.2), calls=%async_computation.4 | async-start | bytes 1048576 | tf_op jit(solution)/shard_map/all_to_all | solution.py:97
  97.8 13.3 %collective-permute-start.8 = (bf16[1024,64]{0,1:T(8,128)(2,1)}, bf16[1024,64]{0,1:T(8,128)(2,1)S(1)}, u32[]{:S(2)}, u32[]{:S(2)}) collective-permute-start(bf16[1024,64]{0,1:T(8,128)(2,1)} %get-tuple-element.33), channel_id=1, source_target_pairs={{1,0},{2,1},{3,2},{4,3},{5,4},{6,5},{7,6},{9,8},{10,9},{11,10},{12... | collective-permute-start | bytes 393224 | tf_op jit(solution)/shard_map/ppermute | solution.py:28
  99.1 10.6 %copy-start.23 = (f32[256]{0:T(256)S(1)}, f32[256]{0:T(256)}, u32[]{:S(2)}) copy-start(f32[256]{0:T(256)} %copy-done.21) | copy-start | bytes 3076
  99.1 12.0 %collective-permute-start.7 = (bf16[1024,64]{0,1:T(8,128)(2,1)}, bf16[1024,64]{0,1:T(8,128)(2,1)S(1)}, u32[]{:S(2)}, u32[]{:S(2)}) collective-permute-start(bf16[1024,64]{0,1:T(8,128)(2,1)} %get-tuple-element.32), channel_id=1, source_target_pairs={{0,1},{1,2},{2,3},{3,4},{4,5},{5,6},{6,7},{8,9},{9,10},{10,11},{11... | collective-permute-start | bytes 393224 | tf_op jit(solution)/shard_map/ppermute | solution.py:27
  107.7 3.4 %copy-start.15 = (f32[8,128]{1,0:T(8,128)S(1)}, f32[8,128]{1,0:T(8,128)}, u32[]{:S(2)}) copy-start(f32[8,128]{1,0:T(8,128)} %copy-done.13) | copy-start | bytes 12292
  107.7 3.5 %copy-start.19 = (f32[1024]{0:T(1024)S(1)}, f32[1024]{0:T(1024)}, u32[]{:S(2)}) copy-start(f32[1024]{0:T(1024)} %param.13) | copy-start | bytes 12292
  107.7 3.5 %copy-start.27 = (f32[256]{0:T(256)S(1)}, f32[256]{0:T(256)}, u32[]{:S(2)}) copy-start(f32[256]{0:T(256)} %copy-done.25) | copy-start | bytes 3076
  107.7 3.5 %copy-start.31 = (f32[256]{0:T(256)S(1)}, f32[256]{0:T(256)}, u32[]{:S(2)}) copy-start(f32[256]{0:T(256)} %copy-done.29) | copy-start | bytes 3076
  107.7 3.5 %copy-start.3 = (bf16[1024,256]{0,1:T(8,128)(2,1)S(1)}, bf16[1024,256]{0,1:T(8,128)(2,1)}, u32[]{:S(2)}) copy-start(bf16[1024,256]{0,1:T(8,128)(2,1)} %copy-done.2) | copy-start | bytes 1572868
  107.7 3.5 %copy-start.10 = (f32[1024,256]{0,1:T(8,128)S(1)}, f32[1024,256]{0,1:T(8,128)}, u32[]{:S(2)}) copy-start(f32[1024,256]{0,1:T(8,128)} %get-tuple-element.17) | copy-start | bytes 3145732
  114.9 15.0 %all-to-all-start.5 = ((bf16[4,256,256]{2,1,0:T(8,128)(2,1)}), bf16[4,256,256]{2,1,0:T(8,128)(2,1)}, u32[]{:S(2)}, u32[]{:S(2)}) async-start(bf16[4,256,256]{2,1,0:T(8,128)(2,1)} %select_select_fusion.1), calls=%async_computation.5 | async-start | bytes 1048576 | tf_op jit(solution)/shard_map/all_to_all | solution.py:97
  119.8 13.5 %collective-permute-start.10 = (bf16[1024,64]{0,1:T(8,128)(2,1)}, bf16[1024,64]{0,1:T(8,128)(2,1)S(1)}, u32[]{:S(2)}, u32[]{:S(2)}) collective-permute-start(bf16[1024,64]{0,1:T(8,128)(2,1)} %get-tuple-element.27), channel_id=1, source_target_pairs={{1,0},{2,1},{3,2},{4,3},{5,4},{6,5},{7,6},{9,8},{10,9},{11,10},{12... | collective-permute-start | bytes 393224 | tf_op jit(solution)/shard_map/ppermute | solution.py:28
  121.1 10.8 %copy-start.24 = (f32[256]{0:T(256)S(1)}, f32[256]{0:T(256)}, u32[]{:S(2)}) copy-start(f32[256]{0:T(256)} %copy-done.21) | copy-start | bytes 3076
  121.1 12.2 %collective-permute-start.9 = (bf16[1024,64]{0,1:T(8,128)(2,1)}, bf16[1024,64]{0,1:T(8,128)(2,1)S(1)}, u32[]{:S(2)}, u32[]{:S(2)}) collective-permute-start(bf16[1024,64]{0,1:T(8,128)(2,1)} %get-tuple-element.26), channel_id=1, source_target_pairs={{0,1},{1,2},{2,3},{3,4},{4,5},{5,6},{6,7},{8,9},{9,10},{10,11},{11... | collective-permute-start | bytes 393224 | tf_op jit(solution)/shard_map/ppermute | solution.py:27
  129.9 3.4 %copy-start.16 = (f32[8,128]{1,0:T(8,128)S(1)}, f32[8,128]{1,0:T(8,128)}, u32[]{:S(2)}) copy-start(f32[8,128]{1,0:T(8,128)} %copy-done.13) | copy-start | bytes 12292
  129.9 3.4 %copy-start.20 = (f32[1024]{0:T(1024)S(1)}, f32[1024]{0:T(1024)}, u32[]{:S(2)}) copy-start(f32[1024]{0:T(1024)} %param.13) | copy-start | bytes 12292
  129.9 3.4 %copy-start.28 = (f32[256]{0:T(256)S(1)}, f32[256]{0:T(256)}, u32[]{:S(2)}) copy-start(f32[256]{0:T(256)} %copy-done.25) | copy-start | bytes 3076
  129.9 3.4 %copy-start.32 = (f32[256]{0:T(256)S(1)}, f32[256]{0:T(256)}, u32[]{:S(2)}) copy-start(f32[256]{0:T(256)} %copy-done.29) | copy-start | bytes 3076
  129.9 3.4 %copy-start.9 = (f32[1024,256]{0,1:T(8,128)S(1)}, f32[1024,256]{0,1:T(8,128)}, u32[]{:S(2)}) copy-start(f32[1024,256]{0,1:T(8,128)} %get-tuple-element.15) | copy-start | bytes 3145732
  135.2 0.9 copy-start.4
  136.2 16.9 %collective-permute-start.12 = (bf16[1024,64]{0,1:T(8,128)(2,1)}, bf16[1024,64]{0,1:T(8,128)(2,1)}, u32[]{:S(2)}, u32[]{:S(2)}) collective-permute-start(bf16[1024,64]{0,1:T(8,128)(2,1)} %get-tuple-element.25), channel_id=1, source_target_pairs={{1,0},{2,1},{3,2},{4,3},{5,4},{6,5},{7,6},{9,8},{10,9},{11,10},{12... | collective-permute-start | bytes 393224 | tf_op jit(solution)/shard_map/ppermute | solution.py:28
  137.5 15.6 %collective-permute-start.11 = (bf16[1024,64]{0,1:T(8,128)(2,1)}, bf16[1024,64]{0,1:T(8,128)(2,1)}, u32[]{:S(2)}, u32[]{:S(2)}) collective-permute-start(bf16[1024,64]{0,1:T(8,128)(2,1)} %get-tuple-element.24), channel_id=1, source_target_pairs={{0,1},{1,2},{2,3},{3,4},{4,5},{5,6},{6,7},{8,9},{9,10},{10,11},{11... | collective-permute-start | bytes 393224 | tf_op jit(solution)/shard_map/ppermute | solution.py:27
  143.7 9.4 %copy-start.5 = (bf16[1024,256]{0,1:T(8,128)(2,1)S(1)}, bf16[1024,256]{0,1:T(8,128)(2,1)}, u32[]{:S(2)}) copy-start(bf16[1024,256]{0,1:T(8,128)(2,1)} %copy-done.4) | copy-start | bytes 1572868
  145.5 13.0 %all-to-all-start.6 = ((bf16[4,256,256]{2,1,0:T(8,128)(2,1)}), bf16[4,256,256]{2,1,0:T(8,128)(2,1)}, u32[]{:S(2)}, u32[]{:S(2)}) async-start(bf16[4,256,256]{2,1,0:T(8,128)(2,1)} %select_select_fusion), calls=%async_computation.6 | async-start | bytes 1048576 | tf_op jit(solution)/shard_map/all_to_all | solution.py:97
  162.4 7.0 %all-to-all-start.7 = ((f32[4,2,256]{2,1,0:T(2,128)}), f32[4,2,256]{2,1,0:T(2,128)S(1)}, u32[]{:S(2)}, u32[]{:S(2)}) async-start(f32[4,2,256]{2,1,0:T(2,128)} %broadcast_in_dim.231), calls=%async_computation.7 | async-start | bytes 16384 | tf_op jit(solution)/shard_map/all_to_all | solution.py:180

commit v16 on v14

--- a/solution.py
+++ b/solution.py
@@ -91,7 +91,7 @@
         total = jnp.dot(field.T, own_t, preferred_element_type=jnp.float32)
         total = total + jnp.dot(lower.T, lower_t, preferred_element_type=jnp.float32)
         total = total + jnp.dot(upper.T, upper_t, preferred_element_type=jnp.float32)
-        return total.T
+        return total.T, lower
 
     def temporal(field):
         arrived = with_halo(field, (("tm", 1),), PROBES)
@@ -103,11 +103,12 @@
 
     solution = relaxation * probe_vals / base_diag
     rounded = lax.optimization_barrier(solution.astype(jnp.bfloat16))
-    first_space = spatial(rounded)
+    first_space, first_lower = spatial(rounded)
+    svc_sent, _ = lax.optimization_barrier((svc_coef, first_lower))
     first_time = temporal(rounded)
     nodes_dev = svc_coef.shape[0]
     tables = [svc_coef] + [
-        lax.ppermute(svc_coef, "space", [(i, (i + k) % space_count) for i in range(space_count)])
+        lax.ppermute(svc_sent, "space", [(i, (i + k) % space_count) for i in range(space_count)])
         for k in range(1, space_count)
     ]
     svc_all = jnp.concatenate(tables, axis=0).astype(jnp.float32)
@@ -145,7 +146,7 @@
     for sweep in range(ITERS - 1):
         rounded = lax.optimization_barrier(solution.astype(jnp.bfloat16))
         applied = (
-            scale_space * spatial(rounded)
+            scale_space * spatial(rounded)[0]
             + scale_time * temporal(rounded)
             + local_diag * rounded.astype(jnp.float32)
         )
@@ -153,7 +154,7 @@
     rounded = solution.astype(jnp.bfloat16)
     partial_sums = jnp.stack(
         [
-            jnp.sum(probe_vals * spatial(rounded), axis=0),
+            jnp.sum(probe_vals * spatial(rounded)[0], axis=0),
             jnp.sum(probe_vals * temporal(rounded), axis=0),
         ]
     )

time: 143 us -> 167 us (1.17)
  waiting for transfers between devices: 15.2 us -> 42.6 us
    ppermute x3, waiting for transfers between devices: 0.01 us -> 18.5 us  [shards(): lax.ppermute(svc_sent, 'space', [(i, (i + k) % space_count) for i in rang...]
    ppermute x5, waiting for transfers between devices: 0.54 us -> 17.7 us  [with_halo(): after = lax.ppermute(initial, axis, down)]
    ppermute x5, waiting for transfers between devices: 12 us -> 3.77 us  [with_halo(): before = lax.ppermute(last, axis, up)]
    ppermute x5, starting transfers between devices: 25.3 us -> 21.5 us  [with_halo(): before = lax.ppermute(last, axis, up)]
    all_to_all x1, starting transfers between devices: 3.23 us -> 6.68 us  [shards(): lax.all_to_all(jnp.broadcast_to(partial_sums[None], (space_count,) + part...]
    unnamed x17 -> x21, local copies, waits for them, and re-layouts: 7.02 us -> 5.46 us
  transfers between devices with their start and end apart: 26 -> 26, of which waited for: 7 -> 12; matrix products, arithmetic and copies ran while one was open for 30% -> 24% of each run, Pallas kernels for 0% -> 0%
where the time goes in v16:
time: 167 us; the launch traced here: 166 us
  starting transfers between devices  66.1 us (40%)
  waiting for transfers between devices  42.6 us (26%)
  local copies, waits for them, and re-layouts  22.3 us (13%)
  matrix products  20.3 us (12%)
  other arithmetic  10.4 us (6%)
  between operations  3.92 us (2%)
    ppermute x5, starting transfers between devices, with_halo(): before = lax.ppermute(last, axis, up)  21.5 us
    ppermute x3, waiting for transfers between devices, shards(): lax.ppermute(svc_sent, 'space', [(i, (i + k) % space_count) for i in rang...  18.5 us
    ppermute x5, waiting for transfers between devices, with_halo(): after = lax.ppermute(initial, axis, down)  17.7 us
    ppermute x5, starting transfers between devices, spatial(): lower = lax.ppermute(pick_blocks(field, upper_wants), 'space', up)  13.7 us
    gather x1, local copies, waits for them, and re-layouts, shards(): coef_rows = svc_all[shift * nodes_dev + obs_cell // T_DEV]  10.8 us
    all_to_all x1, starting transfers between devices, shards(): lax.all_to_all(jnp.broadcast_to(partial_sums[None], (space_count,) + part...  6.68 us
    ppermute x5, starting transfers between devices, with_halo(): after = lax.ppermute(initial, axis, down)  6.63 us
    dot_general x5, matrix products, spatial(): jnp.dot(upper.T, upper_t, preferred_element_type=jnp.float32)  6.47 us
  transfers between devices with their start and end apart: 26, of which 12 were waited for; matrix products, arithmetic and copies ran while one was open for 24% of the time, Pallas kernels for 0%

profile of v16, /device:TPU:0, one launch (start us, length us, event | category | flops | bytes accessed | tf_op | source)
XLA Modules:
  0.0 165.7 jit_solution(17134494071311199791)
XLA Ops:
  0.7 1.4 broadcast_in_dim.80
  2.0 4.3 %all-to-all-start = ((s32[4,1,4]{2,1,0:T(1,128)}), s32[4,1,4]{2,1,0:T(1,128)S(1)}, u32[]{:S(2)}, u32[]{:S(2)}) async-start(s32[4,1,4]{2,1,0:T(1,128)} %broadcast_in_dim.80), calls=%async_computation | async-start | bytes 4096 | tf_op jit(solution)/shard_map/all_to_all | solution.py:74
  6.3 0.7 broadcast_in_dim.76
  7.1 0.7 broadcast_in_dim.79
  8.0 1.2 copy.41
  9.2 1.1 select_reduce_fusion
  10.3 1.1 fusion.56
  11.4 0.7 fusion.91
  12.1 4.5 %collective-permute-start.2 = (bf16[1024,64]{0,1:T(8,128)(2,1)}, bf16[1024,64]{0,1:T(8,128)(2,1)}, u32[]{:S(2)}, u32[]{:S(2)}) collective-permute-start(bf16[1024,64]{0,1:T(8,128)(2,1)} %get-tuple-element.38), channel_id=1, source_target_pairs={{0,1},{1,2},{2,3},{3,4},{4,5},{5,6},{6,7},{8,9},{9,10},{10,11},{11... | collective-permute-start | bytes 393224 | tf_op jit(solution)/shard_map/ppermute | solution.py:27
  16.5 1.3 collective-permute-start.3
  17.8 1.8 %convert_element_type.89 = f32[8,128,128]{2,1,0:T(8,128)} convert(bf16[8,128,128]{2,1,0:T(8,128)(2,1)} %param.16) | non-fusion elementwise | flops 131072 | bytes 786432 | tf_op jit(solution)/shard_map/convert_element_type | solution.py:52
  19.7 0.6 fusion.92
  23.0 2.2 %collective-permute-start = (bf16[256,256]{0,1:T(8,128)(2,1)S(1)}, bf16[256,256]{0,1:T(8,128)(2,1)S(1)}, u32[]{:S(2)}, u32[]{:S(2)}) collective-permute-start(bf16[256,256]{0,1:T(8,128)(2,1)S(1)} %pad_maximum_fusion.10), channel_id=1, source_target_pairs={{0,8},{8,16},{16,24},{1,9},{9,17},{17,25},{2,10},{10,18},{18,26},{... | collective-permute-start | bytes 393224 | tf_op jit(solution)/shard_map/ppermute | solution.py:89
  25.3 3.1 %add_convert_fusion = bf16[8,12,128,128]{3,1,2,0:T(8,128)(2,1)S(1)} fusion(f32[8,128,128]{2,1,0:T(8,128)} %convert_element_type.89, f32[8,12]{1,0:T(8,128)S(1)} %fusion.82, bf16[8,8,128,128]{3,2,1,0:T(8,128)(2,1)S(1)} %copy-done, s32[8,8]{1,0:T(8,128)S(1)} %copy-done.8), kind=kOutput, calls=%fused_computation.2 | convolution fusion | flops 29885184 | bytes 5767808 | tf_op jit(solution)/shard_map/bkm,bkij->bimj/dot_general | solution.py:63
  28.5 0.7 collective-permute-start.6
  29.1 2.9 %collective-permute-start.5 = (bf16[1024,256]{1,0:T(8,128)(2,1)S(1)}, bf16[1024,256]{1,0:T(8,128)(2,1)S(1)}, u32[]{:S(2)}, u32[]{:S(2)}) collective-permute-start(bf16[1024,256]{1,0:T(8,128)(2,1)S(1)} %copy-done.3), channel_id=1, source_target_pairs={{0,16},{8,24},{16,0},{24,8},{1,17},{9,25},{17,1},{25,9},{2,18},{10... | collective-permute-start | bytes 1572872 | tf_op jit(solution)/shard_map/ppermute | solution.py:111
  32.1 1.6 copy.62
  33.8 2.0 %fusion.38 = f32[1024,256]{0,1:T(8,128)} fusion(bf16[1024,256]{0,1:T(8,128)(2,1)S(1)} %fusion.56, bf16[1024,1536]{1,0:T(8,128)(2,1)S(1)} %bitcast.53), kind=kOutput, calls=%fused_computation.67 | convolution fusion | flops 536870912 | bytes 3670016 | tf_op jit(solution)/shard_map/dot_general | solution.py:91
  35.8 3.9 %collective-permute-done.6 = bf16[1024,256]{1,0:T(8,128)(2,1)S(1)} collective-permute-done((bf16[1024,256]{1,0:T(8,128)(2,1)S(1)}, bf16[1024,256]{1,0:T(8,128)(2,1)S(1)}, u32[]{:S(2)}, u32[]{:S(2)}) %collective-permute-start.6) | collective-permute-done | bytes 524320 | tf_op jit(solution)/shard_map/ppermute | solution.py:111
  39.6 1.3 collective-permute-start.1
  40.9 14.7 %collective-permute-done.5 = bf16[1024,256]{1,0:T(8,128)(2,1)S(1)} collective-permute-done((bf16[1024,256]{1,0:T(8,128)(2,1)S(1)}, bf16[1024,256]{1,0:T(8,128)(2,1)S(1)}, u32[]{:S(2)}, u32[]{:S(2)}) %collective-permute-start.5) | collective-permute-done | bytes 524320 | tf_op jit(solution)/shard_map/ppermute | solution.py:111
  55.6 2.3 %maximum_convert_fusion = f32[4096,256]{1,0:T(8,128)} fusion(bf16[1024,256]{1,0:T(8,128)(2,1)S(1)} %collective-permute-done.6, bf16[1024,256]{1,0:T(8,128)(2,1)S(1)} %collective-permute-done.5, bf16[1024,256]{1,0:T(8,128)(2,1)S(1)} %collective-permute-done.4, bf16[1024,256]{1,0:T(8,128)(2,1)S(1)} %copy-done.3), kind=kLoop, calls=%fused_computation.13 | loop fusion | flops 8388608 | bytes 6291456 | tf_op jit(solution)/shard_map/convert_element_type | solution.py:114
  57.9 10.8 %gather_fusion = f32[2048,256]{1,0:T(8,128)} fusion(f32[4096,256]{1,0:T(8,128)} %maximum_convert_fusion, s32[2048]{0:T(1024)S(1)} %get-tuple-element.53), kind=kCustom, calls=%fused_computation | custom fusion | bytes 4202496 | tf_op jit(solution)/shard_map/gather | solution.py:117
  68.6 2.2 %multiply_reduce_fusion = f32[2048]{0:T(1024)S(1)} fusion(f32[2048,256]{1,0:T(8,128)} %gather_fusion, bf16[2048,256]{1,0:T(8,128)(2,1)} %param.20), kind=kLoop, calls=%fused_computation.15 | loop fusion | flops 1570816 | bytes 3153920 | tf_op jit(solution)/shard_map/reduce_sum | solution.py:118
  70.9 1.7 %fusion = f32[48,1024]{1,0:T(8,128)S(1)} fusion(s32[2048]{0:T(1024)S(1)} %get-tuple-element.54, bf16[2048,16]{0,1:T(8,128)(2,1)S(1)} %get-tuple-element.47, bf16[2048,16]{0,1:T(8,128)(2,1)S(1)} %get-tuple-element.48, bf16[2048,16]{0,1:T(8,128)(2,1)S(1)} %get-tuple-element.46), kind=kOutput, calls=%fused_computation.3 | convolution fusion | flops 204013568 | bytes 401408 | tf_op jit(solution)/shard_map/dot_general | solution.py:130
  72.7 0.6 add.198
  73.3 3.3 %all-to-all-start.1 = ((f32[4,4,1024]{2,1,0:T(4,128)}), f32[4,4,1024]{2,1,0:T(4,128)S(1)}, u32[]{:S(2)}, u32[]{:S(2)}) async-start(f32[4,4,1024]{2,1,0:T(4,128)} %add.198), calls=%async_computation.1 | async-start | bytes 131072 | tf_op jit(solution)/shard_map/all_to_all | solution.py:135
  76.6 2.7 %convolution_add_fusion.9 = f32[1024,256]{0,1:T(8,128)} fusion(f32[1024,256]{0,1:T(8,128)} %fusion.38, bf16[256,256]{0,1:T(8,128)(2,1)} %copy-done.4, bf16[1024,1536]{1,0:T(8,128)(2,1)} %bitcast.54), kind=kOutput, calls=%fused_computation.43 | convolution fusion | flops 134479872 | bytes 2752512 | tf_op jit(solution)/shard_map/dot_general | solution.py:92
  79.3 1.3 all-to-all-done.1
  81.1 2.7 %fusion.94 = (bf16[1024,256]{0,1:T(8,128)(2,1)S(1)}, f32[1024,256]{0,1:T(8,128)S(1)}) fusion(f32[1024,256]{0,1:T(8,128)S(1)} %get-tuple-element.45, f32[1024,256]{0,1:T(8,128)S(1)} %get-tuple-element.44, bf16[1024,64]{0,1:T(8,128)(2,1)} %collective-permute-done.3, bf16[1024,256]{0,1:T(8,128)(2,1)S(1)} %fusion.56, ...), kind=kOutput, calls=%fused_computation.193 | convolution fusion | flops 141557760 | bytes 6695936 | tf_op jit(solution)/shard_map/dot_general | solution.py:93
  84.0 0.7 fusion.36
  84.8 1.6 collective-permute-start.7
  86.4 1.3 collective-permute-start.8
  87.7 4.6 %collective-permute-start.9 = (bf16[1024,64]{0,1:T(8,128)(2,1)S(1)}, bf16[1024,64]{0,1:T(8,128)(2,1)S(1)}, u32[]{:S(2)}, u32[]{:S(2)}) collective-permute-start(bf16[1024,64]{0,1:T(8,128)(2,1)S(1)} %get-tuple-element.32), channel_id=1, source_target_pairs={{0,1},{1,2},{2,3},{3,4},{4,5},{5,6},{6,7},{8,9},{9,10},{10,11},{11... | collective-permute-start | bytes 393224 | tf_op jit(solution)/shard_map/ppermute | solution.py:27
  92.3 1.5 collective-permute-start.10
  94.1 1.3 collective-permute-done.9
  95.4 4.6 %collective-permute-done.10 = bf16[1024,64]{0,1:T(8,128)(2,1)S(1)} collective-permute-done((bf16[1024,64]{0,1:T(8,128)(2,1)S(1)}, bf16[1024,64]{0,1:T(8,128)(2,1)S(1)}, u32[]{:S(2)}, u32[]{:S(2)}) %collective-permute-start.10) | collective-permute-done | bytes 131104 | tf_op jit(solution)/shard_map/ppermute | solution.py:28
  100.0 0.8 fusion.95
  101.0 0.7 fusion.34
  101.8 2.3 %collective-permute-start.11 = (bf16[256,256]{0,1:T(8,128)(2,1)S(1)}, bf16[256,256]{0,1:T(8,128)(2,1)S(1)}, u32[]{:S(2)}, u32[]{:S(2)}) collective-permute-start(bf16[256,256]{0,1:T(8,128)(2,1)S(1)} %pad_maximum_fusion.14), channel_id=1, source_target_pairs={{0,8},{8,16},{16,24},{1,9},{9,17},{17,25},{2,10},{10,18},{18,26},{... | collective-permute-start | bytes 393224 | tf_op jit(solution)/shard_map/ppermute | solution.py:89
  104.1 1.3 collective-permute-start.12
  105.4 4.6 %collective-permute-start.13 = (bf16[1024,64]{0,1:T(8,128)(2,1)S(1)}, bf16[1024,64]{0,1:T(8,128)(2,1)S(1)}, u32[]{:S(2)}, u32[]{:S(2)}) collective-permute-start(bf16[1024,64]{0,1:T(8,128)(2,1)S(1)} %get-tuple-element.26), channel_id=1, source_target_pairs={{0,1},{1,2},{2,3},{3,4},{4,5},{5,6},{6,7},{8,9},{9,10},{10,11},{11... | collective-permute-start | bytes 393224 | tf_op jit(solution)/shard_map/ppermute | solution.py:27
  110.1 1.3 collective-permute-start.14
  111.7 0.8 collective-permute-done.13
  112.6 4.4 %collective-permute-done.14 = bf16[1024,64]{0,1:T(8,128)(2,1)S(1)} collective-permute-done((bf16[1024,64]{0,1:T(8,128)(2,1)S(1)}, bf16[1024,64]{0,1:T(8,128)(2,1)S(1)}, u32[]{:S(2)}, u32[]{:S(2)}) %collective-permute-start.14) | collective-permute-done | bytes 131104 | tf_op jit(solution)/shard_map/ppermute | solution.py:28
  116.9 0.8 fusion.96
  117.9 0.7 fusion.32
  118.7 3.4 %collective-permute-start.15 = (bf16[256,256]{0,1:T(8,128)(2,1)S(1)}, bf16[256,256]{0,1:T(8,128)(2,1)S(1)}, u32[]{:S(2)}, u32[]{:S(2)}) collective-permute-start(bf16[256,256]{0,1:T(8,128)(2,1)S(1)} %pad_maximum_fusion.16), channel_id=1, source_target_pairs={{0,8},{8,16},{16,24},{1,9},{9,17},{17,25},{2,10},{10,18},{18,26},{... | collective-permute-start | bytes 393224 | tf_op jit(solution)/shard_map/ppermute | solution.py:89
  122.1 1.3 collective-permute-start.16
  123.4 3.7 %collective-permute-start.17 = (bf16[1024,64]{0,1:T(8,128)(2,1)S(1)}, bf16[1024,64]{0,1:T(8,128)(2,1)S(1)}, u32[]{:S(2)}, u32[]{:S(2)}) collective-permute-start(bf16[1024,64]{0,1:T(8,128)(2,1)S(1)} %get-tuple-element.20), channel_id=1, source_target_pairs={{0,1},{1,2},{2,3},{3,4},{4,5},{5,6},{6,7},{8,9},{9,10},{10,11},{11... | collective-permute-start | bytes 393224 | tf_op jit(solution)/shard_map/ppermute | solution.py:27
  127.1 1.3 collective-permute-start.18
  128.8 0.8 collective-permute-done.17
  129.6 4.4 %collective-permute-done.18 = bf16[1024,64]{0,1:T(8,128)(2,1)S(1)} collective-permute-done((bf16[1024,64]{0,1:T(8,128)(2,1)S(1)}, bf16[1024,64]{0,1:T(8,128)(2,1)S(1)}, u32[]{:S(2)}, u32[]{:S(2)}) %collective-permute-start.18) | collective-permute-done | bytes 131104 | tf_op jit(solution)/shard_map/ppermute | solution.py:28
  134.0 1.8 %fusion.97 = (bf16[1024,256]{0,1:T(8,128)(2,1)S(1)}, f32[1024,256]{0,1:T(8,128)}) fusion(f32[1024,256]{0,1:T(8,128)S(1)} %get-tuple-element.68, f32[1024,256]{0,1:T(8,128)S(1)} %get-tuple-element.45, f32[1024,256]{0,1:T(8,128)S(1)} %fusion.3, bf16[1024,64]{0,1:T(8,128)(2,1)S(1)} %collective-permute-done.18, bf16[1024,256]{0,1:T(8,128)(2,1)S(1)} %get-tuple-element.67, ...), kind=kOutput, calls=%fused_computation.196 | convolution fusion | flops 140247040 | bytes 7735296 | tf_op jit(solution)/shard_map/dot_general | solution.py:93
  135.9 0.7 fusion.40
  136.6 4.2 %collective-permute-start.19 = (bf16[256,256]{0,1:T(8,128)(2,1)S(1)}, bf16[256,256]{0,1:T(8,128)(2,1)S(1)}, u32[]{:S(2)}, u32[]{:S(2)}) collective-permute-start(bf16[256,256]{0,1:T(8,128)(2,1)S(1)} %pad_maximum_fusion.18), channel_id=1, source_target_pairs={{0,8},{8,16},{16,24},{1,9},{9,17},{17,25},{2,10},{10,18},{18,26},{... | collective-permute-start | bytes 393224 | tf_op jit(solution)/shard_map/ppermute | solution.py:89
  140.9 1.3 collective-permute-start.20
  142.2 4.1 %collective-permute-start.21 = (bf16[1024,64]{0,1:T(8,128)(2,1)S(1)}, bf16[1024,64]{0,1:T(8,128)(2,1)S(1)}, u32[]{:S(2)}, u32[]{:S(2)}) collective-permute-start(bf16[1024,64]{0,1:T(8,128)(2,1)S(1)} %get-tuple-element.18), channel_id=1, source_target_pairs={{0,1},{1,2},{2,3},{3,4},{4,5},{5,6},{6,7},{8,9},{9,10},{10,11},{11... | collective-permute-start | bytes 393224 | tf_op jit(solution)/shard_map/ppermute | solution.py:27
  146.3 1.3 collective-permute-start.22
  148.0 0.8 collective-permute-done.21
  148.8 4.4 %collective-permute-done.22 = bf16[1024,64]{0,1:T(8,128)(2,1)S(1)} collective-permute-done((bf16[1024,64]{0,1:T(8,128)(2,1)S(1)}, bf16[1024,64]{0,1:T(8,128)(2,1)S(1)}, u32[]{:S(2)}, u32[]{:S(2)}) %collective-permute-start.22) | collective-permute-done | bytes 131104 | tf_op jit(solution)/shard_map/ppermute | solution.py:28
  154.6 6.7 %all-to-all-start.2 = ((f32[4,2,256]{2,1,0:T(2,128)}), f32[4,2,256]{2,1,0:T(2,128)S(1)}, u32[]{:S(2)}, u32[]{:S(2)}) async-start(f32[4,2,256]{2,1,0:T(2,128)} %broadcast_in_dim.87), calls=%async_computation.2 | async-start | bytes 16384 | tf_op jit(solution)/shard_map/all_to_all | solution.py:162
  161.3 2.5 %copy.48 = f32[1024,256]{1,0:T(8,128)} copy(f32[1024,256]{0,1:T(8,128)} %get-tuple-element.70) | data formatting | bytes 2097152
  163.8 1.3 all-to-all-done.2
  (78 shorter events, 5.2 us)
Async XLA Ops:
  0.6 24.6 %copy-start = (bf16[8,8,128,128]{3,2,1,0:T(8,128)(2,1)S(1)}, bf16[8,8,128,128]{3,2,1,0:T(8,128)(2,1)}, u32[]{:S(2)}) copy-start(bf16[8,8,128,128]{3,2,1,0:T(8,128)(2,1)} %param.17) | copy-start | bytes 6291460
  0.6 19.0 %copy-start.6 = (s32[2048,1]{0,1:T(1,128)S(1)}, s32[2048,1]{0,1:T(1,128)}, u32[]{:S(2)}) copy-start(s32[2048,1]{0,1:T(1,128)} %param.21) | copy-start | bytes 24580
  0.7 24.6 %copy-start.8 = (s32[8,8]{1,0:T(8,128)S(1)}, s32[8,8]{1,0:T(8,128)}, u32[]{:S(2)}) copy-start(s32[8,8]{1,0:T(8,128)} %param.18) | copy-start | bytes 772
  2.0 17.6 %all-to-all-start = ((s32[4,1,4]{2,1,0:T(1,128)}), s32[4,1,4]{2,1,0:T(1,128)S(1)}, u32[]{:S(2)}, u32[]{:S(2)}) async-start(s32[4,1,4]{2,1,0:T(1,128)} %broadcast_in_dim.80), calls=%async_computation | async-start | bytes 4096 | tf_op jit(solution)/shard_map/all_to_all | solution.py:74
  12.1 69.0 %collective-permute-start.2 = (bf16[1024,64]{0,1:T(8,128)(2,1)}, bf16[1024,64]{0,1:T(8,128)(2,1)}, u32[]{:S(2)}, u32[]{:S(2)}) collective-permute-start(bf16[1024,64]{0,1:T(8,128)(2,1)} %get-tuple-element.38), channel_id=1, source_target_pairs={{0,1},{1,2},{2,3},{3,4},{4,5},{5,6},{6,7},{8,9},{9,10},{10,11},{11... | collective-permute-start | bytes 393224 | tf_op jit(solution)/shard_map/ppermute | solution.py:27
  16.5 64.5 %collective-permute-start.3 = (bf16[1024,64]{0,1:T(8,128)(2,1)S(1)}, bf16[1024,64]{0,1:T(8,128)(2,1)}, u32[]{:S(2)}, u32[]{:S(2)}) collective-permute-start(bf16[1024,64]{0,1:T(8,128)(2,1)S(1)} %get-tuple-element.39), channel_id=1, source_target_pairs={{1,0},{2,1},{3,2},{4,3},{5,4},{6,5},{7,6},{9,8},{10,9},{11,10},{12... | collective-permute-start | bytes 393224 | tf_op jit(solution)/shard_map/ppermute | solution.py:28
  23.0 5.4 %copy-start.3 = (bf16[1024,256]{1,0:T(8,128)(2,1)S(1)}, bf16[1024,256]{1,0:T(8,128)(2,1)}, u32[]{:S(2)}) copy-start(bf16[1024,256]{1,0:T(8,128)(2,1)} %param.23) | copy-start | bytes 1572868
  23.0 9.1 %copy-start.7 = (s32[2048]{0:T(1024)S(1)}, s32[2048]{0:T(1024)}, u32[]{:S(2)}) copy-start(s32[2048]{0:T(1024)} %param.22) | copy-start | bytes 24580
  23.0 5.4 %collective-permute-start = (bf16[256,256]{0,1:T(8,128)(2,1)S(1)}, bf16[256,256]{0,1:T(8,128)(2,1)S(1)}, u32[]{:S(2)}, u32[]{:S(2)}) collective-permute-start(bf16[256,256]{0,1:T(8,128)(2,1)S(1)} %pad_maximum_fusion.10), channel_id=1, source_target_pairs={{0,8},{8,16},{16,24},{1,9},{9,17},{17,25},{2,10},{10,18},{18,26},{... | collective-permute-start | bytes 393224 | tf_op jit(solution)/shard_map/ppermute | solution.py:89
  28.5 5.3 %copy-start.4 = (bf16[256,256]{0,1:T(8,128)(2,1)}, bf16[256,256]{0,1:T(8,128)(2,1)S(1)}, u32[]{:S(2)}) copy-start(bf16[256,256]{0,1:T(8,128)(2,1)S(1)} %collective-permute-done) | copy-start | bytes 393220
  28.5 11.2 %collective-permute-start.6 = (bf16[1024,256]{1,0:T(8,128)(2,1)S(1)}, bf16[1024,256]{1,0:T(8,128)(2,1)S(1)}, u32[]{:S(2)}, u32[]{:S(2)}) collective-permute-start(bf16[1024,256]{1,0:T(8,128)(2,1)S(1)} %copy-done.3), channel_id=1, source_target_pairs={{0,24},{8,0},{16,8},{24,16},{1,25},{9,1},{17,9},{25,17},{2,26},{10... | collective-permute-start | bytes 1572872 | tf_op jit(solution)/shard_map/ppermute | solution.py:111
  29.1 26.4 %collective-permute-start.5 = (bf16[1024,256]{1,0:T(8,128)(2,1)S(1)}, bf16[1024,256]{1,0:T(8,128)(2,1)S(1)}, u32[]{:S(2)}, u32[]{:S(2)}) collective-permute-start(bf16[1024,256]{1,0:T(8,128)(2,1)S(1)} %copy-done.3), channel_id=1, source_target_pairs={{0,16},{8,24},{16,0},{24,8},{1,17},{9,25},{17,1},{25,9},{2,18},{10... | collective-permute-start | bytes 1572872 | tf_op jit(solution)/shard_map/ppermute | solution.py:111
  32.1 23.5 %collective-permute-start.4 = (bf16[1024,256]{1,0:T(8,128)(2,1)S(1)}, bf16[1024,256]{1,0:T(8,128)(2,1)S(1)}, u32[]{:S(2)}, u32[]{:S(2)}) collective-permute-start(bf16[1024,256]{1,0:T(8,128)(2,1)S(1)} %copy-done.3), channel_id=1, source_target_pairs={{0,8},{8,16},{16,24},{24,0},{1,9},{9,17},{17,25},{25,1},{2,10},{10... | collective-permute-start | bytes 1572872 | tf_op jit(solution)/shard_map/ppermute | solution.py:111
  33.7 24.1 %copy-start.1 = (bf16[128,8,12,128]{3,1,2,0:T(8,128)(2,1)}, bf16[128,8,12,128]{3,1,2,0:T(8,128)(2,1)S(1)}, u32[]{:S(2)}) copy-start(bf16[128,8,12,128]{3,1,2,0:T(8,128)(2,1)S(1)} %copy.62) | copy-start | bytes 9437188
  39.6 41.5 %collective-permute-start.1 = (bf16[256,256]{0,1:T(8,128)(2,1)S(1)}, bf16[256,256]{0,1:T(8,128)(2,1)}, u32[]{:S(2)}, u32[]{:S(2)}) collective-permute-start(bf16[256,256]{0,1:T(8,128)(2,1)S(1)} %pad_maximum_fusion.11), channel_id=1, source_target_pairs={{8,0},{16,8},{24,16},{9,1},{17,9},{25,17},{10,2},{18,10},{26,18},{... | collective-permute-start | bytes 393224 | tf_op jit(solution)/shard_map/ppermute | solution.py:90
  70.9 9.8 %copy-start.5 = (f32[1024]{0:T(1024)S(1)}, f32[1024]{0:T(1024)}, u32[]{:S(2)}) copy-start(f32[1024]{0:T(1024)} %param.13) | copy-start | bytes 12292
  73.3 7.4 %all-to-all-start.1 = ((f32[4,4,1024]{2,1,0:T(4,128)}), f32[4,4,1024]{2,1,0:T(4,128)S(1)}, u32[]{:S(2)}, u32[]{:S(2)}) async-start(f32[4,4,1024]{2,1,0:T(4,128)} %add.198), calls=%async_computation.1 | async-start | bytes 131072 | tf_op jit(solution)/shard_map/all_to_all | solution.py:135
  81.1 2.9 %copy-start.2 = (bf16[128,8,12,128]{3,1,2,0:T(8,128)(2,1)S(1)}, bf16[128,8,12,128]{3,1,2,0:T(8,128)(2,1)}, u32[]{:S(2)}) copy-start(bf16[128,8,12,128]{3,1,2,0:T(8,128)(2,1)} %copy-done.1) | copy-start | bytes 9437188
  84.8 9.0 %collective-permute-start.7 = (bf16[256,256]{0,1:T(8,128)(2,1)S(1)}, bf16[256,256]{0,1:T(8,128)(2,1)S(1)}, u32[]{:S(2)}, u32[]{:S(2)}) collective-permute-start(bf16[256,256]{0,1:T(8,128)(2,1)S(1)} %pad_maximum_fusion.12), channel_id=1, source_target_pairs={{0,8},{8,16},{16,24},{1,9},{9,17},{17,25},{2,10},{10,18},{18,26},{... | collective-permute-start | bytes 393224 | tf_op jit(solution)/shard_map/ppermute | solution.py:89
  86.4 7.7 %collective-permute-start.8 = (bf16[256,256]{0,1:T(8,128)(2,1)S(1)}, bf16[256,256]{0,1:T(8,128)(2,1)S(1)}, u32[]{:S(2)}, u32[]{:S(2)}) collective-permute-start(bf16[256,256]{0,1:T(8,128)(2,1)S(1)} %pad_maximum_fusion.13), channel_id=1, source_target_pairs={{8,0},{16,8},{24,16},{9,1},{17,9},{25,17},{10,2},{18,10},{26,18},{... | collective-permute-start | bytes 393224 | tf_op jit(solution)/shard_map/ppermute | solution.py:90
  87.7 7.7 %collective-permute-start.9 = (bf16[1024,64]{0,1:T(8,128)(2,1)S(1)}, bf16[1024,64]{0,1:T(8,128)(2,1)S(1)}, u32[]{:S(2)}, u32[]{:S(2)}) collective-permute-start(bf16[1024,64]{0,1:T(8,128)(2,1)S(1)} %get-tuple-element.32), channel_id=1, source_target_pairs={{0,1},{1,2},{2,3},{3,4},{4,5},{5,6},{6,7},{8,9},{9,10},{10,11},{11... | collective-permute-start | bytes 393224 | tf_op jit(solution)/shard_map/ppermute | solution.py:27
  92.3 7.7 %collective-permute-start.10 = (bf16[1024,64]{0,1:T(8,128)(2,1)S(1)}, bf16[1024,64]{0,1:T(8,128)(2,1)S(1)}, u32[]{:S(2)}, u32[]{:S(2)}) collective-permute-start(bf16[1024,64]{0,1:T(8,128)(2,1)S(1)} %get-tuple-element.33), channel_id=1, source_target_pairs={{1,0},{2,1},{3,2},{4,3},{5,4},{6,5},{7,6},{9,8},{10,9},{11,10},{12... | collective-permute-start | bytes 393224 | tf_op jit(solution)/shard_map/ppermute | solution.py:28
  101.8 9.6 %collective-permute-start.11 = (bf16[256,256]{0,1:T(8,128)(2,1)S(1)}, bf16[256,256]{0,1:T(8,128)(2,1)S(1)}, u32[]{:S(2)}, u32[]{:S(2)}) collective-permute-start(bf16[256,256]{0,1:T(8,128)(2,1)S(1)} %pad_maximum_fusion.14), channel_id=1, source_target_pairs={{0,8},{8,16},{16,24},{1,9},{9,17},{17,25},{2,10},{10,18},{18,26},{... | collective-permute-start | bytes 393224 | tf_op jit(solution)/shard_map/ppermute | solution.py:89
  104.1 7.6 %collective-permute-start.12 = (bf16[256,256]{0,1:T(8,128)(2,1)S(1)}, bf16[256,256]{0,1:T(8,128)(2,1)S(1)}, u32[]{:S(2)}, u32[]{:S(2)}) collective-permute-start(bf16[256,256]{0,1:T(8,128)(2,1)S(1)} %pad_maximum_fusion.15), channel_id=1, source_target_pairs={{8,0},{16,8},{24,16},{9,1},{17,9},{25,17},{10,2},{18,10},{26,18},{... | collective-permute-start | bytes 393224 | tf_op jit(solution)/shard_map/ppermute | solution.py:90
  105.4 7.1 %collective-permute-start.13 = (bf16[1024,64]{0,1:T(8,128)(2,1)S(1)}, bf16[1024,64]{0,1:T(8,128)(2,1)S(1)}, u32[]{:S(2)}, u32[]{:S(2)}) collective-permute-start(bf16[1024,64]{0,1:T(8,128)(2,1)S(1)} %get-tuple-element.26), channel_id=1, source_target_pairs={{0,1},{1,2},{2,3},{3,4},{4,5},{5,6},{6,7},{8,9},{9,10},{10,11},{11... | collective-permute-start | bytes 393224 | tf_op jit(solution)/shard_map/ppermute | solution.py:27
  110.1 6.9 %collective-permute-start.14 = (bf16[1024,64]{0,1:T(8,128)(2,1)S(1)}, bf16[1024,64]{0,1:T(8,128)(2,1)S(1)}, u32[]{:S(2)}, u32[]{:S(2)}) collective-permute-start(bf16[1024,64]{0,1:T(8,128)(2,1)S(1)} %get-tuple-element.27), channel_id=1, source_target_pairs={{1,0},{2,1},{3,2},{4,3},{5,4},{6,5},{7,6},{9,8},{10,9},{11,10},{12... | collective-permute-start | bytes 393224 | tf_op jit(solution)/shard_map/ppermute | solution.py:28
  118.7 9.7 %collective-permute-start.15 = (bf16[256,256]{0,1:T(8,128)(2,1)S(1)}, bf16[256,256]{0,1:T(8,128)(2,1)S(1)}, u32[]{:S(2)}, u32[]{:S(2)}) collective-permute-start(bf16[256,256]{0,1:T(8,128)(2,1)S(1)} %pad_maximum_fusion.16), channel_id=1, source_target_pairs={{0,8},{8,16},{16,24},{1,9},{9,17},{17,25},{2,10},{10,18},{18,26},{... | collective-permute-start | bytes 393224 | tf_op jit(solution)/shard_map/ppermute | solution.py:89
  122.1 6.7 %collective-permute-start.16 = (bf16[256,256]{0,1:T(8,128)(2,1)S(1)}, bf16[256,256]{0,1:T(8,128)(2,1)S(1)}, u32[]{:S(2)}, u32[]{:S(2)}) collective-permute-start(bf16[256,256]{0,1:T(8,128)(2,1)S(1)} %pad_maximum_fusion.17), channel_id=1, source_target_pairs={{8,0},{16,8},{24,16},{9,1},{17,9},{25,17},{10,2},{18,10},{26,18},{... | collective-permute-start | bytes 393224 | tf_op jit(solution)/shard_map/ppermute | solution.py:90
  123.4 6.2 %collective-permute-start.17 = (bf16[1024,64]{0,1:T(8,128)(2,1)S(1)}, bf16[1024,64]{0,1:T(8,128)(2,1)S(1)}, u32[]{:S(2)}, u32[]{:S(2)}) collective-permute-start(bf16[1024,64]{0,1:T(8,128)(2,1)S(1)} %get-tuple-element.20), channel_id=1, source_target_pairs={{0,1},{1,2},{2,3},{3,4},{4,5},{5,6},{6,7},{8,9},{9,10},{10,11},{11... | collective-permute-start | bytes 393224 | tf_op jit(solution)/shard_map/ppermute | solution.py:27
  127.1 6.9 %collective-permute-start.18 = (bf16[1024,64]{0,1:T(8,128)(2,1)S(1)}, bf16[1024,64]{0,1:T(8,128)(2,1)S(1)}, u32[]{:S(2)}, u32[]{:S(2)}) collective-permute-start(bf16[1024,64]{0,1:T(8,128)(2,1)S(1)} %get-tuple-element.21), channel_id=1, source_target_pairs={{1,0},{2,1},{3,2},{4,3},{5,4},{6,5},{7,6},{9,8},{10,9},{11,10},{12... | collective-permute-start | bytes 393224 | tf_op jit(solution)/shard_map/ppermute | solution.py:28
  136.6 11.0 %collective-permute-start.19 = (bf16[256,256]{0,1:T(8,128)(2,1)S(1)}, bf16[256,256]{0,1:T(8,128)(2,1)S(1)}, u32[]{:S(2)}, u32[]{:S(2)}) collective-permute-start(bf16[256,256]{0,1:T(8,128)(2,1)S(1)} %pad_maximum_fusion.18), channel_id=1, source_target_pairs={{0,8},{8,16},{16,24},{1,9},{9,17},{17,25},{2,10},{10,18},{18,26},{... | collective-permute-start | bytes 393224 | tf_op jit(solution)/shard_map/ppermute | solution.py:89
  140.9 12.7 %collective-permute-start.20 = (bf16[256,256]{0,1:T(8,128)(2,1)S(1)}, bf16[256,256]{0,1:T(8,128)(2,1)S(1)}, u32[]{:S(2)}, u32[]{:S(2)}) collective-permute-start(bf16[256,256]{0,1:T(8,128)(2,1)S(1)} %pad_maximum_fusion.19), channel_id=1, source_target_pairs={{8,0},{16,8},{24,16},{9,1},{17,9},{25,17},{10,2},{18,10},{26,18},{... | collective-permute-start | bytes 393224 | tf_op jit(solution)/shard_map/ppermute | solution.py:90
  142.2 6.6 %collective-permute-start.21 = (bf16[1024,64]{0,1:T(8,128)(2,1)S(1)}, bf16[1024,64]{0,1:T(8,128)(2,1)S(1)}, u32[]{:S(2)}, u32[]{:S(2)}) collective-permute-start(bf16[1024,64]{0,1:T(8,128)(2,1)S(1)} %get-tuple-element.18), channel_id=1, source_target_pairs={{0,1},{1,2},{2,3},{3,4},{4,5},{5,6},{6,7},{8,9},{9,10},{10,11},{11... | collective-permute-start | bytes 393224 | tf_op jit(solution)/shard_map/ppermute | solution.py:27
  146.3 6.9 %collective-permute-start.22 = (bf16[1024,64]{0,1:T(8,128)(2,1)S(1)}, bf16[1024,64]{0,1:T(8,128)(2,1)S(1)}, u32[]{:S(2)}, u32[]{:S(2)}) collective-permute-start(bf16[1024,64]{0,1:T(8,128)(2,1)S(1)} %get-tuple-element.19), channel_id=1, source_target_pairs={{1,0},{2,1},{3,2},{4,3},{5,4},{6,5},{7,6},{9,8},{10,9},{11,10},{12... | collective-permute-start | bytes 393224 | tf_op jit(solution)/shard_map/ppermute | solution.py:28
  154.6 10.5 %all-to-all-start.2 = ((f32[4,2,256]{2,1,0:T(2,128)}), f32[4,2,256]{2,1,0:T(2,128)S(1)}, u32[]{:S(2)}, u32[]{:S(2)}) async-start(f32[4,2,256]{2,1,0:T(2,128)} %broadcast_in_dim.87), calls=%async_computation.2 | async-start | bytes 16384 | tf_op jit(solution)/shard_map/all_to_all | solution.py:162
